TPU v7x, 256 devices: a whole 4x4x8 slice. The times are simulated.
256 devices in a mesh: space: 16 (over z_lo, y), view: 16 (over x, z_hi, core).
Axes of the slice: x: 4, y: 4, z: 8 (z_hi: 2, z_lo: 4; z = z_hi * 4 + z_lo), core: 2. Of those that a mesh axis runs over, the one named last changes fastest.
Arguments:
- estimate: float32 [16, 64, 4096], P('space', None, 'view'), may hold values from 0.5 to 2
- measured: float32 [16, 16, 64, 4096], P('view', 'space'), may hold values from 0.2 to 5
- kernel_x: float32 [16, 7], P('view'), may hold values from 0.2 to 1
- kernel_y: float32 [16, 7], P('view'), may hold values from 0.2 to 1
- kernel_z: float32 [16, 15], P('view'), may hold values from 0.2 to 1
- neighbors: int32 [16, 6], P('space'), may hold values from -1 to 15, as said below
- inside: int32 [16], P('space'), may hold values 0 or 1
Outputs:
- deconvolved: float32 [16, 64, 4096], P('space', None, 'view')
Inputs may be any that keep to these rules, and one draw needn't show every extreme that they name: neighbors[b, f] is the brick across face f of brick b (faces in order: low and high along the first, second and third cell dimension), or -1 at the window's border; if neighbors[b, f] = c then neighbors[c, f + 1 - 2 (f % 2)] = b; the window is a box of 2 x 2 x (4) bricks, and the 1 bricks of one index of space lie in a row along the third dimension.
All inputs are finite; a program needn't handle non-finite values. No bound on the sum of `inside` on one device may be relied on, other than what follows from the above.
Results may differ from a plain program's by a relative error of at most 0.0001.
Values sent between devices are 32-bit elements; how exact they have to be, the bound alone decides.
No kernel may reach another device: no remote copies, remote signals or barrier semaphores. Data moves between devices by JAX's collectives and lax.ppermute only.
A program may use at most 128 MiB of HBM per device.

v0:
```python
import jax
import jax.numpy as jnp
from jax import lax
from jax.sharding import PartitionSpec as P

ITERS = 2


def normalized(kernel):
    return kernel / jnp.sum(kernel)


def edge_planes(volume, axis_dim, radius):
    length = volume.shape[axis_dim]
    first_part = lax.slice_in_dim(volume, 0, radius, axis=axis_dim)
    last_part = lax.slice_in_dim(volume, length - radius, length, axis=axis_dim)
    stacked = jnp.stack([first_part, last_part], axis=1)
    return jnp.moveaxis(stacked, axis_dim + 1, 2)


def pick_faces(neighbors, axis_dim):
    low_ids = neighbors[:, 2 * axis_dim - 2]
    high_ids = neighbors[:, 2 * axis_dim - 1]

    def fold_faces(running, incoming, first_row):
        count_rows = incoming.shape[0]
        brick_ids = jnp.arange(count_rows, dtype=jnp.int32)
        low_pick = (low_ids[:, None] == brick_ids[None, :]).astype(jnp.float32)
        high_pick = (high_ids[:, None] == brick_ids[None, :]).astype(jnp.float32)
        low_part = jnp.einsum(
            "br,rpac->bpac", low_pick, incoming[:, 1], precision=lax.Precision.HIGHEST
        )
        high_part = jnp.einsum(
            "br,rpac->bpac", high_pick, incoming[:, 0], precision=lax.Precision.HIGHEST
        )
        return jnp.stack([low_part, high_part], axis=1)

    return fold_faces


def with_halo(volume, neighbors, axis_dim, radius, source):
    edge_slabs = edge_planes(volume, axis_dim, radius)
    zeros_halo = jnp.zeros_like(edge_slabs)
    fold_faces = pick_faces(neighbors, axis_dim)
    if source == "estimate":
        halo_faces = fold_faces(
            zeros_halo, lax.all_gather(edge_slabs, "space", axis=0, tiled=True), jnp.int32(0)
        )
    elif source == "blurred":
        halo_faces = fold_faces(
            zeros_halo, lax.all_gather(edge_slabs, "space", axis=0, tiled=True), jnp.int32(0)
        )
    elif source == "blurred_z":
        halo_faces = fold_faces(
            zeros_halo, lax.all_gather(edge_slabs, "space", axis=0, tiled=True), jnp.int32(0)
        )
    elif source == "ratio_z":
        halo_faces = fold_faces(
            zeros_halo, lax.all_gather(edge_slabs, "space", axis=0, tiled=True), jnp.int32(0)
        )
    else:
        halo_faces = fold_faces(
            zeros_halo, lax.all_gather(edge_slabs, "space", axis=0, tiled=True), jnp.int32(0)
        )
    halo_faces = jnp.moveaxis(halo_faces, 2, axis_dim + 1)
    return jnp.concatenate([halo_faces[:, 0], volume, halo_faces[:, 1]], axis=axis_dim)


def convolve(extended, kernel, axis_dim, flipped):
    radius = (kernel.shape[0] - 1) // 2
    length = extended.shape[axis_dim] - 2 * radius
    out_shape = list(extended.shape)
    out_shape[axis_dim] = length
    summed = jnp.zeros(tuple(out_shape), jnp.float32)
    for position in range(2 * radius + 1):
        weight = kernel[2 * radius - position] if flipped else kernel[position]
        summed = summed + weight * lax.slice_in_dim(
            extended, position, position + length, axis=axis_dim
        )
    return summed


def shards(estimate, measured, kernel_x, kernel_y, kernel_z, neighbors, inside):
    brick_side = estimate.shape[1]
    share_cells = estimate.reshape(
        estimate.shape[0], brick_side, estimate.shape[2] // brick_side, brick_side
    )
    recorded_all = measured.reshape(
        measured.shape[0], measured.shape[1], brick_side, brick_side, brick_side
    )
    share_rows = share_cells.shape[2]
    row_start = lax.axis_index("view") * share_rows
    view_count = recorded_all.shape[0] * lax.axis_size("view")
    radius_x = (kernel_x.shape[1] - 1) // 2
    radius_y = (kernel_y.shape[1] - 1) // 2
    radius_z = (kernel_z.shape[1] - 1) // 2
    keep_mask = (inside > 0)[:, None, None, None]
    share_now = share_cells
    full_now = None
    for sweep_no in range(ITERS):
        if full_now is None:
            full_now = lax.all_gather(share_now, "view", axis=2, tiled=True)
            extended = with_halo(full_now, neighbors, 1, radius_x, "estimate")
        else:
            extended = with_halo(full_now, neighbors, 1, radius_x, "estimate")
        along_x = normalized(kernel_x[0])
        along_y = normalized(kernel_y[0])
        along_z = normalized(kernel_z[0])
        blurred = convolve(extended, along_x, 1, False)
        blurred = convolve(with_halo(blurred, neighbors, 2, radius_y, "blurred"), along_y, 2, False)
        blurred = convolve(
            with_halo(blurred, neighbors, 3, radius_z, "blurred_z"), along_z, 3, False
        )
        quotient = recorded_all[0] / blurred
        spread = convolve(with_halo(quotient, neighbors, 3, radius_z, "ratio_z"), along_z, 3, True)
        spread = convolve(with_halo(spread, neighbors, 2, radius_y, "ratio"), along_y, 2, True)
        spread = convolve(with_halo(spread, neighbors, 1, radius_x, "ratio"), along_x, 1, True)
        final_sweep = sweep_no == ITERS - 1
        if not final_sweep:
            summed = lax.psum(spread, "view")
            full_now = full_now * jnp.where(keep_mask, summed / view_count, 1.0)
        else:
            summed = lax.psum_scatter(spread, "view", scatter_dimension=2, tiled=True)
            own_rows = lax.dynamic_slice_in_dim(full_now, row_start, share_rows, 2)
            share_now = own_rows * jnp.where(keep_mask, summed / view_count, 1.0)
            full_now = None
    return share_now.reshape(share_now.shape[0], brick_side, share_rows * brick_side)


def solution(mesh):
    placed = (
        P("space", None, "view"),
        P("view", "space", None, None),
        P("view", None),
        P("view", None),
        P("view", None),
        P("space", None),
        P("space"),
    )
    return jax.shard_map(
        shards, mesh=mesh, in_specs=placed, out_specs=P("space", None, "view"), check_vma=False
    )
```

profile of v0, /device:TPU:8, one launch (start us, length us, event | category | flops | bytes accessed | tf_op | source)
XLA Modules:
  0.0 1770.8 jit_solution(11116695997213249861)
XLA Ops:
  8.3 67.6 %all-gather.14.cloned.1.call-done = f32[1,64,64,64]{3,1,0,2:T(8,128)} async-done(((f32[1,64,4,64]{3,1,0,2:T(8,128)}), f32[1,64,64,64]{3,1,0,2:T(8,128)}) %all-gather.14.cloned.1.call-update) | async-done | bytes 1048592 | tf_op jit(solution)/shard_map/all_gather | solution.py:102
  81.3 2.8 copy.54
  84.2 75.9 %all-gather.16.cloned.1.call-done = f32[16,2,3,64,64]{4,3,2,1,0:T(8,128)} async-done(((f32[1,2,3,64,64]{4,3,2,1,0:T(8,128)}), f32[16,2,3,64,64]{4,3,2,1,0:T(8,128)}) %all-gather.16.cloned.1.call-update) | async-done | bytes 1572880 | tf_op jit(solution)/shard_map/all_gather | solution.py:47
  166.4 6.3 fusion.61
  177.2 82.1 %all-gather.18.cloned.1.call-done = f32[16,2,3,64,64]{4,3,2,1,0:T(8,128)} async-done(((f32[1,2,3,64,64]{4,3,2,1,0:T(8,128)}), f32[16,2,3,64,64]{4,3,2,1,0:T(8,128)}) %all-gather.18.cloned.1.call-update) | async-done | bytes 1572880 | tf_op jit(solution)/shard_map/all_gather | solution.py:51
  261.4 2.2 fusion.300
  266.0 6.6 fusion.117
  272.7 2.7 slice_bitcast_fusion.23
  275.4 2.3 copy.47
  277.7 3.1 copy.48
  287.2 88.8 %all-gather.20.cloned.1.call-done = f32[16,2,7,64,64]{4,3,2,1,0:T(8,128)} async-done(((f32[1,2,7,64,64]{4,3,2,1,0:T(8,128)}), f32[16,2,7,64,64]{4,3,2,1,0:T(8,128)}) %all-gather.20.cloned.1.call-update) | async-done | bytes 3670032 | tf_op jit(solution)/shard_map/all_gather | solution.py:55
  376.0 4.5 slice_bitcast_fusion.7
  380.5 4.0 fusion.14
  384.6 4.0 fusion.12
  388.6 3.5 copy.49
  392.1 2.9 slice_bitcast_fusion.21
  395.0 24.2 %fusion.239 = f32[1,64,64,64]{3,2,1,0:T(8,128)S(1)} fusion(f32[1,64,64,64]{3,2,1,0:T(8,128)S(1)} %copy-done.4, f32[1,64,64,7]{3,2,1,0:T(8,128)S(1)} %get-tuple-element.20, f32[1,64,64,64]{3,2,1,0:T(8,128)S(1)} %fusion.117, f32[1,64,64,7]{3,2,1,0:T(8,128)S(1)} %get-tuple-element.19, f32[]{:T(128)} %bitcast.96, f32[]{:T(128)} %bitcast.95, f32[]{:T(128)} %bitcast.94, ...), kind=kLoop, calls=%fused_computation.402 | loop fusion | flops 11534336 | bytes 3375164 | tf_op jit(solution)/shard_map/div | solution.py:114
  419.2 2.2 slice_bitcast_fusion.19
  421.5 2.3 copy.50
  425.6 93.2 %all-gather.22.cloned.1.call-done = f32[16,2,7,64,64]{4,3,2,1,0:T(8,128)} async-done(((f32[1,2,7,64,64]{4,3,2,1,0:T(8,128)}), f32[16,2,7,64,64]{4,3,2,1,0:T(8,128)}) %all-gather.22.cloned.1.call-update) | async-done | bytes 3670032 | tf_op jit(solution)/shard_map/all_gather | solution.py:59
  518.8 4.5 slice_bitcast_fusion.5
  523.4 4.0 fusion.10
  527.4 4.0 fusion.8
  531.5 3.0 copy.52
  534.5 5.0 slice_bitcast_fusion.17
  539.5 36.4 %fusion.206 = f32[1,64,64,64]{3,2,1,0:T(8,128)} fusion(f32[1,64,64,7]{3,2,1,0:T(8,128)} %get-tuple-element.18, f32[1,64,64,64]{3,2,1,0:T(8,128)S(1)} %copy-done.3, f32[1,64,64,7]{3,2,1,0:T(8,128)} %get-tuple-element.17, f32[]{:T(128)} %bitcast.96, f32[]{:T(128)} %bitcast.95, f32[]{:T(128)} %bitcast.94, f32[]{:T(128)} %bitcast.93, f32[]{:T(128)} %bitcast.92, ...), kind=kLoop, calls=%fused_computation.343 | loop fusion | flops 11272192 | bytes 2326588 | tf_op jit(solution)/shard_map/add | solution.py:77
  577.8 84.3 %all-gather.24.cloned.1.call-done = f32[16,2,3,64,64]{4,3,2,1,0:T(8,128)} async-done(((f32[1,2,3,64,64]{4,3,2,1,0:T(8,128)}), f32[16,2,3,64,64]{4,3,2,1,0:T(8,128)}) %all-gather.24.cloned.1.call-update) | async-done | bytes 1572880 | tf_op jit(solution)/shard_map/all_gather | solution.py:63
  664.2 2.2 fusion.296
  668.8 7.1 fusion.103
  676.7 84.3 %all-gather.26.cloned.1.call-done = f32[16,2,3,64,64]{4,3,2,1,0:T(8,128)} async-done(((f32[1,2,3,64,64]{4,3,2,1,0:T(8,128)}), f32[16,2,3,64,64]{4,3,2,1,0:T(8,128)}) %all-gather.26.cloned.1.call-update) | async-done | bytes 1572880 | tf_op jit(solution)/shard_map/all_gather | solution.py:63
  767.3 7.5 fusion.47
  775.6 199.1 %all-reduce.2.cloned.1.call-done = f32[1,64,64,64]{3,2,1,0:T(8,128)} async-done(((f32[1,64,64,64]{3,2,1,0:T(8,128)}), f32[1,64,64,64]{3,2,1,0:T(8,128)}) %all-reduce.2.cloned.1.call-update) | async-done | bytes 1048592 | tf_op jit(solution)/shard_map/psum | solution.py:120
  974.7 3.5 select_multiply_fusion
  979.2 82.8 %all-gather.28.cloned.1.call-done = f32[16,2,3,64,64]{4,3,2,1,0:T(8,128)} async-done(((f32[1,2,3,64,64]{4,3,2,1,0:T(8,128)}), f32[16,2,3,64,64]{4,3,2,1,0:T(8,128)}) %all-gather.28.cloned.1.call-update) | async-done | bytes 1572880 | tf_op jit(solution)/shard_map/all_gather | solution.py:47
  1068.3 6.3 fusion.33
  1077.0 84.1 %all-gather.30.cloned.1.call-done = f32[16,2,3,64,64]{4,3,2,1,0:T(8,128)} async-done(((f32[1,2,3,64,64]{4,3,2,1,0:T(8,128)}), f32[16,2,3,64,64]{4,3,2,1,0:T(8,128)}) %all-gather.30.cloned.1.call-update) | async-done | bytes 1572880 | tf_op jit(solution)/shard_map/all_gather | solution.py:51
  1163.3 2.2 fusion.284
  1167.9 6.6 fusion.89
  1174.6 2.2 slice_bitcast_fusion.15
  1176.8 2.3 copy.56
  1181.0 93.1 %all-gather.32.cloned.1.call-done = f32[16,2,7,64,64]{4,3,2,1,0:T(8,128)} async-done(((f32[1,2,7,64,64]{4,3,2,1,0:T(8,128)}), f32[16,2,7,64,64]{4,3,2,1,0:T(8,128)}) %all-gather.32.cloned.1.call-update) | async-done | bytes 3670032 | tf_op jit(solution)/shard_map/all_gather | solution.py:55
  1274.1 4.5 slice_bitcast_fusion.3
  1278.7 4.0 fusion.6
  1282.7 4.0 fusion.4
  1286.8 3.0 copy.58
  1289.8 2.9 slice_bitcast_fusion.13
  1293.3 24.2 %fusion.166 = f32[1,64,64,64]{3,2,1,0:T(8,128)S(1)} fusion(f32[1,64,64,64]{3,2,1,0:T(8,128)S(1)} %copy-done.5, f32[1,64,64,7]{3,2,1,0:T(8,128)S(1)} %get-tuple-element.16, f32[1,64,64,64]{3,2,1,0:T(8,128)S(1)} %copy-done.1, f32[1,64,64,7]{3,2,1,0:T(8,128)S(1)} %get-tuple-element.15, f32[]{:T(128)} %bitcast.96, f32[]{:T(128)} %bitcast.95, f32[]{:T(128)} %bitcast.94, ...), kind=kLoop, calls=%fused_computation.269 | loop fusion | flops 11534336 | bytes 3375164 | tf_op jit(solution)/shard_map/div | solution.py:114
  1317.5 2.7 slice_bitcast_fusion.11
  1320.3 2.3 copy.59
  1322.6 2.3 copy.60
  1326.3 92.9 %all-gather.34.cloned.1.call-done = f32[16,2,7,64,64]{4,3,2,1,0:T(8,128)} async-done(((f32[1,2,7,64,64]{4,3,2,1,0:T(8,128)}), f32[16,2,7,64,64]{4,3,2,1,0:T(8,128)}) %all-gather.34.cloned.1.call-update) | async-done | bytes 3670032 | tf_op jit(solution)/shard_map/all_gather | solution.py:59
  1419.2 4.5 slice_bitcast_fusion.1
  1423.7 4.0 fusion.2
  1427.8 4.0 fusion
  1431.8 3.0 copy.61
  1434.9 4.8 slice_bitcast_fusion.9
  1439.7 36.2 %fusion.133 = f32[1,64,64,64]{3,2,1,0:T(8,128)} fusion(f32[1,64,64,7]{3,2,1,0:T(8,128)} %get-tuple-element.14, f32[1,64,64,64]{3,2,1,0:T(8,128)S(1)} %fusion.166, f32[1,64,64,7]{3,2,1,0:T(8,128)} %get-tuple-element.13, f32[]{:T(128)} %bitcast.96, f32[]{:T(128)} %bitcast.95, f32[]{:T(128)} %bitcast.94, f32[]{:T(128)} %bitcast.93, f32[]{:T(128)} %bitcast.92, ...), kind=kLoop, calls=%fused_computation.210 | loop fusion | flops 11272192 | bytes 2326588 | tf_op jit(solution)/shard_map/add | solution.py:77
  1477.8 84.3 %all-gather.36.cloned.1.call-done = f32[16,2,3,64,64]{4,3,2,1,0:T(8,128)} async-done(((f32[1,2,3,64,64]{4,3,2,1,0:T(8,128)}), f32[16,2,3,64,64]{4,3,2,1,0:T(8,128)}) %all-gather.36.cloned.1.call-update) | async-done | bytes 1572880 | tf_op jit(solution)/shard_map/all_gather | solution.py:63
  1564.3 2.2 fusion.280
  1568.9 6.9 fusion.75
  1576.5 84.3 %all-gather.38.cloned.1.call-done = f32[16,2,3,64,64]{4,3,2,1,0:T(8,128)} async-done(((f32[1,2,3,64,64]{4,3,2,1,0:T(8,128)}), f32[16,2,3,64,64]{4,3,2,1,0:T(8,128)}) %all-gather.38.cloned.1.call-update) | async-done | bytes 1572880 | tf_op jit(solution)/shard_map/all_gather | solution.py:63
  1667.2 6.3 fusion.19
  1673.5 2.5 copy.63
  1676.1 86.1 %reduce-scatter.2.cloned.1.call-done = f32[1,64,4,64]{3,1,0,2:T(8,128)} async-done(((f32[1,64,64,64]{3,1,0,2:T(8,128)}), f32[1,64,4,64]{3,1,0,2:T(8,128)}) %reduce-scatter.2.cloned.1.call-update) | async-done | bytes 65552 | tf_op jit(solution)/shard_map/reduce_scatter | solution.py:123
  (148 shorter events, 77.0 us)
Async XLA Ops:
  6.5 72.1 %copy-start.15 = (f32[1,7]{1,0:T(1,128)S(1)}, f32[1,7]{1,0:T(1,128)}, u32[]{:S(2)}) copy-start(f32[1,7]{1,0:T(1,128)} %param.9) | copy-start | bytes 88
  6.5 72.8 %copy-start.14 = (s32[1,6]{1,0:T(1,128)S(1)}, s32[1,6]{1,0:T(1,128)}, u32[]{:S(2)}) copy-start(s32[1,6]{1,0:T(1,128)} %param.12) | copy-start | bytes 76
  6.5 69.3 %all-gather.14.cloned.1.call-start = ((), (), s32[]{:S(2)}) async-start(), calls=%async_computation.1 | async-start | bytes 2228224 | tf_op jit(solution)/shard_map/all_gather | solution.py:102
  8.2 151.9 %all-gather.16.cloned.1.call-start = ((), (), s32[]{:S(2)}) async-start(), calls=%async_computation.2 | async-start | bytes 3342336 | tf_op jit(solution)/shard_map/all_gather | solution.py:47
  78.6 180.7 %all-gather.18.cloned.1.call-start = ((), (), s32[]{:S(2)}) async-start(), calls=%async_computation.3 | async-start | bytes 3342336 | tf_op jit(solution)/shard_map/all_gather | solution.py:51
  166.4 8.9 copy-start.16
  172.7 1.3 copy-start.9
  174.9 201.1 %all-gather.20.cloned.1.call-start = ((), (), s32[]{:S(2)}) async-start(), calls=%async_computation.4 | async-start | bytes 7798784 | tf_op jit(solution)/shard_map/all_gather | solution.py:55
  261.4 4.6 copy-start.10
  277.7 5.3 copy-start.17
  277.7 5.9 copy-start.13
  282.6 236.2 %all-gather.22.cloned.1.call-start = ((), (), s32[]{:S(2)}) async-start(), calls=%async_computation.5 | async-start | bytes 7798784 | tf_op jit(solution)/shard_map/all_gather | solution.py:59
  392.1 2.9 copy-start.4
  419.2 2.2 copy-start.2
  425.4 236.7 %all-gather.24.cloned.1.call-start = ((), (), s32[]{:S(2)}) async-start(), calls=%async_computation.6 | async-start | bytes 3342336 | tf_op jit(solution)/shard_map/all_gather | solution.py:63
  534.5 5.0 copy-start.3
  577.7 183.3 %all-gather.26.cloned.1.call-start = ((), (), s32[]{:S(2)}) async-start(), calls=%async_computation.7 | async-start | bytes 3342336 | tf_op jit(solution)/shard_map/all_gather | solution.py:63
  664.2 4.6 copy-start.8
  676.6 298.1 %all-reduce.2.cloned.1.call-start = ((), (), s32[]{:S(2)}) async-start(), calls=%async_computation.8 | async-start | bytes 4194304 | tf_op jit(solution)/shard_map/psum | solution.py:120
  774.9 287.1 %all-gather.28.cloned.1.call-start = ((), (), s32[]{:S(2)}) async-start(), calls=%async_computation.9 | async-start | bytes 3342336 | tf_op jit(solution)/shard_map/all_gather | solution.py:47
  978.3 90.0 %copy-start.6 = (f32[1,64,64,64]{3,2,1,0:T(8,128)}, f32[1,64,64,64]{3,2,1,0:T(8,128)S(1)}, u32[]{:S(2)}) copy-start(f32[1,64,64,64]{3,2,1,0:T(8,128)S(1)} %select_multiply_fusion) | copy-start | bytes 3145732
  979.1 182.1 %all-gather.30.cloned.1.call-start = ((), (), s32[]{:S(2)}) async-start(), calls=%async_computation.10 | async-start | bytes 3342336 | tf_op jit(solution)/shard_map/all_gather | solution.py:51
  1074.6 1.3 copy-start.11
  1076.8 197.3 %all-gather.32.cloned.1.call-start = ((), (), s32[]{:S(2)}) async-start(), calls=%async_computation.11 | async-start | bytes 7798784 | tf_op jit(solution)/shard_map/all_gather | solution.py:55
  1163.3 4.6 copy-start.12
  1174.6 2.2 copy-start
  1180.7 238.4 %all-gather.34.cloned.1.call-start = ((), (), s32[]{:S(2)}) async-start(), calls=%async_computation.12 | async-start | bytes 7798784 | tf_op jit(solution)/shard_map/all_gather | solution.py:59
  1289.8 2.9 copy-start.1
  1289.8 3.5 copy-start.5
  1325.8 236.4 %all-gather.36.cloned.1.call-start = ((), (), s32[]{:S(2)}) async-start(), calls=%async_computation.13 | async-start | bytes 3342336 | tf_op jit(solution)/shard_map/all_gather | solution.py:63
  1477.8 183.1 %all-gather.38.cloned.1.call-start = ((), (), s32[]{:S(2)}) async-start(), calls=%async_computation.14 | async-start | bytes 3342336 | tf_op jit(solution)/shard_map/all_gather | solution.py:63
  1564.3 4.6 copy-start.7
  1576.5 185.7 %reduce-scatter.2.cloned.1.call-start = ((), (), s32[]{:S(2)}) async-start(), calls=%async_computation.15 | async-start | bytes 2228224 | tf_op jit(solution)/shard_map/reduce_scatter | solution.py:123
Sparse Core Ops, SparseCore 0:
  10.0 65.7 all-gather.13
  78.7 81.3 all-gather.15
  175.0 84.2 all-gather.17
  282.7 93.2 all-gather.19
  425.5 93.2 all-gather.21
  577.9 84.2 all-gather.23
  676.8 84.2 all-gather.25
  775.0 199.6 all-reduce.1
  979.2 82.7 all-gather.27
  1076.9 84.2 all-gather.29
  1180.9 93.2 all-gather.31
  1325.9 93.2 all-gather.33
  1477.9 84.2 all-gather.35
  1576.6 84.2 all-gather.37
  1676.2 85.9 reduce-scatter.1
where the time goes:
time: 1780 us; the launch traced here: 1770 us
  waiting for transfers between devices  1380 us (78%)
  other arithmetic  190 us (11%)
  local copies, waits for them, and re-layouts  114 us (6%)
  matrix products  66 us (4%)
    all_gather x12, waiting for transfers between devices, with_halo(): lax.all_gather(edge_slabs, 'space', axis=0, tiled=True)  1030 us
    psum x1, waiting for transfers between devices, shards(): summed = lax.psum(spread, 'view')  199 us
    add x10, other arithmetic, convolve(): summed + weight * lax.slice_in_dim(extended, position, position + length,...  126 us
    reduce_scatter x1, waiting for transfers between devices, shards(): summed = lax.psum_scatter(spread, 'view', scatter_dimension=2, tiled=True)  86.1 us
    all_gather x1, waiting for transfers between devices, shards(): full_now = lax.all_gather(share_now, 'view', axis=2, tiled=True)  67.6 us
    div x2, other arithmetic, shards(): quotient = recorded_all[0] / blurred  48.4 us
  transfers between devices with their start and end apart: 15, of which 15 were waited for; matrix products, arithmetic and copies ran while one was open for 1% of the time, Pallas kernels for 0%

commit v1 on v0

v1 whole, which is shorter than its diff:
```python
import jax
import jax.numpy as jnp
from jax import lax
from jax.sharding import PartitionSpec as P

ITERS = 2
ROW = 4


def normalized(kernel):
    return kernel / jnp.sum(kernel)


def xor_pairs(n, m):
    return [(i, i ^ m) for i in range(n)]


def gather_rows(row, axis, n):
    me = lax.axis_index(axis)
    buf = jnp.where(jnp.arange(n)[:, None] == me, row, jnp.zeros_like(row))
    m = 1
    while m < n:
        buf = buf + lax.ppermute(buf, axis, xor_pairs(n, m))
        m *= 2
    return buf


def route(x, dest, src_of_me, nsp):
    me = lax.axis_index("space")
    rows = nsp // ROW
    my_row, my_col = me // ROW, me % ROW
    dest_col = dest[me] % ROW
    zero = jnp.zeros_like(x)
    received = []
    for k in range(ROW):
        part = jnp.where((dest_col - my_col) % ROW == k, x, zero)
        if k:
            pairs = [(a * ROW + b, a * ROW + (b + k) % ROW) for a in range(rows) for b in range(ROW)]
            part = lax.ppermute(part, "space", pairs)
        src = my_row * ROW + (my_col - k) % ROW
        received.append((part, dest[src]))
    result = zero
    for j in range(rows):
        target = ((my_row + j) % rows) * ROW + my_col
        part = zero
        for data, d in received:
            part = jnp.where(d == target, data, part)
        if j:
            pairs = [(a * ROW + c, ((a + j) % rows) * ROW + c) for a in range(rows) for c in range(ROW)]
            part = lax.ppermute(part, "space", pairs)
        src_row = src_of_me // ROW
        result = jnp.where((my_row - src_row) % rows == j, part, result)
    return result


def convolve(extended, kernel, axis, flipped):
    radius = (kernel.shape[0] - 1) // 2
    length = extended.shape[axis] - 2 * radius
    summed = None
    for position in range(2 * radius + 1):
        weight = kernel[2 * radius - position] if flipped else kernel[position]
        term = weight * lax.slice_in_dim(extended, position, position + length, axis=axis)
        summed = term if summed is None else summed + term
    return summed


def pair_halo(volume, axis, radius, partner, is_high):
    length = volume.shape[axis]
    first = lax.slice_in_dim(volume, 0, radius, axis=axis)
    last = lax.slice_in_dim(volume, length - radius, length, axis=axis)
    send = jnp.where(is_high, first, last)
    nsp = lax.axis_size("space")
    recv = lax.ppermute(send, "space", [(i, i ^ partner) for i in range(nsp)])
    zero = jnp.zeros_like(recv)
    low = jnp.where(is_high, recv, zero)
    high = jnp.where(is_high, zero, recv)
    return jnp.concatenate([low, volume, high], axis=axis)


def z_halo(volume, axis, radius):
    length = volume.shape[axis]
    nsp = lax.axis_size("space")
    first = lax.slice_in_dim(volume, 0, radius, axis=axis)
    last = lax.slice_in_dim(volume, length - radius, length, axis=axis)
    low = lax.ppermute(last, "space", [(i, i + ROW) for i in range(nsp - ROW)])
    high = lax.ppermute(first, "space", [(i + ROW, i) for i in range(nsp - ROW)])
    return jnp.concatenate([low, volume, high], axis=axis)


RS_BITS = (1, 4, 8, 2)


def bit_axis(present, m):
    order = [8, 4, 2, 1]
    return 1 + sum(1 for b in order if b in present and order.index(b) < order.index(m))


def view_reduce_scatter(full, nv):
    me = lax.axis_index("view")
    s0, s1, s2 = full.shape
    x = full.reshape(s0, 2, 2, 2, 2, s1 // nv, s2)
    present = {8, 4, 2, 1}
    for m in RS_BITS:
        ax = bit_axis(present, m)
        x0 = lax.index_in_dim(x, 0, axis=ax, keepdims=False)
        x1 = lax.index_in_dim(x, 1, axis=ax, keepdims=False)
        mine = (me & m) != 0
        keep = jnp.where(mine, x1, x0)
        send = jnp.where(mine, x0, x1)
        x = keep + lax.ppermute(send, "view", xor_pairs(nv, m))
        present.discard(m)
    return x


def view_all_gather(share, nv):
    me = lax.axis_index("view")
    x = share
    present = set()
    for m in reversed(RS_BITS):
        recv = lax.ppermute(x, "view", xor_pairs(nv, m))
        mine = (me & m) != 0
        lo = jnp.where(mine, recv, x)
        hi = jnp.where(mine, x, recv)
        ax = bit_axis(present | {m}, m)
        x = jnp.stack([lo, hi], axis=ax)
        present.add(m)
    s0 = x.shape[0]
    return x.reshape(s0, -1, x.shape[-1])


def shards(estimate, measured, kernel_x, kernel_y, kernel_z, neighbors, inside):
    side = estimate.shape[1]
    nsp = lax.axis_size("space")
    nv = lax.axis_size("view")
    me = lax.axis_index("space")
    table = gather_rows(
        jnp.concatenate([neighbors[0], inside.astype(jnp.int32)]), "space", nsp
    )
    nbr = table[:, :6]
    inside_all = table[:, 6]
    cx = (nbr[:, 0] >= 0).astype(jnp.int32)
    cy = (nbr[:, 2] >= 0).astype(jnp.int32)
    cz = jnp.zeros_like(cx)
    cur = nbr[:, 4]
    for _ in range(nsp // ROW - 1):
        cz = cz + (cur >= 0).astype(jnp.int32)
        cur = jnp.where(cur >= 0, nbr[jnp.maximum(cur, 0), 4], -1)
    ypos = jnp.where(cy == 0, cx, 3 - cx)
    place = cz * ROW + ypos
    ids = jnp.arange(nsp, dtype=jnp.int32)
    brick_at = jnp.zeros_like(place).at[place].set(ids)
    my_brick = brick_at[me]
    keep = inside_all[my_brick] > 0
    my_x = cx[my_brick]
    my_y = cy[my_brick]

    share = estimate[0].reshape(side, estimate.shape[2] // side, side)
    share = route(share, place, my_brick, nsp)
    recorded = measured[0, 0].reshape(side, side, side)
    recorded = route(recorded, place, my_brick, nsp)

    radius_x = (kernel_x.shape[1] - 1) // 2
    radius_y = (kernel_y.shape[1] - 1) // 2
    radius_z = (kernel_z.shape[1] - 1) // 2
    along_x = normalized(kernel_x[0])
    along_y = normalized(kernel_y[0])
    along_z = normalized(kernel_z[0])
    for sweep_no in range(ITERS):
        full = view_all_gather(share, nv)
        blurred = convolve(pair_halo(full, 0, radius_x, 1, my_x == 1), along_x, 0, False)
        blurred = convolve(pair_halo(blurred, 1, radius_y, 3, my_y == 1), along_y, 1, False)
        blurred = convolve(z_halo(blurred, 2, radius_z), along_z, 2, False)
        quotient = recorded / blurred
        spread = convolve(z_halo(quotient, 2, radius_z), along_z, 2, True)
        spread = convolve(pair_halo(spread, 1, radius_y, 3, my_y == 1), along_y, 1, True)
        spread = convolve(pair_halo(spread, 0, radius_x, 1, my_x == 1), along_x, 0, True)
        summed = view_reduce_scatter(spread, nv)
        share = share * jnp.where(keep, summed / (nv * measured.shape[0]), 1.0)
    share = route(share, brick_at, place[me], nsp)
    return share.reshape(1, side, estimate.shape[2])


def solution(mesh):
    placed = (
        P("space", None, "view"),
        P("view", "space", None, None),
        P("view", None),
        P("view", None),
        P("view", None),
        P("space", None),
        P("space"),
    )
    return jax.shard_map(
        shards, mesh=mesh, in_specs=placed, out_specs=P("space", None, "view"), check_vma=False
    )
```

time: 1780 us -> 849 us (0.48)
  waiting for transfers between devices: 1380 us -> 352 us
  starting transfers between devices: 2.23 us -> 126 us
  matrix products: 66 us -> 0 us
  other arithmetic: 190 us -> 256 us
  local copies, waits for them, and re-layouts: 114 us -> 75.1 us
    all_gather x13 -> x0, waiting for transfers between devices: 1100 us -> none  [the longest x12 1030 us: with_halo(): lax.all_gather(edge_slabs, 'space', axis=0, tiled=True)]
    ppermute x0 -> x54, waiting for transfers between devices: none -> 352 us  [the longest x8 94.6 us: pair_halo(): recv = lax.ppermute(send, 'space', [(i, i ^ partner) for i in range(nsp)])]
    psum x1 -> x0, waiting for transfers between devices: 199 us -> none  [shards(): summed = lax.psum(spread, 'view')]
    ppermute x0 -> x54, starting transfers between devices: none -> 126 us  [the longest x4 28.1 us: z_halo(): low = lax.ppermute(last, 'space', [(i, i + ROW) for i in range(nsp - ROW)])]
    reduce_scatter x1 -> x0, waiting for transfers between devices: 86.1 us -> none  [shards(): summed = lax.psum_scatter(spread, 'view', scatter_dimension=2, tiled=True)]
    dot_general x24 -> x0, matrix products: 66 us -> none  [the longest x12 33.2 us: fold_faces(): jnp.einsum('br,rpac->bpac', low_pick, incoming[:, 1], precision=lax.Preci...]
    squeeze x20 -> x0, local copies, waits for them, and re-layouts: 50.7 us -> none  [the longest x12 35 us: fold_faces(): incoming[:, 1]]
    another operation x28 -> x2, local copies, waits for them, and re-layouts: 45.9 us -> 0.59 us  [view_all_gather(): x = jnp.stack([lo, hi], axis=ax)]
  transfers between devices with their start and end apart: 15 -> 54, of which waited for: 15 -> 34; matrix products, arithmetic and copies ran while one was open for 1% -> 10% of each run, Pallas kernels for 0% -> 0%
where the time goes in v1:
time: 849 us; the launch traced here: 838 us
  waiting for transfers between devices  352 us (41%)
  other arithmetic  256 us (30%)
  starting transfers between devices  126 us (15%)
  local copies, waits for them, and re-layouts  75.1 us (9%)
  between operations  28.8 us (3%)
    add x10, other arithmetic, convolve(): summed = term if summed is None else summed + term  137 us
    ppermute x8, waiting for transfers between devices, pair_halo(): recv = lax.ppermute(send, 'space', [(i, i ^ partner) for i in range(nsp)])  94.6 us
    ppermute x4, waiting for transfers between devices, z_halo(): low = lax.ppermute(last, 'space', [(i, i + ROW) for i in range(nsp - ROW)])  85.5 us
    div x2, other arithmetic, shards(): quotient = recorded / blurred  78.7 us
    ppermute x8, waiting for transfers between devices, view_reduce_scatter(): x = keep + lax.ppermute(send, 'view', xor_pairs(nv, m))  50.7 us
    ppermute x18, waiting for transfers between devices, route(): part = lax.ppermute(part, 'space', pairs)  46.9 us
    ppermute x8, waiting for transfers between devices, view_all_gather(): recv = lax.ppermute(x, 'view', xor_pairs(nv, m))  39.6 us
    ppermute x4, starting transfers between devices, z_halo(): low = lax.ppermute(last, 'space', [(i, i + ROW) for i in range(nsp - ROW)])  28.1 us
  transfers between devices with their start and end apart: 54, of which 34 were waited for; matrix products, arithmetic and copies ran while one was open for 10% of the time, Pallas kernels for 0%

profile of v1, /device:TPU:8, one launch (start us, length us, event | category | flops | bytes accessed | tf_op | source)
XLA Modules:
  0.0 838.1 jit_solution(197288699900356716)
XLA Ops:
  7.4 3.0 collective-permute-done.1
  14.1 3.1 collective-permute-start.3
  38.5 4.4 collective-permute-start.7
  50.3 8.3 collective-permute-start.16
  61.7 3.1 collective-permute-start.17
  65.4 7.1 collective-permute-done.17
  77.1 5.0 collective-permute-done.18
  83.7 2.9 select_select_fusion.4
  91.5 3.2 select_n.1133
  95.8 3.1 select_n.1137
  101.4 3.2 select_n.1162
  104.6 3.1 select_n.1152
  107.7 3.1 select_n.1142
  116.1 75.4 %collective-permute-done.20 = f32[3,64,64]{2,1,0:T(8,128)S(1)} collective-permute-done((f32[3,64,64]{2,1,0:T(8,128)S(1)}, f32[3,64,64]{2,1,0:T(8,128)S(1)}, u32[]{:S(2)}, u32[]{:S(2)}) %collective-permute-start.20) | collective-permute-done | bytes 49184 | tf_op jit(solution)/shard_map/ppermute | solution.py:73
  192.2 7.0 fusion.45
  200.0 7.1 select_select_fusion.1
  211.7 6.4 fusion.101
  218.2 2.7 fusion.286
  224.6 3.0 copy.49
  227.6 5.4 collective-permute-start.22
  236.6 24.0 %collective-permute-done.23 = f32[64,64,7]{1,0,2:T(8,128)} collective-permute-done((f32[64,64,7]{1,0,2:T(8,128)S(1)}, f32[64,64,7]{1,0,2:T(8,128)}, u32[]{:S(2)}, u32[]{:S(2)}) %collective-permute-start.23) | collective-permute-done | bytes 114720 | tf_op jit(solution)/shard_map/ppermute | solution.py:86
  260.6 3.0 copy.52
  263.6 84.3 %collective-permute-done.22 = f32[64,64,7]{1,0,2:T(8,128)} collective-permute-done((f32[64,64,7]{1,0,2:T(8,128)}, f32[64,64,7]{1,0,2:T(8,128)}, u32[]{:S(2)}, u32[]{:S(2)}) %collective-permute-start.22) | collective-permute-done | bytes 114720 | tf_op jit(solution)/shard_map/ppermute | solution.py:85
  347.9 3.0 copy.50
  350.9 39.8 %collective-permute-done.14 = f32[64,64,64]{2,1,0:T(8,128)} collective-permute-done((f32[64,64,64]{2,1,0:T(8,128)}, f32[64,64,64]{2,1,0:T(8,128)}, u32[]{:S(2)}, u32[]{:S(2)}) %collective-permute-start.14) | collective-permute-done | bytes 1048608 | tf_op jit(solution)/shard_map/ppermute | solution.py:50
  390.8 34.7 %fusion.223 = (f32[64,64,64]{2,1,0:T(8,128)S(1)}, f32[64,64,64]{2,1,0:T(8,128)}) fusion(f32[64,64,7]{2,1,0:T(8,128)} %copy.52, f32[64,64,64]{2,1,0:T(8,128)S(1)} %fusion.101, f32[64,64,7]{2,1,0:T(8,128)} %copy.50, f32[]{:T(128)} %bitcast.57, f32[]{:T(128)} %bitcast.56, f32[]{:T(128)} %bitcast.55, f32[]{:T(128)} %bitcast.54, f32[]{:T(128)} %bitcast.53, ...), kind=kLoop, calls=%fused_computation.379 | loop fusion | flops 13369344 | bytes 10715203 | tf_op jit(solution)/shard_map/div | solution.py:173
  432.0 13.0 %collective-permute-start.24 = (f32[64,64,7]{1,0,2:T(8,128)S(1)}, f32[64,64,7]{1,0,2:T(8,128)S(1)}, u32[]{:S(2)}, u32[]{:S(2)}) collective-permute-start(f32[64,64,7]{1,0,2:T(8,128)S(1)} %copy.53), channel_id=1, source_target_pairs={{0,64},{16,80},{32,96},{48,112},{64,128},{80,144},{96,160},{112,17... | collective-permute-start | bytes 344072 | tf_op jit(solution)/shard_map/ppermute | solution.py:85
  450.7 35.9 %fusion.190 = f32[64,64,64]{2,1,0:T(8,128)} fusion(f32[64,64,7]{2,1,0:T(8,128)} %copy.56, f32[64,64,64]{2,1,0:T(8,128)S(1)} %copy-done.1, f32[64,64,7]{2,1,0:T(8,128)} %copy.54, f32[]{:T(128)} %bitcast.57, f32[]{:T(128)} %bitcast.56, f32[]{:T(128)} %bitcast.55, f32[]{:T(128)} %bitcast.54, f32[]{:T(128)} %bitcast.53, f32[]{:T(128)} %bitcast.52, f32[]{:T(128)} %bitcast.51, ...), kind=kLoop, calls=%fused_computation.324 | loop fusion | flops 11272192 | bytes 2326588 | tf_op jit(solution)/shard_map/add | solution.py:63
  489.7 3.5 collective-permute-done.26
  493.9 13.0 %fusion.87 = f32[64,64,64]{2,1,0:T(8,128)S(1)} fusion(f32[64,64,64]{2,1,0:T(8,128)} %fusion.190, f32[64,3,64]{2,1,0:T(4,128)S(1)} %get-tuple-element.60, f32[64,3,64]{2,1,0:T(4,128)S(1)} %get-tuple-element.59, f32[]{:T(128)} %bitcast.44, f32[]{:T(128)} %bitcast.43, f32[]{:T(128)} %bitcast.42, f32[]{:T(128)} %bitcast.41, f32[]{:T(128)} %bitcast.40, ...), kind=kLoop, calls=%fused_computation.164 | loop fusion | flops 4980736 | bytes 2195484 | tf_op jit(solution)/shard_map/add | solution.py:63
  507.5 3.5 collective-permute-start.27
  511.1 2.6 collective-permute-done.27
  514.3 6.5 fusion.31
  521.8 2.6 collective-permute-done.28
  527.1 12.2 %collective-permute-done.29 = f32[64,2,2,4,64]{4,3,0,2,1:T(4,128)S(1)} collective-permute-done((f32[64,2,2,4,64]{4,3,0,2,1:T(4,128)S(1)}, f32[64,2,2,4,64]{4,3,0,2,1:T(4,128)S(1)}, u32[]{:S(2)}, u32[]{:S(2)}) %collective-permute-start.29) | collective-permute-done | bytes 262176 | tf_op jit(solution)/shard_map/ppermute | solution.py:110
  539.5 3.5 collective-permute-start.30
  543.0 5.9 collective-permute-done.30
  549.1 5.9 collective-permute-start.31
  555.7 3.9 collective-permute-done.31
  560.4 6.5 collective-permute-start.32
  566.9 3.9 collective-permute-done.32
  571.3 10.0 %collective-permute-done.33 = f32[64,2,4,64]{3,2,0,1:T(4,128)S(1)} collective-permute-done((f32[64,2,4,64]{3,2,0,1:T(4,128)S(1)}, f32[64,2,4,64]{3,2,0,1:T(4,128)S(1)}, u32[]{:S(2)}, u32[]{:S(2)}) %collective-permute-start.33) | collective-permute-done | bytes 131104 | tf_op jit(solution)/shard_map/ppermute | solution.py:120
  581.7 9.2 %collective-permute-done.34 = f32[64,2,2,4,64]{4,3,0,2,1:T(4,128)S(1)} collective-permute-done((f32[64,2,2,4,64]{4,3,0,2,1:T(4,128)S(1)}, f32[64,2,2,4,64]{4,3,0,2,1:T(4,128)S(1)}, u32[]{:S(2)}, u32[]{:S(2)}) %collective-permute-start.34) | collective-permute-done | bytes 262176 | tf_op jit(solution)/shard_map/ppermute | solution.py:120
  591.5 2.6 collective-permute-done.35
  601.4 6.5 fusion.17
  608.7 4.9 collective-permute-done.37
  614.2 6.4 fusion.73
  627.3 4.6 collective-permute-start.38
  637.5 44.0 %fusion.150 = f32[64,64,64]{2,1,0:T(8,128)S(1)} fusion(f32[64,64,64]{2,1,0:T(8,128)} %get-tuple-element.8, f32[64,64,7]{2,1,0:T(8,128)} %copy.68, f32[64,64,64]{2,1,0:T(8,128)} %copy-done.2, f32[64,64,7]{2,1,0:T(8,128)} %copy.66, f32[]{:T(128)} %bitcast.57, f32[]{:T(128)} %bitcast.56, f32[]{:T(128)} %bitcast.55, f32[]{:T(128)} %bitcast.54, f32[]{:T(128)} %bitcast.53, ...), kind=kLoop, calls=%fused_computation.254 | loop fusion | flops 11534336 | bytes 3375164 | tf_op jit(solution)/shard_map/div | solution.py:173
  681.6 2.8 fusion.282
  690.3 5.1 collective-permute-start.40
  700.8 35.9 %fusion.117 = f32[64,64,64]{2,1,0:T(8,128)} fusion(f32[64,64,7]{2,1,0:T(8,128)} %copy.72, f32[64,64,64]{2,1,0:T(8,128)S(1)} %fusion.150, f32[64,64,7]{2,1,0:T(8,128)} %copy.70, f32[]{:T(128)} %bitcast.57, f32[]{:T(128)} %bitcast.56, f32[]{:T(128)} %bitcast.55, f32[]{:T(128)} %bitcast.54, f32[]{:T(128)} %bitcast.53, f32[]{:T(128)} %bitcast.52, f32[]{:T(128)} %bitcast.51, ...), kind=kLoop, calls=%fused_computation.199 | loop fusion | flops 11272192 | bytes 2326588 | tf_op jit(solution)/shard_map/add | solution.py:63
  738.8 4.6 collective-permute-done.42
  744.0 13.0 %fusion.59 = f32[64,64,64]{2,1,0:T(8,128)S(1)} fusion(f32[64,64,64]{2,1,0:T(8,128)} %fusion.117, f32[64,3,64]{2,1,0:T(4,128)S(1)} %get-tuple-element.56, f32[64,3,64]{2,1,0:T(4,128)S(1)} %get-tuple-element.55, f32[]{:T(128)} %bitcast.44, f32[]{:T(128)} %bitcast.43, f32[]{:T(128)} %bitcast.42, f32[]{:T(128)} %bitcast.41, f32[]{:T(128)} %bitcast.40, ...), kind=kLoop, calls=%fused_computation.136 | loop fusion | flops 4980736 | bytes 2195484 | tf_op jit(solution)/shard_map/add | solution.py:63
  757.6 4.4 collective-permute-start.43
  765.3 6.5 fusion.3
  772.8 2.6 collective-permute-done.44
  777.3 12.8 %collective-permute-done.45 = f32[64,2,2,4,64]{4,3,0,2,1:T(4,128)S(1)} collective-permute-done((f32[64,2,2,4,64]{4,3,0,2,1:T(4,128)S(1)}, f32[64,2,2,4,64]{4,3,0,2,1:T(4,128)S(1)}, u32[]{:S(2)}, u32[]{:S(2)}) %collective-permute-start.45) | collective-permute-done | bytes 262176 | tf_op jit(solution)/shard_map/ppermute | solution.py:110
  790.3 3.0 collective-permute-start.46
  793.3 6.1 collective-permute-done.46
  799.5 6.7 collective-permute-start.47
  806.3 4.5 collective-permute-done.47
  823.4 4.5 collective-permute-start.51
  831.8 4.9 collective-permute-done.52
  (208 shorter events, 132.4 us)
Async XLA Ops:
  1.5 3.8 collective-permute-start
  5.3 5.1 collective-permute-start.1
  10.5 3.6 collective-permute-start.2
  14.1 4.7 collective-permute-start.3
  26.0 32.6 %copy-start.9 = (f32[1,7]{1,0:T(1,128)S(1)}, f32[1,7]{1,0:T(1,128)}, u32[]{:S(2)}) copy-start(f32[1,7]{1,0:T(1,128)} %param.9) | copy-start | bytes 88
  26.0 33.2 %copy-start.10 = (f32[1,7]{1,0:T(1,128)S(1)}, f32[1,7]{1,0:T(1,128)}, u32[]{:S(2)}) copy-start(f32[1,7]{1,0:T(1,128)} %param.10) | copy-start | bytes 88
  27.0 11.4 %collective-permute-start.4 = (f32[64,4,64]{2,1,0:T(4,128)S(1)}, f32[64,4,64]{2,1,0:T(4,128)S(1)}, u32[]{:S(2)}, u32[]{:S(2)}) collective-permute-start(f32[64,4,64]{2,1,0:T(4,128)S(1)} %select_n.1057), channel_id=1, source_target_pairs={{0,48},{16,0},{32,16},{48,32},{64,112},{80,64},{96,80},{112,96},{1... | collective-permute-start | bytes 196616 | tf_op jit(solution)/shard_map/ppermute | solution.py:39
  29.0 9.3 %collective-permute-start.5 = (f32[64,4,64]{2,1,0:T(4,128)S(1)}, f32[64,4,64]{2,1,0:T(4,128)S(1)}, u32[]{:S(2)}, u32[]{:S(2)}) collective-permute-start(f32[64,4,64]{2,1,0:T(4,128)S(1)} %select_n.1063), channel_id=1, source_target_pairs={{0,32},{16,48},{32,0},{48,16},{64,96},{80,112},{96,64},{112,80},{1... | collective-permute-start | bytes 196616 | tf_op jit(solution)/shard_map/ppermute | solution.py:39
  30.4 8.0 collective-permute-start.6
  38.5 9.6 %collective-permute-start.7 = (f32[64,4,64]{2,1,0:T(4,128)S(1)}, f32[64,4,64]{2,1,0:T(4,128)S(1)}, u32[]{:S(2)}, u32[]{:S(2)}) collective-permute-start(f32[64,4,64]{2,1,0:T(4,128)S(1)} %bitcast.197), channel_id=1, source_target_pairs={{0,192},{16,208},{32,224},{48,240},{64,0},{80,16},{96,32},{112,48}... | collective-permute-start | bytes 196616 | tf_op jit(solution)/shard_map/ppermute | solution.py:50
  42.8 7.3 collective-permute-start.8
  42.8 7.3 collective-permute-start.9
  48.0 27.1 %copy-start.11 = (f32[1,15]{1,0:T(1,128)S(1)}, f32[1,15]{1,0:T(1,128)}, u32[]{:S(2)}) copy-start(f32[1,15]{1,0:T(1,128)} %param.11) | copy-start | bytes 184
  50.3 11.3 %collective-permute-start.16 = (f32[64,4,64]{2,1,0:T(4,128)S(1)}, f32[64,4,64]{2,1,0:T(4,128)S(1)}, u32[]{:S(2)}, u32[]{:S(2)}) collective-permute-start(f32[64,4,64]{2,1,0:T(4,128)S(1)} %select_select_fusion.12), channel_id=1, source_target_pairs={{0,2},{1,3},{2,0},{3,1},{4,6},{5,7},{6,4},{7,5},{8,10},{9,11},{10,... | collective-permute-start | bytes 196616 | tf_op jit(solution)/shard_map/ppermute | solution.py:120
  61.7 10.8 %collective-permute-start.17 = (f32[64,2,4,64]{3,2,0,1:T(4,128)S(1)}, f32[64,2,4,64]{3,2,0,1:T(4,128)S(1)}, u32[]{:S(2)}, u32[]{:S(2)}) collective-permute-start(f32[64,2,4,64]{3,2,0,1:T(4,128)S(1)} %pad_maximum_fusion.30), channel_id=1, source_target_pairs={{0,8},{1,9},{2,10},{3,11},{4,12},{5,13},{6,14},{7,15},{8,0},{9,1},... | collective-permute-start | bytes 393224 | tf_op jit(solution)/shard_map/ppermute | solution.py:120
  72.8 9.3 %collective-permute-start.18 = (f32[64,2,2,4,64]{4,3,0,2,1:T(4,128)S(1)}, f32[64,2,2,4,64]{4,3,0,2,1:T(4,128)S(1)}, u32[]{:S(2)}, u32[]{:S(2)}) collective-permute-start(f32[64,2,2,4,64]{4,3,0,2,1:T(4,128)S(1)} %pad_maximum_fusion.28), channel_id=1, source_target_pairs={{0,4},{1,5},{2,6},{3,7},{4,0},{5,1},{6,2},{7,3},{8,12},{9,13},{10,... | collective-permute-start | bytes 786440 | tf_op jit(solution)/shard_map/ppermute | solution.py:120
  77.1 6.6 copy-start.8
  83.5 27.2 %collective-permute-start.19 = (f32[64,2,2,2,4,64]{5,4,0,3,1,2:T(4,128)}, f32[64,2,2,2,4,64]{5,4,0,3,1,2:T(4,128)}, u32[]{:S(2)}, u32[]{:S(2)}) collective-permute-start(f32[64,2,2,2,4,64]{5,4,0,3,1,2:T(4,128)} %pad_maximum_fusion.26), channel_id=1, source_target_pairs={{0,1},{1,0},{2,3},{3,2},{4,5},{5,4},{6,7},{7,6},{8,9},{9,8},{10,11... | collective-permute-start | bytes 1572872 | tf_op jit(solution)/shard_map/ppermute | solution.py:120
  91.2 108.7 %collective-permute-start.10 = (f32[64,64,64]{2,1,0:T(8,128)}, f32[64,64,64]{2,1,0:T(8,128)S(1)}, u32[]{:S(2)}, u32[]{:S(2)}) collective-permute-start(f32[64,64,64]{2,1,0:T(8,128)} %select_n.1129), channel_id=1, source_target_pairs={{0,48},{16,0},{32,16},{48,32},{64,112},{80,64},{96,80},{112,96},{1... | collective-permute-start | bytes 3145736 | tf_op jit(solution)/shard_map/ppermute | solution.py:39
  94.6 105.3 %collective-permute-start.11 = (f32[64,64,64]{2,1,0:T(8,128)}, f32[64,64,64]{2,1,0:T(8,128)}, u32[]{:S(2)}, u32[]{:S(2)}) collective-permute-start(f32[64,64,64]{2,1,0:T(8,128)} %select_n.1133), channel_id=1, source_target_pairs={{0,32},{16,48},{32,0},{48,16},{64,96},{80,112},{96,64},{112,80},{1... | collective-permute-start | bytes 3145736 | tf_op jit(solution)/shard_map/ppermute | solution.py:39
  98.9 101.1 %collective-permute-start.12 = (f32[64,64,64]{2,1,0:T(8,128)}, f32[64,64,64]{2,1,0:T(8,128)}, u32[]{:S(2)}, u32[]{:S(2)}) collective-permute-start(f32[64,64,64]{2,1,0:T(8,128)} %select_n.1137), channel_id=1, source_target_pairs={{0,16},{16,32},{32,48},{48,0},{64,80},{80,96},{96,112},{112,64},{1... | collective-permute-start | bytes 3145736 | tf_op jit(solution)/shard_map/ppermute | solution.py:39
  113.2 78.3 %collective-permute-start.20 = (f32[3,64,64]{2,1,0:T(8,128)S(1)}, f32[3,64,64]{2,1,0:T(8,128)S(1)}, u32[]{:S(2)}, u32[]{:S(2)}) collective-permute-start(f32[3,64,64]{2,1,0:T(8,128)S(1)} %bitcast.198), channel_id=1, source_target_pairs={{0,16},{16,0},{32,48},{48,32},{64,80},{80,64},{96,112},{112,96},{1... | collective-permute-start | bytes 147464 | tf_op jit(solution)/shard_map/ppermute | solution.py:73
  114.9 85.1 %copy-start.6 = (f32[64,64,64]{2,1,0:T(8,128)S(1)}, f32[64,64,64]{2,1,0:T(8,128)}, u32[]{:S(2)}) copy-start(f32[64,64,64]{2,1,0:T(8,128)} %select_n.1142) | copy-start | bytes 3145732
  192.2 7.8 copy-start.4
  192.2 7.8 copy-start.5
  199.8 11.3 %collective-permute-start.21 = (f32[64,3,64]{2,1,0:T(4,128)S(1)}, f32[64,3,64]{2,1,0:T(4,128)S(1)}, u32[]{:S(2)}, u32[]{:S(2)}) collective-permute-start(f32[64,3,64]{2,1,0:T(4,128)S(1)} %slice_select_fusion.3), channel_id=1, source_target_pairs={{0,48},{16,32},{32,16},{48,0},{64,112},{80,96},{96,80},{112,64},{1... | collective-permute-start | bytes 147464 | tf_op jit(solution)/shard_map/ppermute | solution.py:73
  199.9 7.2 copy-start.3
  207.1 143.8 %collective-permute-start.13 = (f32[64,64,64]{2,1,0:T(8,128)}, f32[64,64,64]{2,1,0:T(8,128)}, u32[]{:S(2)}, u32[]{:S(2)}) collective-permute-start(f32[64,64,64]{2,1,0:T(8,128)} %get-tuple-element.11), channel_id=1, source_target_pairs={{0,192},{16,208},{32,224},{48,240},{64,0},{80,16},{96,32},{112,48}... | collective-permute-start | bytes 3145736 | tf_op jit(solution)/shard_map/ppermute | solution.py:50
  208.3 182.4 %collective-permute-start.14 = (f32[64,64,64]{2,1,0:T(8,128)}, f32[64,64,64]{2,1,0:T(8,128)}, u32[]{:S(2)}, u32[]{:S(2)}) collective-permute-start(f32[64,64,64]{2,1,0:T(8,128)} %get-tuple-element.10), channel_id=1, source_target_pairs={{0,128},{16,144},{32,160},{48,176},{64,192},{80,208},{96,224},{112... | collective-permute-start | bytes 3145736 | tf_op jit(solution)/shard_map/ppermute | solution.py:50
  209.1 181.7 %collective-permute-start.15 = (f32[64,64,64]{2,1,0:T(8,128)}, f32[64,64,64]{2,1,0:T(8,128)}, u32[]{:S(2)}, u32[]{:S(2)}) collective-permute-start(f32[64,64,64]{2,1,0:T(8,128)} %get-tuple-element.9), channel_id=1, source_target_pairs={{0,64},{16,80},{32,96},{48,112},{64,128},{80,144},{96,160},{112,17... | collective-permute-start | bytes 3145736 | tf_op jit(solution)/shard_map/ppermute | solution.py:50
  220.9 13.4 %copy-start.7 = (f32[1,1,64,4096]{3,2,1,0:T(8,128)S(1)}, f32[1,1,64,4096]{3,2,1,0:T(8,128)}, u32[]{:S(2)}) copy-start(f32[1,1,64,4096]{3,2,1,0:T(8,128)} %get-tuple-element.30) | copy-start | bytes 3145732
  223.3 37.2 %collective-permute-start.23 = (f32[64,64,7]{1,0,2:T(8,128)S(1)}, f32[64,64,7]{1,0,2:T(8,128)}, u32[]{:S(2)}, u32[]{:S(2)}) collective-permute-start(f32[64,64,7]{1,0,2:T(8,128)S(1)} %copy.51), channel_id=1, source_target_pairs={{64,0},{80,16},{96,32},{112,48},{128,64},{144,80},{160,96},{176,11... | collective-permute-start | bytes 344072 | tf_op jit(solution)/shard_map/ppermute | solution.py:86
  227.6 120.3 %collective-permute-start.22 = (f32[64,64,7]{1,0,2:T(8,128)}, f32[64,64,7]{1,0,2:T(8,128)}, u32[]{:S(2)}, u32[]{:S(2)}) collective-permute-start(f32[64,64,7]{1,0,2:T(8,128)} %copy.49), channel_id=1, source_target_pairs={{0,64},{16,80},{32,96},{48,112},{64,128},{80,144},{96,160},{112,17... | collective-permute-start | bytes 344072 | tf_op jit(solution)/shard_map/ppermute | solution.py:85
  430.0 16.6 %collective-permute-start.25 = (f32[64,64,7]{1,0,2:T(8,128)S(1)}, f32[64,64,7]{1,0,2:T(8,128)S(1)}, u32[]{:S(2)}, u32[]{:S(2)}) collective-permute-start(f32[64,64,7]{1,0,2:T(8,128)S(1)} %copy.55), channel_id=1, source_target_pairs={{64,0},{80,16},{96,32},{112,48},{128,64},{144,80},{160,96},{176,11... | collective-permute-start | bytes 344072 | tf_op jit(solution)/shard_map/ppermute | solution.py:86
  432.0 18.7 %copy-start.1 = (f32[64,64,64]{2,1,0:T(8,128)S(1)}, f32[64,64,64]{2,1,0:T(8,128)}, u32[]{:S(2)}) copy-start(f32[64,64,64]{2,1,0:T(8,128)} %copy-done) | copy-start | bytes 3145732
  432.0 16.6 %collective-permute-start.24 = (f32[64,64,7]{1,0,2:T(8,128)S(1)}, f32[64,64,7]{1,0,2:T(8,128)S(1)}, u32[]{:S(2)}, u32[]{:S(2)}) collective-permute-start(f32[64,64,7]{1,0,2:T(8,128)S(1)} %copy.53), channel_id=1, source_target_pairs={{0,64},{16,80},{32,96},{48,112},{64,128},{80,144},{96,160},{112,17... | collective-permute-start | bytes 344072 | tf_op jit(solution)/shard_map/ppermute | solution.py:85
  488.2 5.1 collective-permute-start.26
  507.5 6.1 collective-permute-start.27
  521.7 2.7 collective-permute-start.28
  525.0 14.3 %collective-permute-start.29 = (f32[64,2,2,4,64]{4,3,0,2,1:T(4,128)S(1)}, f32[64,2,2,4,64]{4,3,0,2,1:T(4,128)S(1)}, u32[]{:S(2)}, u32[]{:S(2)}) collective-permute-start(f32[64,2,2,4,64]{4,3,0,2,1:T(4,128)S(1)} %select_bitcast_fusion.9), channel_id=1, source_target_pairs={{0,4},{1,5},{2,6},{3,7},{4,0},{5,1},{6,2},{7,3},{8,12},{9,13},{10,... | collective-permute-start | bytes 786440 | tf_op jit(solution)/shard_map/ppermute | solution.py:110
  539.5 9.4 %collective-permute-start.30 = (f32[64,2,4,64]{3,2,0,1:T(4,128)S(1)}, f32[64,2,4,64]{3,2,0,1:T(4,128)S(1)}, u32[]{:S(2)}, u32[]{:S(2)}) collective-permute-start(f32[64,2,4,64]{3,2,0,1:T(4,128)S(1)} %select_bitcast_fusion.15), channel_id=1, source_target_pairs={{0,8},{1,9},{2,10},{3,11},{4,12},{5,13},{6,14},{7,15},{8,0},{9,1},... | collective-permute-start | bytes 393224 | tf_op jit(solution)/shard_map/ppermute | solution.py:110
  549.1 10.5 %collective-permute-start.31 = (f32[64,4,64]{2,1,0:T(4,128)S(1)}, f32[64,4,64]{2,1,0:T(4,128)S(1)}, u32[]{:S(2)}, u32[]{:S(2)}) collective-permute-start(f32[64,4,64]{2,1,0:T(4,128)S(1)} %select_bitcast_fusion.21), channel_id=1, source_target_pairs={{0,2},{1,3},{2,0},{3,1},{4,6},{5,7},{6,4},{7,5},{8,10},{9,11},{10,... | collective-permute-start | bytes 196616 | tf_op jit(solution)/shard_map/ppermute | solution.py:110
  560.4 10.4 %collective-permute-start.32 = (f32[64,4,64]{2,1,0:T(4,128)S(1)}, f32[64,4,64]{2,1,0:T(4,128)S(1)}, u32[]{:S(2)}, u32[]{:S(2)}) collective-permute-start(f32[64,4,64]{2,1,0:T(4,128)S(1)} %fusion.263), channel_id=1, source_target_pairs={{0,2},{1,3},{2,0},{3,1},{4,6},{5,7},{6,4},{7,5},{8,10},{9,11},{10,... | collective-permute-start | bytes 196616 | tf_op jit(solution)/shard_map/ppermute | solution.py:120
  570.9 10.4 %collective-permute-start.33 = (f32[64,2,4,64]{3,2,0,1:T(4,128)S(1)}, f32[64,2,4,64]{3,2,0,1:T(4,128)S(1)}, u32[]{:S(2)}, u32[]{:S(2)}) collective-permute-start(f32[64,2,4,64]{3,2,0,1:T(4,128)S(1)} %pad_maximum_fusion.31), channel_id=1, source_target_pairs={{0,8},{1,9},{2,10},{3,11},{4,12},{5,13},{6,14},{7,15},{8,0},{9,1},... | collective-permute-start | bytes 393224 | tf_op jit(solution)/shard_map/ppermute | solution.py:120
  581.6 9.3 %collective-permute-start.34 = (f32[64,2,2,4,64]{4,3,0,2,1:T(4,128)S(1)}, f32[64,2,2,4,64]{4,3,0,2,1:T(4,128)S(1)}, u32[]{:S(2)}, u32[]{:S(2)}) collective-permute-start(f32[64,2,2,4,64]{4,3,0,2,1:T(4,128)S(1)} %pad_maximum_fusion.29), channel_id=1, source_target_pairs={{0,4},{1,5},{2,6},{3,7},{4,0},{5,1},{6,2},{7,3},{8,12},{9,13},{10,... | collective-permute-start | bytes 786440 | tf_op jit(solution)/shard_map/ppermute | solution.py:120
  591.4 2.7 collective-permute-start.35
  595.4 5.4 collective-permute-start.36
  608.5 5.1 collective-permute-start.37
  625.2 8.1 collective-permute-start.39
  627.3 8.2 collective-permute-start.38
  686.7 8.8 %collective-permute-start.41 = (f32[64,64,7]{1,0,2:T(8,128)S(1)}, f32[64,64,7]{1,0,2:T(8,128)S(1)}, u32[]{:S(2)}, u32[]{:S(2)}) collective-permute-start(f32[64,64,7]{1,0,2:T(8,128)S(1)} %copy.71), channel_id=1, source_target_pairs={{64,0},{80,16},{96,32},{112,48},{128,64},{144,80},{160,96},{176,11... | collective-permute-start | bytes 344072 | tf_op jit(solution)/shard_map/ppermute | solution.py:86
  690.3 8.4 %collective-permute-start.40 = (f32[64,64,7]{1,0,2:T(8,128)S(1)}, f32[64,64,7]{1,0,2:T(8,128)S(1)}, u32[]{:S(2)}, u32[]{:S(2)}) collective-permute-start(f32[64,64,7]{1,0,2:T(8,128)S(1)} %copy.69), channel_id=1, source_target_pairs={{0,64},{16,80},{32,96},{48,112},{64,128},{80,144},{96,160},{112,17... | collective-permute-start | bytes 344072 | tf_op jit(solution)/shard_map/ppermute | solution.py:85
  738.3 5.1 collective-permute-start.42
  757.6 7.0 collective-permute-start.43
  772.7 2.7 collective-permute-start.44
  776.0 14.1 %collective-permute-start.45 = (f32[64,2,2,4,64]{4,3,0,2,1:T(4,128)S(1)}, f32[64,2,2,4,64]{4,3,0,2,1:T(4,128)S(1)}, u32[]{:S(2)}, u32[]{:S(2)}) collective-permute-start(f32[64,2,2,4,64]{4,3,0,2,1:T(4,128)S(1)} %select_bitcast_fusion.6), channel_id=1, source_target_pairs={{0,4},{1,5},{2,6},{3,7},{4,0},{5,1},{6,2},{7,3},{8,12},{9,13},{10,... | collective-permute-start | bytes 786440 | tf_op jit(solution)/shard_map/ppermute | solution.py:110
  790.3 9.1 %collective-permute-start.46 = (f32[64,2,4,64]{3,2,0,1:T(4,128)S(1)}, f32[64,2,4,64]{3,2,0,1:T(4,128)S(1)}, u32[]{:S(2)}, u32[]{:S(2)}) collective-permute-start(f32[64,2,4,64]{3,2,0,1:T(4,128)S(1)} %select_bitcast_fusion.12), channel_id=1, source_target_pairs={{0,8},{1,9},{2,10},{3,11},{4,12},{5,13},{6,14},{7,15},{8,0},{9,1},... | collective-permute-start | bytes 393224 | tf_op jit(solution)/shard_map/ppermute | solution.py:110
  799.5 11.2 %collective-permute-start.47 = (f32[64,4,64]{2,1,0:T(4,128)S(1)}, f32[64,4,64]{2,1,0:T(4,128)S(1)}, u32[]{:S(2)}, u32[]{:S(2)}) collective-permute-start(f32[64,4,64]{2,1,0:T(4,128)S(1)} %select_bitcast_fusion.18), channel_id=1, source_target_pairs={{0,2},{1,3},{2,0},{3,1},{4,6},{5,7},{6,4},{7,5},{8,10},{9,11},{10,... | collective-permute-start | bytes 196616 | tf_op jit(solution)/shard_map/ppermute | solution.py:110
  811.6 11.6 %collective-permute-start.48 = (f32[64,4,64]{2,1,0:T(4,128)S(1)}, f32[64,4,64]{2,1,0:T(4,128)S(1)}, u32[]{:S(2)}, u32[]{:S(2)}) collective-permute-start(f32[64,4,64]{2,1,0:T(4,128)S(1)} %get-tuple-element.54), channel_id=1, source_target_pairs={{0,48},{16,0},{32,16},{48,32},{64,112},{80,64},{96,80},{112,96},{1... | collective-permute-start | bytes 196616 | tf_op jit(solution)/shard_map/ppermute | solution.py:39
  813.7 9.5 %collective-permute-start.49 = (f32[64,4,64]{2,1,0:T(4,128)S(1)}, f32[64,4,64]{2,1,0:T(4,128)S(1)}, u32[]{:S(2)}, u32[]{:S(2)}) collective-permute-start(f32[64,4,64]{2,1,0:T(4,128)S(1)} %get-tuple-element.53), channel_id=1, source_target_pairs={{0,32},{16,48},{32,0},{48,16},{64,96},{80,112},{96,64},{112,80},{1... | collective-permute-start | bytes 196616 | tf_op jit(solution)/shard_map/ppermute | solution.py:39
  813.7 9.5 %collective-permute-start.50 = (f32[64,4,64]{2,1,0:T(4,128)S(1)}, f32[64,4,64]{2,1,0:T(4,128)S(1)}, u32[]{:S(2)}, u32[]{:S(2)}) collective-permute-start(f32[64,4,64]{2,1,0:T(4,128)S(1)} %get-tuple-element.5), channel_id=1, source_target_pairs={{0,16},{16,32},{32,48},{48,0},{64,80},{80,96},{96,112},{112,64},{1... | collective-permute-start | bytes 196616 | tf_op jit(solution)/shard_map/ppermute | solution.py:39
  823.4 8.4 %collective-permute-start.51 = (f32[64,4,64]{2,1,0:T(4,128)S(1)}, f32[64,4,64]{2,1,0:T(4,128)S(1)}, u32[]{:S(2)}, u32[]{:S(2)}) collective-permute-start(f32[64,4,64]{2,1,0:T(4,128)S(1)} %get-tuple-element.41), channel_id=1, source_target_pairs={{0,192},{16,208},{32,224},{48,240},{64,0},{80,16},{96,32},{112,48}... | collective-permute-start | bytes 196616 | tf_op jit(solution)/shard_map/ppermute | solution.py:50
  827.9 8.8 %collective-permute-start.52 = (f32[64,4,64]{2,1,0:T(4,128)S(1)}, f32[64,4,64]{2,1,0:T(4,128)S(1)}, u32[]{:S(2)}, u32[]{:S(2)}) collective-permute-start(f32[64,4,64]{2,1,0:T(4,128)S(1)} %get-tuple-element.40), channel_id=1, source_target_pairs={{0,128},{16,144},{32,160},{48,176},{64,192},{80,208},{96,224},{112... | collective-permute-start | bytes 196616 | tf_op jit(solution)/shard_map/ppermute | solution.py:50
  827.9 8.8 %collective-permute-start.53 = (f32[64,4,64]{2,1,0:T(4,128)S(1)}, f32[64,4,64]{2,1,0:T(4,128)S(1)}, u32[]{:S(2)}, u32[]{:S(2)}) collective-permute-start(f32[64,4,64]{2,1,0:T(4,128)S(1)} %get-tuple-element.39), channel_id=1, source_target_pairs={{0,64},{16,80},{32,96},{48,112},{64,128},{80,144},{96,160},{112,17... | collective-permute-start | bytes 196616 | tf_op jit(solution)/shard_map/ppermute | solution.py:50
  (2 other events, 4.4 us)

commit v2 on v1

--- a/solution.py
+++ b/solution.py
@@ -33,7 +33,7 @@
     zero = jnp.zeros_like(x)
     received = []
     for k in range(ROW):
-        part = jnp.where((dest_col - my_col) % ROW == k, x, zero)
+        part = jnp.where(((dest_col - my_col) % ROW == k) & (dest[me] >= 0), x, zero)
         if k:
             pairs = [(a * ROW + b, a * ROW + (b + k) % ROW) for a in range(rows) for b in range(ROW)]
             part = lax.ppermute(part, "space", pairs)
@@ -49,7 +49,7 @@
             pairs = [(a * ROW + c, ((a + j) % rows) * ROW + c) for a in range(rows) for c in range(ROW)]
             part = lax.ppermute(part, "space", pairs)
         src_row = src_of_me // ROW
-        result = jnp.where((my_row - src_row) % rows == j, part, result)
+        result = jnp.where(((my_row - src_row) % rows == j) & (src_of_me >= 0), part, result)
     return result
 
 
@@ -64,26 +64,31 @@
     return summed
 
 
-def pair_halo(volume, axis, radius, partner, is_high):
+def pair_halo(volume, axis, radius, nbr):
     length = volume.shape[axis]
+    me = lax.axis_index("space")
+    nsp = lax.axis_size("space")
+    lo_ids = nbr[:, 2 * axis]
+    partner = jnp.maximum(lo_ids, nbr[:, 2 * axis + 1])
+    is_high = lo_ids[me] >= 0
     first = lax.slice_in_dim(volume, 0, radius, axis=axis)
     last = lax.slice_in_dim(volume, length - radius, length, axis=axis)
     send = jnp.where(is_high, first, last)
-    nsp = lax.axis_size("space")
-    recv = lax.ppermute(send, "space", [(i, i ^ partner) for i in range(nsp)])
+    recv = route(send, partner, partner[me], nsp)
     zero = jnp.zeros_like(recv)
     low = jnp.where(is_high, recv, zero)
     high = jnp.where(is_high, zero, recv)
     return jnp.concatenate([low, volume, high], axis=axis)
 
 
-def z_halo(volume, axis, radius):
+def z_halo(volume, axis, radius, nbr):
     length = volume.shape[axis]
+    me = lax.axis_index("space")
     nsp = lax.axis_size("space")
     first = lax.slice_in_dim(volume, 0, radius, axis=axis)
     last = lax.slice_in_dim(volume, length - radius, length, axis=axis)
-    low = lax.ppermute(last, "space", [(i, i + ROW) for i in range(nsp - ROW)])
-    high = lax.ppermute(first, "space", [(i + ROW, i) for i in range(nsp - ROW)])
+    low = route(last, nbr[:, 2 * axis + 1], nbr[me, 2 * axis], nsp)
+    high = route(first, nbr[:, 2 * axis], nbr[me, 2 * axis + 1], nsp)
     return jnp.concatenate([low, volume, high], axis=axis)
 
 
@@ -138,26 +143,9 @@
     )
     nbr = table[:, :6]
     inside_all = table[:, 6]
-    cx = (nbr[:, 0] >= 0).astype(jnp.int32)
-    cy = (nbr[:, 2] >= 0).astype(jnp.int32)
-    cz = jnp.zeros_like(cx)
-    cur = nbr[:, 4]
-    for _ in range(nsp // ROW - 1):
-        cz = cz + (cur >= 0).astype(jnp.int32)
-        cur = jnp.where(cur >= 0, nbr[jnp.maximum(cur, 0), 4], -1)
-    ypos = jnp.where(cy == 0, cx, 3 - cx)
-    place = cz * ROW + ypos
-    ids = jnp.arange(nsp, dtype=jnp.int32)
-    brick_at = jnp.zeros_like(place).at[place].set(ids)
-    my_brick = brick_at[me]
-    keep = inside_all[my_brick] > 0
-    my_x = cx[my_brick]
-    my_y = cy[my_brick]
-
+    keep = inside_all[me] > 0
     share = estimate[0].reshape(side, estimate.shape[2] // side, side)
-    share = route(share, place, my_brick, nsp)
     recorded = measured[0, 0].reshape(side, side, side)
-    recorded = route(recorded, place, my_brick, nsp)
 
     radius_x = (kernel_x.shape[1] - 1) // 2
     radius_y = (kernel_y.shape[1] - 1) // 2
@@ -167,16 +155,15 @@
     along_z = normalized(kernel_z[0])
     for sweep_no in range(ITERS):
         full = view_all_gather(share, nv)
-        blurred = convolve(pair_halo(full, 0, radius_x, 1, my_x == 1), along_x, 0, False)
-        blurred = convolve(pair_halo(blurred, 1, radius_y, 3, my_y == 1), along_y, 1, False)
-        blurred = convolve(z_halo(blurred, 2, radius_z), along_z, 2, False)
+        blurred = convolve(pair_halo(full, 0, radius_x, nbr), along_x, 0, False)
+        blurred = convolve(pair_halo(blurred, 1, radius_y, nbr), along_y, 1, False)
+        blurred = convolve(z_halo(blurred, 2, radius_z, nbr), along_z, 2, False)
         quotient = recorded / blurred
-        spread = convolve(z_halo(quotient, 2, radius_z), along_z, 2, True)
-        spread = convolve(pair_halo(spread, 1, radius_y, 3, my_y == 1), along_y, 1, True)
-        spread = convolve(pair_halo(spread, 0, radius_x, 1, my_x == 1), along_x, 0, True)
+        spread = convolve(z_halo(quotient, 2, radius_z, nbr), along_z, 2, True)
+        spread = convolve(pair_halo(spread, 1, radius_y, nbr), along_y, 1, True)
+        spread = convolve(pair_halo(spread, 0, radius_x, nbr), along_x, 0, True)
         summed = view_reduce_scatter(spread, nv)
         share = share * jnp.where(keep, summed / (nv * measured.shape[0]), 1.0)
-    share = route(share, brick_at, place[me], nsp)
     return share.reshape(1, side, estimate.shape[2])
 
 

time: 849 us -> 1080 us (1.27)
  local copies, waits for them, and re-layouts: 75.1 us -> 251 us
  waiting for transfers between devices: 352 us -> 182 us
  starting transfers between devices: 126 us -> 231 us
  other arithmetic: 256 us -> 336 us
  between operations: 28.8 us -> 61.1 us
    ppermute x16 -> x0, waiting for transfers between devices: 207 us -> none  [the longest x8 94.6 us: pair_halo(): recv = lax.ppermute(send, 'space', [(i, i ^ partner) for i in range(nsp)])]
    ppermute x18 -> x96, starting transfers between devices: 27.2 us -> 179 us  [route(): part = lax.ppermute(part, 'space', pairs)]
    ppermute x8 -> x48, local copies, waits for them, and re-layouts: 18.4 us -> 122 us  [route(): part = lax.ppermute(part, 'space', pairs)]
    select_n x12 -> x32, other arithmetic: 8.03 us -> 63.1 us  [the longest x8 32.1 us: route(): jnp.where(((my_row - src_row) % rows == j) & (src_of_me >= 0), part, result)]
    select_n x8 -> x32, local copies, waits for them, and re-layouts: 12.1 us -> 61.4 us  [route(): part = jnp.where(d == target, data, part)]
    select_n x5 -> x20, other arithmetic: 11.1 us -> 59.7 us  [route(): part = jnp.where(d == target, data, part)]
    ppermute x16 -> x0, starting transfers between devices: 46.5 us -> none  [the longest x4 28.1 us: z_halo(): low = lax.ppermute(last, 'space', [(i, i + ROW) for i in range(nsp - ROW)])]
    select_n x8 -> x30, local copies, waits for them, and re-layouts: 8.79 us -> 54.3 us  [route(): jnp.where(((dest_col - my_col) % ROW == k) & (dest[me] >= 0), x, zero)]
  transfers between devices with their start and end apart: 54 -> 116, of which waited for: 34 -> 61; matrix products, arithmetic and copies ran while one was open for 10% -> 17% of each run, Pallas kernels for 0% -> 0%
where the time goes in v2:
time: 1080 us; the launch traced here: 1060 us
  other arithmetic  336 us (31%)
  local copies, waits for them, and re-layouts  251 us (23%)
  starting transfers between devices  231 us (21%)
  waiting for transfers between devices  182 us (17%)
  between operations  61.1 us (6%)
    ppermute x96, starting transfers between devices, route(): part = lax.ppermute(part, 'space', pairs)  179 us
    add x10, other arithmetic, convolve(): summed = term if summed is None else summed + term  132 us
    ppermute x48, local copies, waits for them, and re-layouts, route(): part = lax.ppermute(part, 'space', pairs)  122 us
    ppermute x96, waiting for transfers between devices, route(): part = lax.ppermute(part, 'space', pairs)  86.3 us
    select_n x32, local copies, waits for them, and re-layouts, route(): part = jnp.where(d == target, data, part)  61.4 us
    select_n x20, other arithmetic, route(): part = jnp.where(d == target, data, part)  59.7 us
    div x2, other arithmetic, shards(): quotient = recorded / blurred  59.5 us
    select_n x30, local copies, waits for them, and re-layouts, route(): jnp.where(((dest_col - my_col) % ROW == k) & (dest[me] >= 0), x, zero)  54.3 us
  transfers between devices with their start and end apart: 116, of which 61 were waited for; matrix products, arithmetic and copies ran while one was open for 17% of the time, Pallas kernels for 0%

profile of v2, /device:TPU:8, one launch (start us, length us, event | category | flops | bytes accessed | tf_op | source)
XLA Modules:
  0.0 1060.9 jit_solution(1964045410976320573)
XLA Ops:
  1.0 7.3 collective-permute-start.4
  8.2 3.6 collective-permute-done.4
  16.5 4.5 collective-permute-done.5
  24.6 8.8 collective-permute-done.6
  43.0 4.7 collective-permute-start.3
  85.8 6.6 fusion.45
  123.3 13.4 %fusion.101 = f32[64,64,64]{2,1,0:T(8,128)S(1)} fusion(f32[64,64,64]{2,1,0:T(8,128)} %copy-done.7, f32[64,3,64]{2,1,0:T(4,128)S(1)} %broadcast_select_fusion.14, f32[64,3,64]{2,1,0:T(4,128)S(1)} %get-tuple-element.29, f32[]{:T(128)} %bitcast.48, f32[]{:T(128)} %bitcast.47, f32[]{:T(128)} %bitcast.46, f32[]{:T(128)} %bitcast.45, f32[]{:T(128)} %bitcast.44, ...), kind=kLoop, calls=%fused_computation.175 | loop fusion | flops 4980736 | bytes 2195484 | tf_op jit(solution)/shard_map/add | solution.py:63
  136.7 4.9 slice_select_fusion.29
  167.5 7.1 select_select_fusion.29
  213.1 3.8 select_select_fusion.28
  236.7 7.3 select_select_fusion.25
  251.1 3.6 collective-permute-start.29
  271.8 3.6 select_select_fusion.24
  275.4 24.4 %fusion.223 = f32[64,64,64]{2,1,0:T(8,128)S(1)} fusion(f32[64,64,64]{2,1,0:T(8,128)S(1)} %copy-done.3, f32[64,64,7]{2,1,0:T(8,128)S(1)} %select_select_fusion.24, f32[64,64,64]{2,1,0:T(8,128)S(1)} %fusion.101, f32[64,64,7]{2,1,0:T(8,128)S(1)} %copy-done.8, f32[]{:T(128)} %bitcast.70, f32[]{:T(128)} %bitcast.69, f32[]{:T(128)} %bitcast.68, f32[]{:T(128)} %bitcast.67, ...), kind=kLoop, calls=%fused_computation.376 | loop fusion | flops 11534336 | bytes 3375164 | tf_op jit(solution)/shard_map/div | solution.py:161
  299.9 4.4 slice_select_fusion.21
  322.3 7.1 select_select_fusion.21
  349.8 4.6 collective-permute-start.38
  363.4 3.9 select_select_fusion.20
  380.5 7.3 select_select_fusion.17
  409.3 4.7 select_select_fusion.16
  414.0 36.1 %fusion.190 = f32[64,64,64]{2,1,0:T(8,128)} fusion(f32[64,64,7]{2,1,0:T(8,128)} %select_select_fusion.16, f32[64,64,64]{2,1,0:T(8,128)S(1)} %copy-done.2, f32[64,64,7]{2,1,0:T(8,128)} %get-tuple-element.81, f32[]{:T(128)} %bitcast.70, f32[]{:T(128)} %bitcast.69, f32[]{:T(128)} %bitcast.68, f32[]{:T(128)} %bitcast.67, f32[]{:T(128)} %bitcast.66, ...), kind=kLoop, calls=%fused_computation.321 | loop fusion | flops 11272192 | bytes 2326588 | tf_op jit(solution)/shard_map/add | solution.py:63
  452.2 4.2 collective-permute-start.45
  472.1 6.7 fusion.87
  498.6 6.6 fusion.31
  511.0 12.5 %collective-permute-done.57 = f32[64,2,2,4,64]{4,3,0,2,1:T(4,128)S(1)} collective-permute-done((f32[64,2,2,4,64]{4,3,0,2,1:T(4,128)S(1)}, f32[64,2,2,4,64]{4,3,0,2,1:T(4,128)S(1)}, u32[]{:S(2)}, u32[]{:S(2)}) %collective-permute-start.57) | collective-permute-done | bytes 262176 | tf_op jit(solution)/shard_map/ppermute | solution.py:115
  527.0 6.0 collective-permute-done.58
  533.1 6.6 collective-permute-start.59
  540.3 3.8 collective-permute-done.59
  544.8 5.0 collective-permute-start.60
  549.8 4.0 collective-permute-done.60
  557.0 6.2 collective-permute-done.61
  565.0 8.2 collective-permute-done.62
  586.8 3.8 collective-permute-start.69
  599.5 6.6 fusion.17
  626.2 3.9 collective-permute-done.74
  631.5 6.7 fusion.73
  638.3 4.8 slice_select_fusion.13
  648.1 3.7 collective-permute-start.77
  664.4 7.1 select_select_fusion.13
  690.4 4.1 collective-permute-start.82
  703.5 3.9 select_select_fusion.12
  720.8 7.2 select_select_fusion.9
  732.6 5.3 collective-permute-start.87
  750.5 4.9 collective-permute-done.86
  759.6 3.6 select_select_fusion.8
  763.2 35.0 %fusion.150 = f32[64,64,64]{2,1,0:T(8,128)S(1)} fusion(f32[64,64,64]{2,1,0:T(8,128)S(1)} %copy-done.4, f32[64,64,7]{2,1,0:T(8,128)S(1)} %select_select_fusion.8, f32[64,64,64]{2,1,0:T(8,128)} %copy-done, f32[64,64,7]{2,1,0:T(8,128)S(1)} %copy-done.9, f32[]{:T(128)} %bitcast.70, f32[]{:T(128)} %bitcast.69, f32[]{:T(128)} %bitcast.68, f32[]{:T(128)} %bitcast.67, ...), kind=kLoop, calls=%fused_computation.251 | loop fusion | flops 11534336 | bytes 3375164 | tf_op jit(solution)/shard_map/div | solution.py:161
  798.2 5.0 slice_select_fusion.5
  824.0 7.1 select_select_fusion.5
  850.0 3.5 collective-permute-start.94
  862.6 4.0 select_select_fusion.4
  880.4 7.2 select_select_fusion.1
  892.2 5.5 collective-permute-start.99
  903.6 3.7 collective-permute-done.99
  910.3 4.5 collective-permute-done.98
  919.0 4.7 select_select_fusion
  923.7 36.0 %fusion.117 = f32[64,64,64]{2,1,0:T(8,128)} fusion(f32[64,64,7]{2,1,0:T(8,128)} %select_select_fusion, f32[64,64,64]{2,1,0:T(8,128)S(1)} %fusion.150, f32[64,64,7]{2,1,0:T(8,128)} %get-tuple-element.63, f32[]{:T(128)} %bitcast.70, f32[]{:T(128)} %bitcast.69, f32[]{:T(128)} %bitcast.68, f32[]{:T(128)} %bitcast.67, f32[]{:T(128)} %bitcast.66, f32[]{:T(128)} %bitcast.59, ...), kind=kLoop, calls=%fused_computation.196 | loop fusion | flops 11272192 | bytes 2326588 | tf_op jit(solution)/shard_map/add | solution.py:63
  979.5 4.8 collective-permute-done.104
  985.7 6.7 fusion.59
  1013.8 6.6 fusion.3
  1026.2 12.4 %collective-permute-done.113 = f32[64,2,2,4,64]{4,3,0,2,1:T(4,128)S(1)} collective-permute-done((f32[64,2,2,4,64]{4,3,0,2,1:T(4,128)S(1)}, f32[64,2,2,4,64]{4,3,0,2,1:T(4,128)S(1)}, u32[]{:S(2)}, u32[]{:S(2)}) %collective-permute-start.113) | collective-permute-done | bytes 262176 | tf_op jit(solution)/shard_map/ppermute | solution.py:115
  1038.9 3.7 collective-permute-start.114
  1042.6 5.8 collective-permute-done.114
  1048.6 5.1 collective-permute-start.115
  1053.7 5.3 collective-permute-done.115
  (442 shorter events, 526.4 us)
Async XLA Ops:
  1.0 10.9 %collective-permute-start.4 = (f32[64,4,64]{2,1,0:T(4,128)S(1)}, f32[64,4,64]{2,1,0:T(4,128)S(1)}, u32[]{:S(2)}, u32[]{:S(2)}) collective-permute-start(f32[64,4,64]{2,1,0:T(4,128)S(1)} %reshape_squeeze.6), channel_id=1, source_target_pairs={{0,2},{1,3},{2,0},{3,1},{4,6},{5,7},{6,4},{7,5},{8,10},{9,11},{10,... | collective-permute-start | bytes 196616 | tf_op jit(solution)/shard_map/ppermute | solution.py:125
  12.0 9.0 collective-permute-start.5
  21.2 12.2 %collective-permute-start.6 = (f32[64,2,2,4,64]{4,3,0,2,1:T(4,128)S(1)}, f32[64,2,2,4,64]{4,3,0,2,1:T(4,128)S(1)}, u32[]{:S(2)}, u32[]{:S(2)}) collective-permute-start(f32[64,2,2,4,64]{4,3,0,2,1:T(4,128)S(1)} %pad_maximum_fusion.28), channel_id=1, source_target_pairs={{0,4},{1,5},{2,6},{3,7},{4,0},{5,1},{6,2},{7,3},{8,12},{9,13},{10,... | collective-permute-start | bytes 786440 | tf_op jit(solution)/shard_map/ppermute | solution.py:125
  22.9 11.1 %collective-permute-start = (s32[16,7]{1,0:T(8,128)S(1)}, s32[16,7]{1,0:T(8,128)S(1)}, u32[]{:S(2)}, u32[]{:S(2)}) collective-permute-start(s32[16,7]{1,0:T(8,128)S(1)} %broadcast_select_fusion.40), channel_id=1, source_target_pairs={{0,16},{16,0},{32,48},{48,32},{64,80},{80,64},{96,112},{112,96},{1... | collective-permute-start | bytes 1352 | tf_op jit(solution)/shard_map/ppermute | solution.py:23
  33.9 21.9 %collective-permute-start.7 = (f32[64,2,2,2,4,64]{5,4,0,3,1,2:T(4,128)S(1)}, f32[64,2,2,2,4,64]{5,4,0,3,1,2:T(4,128)}, u32[]{:S(2)}, u32[]{:S(2)}) collective-permute-start(f32[64,2,2,2,4,64]{5,4,0,3,1,2:T(4,128)S(1)} %pad_maximum_fusion.26), channel_id=1, source_target_pairs={{0,1},{1,0},{2,3},{3,2},{4,5},{5,4},{6,7},{7,6},{8,9},{9,8},{10,11... | collective-permute-start | bytes 1572872 | tf_op jit(solution)/shard_map/ppermute | solution.py:125
  58.6 17.4 %collective-permute-start.8 = (f32[3,64,64]{2,1,0:T(8,128)S(1)}, f32[3,64,64]{2,1,0:T(8,128)S(1)}, u32[]{:S(2)}, u32[]{:S(2)}) collective-permute-start(f32[3,64,64]{2,1,0:T(8,128)S(1)} %bitcast.167), channel_id=1, source_target_pairs={{0,48},{16,0},{32,16},{48,32},{64,112},{80,64},{96,80},{112,96},{1... | collective-permute-start | bytes 147464 | tf_op jit(solution)/shard_map/ppermute | solution.py:39
  59.1 16.9 %collective-permute-start.9 = (f32[3,64,64]{2,1,0:T(8,128)S(1)}, f32[3,64,64]{2,1,0:T(8,128)S(1)}, u32[]{:S(2)}, u32[]{:S(2)}) collective-permute-start(f32[3,64,64]{2,1,0:T(8,128)S(1)} %bitcast.166), channel_id=1, source_target_pairs={{0,32},{16,48},{32,0},{48,16},{64,96},{80,112},{96,64},{112,80},{1... | collective-permute-start | bytes 147464 | tf_op jit(solution)/shard_map/ppermute | solution.py:39
  61.7 14.4 %collective-permute-start.10 = (f32[3,64,64]{2,1,0:T(8,128)S(1)}, f32[3,64,64]{2,1,0:T(8,128)S(1)}, u32[]{:S(2)}, u32[]{:S(2)}) collective-permute-start(f32[3,64,64]{2,1,0:T(8,128)S(1)} %bitcast.165), channel_id=1, source_target_pairs={{0,16},{16,32},{32,48},{48,0},{64,80},{80,96},{96,112},{112,64},{1... | collective-permute-start | bytes 147464 | tf_op jit(solution)/shard_map/ppermute | solution.py:39
  94.5 12.7 %collective-permute-start.16 = (f32[64,3,64]{2,1,0:T(4,128)S(1)}, f32[64,3,64]{2,1,0:T(4,128)S(1)}, u32[]{:S(2)}, u32[]{:S(2)}) collective-permute-start(f32[64,3,64]{2,1,0:T(4,128)S(1)} %get-tuple-element.31), channel_id=1, source_target_pairs={{0,16},{16,32},{32,48},{48,0},{64,80},{80,96},{96,112},{112,64},{1... | collective-permute-start | bytes 147464 | tf_op jit(solution)/shard_map/ppermute | solution.py:39
  94.6 12.6 %collective-permute-start.15 = (f32[64,3,64]{2,1,0:T(4,128)S(1)}, f32[64,3,64]{2,1,0:T(4,128)S(1)}, u32[]{:S(2)}, u32[]{:S(2)}) collective-permute-start(f32[64,3,64]{2,1,0:T(4,128)S(1)} %get-tuple-element.139), channel_id=1, source_target_pairs={{0,32},{16,48},{32,0},{48,16},{64,96},{80,112},{96,64},{112,80},{1... | collective-permute-start | bytes 147464 | tf_op jit(solution)/shard_map/ppermute | solution.py:39
  96.9 10.3 collective-permute-start.14
  107.3 14.6 %collective-permute-start.19 = (f32[64,3,64]{2,1,0:T(4,128)S(1)}, f32[64,3,64]{2,1,0:T(4,128)S(1)}, u32[]{:S(2)}, u32[]{:S(2)}) collective-permute-start(f32[64,3,64]{2,1,0:T(4,128)S(1)} %get-tuple-element.112), channel_id=1, source_target_pairs={{0,64},{16,80},{32,96},{48,112},{64,128},{80,144},{96,160},{112,17... | collective-permute-start | bytes 147464 | tf_op jit(solution)/shard_map/ppermute | solution.py:50
  109.2 12.7 %collective-permute-start.18 = (f32[64,3,64]{2,1,0:T(4,128)S(1)}, f32[64,3,64]{2,1,0:T(4,128)S(1)}, u32[]{:S(2)}, u32[]{:S(2)}) collective-permute-start(f32[64,3,64]{2,1,0:T(4,128)S(1)} %get-tuple-element.113), channel_id=1, source_target_pairs={{0,128},{16,144},{32,160},{48,176},{64,192},{80,208},{96,224},{112... | collective-permute-start | bytes 147464 | tf_op jit(solution)/shard_map/ppermute | solution.py:50
  112.2 9.7 collective-permute-start.17
  146.2 14.1 %collective-permute-start.22 = (f32[64,64,7]{1,0,2:T(8,128)S(1)}, f32[64,64,7]{1,0,2:T(8,128)}, u32[]{:S(2)}, u32[]{:S(2)}) collective-permute-start(f32[64,64,7]{1,0,2:T(8,128)S(1)} %copy.81), channel_id=1, source_target_pairs={{0,16},{16,32},{32,48},{48,0},{64,80},{80,96},{96,112},{112,64},{1... | collective-permute-start | bytes 344072 | tf_op jit(solution)/shard_map/ppermute | solution.py:39
  146.7 16.7 %collective-permute-start.21 = (f32[64,64,7]{1,0,2:T(8,128)S(1)}, f32[64,64,7]{1,0,2:T(8,128)S(1)}, u32[]{:S(2)}, u32[]{:S(2)}) collective-permute-start(f32[64,64,7]{1,0,2:T(8,128)S(1)} %copy.80), channel_id=1, source_target_pairs={{0,32},{16,48},{32,0},{48,16},{64,96},{80,112},{96,64},{112,80},{1... | collective-permute-start | bytes 344072 | tf_op jit(solution)/shard_map/ppermute | solution.py:39
  152.0 13.5 %collective-permute-start.20 = (f32[64,64,7]{1,0,2:T(8,128)S(1)}, f32[64,64,7]{1,0,2:T(8,128)S(1)}, u32[]{:S(2)}, u32[]{:S(2)}) collective-permute-start(f32[64,64,7]{1,0,2:T(8,128)S(1)} %copy.79), channel_id=1, source_target_pairs={{0,48},{16,0},{32,16},{48,32},{64,112},{80,64},{96,80},{112,96},{1... | collective-permute-start | bytes 344072 | tf_op jit(solution)/shard_map/ppermute | solution.py:39
  180.1 24.0 %collective-permute-start.25 = (f32[64,64,7]{1,0,2:T(8,128)}, f32[64,64,7]{1,0,2:T(8,128)}, u32[]{:S(2)}, u32[]{:S(2)}) collective-permute-start(f32[64,64,7]{1,0,2:T(8,128)} %copy.93), channel_id=1, source_target_pairs={{0,64},{16,80},{32,96},{48,112},{64,128},{80,144},{96,160},{112,17... | collective-permute-start | bytes 344072 | tf_op jit(solution)/shard_map/ppermute | solution.py:50
  182.2 25.0 %collective-permute-start.24 = (f32[64,64,7]{1,0,2:T(8,128)S(1)}, f32[64,64,7]{1,0,2:T(8,128)}, u32[]{:S(2)}, u32[]{:S(2)}) collective-permute-start(f32[64,64,7]{1,0,2:T(8,128)S(1)} %copy.89), channel_id=1, source_target_pairs={{0,128},{16,144},{32,160},{48,176},{64,192},{80,208},{96,224},{112... | collective-permute-start | bytes 344072 | tf_op jit(solution)/shard_map/ppermute | solution.py:50
  185.2 25.0 %collective-permute-start.23 = (f32[64,64,7]{1,0,2:T(8,128)}, f32[64,64,7]{1,0,2:T(8,128)}, u32[]{:S(2)}, u32[]{:S(2)}) collective-permute-start(f32[64,64,7]{1,0,2:T(8,128)} %copy.85), channel_id=1, source_target_pairs={{0,192},{16,208},{32,224},{48,240},{64,0},{80,16},{96,32},{112,48}... | collective-permute-start | bytes 344072 | tf_op jit(solution)/shard_map/ppermute | solution.py:50
  201.9 29.8 %collective-permute-start.26 = (f32[64,64,7]{1,0,2:T(8,128)S(1)}, f32[64,64,7]{1,0,2:T(8,128)S(1)}, u32[]{:S(2)}, u32[]{:S(2)}) collective-permute-start(f32[64,64,7]{1,0,2:T(8,128)S(1)} %copy.100), channel_id=1, source_target_pairs={{0,48},{16,0},{32,16},{48,32},{64,112},{80,64},{96,80},{112,96},{1... | collective-permute-start | bytes 344072 | tf_op jit(solution)/shard_map/ppermute | solution.py:39
  203.3 26.3 %collective-permute-start.28 = (f32[64,64,7]{1,0,2:T(8,128)S(1)}, f32[64,64,7]{1,0,2:T(8,128)S(1)}, u32[]{:S(2)}, u32[]{:S(2)}) collective-permute-start(f32[64,64,7]{1,0,2:T(8,128)S(1)} %copy.102), channel_id=1, source_target_pairs={{0,16},{16,32},{32,48},{48,0},{64,80},{80,96},{96,112},{112,64},{1... | collective-permute-start | bytes 344072 | tf_op jit(solution)/shard_map/ppermute | solution.py:39
  219.3 14.5 %collective-permute-start.27 = (f32[64,64,7]{1,0,2:T(8,128)S(1)}, f32[64,64,7]{1,0,2:T(8,128)}, u32[]{:S(2)}, u32[]{:S(2)}) collective-permute-start(f32[64,64,7]{1,0,2:T(8,128)S(1)} %copy.101), channel_id=1, source_target_pairs={{0,32},{16,48},{32,0},{48,16},{64,96},{80,112},{96,64},{112,80},{1... | collective-permute-start | bytes 344072 | tf_op jit(solution)/shard_map/ppermute | solution.py:39
  251.1 18.7 %collective-permute-start.29 = (f32[64,64,7]{1,0,2:T(8,128)S(1)}, f32[64,64,7]{1,0,2:T(8,128)S(1)}, u32[]{:S(2)}, u32[]{:S(2)}) collective-permute-start(f32[64,64,7]{1,0,2:T(8,128)S(1)} %copy.106), channel_id=1, source_target_pairs={{0,192},{16,208},{32,224},{48,240},{64,0},{80,16},{96,32},{112,48}... | collective-permute-start | bytes 344072 | tf_op jit(solution)/shard_map/ppermute | solution.py:50
  254.6 13.1 %collective-permute-start.30 = (f32[64,64,7]{1,0,2:T(8,128)S(1)}, f32[64,64,7]{1,0,2:T(8,128)S(1)}, u32[]{:S(2)}, u32[]{:S(2)}) collective-permute-start(f32[64,64,7]{1,0,2:T(8,128)S(1)} %copy.110), channel_id=1, source_target_pairs={{0,128},{16,144},{32,160},{48,176},{64,192},{80,208},{96,224},{112... | collective-permute-start | bytes 344072 | tf_op jit(solution)/shard_map/ppermute | solution.py:50
  254.6 10.0 collective-permute-start.31
  334.7 19.7 %collective-permute-start.37 = (f32[64,64,7]{1,0,2:T(8,128)}, f32[64,64,7]{1,0,2:T(8,128)}, u32[]{:S(2)}, u32[]{:S(2)}) collective-permute-start(f32[64,64,7]{1,0,2:T(8,128)} %copy.135), channel_id=1, source_target_pairs={{0,64},{16,80},{32,96},{48,112},{64,128},{80,144},{96,160},{112,17... | collective-permute-start | bytes 344072 | tf_op jit(solution)/shard_map/ppermute | solution.py:50
  337.2 20.3 %collective-permute-start.36 = (f32[64,64,7]{1,0,2:T(8,128)S(1)}, f32[64,64,7]{1,0,2:T(8,128)}, u32[]{:S(2)}, u32[]{:S(2)}) collective-permute-start(f32[64,64,7]{1,0,2:T(8,128)S(1)} %copy.131), channel_id=1, source_target_pairs={{0,128},{16,144},{32,160},{48,176},{64,192},{80,208},{96,224},{112... | collective-permute-start | bytes 344072 | tf_op jit(solution)/shard_map/ppermute | solution.py:50
  342.3 18.1 %collective-permute-start.35 = (f32[64,64,7]{1,0,2:T(8,128)}, f32[64,64,7]{1,0,2:T(8,128)}, u32[]{:S(2)}, u32[]{:S(2)}) collective-permute-start(f32[64,64,7]{1,0,2:T(8,128)} %copy.127), channel_id=1, source_target_pairs={{0,192},{16,208},{32,224},{48,240},{64,0},{80,16},{96,32},{112,48}... | collective-permute-start | bytes 344072 | tf_op jit(solution)/shard_map/ppermute | solution.py:50
  349.8 24.2 %collective-permute-start.38 = (f32[64,64,7]{1,0,2:T(8,128)S(1)}, f32[64,64,7]{1,0,2:T(8,128)S(1)}, u32[]{:S(2)}, u32[]{:S(2)}) collective-permute-start(f32[64,64,7]{1,0,2:T(8,128)S(1)} %copy.142), channel_id=1, source_target_pairs={{0,48},{16,0},{32,16},{48,32},{64,112},{80,64},{96,80},{112,96},{1... | collective-permute-start | bytes 344072 | tf_op jit(solution)/shard_map/ppermute | solution.py:39
  354.4 17.6 %collective-permute-start.40 = (f32[64,64,7]{1,0,2:T(8,128)S(1)}, f32[64,64,7]{1,0,2:T(8,128)S(1)}, u32[]{:S(2)}, u32[]{:S(2)}) collective-permute-start(f32[64,64,7]{1,0,2:T(8,128)S(1)} %copy.144), channel_id=1, source_target_pairs={{0,16},{16,32},{32,48},{48,0},{64,80},{80,96},{96,112},{112,64},{1... | collective-permute-start | bytes 344072 | tf_op jit(solution)/shard_map/ppermute | solution.py:39
  393.3 11.9 %collective-permute-start.42 = (f32[64,64,7]{1,0,2:T(8,128)S(1)}, f32[64,64,7]{1,0,2:T(8,128)S(1)}, u32[]{:S(2)}, u32[]{:S(2)}) collective-permute-start(f32[64,64,7]{1,0,2:T(8,128)S(1)} %copy.152), channel_id=1, source_target_pairs={{0,128},{16,144},{32,160},{48,176},{64,192},{80,208},{96,224},{112... | collective-permute-start | bytes 344072 | tf_op jit(solution)/shard_map/ppermute | solution.py:50
  397.0 10.3 collective-permute-start.41
  509.4 14.1 %collective-permute-start.57 = (f32[64,2,2,4,64]{4,3,0,2,1:T(4,128)S(1)}, f32[64,2,2,4,64]{4,3,0,2,1:T(4,128)S(1)}, u32[]{:S(2)}, u32[]{:S(2)}) collective-permute-start(f32[64,2,2,4,64]{4,3,0,2,1:T(4,128)S(1)} %select_bitcast_fusion.9), channel_id=1, source_target_pairs={{0,4},{1,5},{2,6},{3,7},{4,0},{5,1},{6,2},{7,3},{8,12},{9,13},{10,... | collective-permute-start | bytes 786440 | tf_op jit(solution)/shard_map/ppermute | solution.py:115
  523.7 9.3 collective-permute-start.58
  533.1 10.9 %collective-permute-start.59 = (f32[64,4,64]{2,1,0:T(4,128)S(1)}, f32[64,4,64]{2,1,0:T(4,128)S(1)}, u32[]{:S(2)}, u32[]{:S(2)}) collective-permute-start(f32[64,4,64]{2,1,0:T(4,128)S(1)} %select_bitcast_fusion.21), channel_id=1, source_target_pairs={{0,2},{1,3},{2,0},{3,1},{4,6},{5,7},{6,4},{7,5},{8,10},{9,11},{10,... | collective-permute-start | bytes 196616 | tf_op jit(solution)/shard_map/ppermute | solution.py:115
  544.8 9.0 collective-permute-start.60
  553.9 9.3 collective-permute-start.61
  563.5 9.7 collective-permute-start.62
  620.6 9.5 collective-permute-start.74
  647.8 8.9 collective-permute-start.78
  648.1 11.6 %collective-permute-start.77 = (f32[64,64,7]{1,0,2:T(8,128)S(1)}, f32[64,64,7]{1,0,2:T(8,128)S(1)}, u32[]{:S(2)}, u32[]{:S(2)}) collective-permute-start(f32[64,64,7]{1,0,2:T(8,128)S(1)} %copy.178), channel_id=1, source_target_pairs={{0,32},{16,48},{32,0},{48,16},{64,96},{80,112},{96,64},{112,80},{1... | collective-permute-start | bytes 344072 | tf_op jit(solution)/shard_map/ppermute | solution.py:39
  676.8 17.8 %collective-permute-start.81 = (f32[64,64,7]{1,0,2:T(8,128)}, f32[64,64,7]{1,0,2:T(8,128)}, u32[]{:S(2)}, u32[]{:S(2)}) collective-permute-start(f32[64,64,7]{1,0,2:T(8,128)} %copy.191), channel_id=1, source_target_pairs={{0,64},{16,80},{32,96},{48,112},{64,128},{80,144},{96,160},{112,17... | collective-permute-start | bytes 344072 | tf_op jit(solution)/shard_map/ppermute | solution.py:50
  680.3 17.3 %collective-permute-start.80 = (f32[64,64,7]{1,0,2:T(8,128)S(1)}, f32[64,64,7]{1,0,2:T(8,128)}, u32[]{:S(2)}, u32[]{:S(2)}) collective-permute-start(f32[64,64,7]{1,0,2:T(8,128)S(1)} %copy.187), channel_id=1, source_target_pairs={{0,128},{16,144},{32,160},{48,176},{64,192},{80,208},{96,224},{112... | collective-permute-start | bytes 344072 | tf_op jit(solution)/shard_map/ppermute | solution.py:50
  684.3 16.2 %collective-permute-start.79 = (f32[64,64,7]{1,0,2:T(8,128)}, f32[64,64,7]{1,0,2:T(8,128)}, u32[]{:S(2)}, u32[]{:S(2)}) collective-permute-start(f32[64,64,7]{1,0,2:T(8,128)} %copy.183), channel_id=1, source_target_pairs={{0,192},{16,208},{32,224},{48,240},{64,0},{80,16},{96,32},{112,48}... | collective-permute-start | bytes 344072 | tf_op jit(solution)/shard_map/ppermute | solution.py:50
  690.4 24.1 %collective-permute-start.82 = (f32[64,64,7]{1,0,2:T(8,128)S(1)}, f32[64,64,7]{1,0,2:T(8,128)S(1)}, u32[]{:S(2)}, u32[]{:S(2)}) collective-permute-start(f32[64,64,7]{1,0,2:T(8,128)S(1)} %copy.198), channel_id=1, source_target_pairs={{0,48},{16,0},{32,16},{48,32},{64,112},{80,64},{96,80},{112,96},{1... | collective-permute-start | bytes 344072 | tf_op jit(solution)/shard_map/ppermute | solution.py:39
  694.5 17.9 %collective-permute-start.84 = (f32[64,64,7]{1,0,2:T(8,128)S(1)}, f32[64,64,7]{1,0,2:T(8,128)S(1)}, u32[]{:S(2)}, u32[]{:S(2)}) collective-permute-start(f32[64,64,7]{1,0,2:T(8,128)S(1)} %copy.200), channel_id=1, source_target_pairs={{0,16},{16,32},{32,48},{48,0},{64,80},{80,96},{96,112},{112,64},{1... | collective-permute-start | bytes 344072 | tf_op jit(solution)/shard_map/ppermute | solution.py:39
  732.6 14.9 %collective-permute-start.87 = (f32[64,64,7]{1,0,2:T(8,128)S(1)}, f32[64,64,7]{1,0,2:T(8,128)}, u32[]{:S(2)}, u32[]{:S(2)}) collective-permute-start(f32[64,64,7]{1,0,2:T(8,128)S(1)} %copy.212), channel_id=1, source_target_pairs={{0,64},{16,80},{32,96},{48,112},{64,128},{80,144},{96,160},{112,17... | collective-permute-start | bytes 344072 | tf_op jit(solution)/shard_map/ppermute | solution.py:50
  737.9 17.5 %collective-permute-start.86 = (f32[64,64,7]{1,0,2:T(8,128)S(1)}, f32[64,64,7]{1,0,2:T(8,128)S(1)}, u32[]{:S(2)}, u32[]{:S(2)}) collective-permute-start(f32[64,64,7]{1,0,2:T(8,128)S(1)} %copy.208), channel_id=1, source_target_pairs={{0,128},{16,144},{32,160},{48,176},{64,192},{80,208},{96,224},{112... | collective-permute-start | bytes 344072 | tf_op jit(solution)/shard_map/ppermute | solution.py:50
  743.7 13.8 %collective-permute-start.85 = (f32[64,64,7]{1,0,2:T(8,128)S(1)}, f32[64,64,7]{1,0,2:T(8,128)S(1)}, u32[]{:S(2)}, u32[]{:S(2)}) collective-permute-start(f32[64,64,7]{1,0,2:T(8,128)S(1)} %copy.204), channel_id=1, source_target_pairs={{0,192},{16,208},{32,224},{48,240},{64,0},{80,16},{96,32},{112,48}... | collective-permute-start | bytes 344072 | tf_op jit(solution)/shard_map/ppermute | solution.py:50
  808.0 11.6 %collective-permute-start.89 = (f32[64,64,7]{1,0,2:T(8,128)S(1)}, f32[64,64,7]{1,0,2:T(8,128)S(1)}, u32[]{:S(2)}, u32[]{:S(2)}) collective-permute-start(f32[64,64,7]{1,0,2:T(8,128)S(1)} %copy.220), channel_id=1, source_target_pairs={{0,32},{16,48},{32,0},{48,16},{64,96},{80,112},{96,64},{112,80},{1... | collective-permute-start | bytes 344072 | tf_op jit(solution)/shard_map/ppermute | solution.py:39
  836.4 17.1 %collective-permute-start.93 = (f32[64,64,7]{1,0,2:T(8,128)}, f32[64,64,7]{1,0,2:T(8,128)}, u32[]{:S(2)}, u32[]{:S(2)}) collective-permute-start(f32[64,64,7]{1,0,2:T(8,128)} %copy.233), channel_id=1, source_target_pairs={{0,64},{16,80},{32,96},{48,112},{64,128},{80,144},{96,160},{112,17... | collective-permute-start | bytes 344072 | tf_op jit(solution)/shard_map/ppermute | solution.py:50
  839.9 16.6 %collective-permute-start.92 = (f32[64,64,7]{1,0,2:T(8,128)S(1)}, f32[64,64,7]{1,0,2:T(8,128)}, u32[]{:S(2)}, u32[]{:S(2)}) collective-permute-start(f32[64,64,7]{1,0,2:T(8,128)S(1)} %copy.229), channel_id=1, source_target_pairs={{0,128},{16,144},{32,160},{48,176},{64,192},{80,208},{96,224},{112... | collective-permute-start | bytes 344072 | tf_op jit(solution)/shard_map/ppermute | solution.py:50
  843.9 15.6 %collective-permute-start.91 = (f32[64,64,7]{1,0,2:T(8,128)}, f32[64,64,7]{1,0,2:T(8,128)}, u32[]{:S(2)}, u32[]{:S(2)}) collective-permute-start(f32[64,64,7]{1,0,2:T(8,128)} %copy.225), channel_id=1, source_target_pairs={{0,192},{16,208},{32,224},{48,240},{64,0},{80,16},{96,32},{112,48}... | collective-permute-start | bytes 344072 | tf_op jit(solution)/shard_map/ppermute | solution.py:50
  850.0 24.1 %collective-permute-start.94 = (f32[64,64,7]{1,0,2:T(8,128)S(1)}, f32[64,64,7]{1,0,2:T(8,128)S(1)}, u32[]{:S(2)}, u32[]{:S(2)}) collective-permute-start(f32[64,64,7]{1,0,2:T(8,128)S(1)} %copy.240), channel_id=1, source_target_pairs={{0,48},{16,0},{32,16},{48,32},{64,112},{80,64},{96,80},{112,96},{1... | collective-permute-start | bytes 344072 | tf_op jit(solution)/shard_map/ppermute | solution.py:39
  853.6 18.4 %collective-permute-start.96 = (f32[64,64,7]{1,0,2:T(8,128)S(1)}, f32[64,64,7]{1,0,2:T(8,128)S(1)}, u32[]{:S(2)}, u32[]{:S(2)}) collective-permute-start(f32[64,64,7]{1,0,2:T(8,128)S(1)} %copy.242), channel_id=1, source_target_pairs={{0,16},{16,32},{32,48},{48,0},{64,80},{80,96},{96,112},{112,64},{1... | collective-permute-start | bytes 344072 | tf_op jit(solution)/shard_map/ppermute | solution.py:39
  892.2 15.1 %collective-permute-start.99 = (f32[64,64,7]{1,0,2:T(8,128)S(1)}, f32[64,64,7]{1,0,2:T(8,128)}, u32[]{:S(2)}, u32[]{:S(2)}) collective-permute-start(f32[64,64,7]{1,0,2:T(8,128)S(1)} %copy.254), channel_id=1, source_target_pairs={{0,64},{16,80},{32,96},{48,112},{64,128},{80,144},{96,160},{112,17... | collective-permute-start | bytes 344072 | tf_op jit(solution)/shard_map/ppermute | solution.py:50
  897.7 17.1 %collective-permute-start.98 = (f32[64,64,7]{1,0,2:T(8,128)S(1)}, f32[64,64,7]{1,0,2:T(8,128)S(1)}, u32[]{:S(2)}, u32[]{:S(2)}) collective-permute-start(f32[64,64,7]{1,0,2:T(8,128)S(1)} %copy.250), channel_id=1, source_target_pairs={{0,128},{16,144},{32,160},{48,176},{64,192},{80,208},{96,224},{112... | collective-permute-start | bytes 344072 | tf_op jit(solution)/shard_map/ppermute | solution.py:50
  903.5 13.4 %collective-permute-start.97 = (f32[64,64,7]{1,0,2:T(8,128)S(1)}, f32[64,64,7]{1,0,2:T(8,128)S(1)}, u32[]{:S(2)}, u32[]{:S(2)}) collective-permute-start(f32[64,64,7]{1,0,2:T(8,128)S(1)} %copy.246), channel_id=1, source_target_pairs={{0,192},{16,208},{32,224},{48,240},{64,0},{80,16},{96,32},{112,48}... | collective-permute-start | bytes 344072 | tf_op jit(solution)/shard_map/ppermute | solution.py:50
  974.9 9.4 collective-permute-start.104
  975.0 9.3 collective-permute-start.103
  1024.6 14.1 %collective-permute-start.113 = (f32[64,2,2,4,64]{4,3,0,2,1:T(4,128)S(1)}, f32[64,2,2,4,64]{4,3,0,2,1:T(4,128)S(1)}, u32[]{:S(2)}, u32[]{:S(2)}) collective-permute-start(f32[64,2,2,4,64]{4,3,0,2,1:T(4,128)S(1)} %select_bitcast_fusion.6), channel_id=1, source_target_pairs={{0,4},{1,5},{2,6},{3,7},{4,0},{5,1},{6,2},{7,3},{8,12},{9,13},{10,... | collective-permute-start | bytes 786440 | tf_op jit(solution)/shard_map/ppermute | solution.py:115
  1038.9 9.5 collective-permute-start.114
  1048.6 10.4 collective-permute-start.115
  (66 other events, 594.8 us)

commit v3 on v1

--- a/solution.py
+++ b/solution.py
@@ -154,9 +154,9 @@
     my_x = cx[my_brick]
     my_y = cy[my_brick]
 
-    share = estimate[0].reshape(side, estimate.shape[2] // side, side)
+    share = jnp.transpose(estimate[0].reshape(side, estimate.shape[2] // side, side), (2, 1, 0))
     share = route(share, place, my_brick, nsp)
-    recorded = measured[0, 0].reshape(side, side, side)
+    recorded = jnp.transpose(measured[0, 0].reshape(side, side, side), (2, 1, 0))
     recorded = route(recorded, place, my_brick, nsp)
 
     radius_x = (kernel_x.shape[1] - 1) // 2
@@ -167,17 +167,17 @@
     along_z = normalized(kernel_z[0])
     for sweep_no in range(ITERS):
         full = view_all_gather(share, nv)
-        blurred = convolve(pair_halo(full, 0, radius_x, 1, my_x == 1), along_x, 0, False)
+        blurred = convolve(pair_halo(full, 2, radius_x, 1, my_x == 1), along_x, 2, False)
         blurred = convolve(pair_halo(blurred, 1, radius_y, 3, my_y == 1), along_y, 1, False)
-        blurred = convolve(z_halo(blurred, 2, radius_z), along_z, 2, False)
+        blurred = convolve(z_halo(blurred, 0, radius_z), along_z, 0, False)
         quotient = recorded / blurred
-        spread = convolve(z_halo(quotient, 2, radius_z), along_z, 2, True)
+        spread = convolve(z_halo(quotient, 0, radius_z), along_z, 0, True)
         spread = convolve(pair_halo(spread, 1, radius_y, 3, my_y == 1), along_y, 1, True)
-        spread = convolve(pair_halo(spread, 0, radius_x, 1, my_x == 1), along_x, 0, True)
+        spread = convolve(pair_halo(spread, 2, radius_x, 1, my_x == 1), along_x, 2, True)
         summed = view_reduce_scatter(spread, nv)
         share = share * jnp.where(keep, summed / (nv * measured.shape[0]), 1.0)
     share = route(share, brick_at, place[me], nsp)
-    return share.reshape(1, side, estimate.shape[2])
+    return jnp.transpose(share, (2, 1, 0)).reshape(1, side, estimate.shape[2])
 
 
 def solution(mesh):

time: 849 us -> 793 us (0.934)
  other arithmetic: 256 us -> 203 us
  waiting for transfers between devices: 352 us -> 337 us
  local copies, waits for them, and re-layouts: 75.1 us -> 88.2 us
    ppermute x8, waiting for transfers between devices: 94.6 us -> 19.8 us  [pair_halo(): recv = lax.ppermute(send, 'space', [(i, i ^ partner) for i in range(nsp)])]
    ppermute x18, waiting for transfers between devices: 46.9 us -> 107 us  [route(): part = lax.ppermute(part, 'space', pairs)]
    div x2, other arithmetic: 78.7 us -> 31.6 us  [shards(): quotient = recorded / blurred]
    select_n x0 -> x8, local copies, waits for them, and re-layouts: none -> 23.3 us  [the longest x4 11.7 us: pair_halo(): low = jnp.where(is_high, recv, zero)]
    ppermute x8 -> x0, local copies, waits for them, and re-layouts: 18.4 us -> none  [the longest x4 9.33 us: z_halo(): lax.ppermute(first, 'space', [(i + ROW, i) for i in range(nsp - ROW)])]
    slice x8 -> x4, local copies, waits for them, and re-layouts: 16.7 us -> 0.94 us  [z_halo(): last = lax.slice_in_dim(volume, length - radius, length, axis=axis)]
    add x10, other arithmetic: 137 us -> 125 us  [convolve(): summed = term if summed is None else summed + term]
    select_n x2 -> x4, local copies, waits for them, and re-layouts: 0.04 us -> 10.5 us  [pair_halo(): send = jnp.where(is_high, first, last)]
  transfers between devices with their start and end apart: 54 -> 54, of which waited for: 34 -> 38; matrix products, arithmetic and copies ran while one was open for 10% -> 12% of each run, Pallas kernels for 0% -> 0%
where the time goes in v3:
time: 793 us; the launch traced here: 781 us
  waiting for transfers between devices  337 us (42%)
  other arithmetic  203 us (26%)
  starting transfers between devices  125 us (16%)
  local copies, waits for them, and re-layouts  88.2 us (11%)
  between operations  27.7 us (3%)
    add x10, other arithmetic, convolve(): summed = term if summed is None else summed + term  125 us
    ppermute x18, waiting for transfers between devices, route(): part = lax.ppermute(part, 'space', pairs)  107 us
    ppermute x4, waiting for transfers between devices, z_halo(): low = lax.ppermute(last, 'space', [(i, i + ROW) for i in range(nsp - ROW)])  90.8 us
    ppermute x8, waiting for transfers between devices, view_reduce_scatter(): x = keep + lax.ppermute(send, 'view', xor_pairs(nv, m))  50.6 us
    ppermute x8, waiting for transfers between devices, view_all_gather(): recv = lax.ppermute(x, 'view', xor_pairs(nv, m))  40.7 us
    div x2, other arithmetic, shards(): quotient = recorded / blurred  31.6 us
    ppermute x18, starting transfers between devices, route(): part = lax.ppermute(part, 'space', pairs)  29.7 us
    ppermute x4, starting transfers between devices, z_halo(): low = lax.ppermute(last, 'space', [(i, i + ROW) for i in range(nsp - ROW)])  23.6 us
  transfers between devices with their start and end apart: 54, of which 38 were waited for; matrix products, arithmetic and copies ran while one was open for 12% of the time, Pallas kernels for 0%

profile of v3, /device:TPU:8, one launch (start us, length us, event | category | flops | bytes accessed | tf_op | source)
XLA Modules:
  0.0 780.6 jit_solution(15618781576512617865)
XLA Ops:
  7.4 3.0 collective-permute-done.1
  14.1 3.1 collective-permute-start.3
  37.7 4.4 collective-permute-start.7
  49.4 8.3 %collective-permute-start.16 = (f32[64,4,64]{2,0,1:T(8,128)S(1)}, f32[64,4,64]{2,0,1:T(8,128)S(1)}, u32[]{:S(2)}, u32[]{:S(2)}) collective-permute-start(f32[64,4,64]{2,0,1:T(8,128)S(1)} %select_select_fusion.8), channel_id=1, source_target_pairs={{0,2},{1,3},{2,0},{3,1},{4,6},{5,7},{6,4},{7,5},{8,10},{9,11},{10,... | collective-permute-start | bytes 196616 | tf_op jit(solution)/shard_map/ppermute | solution.py:120
  57.7 3.0 collective-permute-done.16
  60.8 3.1 collective-permute-start.17
  65.9 5.8 collective-permute-done.17
  74.6 6.4 collective-permute-done.18
  87.2 3.3 copy.167
  92.5 4.1 select_select_fusion
  124.5 11.7 %fusion.45 = f32[64,64,64]{1,0,2:T(8,128)S(1)} fusion(f32[64,64,64]{1,0,2:T(8,128)} %copy-done.2, f32[64,64,3]{1,0,2:T(8,128)S(1)} %get-tuple-element.70, f32[64,64,3]{1,0,2:T(8,128)S(1)} %get-tuple-element.69, f32[]{:T(128)} %bitcast.61, f32[]{:T(128)} %bitcast.60, f32[]{:T(128)} %bitcast.59, f32[]{:T(128)} %bitcast.58, f32[]{:T(128)} %bitcast.57, ...), kind=kLoop, calls=%fused_computation.176 | loop fusion | flops 4980736 | bytes 2195484 | tf_op jit(solution)/shard_map/add | solution.py:63
  143.7 51.1 %collective-permute-done.10 = f32[64,64,64]{1,0,2:T(8,128)} collective-permute-done((f32[64,64,64]{1,0,2:T(8,128)}, f32[64,64,64]{1,0,2:T(8,128)}, u32[]{:S(2)}, u32[]{:S(2)}) %collective-permute-start.10) | collective-permute-done | bytes 1048608 | tf_op jit(solution)/shard_map/ppermute | solution.py:39
  194.8 5.1 collective-permute-done.12
  199.9 9.5 %fusion.265 = (f32[64,64,64]{1,0,2:T(8,128)}, f32[64,64,64]{1,0,2:T(8,128)}, f32[64,64,64]{1,0,2:T(8,128)}) fusion(f32[64,64,64]{1,0,2:T(8,128)} %collective-permute-done.10, f32[64,64,64]{1,0,2:T(8,128)} %collective-permute-done.11, f32[64,64,64]{1,0,2:T(8,128)} %collective-permute-done.12, f32[64,64,64]{1,2,0:T(8,128)} %copy.161, pred[]{:T(512)S(6)} %eq.285, ...), kind=kLoop, calls=%fused_computation.444 | loop fusion | flops 2359296 | bytes 9437193 | tf_op jit(solution)/shard_map/jit(_where)/select_n | solution.py:47
  215.0 2.9 copy.178
  217.9 2.9 copy.175
  220.8 15.2 %fusion.249 = f32[64,64,64]{1,0,2:T(8,128)S(1)} fusion(f32[64,3,64]{1,0,2:T(8,128)} %copy.178, f32[64,64,64]{1,0,2:T(8,128)S(1)} %fusion.45, f32[64,3,64]{1,0,2:T(8,128)} %copy.175, f32[]{:T(128)} %bitcast.66, f32[]{:T(128)} %bitcast.65, f32[]{:T(128)} %bitcast.64, f32[]{:T(128)} %bitcast.63, f32[]{:T(128)} %bitcast.62, f32[]{:T(128)} %bitcast.44, f32[]{:T(128)} %bitcast.33), kind=kLoop, calls=%fused_computation.416 | loop fusion | flops 4980736 | bytes 2195484 | tf_op jit(solution)/shard_map/add | solution.py:63
  239.5 5.3 collective-permute-start.22
  248.4 3.1 copy.162
  251.4 11.9 %collective-permute-done.23 = f32[7,64,64]{1,0,2:T(8,128)S(1)} collective-permute-done((f32[7,64,64]{1,0,2:T(8,128)}, f32[7,64,64]{1,0,2:T(8,128)S(1)}, u32[]{:S(2)}, u32[]{:S(2)}) %collective-permute-start.23) | collective-permute-done | bytes 114720 | tf_op jit(solution)/shard_map/ppermute | solution.py:86
  263.3 87.0 %collective-permute-done.22 = f32[7,64,64]{1,0,2:T(8,128)} collective-permute-done((f32[7,64,64]{1,0,2:T(8,128)}, f32[7,64,64]{1,0,2:T(8,128)}, u32[]{:S(2)}, u32[]{:S(2)}) %collective-permute-start.22) | collective-permute-done | bytes 114720 | tf_op jit(solution)/shard_map/ppermute | solution.py:85
  350.3 43.5 %collective-permute-done.14 = f32[64,64,64]{1,0,2:T(8,128)} collective-permute-done((f32[64,64,64]{1,0,2:T(8,128)}, f32[64,64,64]{1,0,2:T(8,128)}, u32[]{:S(2)}, u32[]{:S(2)}) %collective-permute-start.14) | collective-permute-done | bytes 1048608 | tf_op jit(solution)/shard_map/ppermute | solution.py:50
  393.8 17.4 %fusion.175 = (f32[64,64,64]{1,0,2:T(8,128)S(1)}, f32[64,64,64]{1,0,2:T(8,128)}) fusion(f32[64,64,64]{1,0,2:T(8,128)S(1)} %copy-done.1, f32[7,64,64]{1,0,2:T(8,128)S(1)} %collective-permute-done.23, f32[7,64,64]{1,0,2:T(8,128)} %collective-permute-done.22, f32[]{:T(128)} %bitcast.79, f32[]{:T(128)} %bitcast.78, f32[]{:T(128)} %bitcast.77, f32[]{:T(128)} %bitcast.76, ...), kind=kLoop, calls=%fused_computation.306 | loop fusion | flops 13369344 | bytes 10715203 | tf_op jit(solution)/shard_map/div | solution.py:173
  412.6 7.0 collective-permute-start.24
  419.6 3.0 collective-permute-done.25
  423.8 14.1 %fusion.136 = f32[64,64,64]{1,0,2:T(8,128)S(1)} fusion(f32[64,64,64]{1,0,2:T(8,128)S(1)} %get-tuple-element.7, f32[7,64,64]{1,0,2:T(8,128)S(1)} %collective-permute-done.25, f32[7,64,64]{1,0,2:T(8,128)S(1)} %collective-permute-done.24, f32[]{:T(128)} %bitcast.79, f32[]{:T(128)} %bitcast.78, f32[]{:T(128)} %bitcast.77, f32[]{:T(128)} %bitcast.76, ...), kind=kLoop, calls=%fused_computation.267 | loop fusion | flops 11272192 | bytes 2326588 | tf_op jit(solution)/shard_map/add | solution.py:63
  443.1 3.7 collective-permute-start.26
  453.0 2.9 copy.182
  455.9 15.3 %fusion.237 = f32[64,64,64]{1,0,2:T(8,128)S(1)} fusion(f32[64,3,64]{1,0,2:T(8,128)} %copy.185, f32[64,64,64]{1,0,2:T(8,128)S(1)} %fusion.136, f32[64,3,64]{1,0,2:T(8,128)} %copy.182, f32[]{:T(128)} %bitcast.66, f32[]{:T(128)} %bitcast.65, f32[]{:T(128)} %bitcast.64, f32[]{:T(128)} %bitcast.63, f32[]{:T(128)} %bitcast.62, f32[]{:T(128)} %bitcast.44, f32[]{:T(128)} %bitcast.33), kind=kLoop, calls=%fused_computation.393 | loop fusion | flops 4980736 | bytes 2195484 | tf_op jit(solution)/shard_map/add | solution.py:63
  477.8 6.1 fusion.31
  483.9 3.1 copy.186
  493.9 12.2 %collective-permute-done.29 = f32[64,2,2,4,64]{4,0,3,2,1:T(8,128)S(1)} collective-permute-done((f32[64,2,2,4,64]{4,0,3,2,1:T(8,128)S(1)}, f32[64,2,2,4,64]{4,0,3,2,1:T(8,128)S(1)}, u32[]{:S(2)}, u32[]{:S(2)}) %collective-permute-start.29) | collective-permute-done | bytes 262176 | tf_op jit(solution)/shard_map/ppermute | solution.py:110
  506.3 3.4 collective-permute-start.30
  509.7 5.8 collective-permute-done.30
  515.6 6.0 collective-permute-start.31
  522.2 3.9 collective-permute-done.31
  526.7 6.5 collective-permute-start.32
  533.2 3.9 collective-permute-done.32
  537.9 9.8 %collective-permute-done.33 = f32[64,2,4,64]{3,0,2,1:T(8,128)S(1)} collective-permute-done((f32[64,2,4,64]{3,0,2,1:T(8,128)S(1)}, f32[64,2,4,64]{3,0,2,1:T(8,128)S(1)}, u32[]{:S(2)}, u32[]{:S(2)}) %collective-permute-start.33) | collective-permute-done | bytes 131104 | tf_op jit(solution)/shard_map/ppermute | solution.py:120
  547.9 9.2 %collective-permute-done.34 = f32[64,2,2,4,64]{4,0,3,2,1:T(8,128)S(1)} collective-permute-done((f32[64,2,2,4,64]{4,0,3,2,1:T(8,128)S(1)}, f32[64,2,2,4,64]{4,0,3,2,1:T(8,128)S(1)}, u32[]{:S(2)}, u32[]{:S(2)}) %collective-permute-start.34) | collective-permute-done | bytes 262176 | tf_op jit(solution)/shard_map/ppermute | solution.py:120
  562.1 3.3 copy.190
  568.2 3.1 collective-permute-done.36
  572.0 11.4 %fusion.17 = f32[64,64,64]{1,0,2:T(8,128)S(1)} fusion(f32[64,64,64]{1,0,2:T(8,128)} %copy-done.3, f32[64,64,3]{1,0,2:T(8,128)S(1)} %get-tuple-element.62, f32[64,64,3]{1,0,2:T(8,128)S(1)} %get-tuple-element.61, f32[]{:T(128)} %bitcast.61, f32[]{:T(128)} %bitcast.60, f32[]{:T(128)} %bitcast.59, f32[]{:T(128)} %bitcast.58, f32[]{:T(128)} %bitcast.57, ...), kind=kLoop, calls=%fused_computation.148 | loop fusion | flops 4980736 | bytes 2195484 | tf_op jit(solution)/shard_map/add | solution.py:63
  588.7 4.6 collective-permute-done.37
  594.0 2.9 copy.201
  596.9 2.9 copy.198
  599.9 15.4 %fusion.225 = f32[64,64,64]{1,0,2:T(8,128)S(1)} fusion(f32[64,3,64]{1,0,2:T(8,128)} %copy.201, f32[64,64,64]{1,0,2:T(8,128)S(1)} %fusion.17, f32[64,3,64]{1,0,2:T(8,128)} %copy.198, f32[]{:T(128)} %bitcast.66, f32[]{:T(128)} %bitcast.65, f32[]{:T(128)} %bitcast.64, f32[]{:T(128)} %bitcast.63, f32[]{:T(128)} %bitcast.62, f32[]{:T(128)} %bitcast.44, f32[]{:T(128)} %bitcast.33), kind=kLoop, calls=%fused_computation.370 | loop fusion | flops 4980736 | bytes 2195484 | tf_op jit(solution)/shard_map/add | solution.py:63
  616.6 6.4 collective-permute-start.38
  627.0 14.2 %fusion.98 = f32[64,64,64]{1,0,2:T(8,128)S(1)} fusion(f32[64,64,64]{1,0,2:T(8,128)S(1)} %copy-done.4, f32[64,64,64]{1,0,2:T(8,128)S(1)} %fusion.225, f32[7,64,64]{1,0,2:T(8,128)S(1)} %collective-permute-done.39, f32[7,64,64]{1,0,2:T(8,128)S(1)} %collective-permute-done.38, f32[]{:T(128)} %bitcast.79, f32[]{:T(128)} %bitcast.78, f32[]{:T(128)} %bitcast.77, ...), kind=kLoop, calls=%fused_computation.229 | loop fusion | flops 11534336 | bytes 3375164 | tf_op jit(solution)/shard_map/div | solution.py:173
  642.6 5.0 collective-permute-start.40
  651.4 14.1 %fusion.59 = f32[64,64,64]{1,0,2:T(8,128)S(1)} fusion(f32[64,64,64]{1,0,2:T(8,128)S(1)} %fusion.98, f32[7,64,64]{1,0,2:T(8,128)S(1)} %collective-permute-done.41, f32[7,64,64]{1,0,2:T(8,128)S(1)} %collective-permute-done.40, f32[]{:T(128)} %bitcast.79, f32[]{:T(128)} %bitcast.78, f32[]{:T(128)} %bitcast.77, f32[]{:T(128)} %bitcast.76, f32[]{:T(128)} %bitcast.75, ...), kind=kLoop, calls=%fused_computation.190 | loop fusion | flops 11272192 | bytes 2326588 | tf_op jit(solution)/shard_map/add | solution.py:63
  671.2 4.3 collective-permute-done.42
  679.1 2.9 copy.205
  682.0 15.3 %fusion.213 = f32[64,64,64]{1,0,2:T(8,128)S(1)} fusion(f32[64,3,64]{1,0,2:T(8,128)} %copy.208, f32[64,64,64]{1,0,2:T(8,128)S(1)} %fusion.59, f32[64,3,64]{1,0,2:T(8,128)} %copy.205, f32[]{:T(128)} %bitcast.66, f32[]{:T(128)} %bitcast.65, f32[]{:T(128)} %bitcast.64, f32[]{:T(128)} %bitcast.63, f32[]{:T(128)} %bitcast.62, f32[]{:T(128)} %bitcast.44, f32[]{:T(128)} %bitcast.33), kind=kLoop, calls=%fused_computation.347 | loop fusion | flops 4980736 | bytes 2195484 | tf_op jit(solution)/shard_map/add | solution.py:63
  698.0 4.2 collective-permute-start.43
  705.4 6.1 fusion.3
  711.5 3.1 copy.209
  719.8 14.0 %collective-permute-done.45 = f32[64,2,2,4,64]{4,0,3,2,1:T(8,128)S(1)} collective-permute-done((f32[64,2,2,4,64]{4,0,3,2,1:T(8,128)S(1)}, f32[64,2,2,4,64]{4,0,3,2,1:T(8,128)S(1)}, u32[]{:S(2)}, u32[]{:S(2)}) %collective-permute-start.45) | collective-permute-done | bytes 262176 | tf_op jit(solution)/shard_map/ppermute | solution.py:110
  733.9 2.9 collective-permute-start.46
  736.8 6.2 collective-permute-done.46
  743.1 5.8 collective-permute-start.47
  748.8 3.3 collective-permute-done.47
  764.4 6.6 collective-permute-start.51
  774.8 4.6 collective-permute-done.52
  (202 shorter events, 163.2 us)
Async XLA Ops:
  1.5 3.8 collective-permute-start
  5.3 5.1 collective-permute-start.1
  10.5 3.6 collective-permute-start.2
  14.1 4.7 collective-permute-start.3
  26.7 10.9 %collective-permute-start.4 = (f32[64,4,64]{2,0,1:T(8,128)S(1)}, f32[64,4,64]{2,0,1:T(8,128)S(1)}, u32[]{:S(2)}, u32[]{:S(2)}) collective-permute-start(f32[64,4,64]{2,0,1:T(8,128)S(1)} %bitcast.250), channel_id=1, source_target_pairs={{0,48},{16,0},{32,16},{48,32},{64,112},{80,64},{96,80},{112,96},{1... | collective-permute-start | bytes 196616 | tf_op jit(solution)/shard_map/ppermute | solution.py:39
  28.7 8.9 %collective-permute-start.5 = (f32[64,4,64]{2,0,1:T(8,128)S(1)}, f32[64,4,64]{2,0,1:T(8,128)S(1)}, u32[]{:S(2)}, u32[]{:S(2)}) collective-permute-start(f32[64,4,64]{2,0,1:T(8,128)S(1)} %bitcast.251), channel_id=1, source_target_pairs={{0,32},{16,48},{32,0},{48,16},{64,96},{80,112},{96,64},{112,80},{1... | collective-permute-start | bytes 196616 | tf_op jit(solution)/shard_map/ppermute | solution.py:39
  30.1 7.6 collective-permute-start.6
  34.9 29.0 %copy-start.5 = (f32[1,7]{1,0:T(1,128)S(1)}, f32[1,7]{1,0:T(1,128)}, u32[]{:S(2)}) copy-start(f32[1,7]{1,0:T(1,128)} %param.9) | copy-start | bytes 88
  35.5 29.0 %copy-start.6 = (f32[1,7]{1,0:T(1,128)S(1)}, f32[1,7]{1,0:T(1,128)}, u32[]{:S(2)}) copy-start(f32[1,7]{1,0:T(1,128)} %param.10) | copy-start | bytes 88
  36.1 29.1 %copy-start.7 = (f32[1,15]{1,0:T(1,128)S(1)}, f32[1,15]{1,0:T(1,128)}, u32[]{:S(2)}) copy-start(f32[1,15]{1,0:T(1,128)} %param.11) | copy-start | bytes 184
  37.7 9.4 %collective-permute-start.7 = (f32[64,4,64]{2,0,1:T(8,128)S(1)}, f32[64,4,64]{2,0,1:T(8,128)S(1)}, u32[]{:S(2)}, u32[]{:S(2)}) collective-permute-start(f32[64,4,64]{2,0,1:T(8,128)S(1)} %get-tuple-element.48), channel_id=1, source_target_pairs={{0,192},{16,208},{32,224},{48,240},{64,0},{80,16},{96,32},{112,48}... | collective-permute-start | bytes 196616 | tf_op jit(solution)/shard_map/ppermute | solution.py:50
  42.1 7.3 collective-permute-start.8
  42.1 7.3 collective-permute-start.9
  49.4 11.3 %collective-permute-start.16 = (f32[64,4,64]{2,0,1:T(8,128)S(1)}, f32[64,4,64]{2,0,1:T(8,128)S(1)}, u32[]{:S(2)}, u32[]{:S(2)}) collective-permute-start(f32[64,4,64]{2,0,1:T(8,128)S(1)} %select_select_fusion.8), channel_id=1, source_target_pairs={{0,2},{1,3},{2,0},{3,1},{4,6},{5,7},{6,4},{7,5},{8,10},{9,11},{10,... | collective-permute-start | bytes 196616 | tf_op jit(solution)/shard_map/ppermute | solution.py:120
  60.8 10.8 %collective-permute-start.17 = (f32[64,2,4,64]{3,0,2,1:T(8,128)S(1)}, f32[64,2,4,64]{3,0,2,1:T(8,128)S(1)}, u32[]{:S(2)}, u32[]{:S(2)}) collective-permute-start(f32[64,2,4,64]{3,0,2,1:T(8,128)S(1)} %pad_maximum_fusion.30), channel_id=1, source_target_pairs={{0,8},{1,9},{2,10},{3,11},{4,12},{5,13},{6,14},{7,15},{8,0},{9,1},... | collective-permute-start | bytes 393224 | tf_op jit(solution)/shard_map/ppermute | solution.py:120
  71.8 9.3 %collective-permute-start.18 = (f32[64,2,2,4,64]{4,0,3,2,1:T(8,128)S(1)}, f32[64,2,2,4,64]{4,0,3,2,1:T(8,128)S(1)}, u32[]{:S(2)}, u32[]{:S(2)}) collective-permute-start(f32[64,2,2,4,64]{4,0,3,2,1:T(8,128)S(1)} %pad_maximum_fusion.28), channel_id=1, source_target_pairs={{0,4},{1,5},{2,6},{3,7},{4,0},{5,1},{6,2},{7,3},{8,12},{9,13},{10,... | collective-permute-start | bytes 786440 | tf_op jit(solution)/shard_map/ppermute | solution.py:120
  82.2 3.3 collective-permute-start.19
  90.5 6.1 copy-start.2
  91.2 32.7 %collective-permute-start.20 = (f32[64,64,3]{1,0,2:T(8,128)S(1)}, f32[64,64,3]{1,0,2:T(8,128)S(1)}, u32[]{:S(2)}, u32[]{:S(2)}) collective-permute-start(f32[64,64,3]{1,0,2:T(8,128)S(1)} %slice_select_fusion.7), channel_id=1, source_target_pairs={{0,16},{16,0},{32,48},{48,32},{64,80},{80,64},{96,112},{112,96},{1... | collective-permute-start | bytes 147464 | tf_op jit(solution)/shard_map/ppermute | solution.py:73
  101.1 93.7 %collective-permute-start.10 = (f32[64,64,64]{1,0,2:T(8,128)}, f32[64,64,64]{1,0,2:T(8,128)}, u32[]{:S(2)}, u32[]{:S(2)}) collective-permute-start(f32[64,64,64]{1,0,2:T(8,128)} %bitcast.242), channel_id=1, source_target_pairs={{0,48},{16,0},{32,16},{48,32},{64,112},{80,64},{96,80},{112,96},{1... | collective-permute-start | bytes 3145736 | tf_op jit(solution)/shard_map/ppermute | solution.py:39
  106.0 88.8 %collective-permute-start.11 = (f32[64,64,64]{1,0,2:T(8,128)}, f32[64,64,64]{1,0,2:T(8,128)}, u32[]{:S(2)}, u32[]{:S(2)}) collective-permute-start(f32[64,64,64]{1,0,2:T(8,128)} %bitcast.243), channel_id=1, source_target_pairs={{0,32},{16,48},{32,0},{48,16},{64,96},{80,112},{96,64},{112,80},{1... | collective-permute-start | bytes 3145736 | tf_op jit(solution)/shard_map/ppermute | solution.py:39
  111.1 88.7 %collective-permute-start.12 = (f32[64,64,64]{1,0,2:T(8,128)}, f32[64,64,64]{1,0,2:T(8,128)}, u32[]{:S(2)}, u32[]{:S(2)}) collective-permute-start(f32[64,64,64]{1,0,2:T(8,128)} %bitcast.244), channel_id=1, source_target_pairs={{0,16},{16,32},{32,48},{48,0},{64,80},{80,96},{96,112},{112,64},{1... | collective-permute-start | bytes 3145736 | tf_op jit(solution)/shard_map/ppermute | solution.py:39
  141.5 72.8 %collective-permute-start.21 = (f32[64,3,64]{2,0,1:T(8,128)S(1)}, f32[64,3,64]{2,0,1:T(8,128)S(1)}, u32[]{:S(2)}, u32[]{:S(2)}) collective-permute-start(f32[64,3,64]{2,0,1:T(8,128)S(1)} %copy.172), channel_id=1, source_target_pairs={{0,48},{16,32},{32,16},{48,0},{64,112},{80,96},{96,80},{112,64},{1... | collective-permute-start | bytes 147464 | tf_op jit(solution)/shard_map/ppermute | solution.py:73
  209.4 140.9 %collective-permute-start.13 = (f32[64,64,64]{1,0,2:T(8,128)}, f32[64,64,64]{1,0,2:T(8,128)}, u32[]{:S(2)}, u32[]{:S(2)}) collective-permute-start(f32[64,64,64]{1,0,2:T(8,128)} %get-tuple-element.11), channel_id=1, source_target_pairs={{0,192},{16,208},{32,224},{48,240},{64,0},{80,16},{96,32},{112,48}... | collective-permute-start | bytes 3145736 | tf_op jit(solution)/shard_map/ppermute | solution.py:50
  210.3 183.5 %collective-permute-start.14 = (f32[64,64,64]{1,0,2:T(8,128)}, f32[64,64,64]{1,0,2:T(8,128)}, u32[]{:S(2)}, u32[]{:S(2)}) collective-permute-start(f32[64,64,64]{1,0,2:T(8,128)} %get-tuple-element.10), channel_id=1, source_target_pairs={{0,128},{16,144},{32,160},{48,176},{64,192},{80,208},{96,224},{112... | collective-permute-start | bytes 3145736 | tf_op jit(solution)/shard_map/ppermute | solution.py:50
  212.1 181.7 %collective-permute-start.15 = (f32[64,64,64]{1,0,2:T(8,128)}, f32[64,64,64]{1,0,2:T(8,128)}, u32[]{:S(2)}, u32[]{:S(2)}) collective-permute-start(f32[64,64,64]{1,0,2:T(8,128)} %get-tuple-element.9), channel_id=1, source_target_pairs={{0,64},{16,80},{32,96},{48,112},{64,128},{80,144},{96,160},{112,17... | collective-permute-start | bytes 3145736 | tf_op jit(solution)/shard_map/ppermute | solution.py:50
  236.1 1.3 copy-start
  238.2 25.1 %collective-permute-start.23 = (f32[7,64,64]{1,0,2:T(8,128)}, f32[7,64,64]{1,0,2:T(8,128)S(1)}, u32[]{:S(2)}, u32[]{:S(2)}) collective-permute-start(f32[7,64,64]{1,0,2:T(8,128)} %get-tuple-element.25), channel_id=1, source_target_pairs={{64,0},{80,16},{96,32},{112,48},{128,64},{144,80},{160,96},{176,11... | collective-permute-start | bytes 344072 | tf_op jit(solution)/shard_map/ppermute | solution.py:86
  239.5 110.8 %collective-permute-start.22 = (f32[7,64,64]{1,0,2:T(8,128)}, f32[7,64,64]{1,0,2:T(8,128)}, u32[]{:S(2)}, u32[]{:S(2)}) collective-permute-start(f32[7,64,64]{1,0,2:T(8,128)} %get-tuple-element.24), channel_id=1, source_target_pairs={{0,64},{16,80},{32,96},{48,112},{64,128},{80,144},{96,160},{112,17... | collective-permute-start | bytes 344072 | tf_op jit(solution)/shard_map/ppermute | solution.py:85
  248.4 145.4 %copy-start.1 = (f32[64,64,64]{1,0,2:T(8,128)S(1)}, f32[64,64,64]{1,0,2:T(8,128)}, u32[]{:S(2)}) copy-start(f32[64,64,64]{1,0,2:T(8,128)} %copy-done) | copy-start | bytes 3145732
  411.3 11.3 %collective-permute-start.25 = (f32[7,64,64]{1,0,2:T(8,128)S(1)}, f32[7,64,64]{1,0,2:T(8,128)S(1)}, u32[]{:S(2)}, u32[]{:S(2)}) collective-permute-start(f32[7,64,64]{1,0,2:T(8,128)S(1)} %get-tuple-element.23), channel_id=1, source_target_pairs={{64,0},{80,16},{96,32},{112,48},{128,64},{144,80},{160,96},{176,11... | collective-permute-start | bytes 344072 | tf_op jit(solution)/shard_map/ppermute | solution.py:86
  412.6 11.2 %collective-permute-start.24 = (f32[7,64,64]{1,0,2:T(8,128)S(1)}, f32[7,64,64]{1,0,2:T(8,128)S(1)}, u32[]{:S(2)}, u32[]{:S(2)}) collective-permute-start(f32[7,64,64]{1,0,2:T(8,128)S(1)} %get-tuple-element.22), channel_id=1, source_target_pairs={{0,64},{16,80},{32,96},{48,112},{64,128},{80,144},{96,160},{112,17... | collective-permute-start | bytes 344072 | tf_op jit(solution)/shard_map/ppermute | solution.py:85
  443.1 6.3 collective-permute-start.26
  471.9 5.3 collective-permute-start.27
  488.9 2.7 collective-permute-start.28
  492.0 14.1 %collective-permute-start.29 = (f32[64,2,2,4,64]{4,0,3,2,1:T(8,128)S(1)}, f32[64,2,2,4,64]{4,0,3,2,1:T(8,128)S(1)}, u32[]{:S(2)}, u32[]{:S(2)}) collective-permute-start(f32[64,2,2,4,64]{4,0,3,2,1:T(8,128)S(1)} %select_bitcast_fusion.9), channel_id=1, source_target_pairs={{0,4},{1,5},{2,6},{3,7},{4,0},{5,1},{6,2},{7,3},{8,12},{9,13},{10,... | collective-permute-start | bytes 786440 | tf_op jit(solution)/shard_map/ppermute | solution.py:110
  506.3 9.2 %collective-permute-start.30 = (f32[64,2,4,64]{3,0,2,1:T(8,128)S(1)}, f32[64,2,4,64]{3,0,2,1:T(8,128)S(1)}, u32[]{:S(2)}, u32[]{:S(2)}) collective-permute-start(f32[64,2,4,64]{3,0,2,1:T(8,128)S(1)} %select_bitcast_fusion.15), channel_id=1, source_target_pairs={{0,8},{1,9},{2,10},{3,11},{4,12},{5,13},{6,14},{7,15},{8,0},{9,1},... | collective-permute-start | bytes 393224 | tf_op jit(solution)/shard_map/ppermute | solution.py:110
  515.6 10.5 %collective-permute-start.31 = (f32[64,4,64]{2,0,1:T(8,128)S(1)}, f32[64,4,64]{2,0,1:T(8,128)S(1)}, u32[]{:S(2)}, u32[]{:S(2)}) collective-permute-start(f32[64,4,64]{2,0,1:T(8,128)S(1)} %select_bitcast_fusion.21), channel_id=1, source_target_pairs={{0,2},{1,3},{2,0},{3,1},{4,6},{5,7},{6,4},{7,5},{8,10},{9,11},{10,... | collective-permute-start | bytes 196616 | tf_op jit(solution)/shard_map/ppermute | solution.py:110
  526.7 10.4 %collective-permute-start.32 = (f32[64,4,64]{2,0,1:T(8,128)S(1)}, f32[64,4,64]{2,0,1:T(8,128)S(1)}, u32[]{:S(2)}, u32[]{:S(2)}) collective-permute-start(f32[64,4,64]{2,0,1:T(8,128)S(1)} %fusion.275), channel_id=1, source_target_pairs={{0,2},{1,3},{2,0},{3,1},{4,6},{5,7},{6,4},{7,5},{8,10},{9,11},{10,... | collective-permute-start | bytes 196616 | tf_op jit(solution)/shard_map/ppermute | solution.py:120
  537.2 10.6 %collective-permute-start.33 = (f32[64,2,4,64]{3,0,2,1:T(8,128)S(1)}, f32[64,2,4,64]{3,0,2,1:T(8,128)S(1)}, u32[]{:S(2)}, u32[]{:S(2)}) collective-permute-start(f32[64,2,4,64]{3,0,2,1:T(8,128)S(1)} %pad_maximum_fusion.31), channel_id=1, source_target_pairs={{0,8},{1,9},{2,10},{3,11},{4,12},{5,13},{6,14},{7,15},{8,0},{9,1},... | collective-permute-start | bytes 393224 | tf_op jit(solution)/shard_map/ppermute | solution.py:120
  547.8 9.3 %collective-permute-start.34 = (f32[64,2,2,4,64]{4,0,3,2,1:T(8,128)S(1)}, f32[64,2,2,4,64]{4,0,3,2,1:T(8,128)S(1)}, u32[]{:S(2)}, u32[]{:S(2)}) collective-permute-start(f32[64,2,2,4,64]{4,0,3,2,1:T(8,128)S(1)} %pad_maximum_fusion.29), channel_id=1, source_target_pairs={{0,4},{1,5},{2,6},{3,7},{4,0},{5,1},{6,2},{7,3},{8,12},{9,13},{10,... | collective-permute-start | bytes 786440 | tf_op jit(solution)/shard_map/ppermute | solution.py:120
  557.3 2.7 collective-permute-start.35
  565.4 6.5 copy-start.3
  566.1 5.2 collective-permute-start.36
  588.6 4.7 collective-permute-start.37
  599.9 27.1 %copy-start.4 = (f32[64,64,64]{1,0,2:T(8,128)S(1)}, f32[64,64,64]{1,0,2:T(8,128)}, u32[]{:S(2)}) copy-start(f32[64,64,64]{1,0,2:T(8,128)} %get-tuple-element.8) | copy-start | bytes 3145732
  615.3 10.5 %collective-permute-start.39 = (f32[7,64,64]{1,0,2:T(8,128)S(1)}, f32[7,64,64]{1,0,2:T(8,128)S(1)}, u32[]{:S(2)}, u32[]{:S(2)}) collective-permute-start(f32[7,64,64]{1,0,2:T(8,128)S(1)} %get-tuple-element.17), channel_id=1, source_target_pairs={{64,0},{80,16},{96,32},{112,48},{128,64},{144,80},{160,96},{176,11... | collective-permute-start | bytes 344072 | tf_op jit(solution)/shard_map/ppermute | solution.py:86
  616.6 10.3 %collective-permute-start.38 = (f32[7,64,64]{1,0,2:T(8,128)S(1)}, f32[7,64,64]{1,0,2:T(8,128)S(1)}, u32[]{:S(2)}, u32[]{:S(2)}) collective-permute-start(f32[7,64,64]{1,0,2:T(8,128)S(1)} %get-tuple-element.16), channel_id=1, source_target_pairs={{0,64},{16,80},{32,96},{48,112},{64,128},{80,144},{96,160},{112,17... | collective-permute-start | bytes 344072 | tf_op jit(solution)/shard_map/ppermute | solution.py:85
  641.3 8.7 %collective-permute-start.41 = (f32[7,64,64]{1,0,2:T(8,128)S(1)}, f32[7,64,64]{1,0,2:T(8,128)S(1)}, u32[]{:S(2)}, u32[]{:S(2)}) collective-permute-start(f32[7,64,64]{1,0,2:T(8,128)S(1)} %get-tuple-element.15), channel_id=1, source_target_pairs={{64,0},{80,16},{96,32},{112,48},{128,64},{144,80},{160,96},{176,11... | collective-permute-start | bytes 344072 | tf_op jit(solution)/shard_map/ppermute | solution.py:86
  642.6 8.9 %collective-permute-start.40 = (f32[7,64,64]{1,0,2:T(8,128)S(1)}, f32[7,64,64]{1,0,2:T(8,128)S(1)}, u32[]{:S(2)}, u32[]{:S(2)}) collective-permute-start(f32[7,64,64]{1,0,2:T(8,128)S(1)} %get-tuple-element.14), channel_id=1, source_target_pairs={{0,64},{16,80},{32,96},{48,112},{64,128},{80,144},{96,160},{112,17... | collective-permute-start | bytes 344072 | tf_op jit(solution)/shard_map/ppermute | solution.py:85
  670.8 4.7 collective-permute-start.42
  698.0 6.8 collective-permute-start.43
  716.5 2.7 collective-permute-start.44
  719.6 14.1 %collective-permute-start.45 = (f32[64,2,2,4,64]{4,0,3,2,1:T(8,128)S(1)}, f32[64,2,2,4,64]{4,0,3,2,1:T(8,128)S(1)}, u32[]{:S(2)}, u32[]{:S(2)}) collective-permute-start(f32[64,2,2,4,64]{4,0,3,2,1:T(8,128)S(1)} %select_bitcast_fusion.6), channel_id=1, source_target_pairs={{0,4},{1,5},{2,6},{3,7},{4,0},{5,1},{6,2},{7,3},{8,12},{9,13},{10,... | collective-permute-start | bytes 786440 | tf_op jit(solution)/shard_map/ppermute | solution.py:110
  733.9 9.1 %collective-permute-start.46 = (f32[64,2,4,64]{3,0,2,1:T(8,128)S(1)}, f32[64,2,4,64]{3,0,2,1:T(8,128)S(1)}, u32[]{:S(2)}, u32[]{:S(2)}) collective-permute-start(f32[64,2,4,64]{3,0,2,1:T(8,128)S(1)} %select_bitcast_fusion.12), channel_id=1, source_target_pairs={{0,8},{1,9},{2,10},{3,11},{4,12},{5,13},{6,14},{7,15},{8,0},{9,1},... | collective-permute-start | bytes 393224 | tf_op jit(solution)/shard_map/ppermute | solution.py:110
  743.1 9.1 %collective-permute-start.47 = (f32[64,4,64]{2,0,1:T(8,128)S(1)}, f32[64,4,64]{2,0,1:T(8,128)S(1)}, u32[]{:S(2)}, u32[]{:S(2)}) collective-permute-start(f32[64,4,64]{2,0,1:T(8,128)S(1)} %select_bitcast_fusion.18), channel_id=1, source_target_pairs={{0,2},{1,3},{2,0},{3,1},{4,6},{5,7},{6,4},{7,5},{8,10},{9,11},{10,... | collective-permute-start | bytes 196616 | tf_op jit(solution)/shard_map/ppermute | solution.py:110
  752.8 11.4 %collective-permute-start.48 = (f32[64,4,64]{2,0,1:T(8,128)S(1)}, f32[64,4,64]{2,0,1:T(8,128)S(1)}, u32[]{:S(2)}, u32[]{:S(2)}) collective-permute-start(f32[64,4,64]{2,0,1:T(8,128)S(1)} %get-tuple-element.54), channel_id=1, source_target_pairs={{0,48},{16,0},{32,16},{48,32},{64,112},{80,64},{96,80},{112,96},{1... | collective-permute-start | bytes 196616 | tf_op jit(solution)/shard_map/ppermute | solution.py:39
  754.9 9.4 %collective-permute-start.49 = (f32[64,4,64]{2,0,1:T(8,128)S(1)}, f32[64,4,64]{2,0,1:T(8,128)S(1)}, u32[]{:S(2)}, u32[]{:S(2)}) collective-permute-start(f32[64,4,64]{2,0,1:T(8,128)S(1)} %get-tuple-element.53), channel_id=1, source_target_pairs={{0,32},{16,48},{32,0},{48,16},{64,96},{80,112},{96,64},{112,80},{1... | collective-permute-start | bytes 196616 | tf_op jit(solution)/shard_map/ppermute | solution.py:39
  754.9 9.4 %collective-permute-start.50 = (f32[64,4,64]{2,0,1:T(8,128)S(1)}, f32[64,4,64]{2,0,1:T(8,128)S(1)}, u32[]{:S(2)}, u32[]{:S(2)}) collective-permute-start(f32[64,4,64]{2,0,1:T(8,128)S(1)} %get-tuple-element.5), channel_id=1, source_target_pairs={{0,16},{16,32},{32,48},{48,0},{64,80},{80,96},{96,112},{112,64},{1... | collective-permute-start | bytes 196616 | tf_op jit(solution)/shard_map/ppermute | solution.py:39
  764.4 10.4 %collective-permute-start.51 = (f32[64,4,64]{2,0,1:T(8,128)S(1)}, f32[64,4,64]{2,0,1:T(8,128)S(1)}, u32[]{:S(2)}, u32[]{:S(2)}) collective-permute-start(f32[64,4,64]{2,0,1:T(8,128)S(1)} %get-tuple-element.41), channel_id=1, source_target_pairs={{0,192},{16,208},{32,224},{48,240},{64,0},{80,16},{96,32},{112,48}... | collective-permute-start | bytes 196616 | tf_op jit(solution)/shard_map/ppermute | solution.py:50
  771.0 8.4 %collective-permute-start.52 = (f32[64,4,64]{2,0,1:T(8,128)S(1)}, f32[64,4,64]{2,0,1:T(8,128)S(1)}, u32[]{:S(2)}, u32[]{:S(2)}) collective-permute-start(f32[64,4,64]{2,0,1:T(8,128)S(1)} %get-tuple-element.40), channel_id=1, source_target_pairs={{0,128},{16,144},{32,160},{48,176},{64,192},{80,208},{96,224},{112... | collective-permute-start | bytes 196616 | tf_op jit(solution)/shard_map/ppermute | solution.py:50
  771.0 8.4 %collective-permute-start.53 = (f32[64,4,64]{2,0,1:T(8,128)S(1)}, f32[64,4,64]{2,0,1:T(8,128)S(1)}, u32[]{:S(2)}, u32[]{:S(2)}) collective-permute-start(f32[64,4,64]{2,0,1:T(8,128)S(1)} %get-tuple-element.39), channel_id=1, source_target_pairs={{0,64},{16,80},{32,96},{48,112},{64,128},{80,144},{96,160},{112,17... | collective-permute-start | bytes 196616 | tf_op jit(solution)/shard_map/ppermute | solution.py:50

commit v4 on v3

--- a/solution.py
+++ b/solution.py
@@ -56,12 +56,17 @@
 def convolve(extended, kernel, axis, flipped):
     radius = (kernel.shape[0] - 1) // 2
     length = extended.shape[axis] - 2 * radius
-    summed = None
-    for position in range(2 * radius + 1):
-        weight = kernel[2 * radius - position] if flipped else kernel[position]
-        term = weight * lax.slice_in_dim(extended, position, position + length, axis=axis)
-        summed = term if summed is None else summed + term
-    return summed
+    taps = kernel[::-1] if flipped else kernel
+    offset = jnp.arange(length + 2 * radius)[None, :] - jnp.arange(length)[:, None]
+    band = jnp.where(
+        (offset >= 0) & (offset <= 2 * radius), taps[jnp.clip(offset, 0, 2 * radius)], 0.0
+    )
+    hi = lax.Precision.HIGHEST
+    if axis == 0:
+        return jnp.einsum("ot,tab->oab", band, extended, precision=hi)
+    if axis == 1:
+        return jnp.einsum("ot,atb->aob", band, extended, precision=hi)
+    return jnp.einsum("abt,ot->abo", extended, band, precision=hi)
 
 
 def pair_halo(volume, axis, radius, partner, is_high):

time: 793 us -> 739 us (0.932)
  other arithmetic: 203 us -> 50.6 us
  matrix products: 0 us -> 87.2 us
  local copies, waits for them, and re-layouts: 88.2 us -> 144 us
  waiting for transfers between devices: 337 us -> 285 us
    add x10 -> x0, other arithmetic: 125 us -> none  [convolve(): summed = term if summed is None else summed + term]
    dot_general x0 -> x12, matrix products: none -> 87.2 us  [the longest x4 36.1 us: convolve(): return jnp.einsum('abt,ot->abo', extended, band, precision=hi)]
    gather x0 -> x8, local copies, waits for them, and re-layouts: none -> 71.8 us  [convolve(): taps[jnp.clip(offset, 0, 2 * radius)]]
    ppermute x4, waiting for transfers between devices: 90.8 us -> 54.1 us  [z_halo(): low = lax.ppermute(last, 'space', [(i, i + ROW) for i in range(nsp - ROW)])]
    div x2 -> x0, other arithmetic: 31.6 us -> none  [shards(): quotient = recorded / blurred]
    ppermute x4, waiting for transfers between devices: 20.1 us -> 4.73 us  [z_halo(): lax.ppermute(first, 'space', [(i + ROW, i) for i in range(nsp - ROW)])]
    concatenate x0 -> x4, local copies, waits for them, and re-layouts: none -> 14.3 us  [the longest x2 7.86 us: z_halo(): return jnp.concatenate([low, volume, high], axis=axis)]
    unnamed x16 -> x24, local copies, waits for them, and re-layouts: 1.35 us -> 10.6 us
  transfers between devices with their start and end apart: 54 -> 54, of which waited for: 38 -> 36; matrix products, arithmetic and copies ran while one was open for 12% -> 22% of each run, Pallas kernels for 0% -> 0%
where the time goes in v4:
time: 739 us; the launch traced here: 727 us
  waiting for transfers between devices  285 us (39%)
  local copies, waits for them, and re-layouts  144 us (19%)
  starting transfers between devices  132 us (18%)
  matrix products  87.2 us (12%)
  other arithmetic  50.6 us (7%)
  between operations  28 us (4%)
    ppermute x18, waiting for transfers between devices, route(): part = lax.ppermute(part, 'space', pairs)  110 us
    gather x8, local copies, waits for them, and re-layouts, convolve(): taps[jnp.clip(offset, 0, 2 * radius)]  71.8 us
    ppermute x4, waiting for transfers between devices, z_halo(): low = lax.ppermute(last, 'space', [(i, i + ROW) for i in range(nsp - ROW)])  54.1 us
    ppermute x8, waiting for transfers between devices, view_reduce_scatter(): x = keep + lax.ppermute(send, 'view', xor_pairs(nv, m))  48.8 us
    ppermute x8, waiting for transfers between devices, view_all_gather(): recv = lax.ppermute(x, 'view', xor_pairs(nv, m))  39.8 us
    dot_general x4, matrix products, convolve(): return jnp.einsum('abt,ot->abo', extended, band, precision=hi)  36.1 us
    dot_general x4, matrix products, convolve(): return jnp.einsum('ot,atb->aob', band, extended, precision=hi)  32.1 us
    ppermute x18, starting transfers between devices, route(): part = lax.ppermute(part, 'space', pairs)  28.8 us
  transfers between devices with their start and end apart: 54, of which 36 were waited for; matrix products, arithmetic and copies ran while one was open for 22% of the time, Pallas kernels for 0%

profile of v4, /device:TPU:8, one launch (start us, length us, event | category | flops | bytes accessed | tf_op | source)
XLA Modules:
  0.0 726.9 jit_solution(6803201437505582343)
XLA Ops:
  7.4 3.0 collective-permute-done.1
  14.1 3.1 collective-permute-start.3
  38.2 4.4 collective-permute-start.7
  49.9 8.3 %collective-permute-start.16 = (f32[64,4,64]{2,0,1:T(8,128)S(1)}, f32[64,4,64]{2,0,1:T(8,128)S(1)}, u32[]{:S(2)}, u32[]{:S(2)}) collective-permute-start(f32[64,4,64]{2,0,1:T(8,128)S(1)} %select_select_fusion.12), channel_id=1, source_target_pairs={{0,2},{1,3},{2,0},{3,1},{4,6},{5,7},{6,4},{7,5},{8,10},{9,11},{10,... | collective-permute-start | bytes 196616 | tf_op jit(solution)/shard_map/ppermute | solution.py:125
  61.4 3.1 collective-permute-start.17
  65.1 7.1 collective-permute-done.17
  76.0 5.6 collective-permute-done.18
  86.1 3.1 copy.239
  89.6 3.1 copy.240
  94.0 3.2 copy.241
  99.6 3.2 copy.244
  102.8 3.2 copy.243
  111.6 2.8 fusion.206
  120.7 62.1 %collective-permute-done.10 = f32[64,64,64]{2,0,1:T(8,128)} collective-permute-done((f32[64,64,64]{2,0,1:T(8,128)}, f32[64,64,64]{2,0,1:T(8,128)}, u32[]{:S(2)}, u32[]{:S(2)}) %collective-permute-start.10) | collective-permute-done | bytes 1048608 | tf_op jit(solution)/shard_map/ppermute | solution.py:39
  182.8 5.7 collective-permute-done.12
  188.4 9.5 %select_select_fusion.1 = (f32[64,64,64]{2,0,1:T(8,128)}, f32[64,64,64]{2,0,1:T(8,128)}, f32[64,64,64]{2,0,1:T(8,128)}) fusion(f32[64,64,64]{2,0,1:T(8,128)} %collective-permute-done.10, f32[64,64,64]{2,0,1:T(8,128)} %collective-permute-done.11, f32[64,64,64]{2,0,1:T(8,128)} %collective-permute-done.12, f32[64,64,64]{2,0,1:T(8,128)} %bitcast.294, ...), kind=kLoop, calls=%fused_computation.54 | loop fusion | flops 2359296 | bytes 9437193 | tf_op jit(solution)/shard_map/jit(_where)/select_n | solution.py:47
  209.9 8.9 %fusion.28 = f32[64,64,64]{2,1,0:T(8,128)S(1)} fusion(f32[64,64,3]{2,1,0:T(8,128)} %copy.254, f32[64,64,64]{2,1,0:T(8,128)S(1)} %copy-done.1, f32[64,64,3]{2,1,0:T(8,128)} %copy.252, f32[]{:T(128)} %bitcast.62, f32[]{:T(128)} %bitcast.63, f32[]{:T(128)} %bitcast.64, f32[]{:T(128)} %bitcast.65, f32[]{:T(128)} %bitcast.66, f32[]{:T(128)} %bitcast.68, f32[]{:T(128)} %bitcast.67), kind=kOutput, calls=%fused_computation.40 | convolution fusion | flops 220872960 | bytes 2195484 | tf_op jit(solution)/shard_map/abt,ot->abo/dot_general | solution.py:69
  220.9 3.6 collective-permute-done.21
  225.2 8.2 %fusion.43 = f32[64,64,64]{1,2,0:T(8,128)S(1)} fusion(f32[64,3,64]{2,1,0:T(4,128)S(1)} %get-tuple-element.68, f32[64,64,64]{2,1,0:T(8,128)S(1)} %fusion.28, f32[64,3,64]{2,1,0:T(4,128)S(1)} %get-tuple-element.67, f32[]{:T(128)} %bitcast.72, f32[]{:T(128)} %bitcast.73, f32[]{:T(128)} %bitcast.74, f32[]{:T(128)} %bitcast.75, f32[]{:T(128)} %bitcast.76, ...), kind=kOutput, calls=%fused_computation.58 | convolution fusion | flops 220872960 | bytes 2195484 | tf_op jit(solution)/shard_map/ot,atb->aob/dot_general | solution.py:68
  235.4 5.4 collective-permute-start.22
  243.7 39.3 %gather_fusion.3 = f32[4992]{0:T(1024)} fusion(f32[15]{0:T(128)S(1)} %get-tuple-element.135, s32[5120]{0:T(1024)S(1)} %pad_clamp_fusion), kind=kCustom, calls=%fused_computation.3 | custom fusion | bytes 59904 | tf_op jit(solution)/shard_map/gather | solution.py:62
  286.5 51.5 %collective-permute-done.22 = f32[7,64,64]{1,2,0:T(8,128)} collective-permute-done((f32[7,64,64]{1,2,0:T(8,128)S(1)}, f32[7,64,64]{1,2,0:T(8,128)}, u32[]{:S(2)}, u32[]{:S(2)}) %collective-permute-start.22) | collective-permute-done | bytes 114720 | tf_op jit(solution)/shard_map/ppermute | solution.py:90
  337.9 2.8 pad_maximum_fusion
  340.8 4.6 copy.256
  345.3 36.3 %collective-permute-done.14 = f32[64,64,64]{2,0,1:T(8,128)} collective-permute-done((f32[64,64,64]{2,0,1:T(8,128)}, f32[64,64,64]{2,0,1:T(8,128)}, u32[]{:S(2)}, u32[]{:S(2)}) %collective-permute-start.14) | collective-permute-done | bytes 1048608 | tf_op jit(solution)/shard_map/ppermute | solution.py:50
  381.7 3.5 select_select_fusion
  385.3 6.1 convolution_divide_fusion.1
  393.4 11.7 %collective-permute-start.24 = (f32[7,64,64]{2,0,1:T(8,128)S(1)}, f32[7,64,64]{2,0,1:T(8,128)S(1)}, u32[]{:S(2)}, u32[]{:S(2)}) collective-permute-start(f32[7,64,64]{2,0,1:T(8,128)S(1)} %get-tuple-element.26), channel_id=1, source_target_pairs={{0,64},{16,80},{32,96},{48,112},{64,128},{80,144},{96,160},{112,17... | collective-permute-start | bytes 344072 | tf_op jit(solution)/shard_map/ppermute | solution.py:90
  405.1 28.2 %gather_fusion.2 = f32[4992]{0:T(1024)S(1)} fusion(f32[15]{0:T(128)S(1)} %get-tuple-element.136, s32[5120]{0:T(1024)S(1)} %pad_clamp_fusion), kind=kCustom, calls=%fused_computation.2 | custom fusion | bytes 59904 | tf_op jit(solution)/shard_map/gather | solution.py:62
  436.5 4.0 collective-permute-start.26
  444.4 3.2 copy.288
  447.7 7.8 %convolution_bitcast_fusion.1 = f32[64,64,64]{1,0,2:T(8,128)S(1)} fusion(f32[64,70,64]{1,0,2:T(8,128)} %copy.288, f32[]{:T(128)} %bitcast.82, f32[]{:T(128)} %bitcast.83, f32[]{:T(128)} %bitcast.84, f32[]{:T(128)} %bitcast.85, f32[]{:T(128)} %bitcast.86, f32[]{:T(128)} %bitcast.88, f32[]{:T(128)} %bitcast.87), kind=kOutput, calls=%fused_computation.61 | convolution fusion | flops 220299520 | bytes 2195484 | tf_op jit(solution)/shard_map/ot,atb->aob/dot_general | solution.py:68
  456.2 3.7 collective-permute-start.27
  463.6 9.2 %fusion.26 = f32[64,64,64]{2,1,0:T(8,128)S(1)} fusion(f32[64,64,70]{1,0,2:T(8,128)S(1)} %pad_maximum_fusion.3, f32[]{:T(128)} %bitcast.92, f32[]{:T(128)} %bitcast.93, f32[]{:T(128)} %bitcast.94, f32[]{:T(128)} %bitcast.95, f32[]{:T(128)} %bitcast.96, f32[]{:T(128)} %bitcast.98, f32[]{:T(128)} %bitcast.97), kind=kOutput, calls=%fused_computation.33 | convolution fusion | flops 220299520 | bytes 2195484 | tf_op jit(solution)/shard_map/abt,ot->abo/dot_general | solution.py:69
  475.1 2.6 collective-permute-done.28
  481.0 12.2 %collective-permute-done.29 = f32[64,2,2,4,64]{4,0,3,2,1:T(8,128)S(1)} collective-permute-done((f32[64,2,2,4,64]{4,0,3,2,1:T(8,128)S(1)}, f32[64,2,2,4,64]{4,0,3,2,1:T(8,128)S(1)}, u32[]{:S(2)}, u32[]{:S(2)}) %collective-permute-start.29) | collective-permute-done | bytes 262176 | tf_op jit(solution)/shard_map/ppermute | solution.py:115
  493.4 3.5 collective-permute-start.30
  496.9 5.9 collective-permute-done.30
  502.8 5.8 collective-permute-start.31
  512.6 7.5 %collective-permute-start.32 = (f32[64,4,64]{2,0,1:T(8,128)S(1)}, f32[64,4,64]{2,0,1:T(8,128)S(1)}, u32[]{:S(2)}, u32[]{:S(2)}) collective-permute-start(f32[64,4,64]{2,0,1:T(8,128)S(1)} %fusion.51), channel_id=1, source_target_pairs={{0,2},{1,3},{2,0},{3,1},{4,6},{5,7},{6,4},{7,5},{8,10},{9,11},{10,... | collective-permute-start | bytes 196616 | tf_op jit(solution)/shard_map/ppermute | solution.py:125
  520.1 3.9 collective-permute-done.32
  524.9 9.6 %collective-permute-done.33 = f32[64,2,4,64]{3,0,2,1:T(8,128)S(1)} collective-permute-done((f32[64,2,4,64]{3,0,2,1:T(8,128)S(1)}, f32[64,2,4,64]{3,0,2,1:T(8,128)S(1)}, u32[]{:S(2)}, u32[]{:S(2)}) %collective-permute-start.33) | collective-permute-done | bytes 131104 | tf_op jit(solution)/shard_map/ppermute | solution.py:125
  534.7 9.2 %collective-permute-done.34 = f32[64,2,2,4,64]{4,0,3,2,1:T(8,128)S(1)} collective-permute-done((f32[64,2,2,4,64]{4,0,3,2,1:T(8,128)S(1)}, f32[64,2,2,4,64]{4,0,3,2,1:T(8,128)S(1)}, u32[]{:S(2)}, u32[]{:S(2)}) %collective-permute-start.34) | collective-permute-done | bytes 262176 | tf_op jit(solution)/shard_map/ppermute | solution.py:125
  544.2 2.6 collective-permute-done.35
  547.7 2.7 fusion.201
  566.6 8.9 %fusion.34 = f32[64,64,64]{2,1,0:T(8,128)S(1)} fusion(f32[64,64,3]{2,1,0:T(8,128)} %copy.272, f32[64,64,64]{2,1,0:T(8,128)S(1)} %copy-done, f32[64,64,3]{2,1,0:T(8,128)} %copy.270, f32[]{:T(128)} %bitcast.62, f32[]{:T(128)} %bitcast.63, f32[]{:T(128)} %bitcast.64, f32[]{:T(128)} %bitcast.65, f32[]{:T(128)} %bitcast.66, f32[]{:T(128)} %bitcast.68, f32[]{:T(128)} %bitcast.67), kind=kOutput, calls=%fused_computation.47 | convolution fusion | flops 220872960 | bytes 2195484 | tf_op jit(solution)/shard_map/abt,ot->abo/dot_general | solution.py:69
  576.4 4.9 collective-permute-done.37
  582.0 8.2 %fusion.40 = f32[64,64,64]{1,2,0:T(8,128)S(1)} fusion(f32[64,3,64]{2,1,0:T(4,128)S(1)} %get-tuple-element.64, f32[64,64,64]{2,1,0:T(8,128)S(1)} %fusion.34, f32[64,3,64]{2,1,0:T(4,128)S(1)} %get-tuple-element.63, f32[]{:T(128)} %bitcast.72, f32[]{:T(128)} %bitcast.73, f32[]{:T(128)} %bitcast.74, f32[]{:T(128)} %bitcast.75, f32[]{:T(128)} %bitcast.76, ...), kind=kOutput, calls=%fused_computation.57 | convolution fusion | flops 220872960 | bytes 2195484 | tf_op jit(solution)/shard_map/ot,atb->aob/dot_general | solution.py:68
  591.5 5.5 collective-permute-start.38
  600.8 3.3 copy.274
  604.1 8.3 %convolution_divide_fusion = f32[64,64,64]{2,0,1:T(8,128)S(1)} fusion(f32[64,64,64]{2,0,1:T(8,128)} %copy-done.4, f32[78,64,64]{0,2,1:T(8,128)} %copy.274, f32[64,78]{1,0:T(8,128)S(1)} %copy-done.6), kind=kOutput, calls=%fused_computation.60 | convolution fusion | flops 245653888 | bytes 3395072 | tf_op jit(solution)/shard_map/ot,tab->oab/dot_general | solution.py:66
  613.8 5.0 collective-permute-start.40
  626.4 4.4 collective-permute-done.42
  631.7 3.2 copy.292
  634.9 7.9 %convolution_bitcast_fusion = f32[64,64,64]{1,0,2:T(8,128)S(1)} fusion(f32[64,70,64]{1,0,2:T(8,128)} %copy.292, f32[]{:T(128)} %bitcast.82, f32[]{:T(128)} %bitcast.83, f32[]{:T(128)} %bitcast.84, f32[]{:T(128)} %bitcast.85, f32[]{:T(128)} %bitcast.86, f32[]{:T(128)} %bitcast.88, f32[]{:T(128)} %bitcast.87), kind=kOutput, calls=%fused_computation.59 | convolution fusion | flops 220299520 | bytes 2195484 | tf_op jit(solution)/shard_map/ot,atb->aob/dot_general | solution.py:68
  643.5 4.4 collective-permute-start.43
  651.5 9.2 %fusion.24 = f32[64,64,64]{2,1,0:T(8,128)S(1)} fusion(f32[64,64,70]{1,0,2:T(8,128)S(1)} %pad_maximum_fusion.5, f32[]{:T(128)} %bitcast.92, f32[]{:T(128)} %bitcast.93, f32[]{:T(128)} %bitcast.94, f32[]{:T(128)} %bitcast.95, f32[]{:T(128)} %bitcast.96, f32[]{:T(128)} %bitcast.98, f32[]{:T(128)} %bitcast.97), kind=kOutput, calls=%fused_computation.31 | convolution fusion | flops 220299520 | bytes 2195484 | tf_op jit(solution)/shard_map/abt,ot->abo/dot_general | solution.py:69
  668.3 12.2 %collective-permute-done.45 = f32[64,2,2,4,64]{4,0,3,2,1:T(8,128)S(1)} collective-permute-done((f32[64,2,2,4,64]{4,0,3,2,1:T(8,128)S(1)}, f32[64,2,2,4,64]{4,0,3,2,1:T(8,128)S(1)}, u32[]{:S(2)}, u32[]{:S(2)}) %collective-permute-start.45) | collective-permute-done | bytes 262176 | tf_op jit(solution)/shard_map/ppermute | solution.py:115
  680.7 3.0 collective-permute-start.46
  683.6 6.1 collective-permute-done.46
  689.9 6.1 collective-permute-start.47
  695.9 4.5 collective-permute-done.47
  712.2 5.4 collective-permute-start.51
  721.4 4.5 collective-permute-done.52
  (223 shorter events, 149.7 us)
Async XLA Ops:
  1.5 3.8 collective-permute-start
  5.3 5.1 collective-permute-start.1
  7.4 35.8 %copy-start.7 = (f32[1,7]{1,0:T(1,128)S(1)}, f32[1,7]{1,0:T(1,128)}, u32[]{:S(2)}) copy-start(f32[1,7]{1,0:T(1,128)} %param.9) | copy-start | bytes 88
  10.5 3.6 collective-permute-start.2
  14.1 4.7 collective-permute-start.3
  25.7 33.1 %copy-start.8 = (f32[1,7]{1,0:T(1,128)S(1)}, f32[1,7]{1,0:T(1,128)}, u32[]{:S(2)}) copy-start(f32[1,7]{1,0:T(1,128)} %param.10) | copy-start | bytes 88
  26.7 11.4 %collective-permute-start.4 = (f32[64,4,64]{2,0,1:T(8,128)S(1)}, f32[64,4,64]{2,0,1:T(8,128)S(1)}, u32[]{:S(2)}, u32[]{:S(2)}) collective-permute-start(f32[64,4,64]{2,0,1:T(8,128)S(1)} %bitcast.308), channel_id=1, source_target_pairs={{0,48},{16,0},{32,16},{48,32},{64,112},{80,64},{96,80},{112,96},{1... | collective-permute-start | bytes 196616 | tf_op jit(solution)/shard_map/ppermute | solution.py:39
  28.8 9.4 %collective-permute-start.5 = (f32[64,4,64]{2,0,1:T(8,128)S(1)}, f32[64,4,64]{2,0,1:T(8,128)S(1)}, u32[]{:S(2)}, u32[]{:S(2)}) collective-permute-start(f32[64,4,64]{2,0,1:T(8,128)S(1)} %bitcast.309), channel_id=1, source_target_pairs={{0,32},{16,48},{32,0},{48,16},{64,96},{80,112},{96,64},{112,80},{1... | collective-permute-start | bytes 196616 | tf_op jit(solution)/shard_map/ppermute | solution.py:39
  30.1 8.0 %collective-permute-start.6 = (f32[64,4,64]{2,0,1:T(8,128)S(1)}, f32[64,4,64]{2,0,1:T(8,128)S(1)}, u32[]{:S(2)}, u32[]{:S(2)}) collective-permute-start(f32[64,4,64]{2,0,1:T(8,128)S(1)} %bitcast.310), channel_id=1, source_target_pairs={{0,16},{16,32},{32,48},{48,0},{64,80},{80,96},{96,112},{112,64},{1... | collective-permute-start | bytes 196616 | tf_op jit(solution)/shard_map/ppermute | solution.py:39
  38.2 10.3 %collective-permute-start.7 = (f32[64,4,64]{2,0,1:T(8,128)S(1)}, f32[64,4,64]{2,0,1:T(8,128)S(1)}, u32[]{:S(2)}, u32[]{:S(2)}) collective-permute-start(f32[64,4,64]{2,0,1:T(8,128)S(1)} %get-tuple-element.54), channel_id=1, source_target_pairs={{0,192},{16,208},{32,224},{48,240},{64,0},{80,16},{96,32},{112,48}... | collective-permute-start | bytes 196616 | tf_op jit(solution)/shard_map/ppermute | solution.py:50
  42.6 7.3 %collective-permute-start.8 = (f32[64,4,64]{2,0,1:T(8,128)S(1)}, f32[64,4,64]{2,0,1:T(8,128)S(1)}, u32[]{:S(2)}, u32[]{:S(2)}) collective-permute-start(f32[64,4,64]{2,0,1:T(8,128)S(1)} %get-tuple-element.53), channel_id=1, source_target_pairs={{0,128},{16,144},{32,160},{48,176},{64,192},{80,208},{96,224},{112... | collective-permute-start | bytes 196616 | tf_op jit(solution)/shard_map/ppermute | solution.py:50
  42.6 7.3 %collective-permute-start.9 = (f32[64,4,64]{2,0,1:T(8,128)S(1)}, f32[64,4,64]{2,0,1:T(8,128)S(1)}, u32[]{:S(2)}, u32[]{:S(2)}) collective-permute-start(f32[64,4,64]{2,0,1:T(8,128)S(1)} %get-tuple-element.52), channel_id=1, source_target_pairs={{0,64},{16,80},{32,96},{48,112},{64,128},{80,144},{96,160},{112,17... | collective-permute-start | bytes 196616 | tf_op jit(solution)/shard_map/ppermute | solution.py:50
  49.9 24.7 %copy-start.9 = (f32[1,15]{1,0:T(1,128)S(1)}, f32[1,15]{1,0:T(1,128)}, u32[]{:S(2)}) copy-start(f32[1,15]{1,0:T(1,128)} %param.11) | copy-start | bytes 184
  49.9 11.4 %collective-permute-start.16 = (f32[64,4,64]{2,0,1:T(8,128)S(1)}, f32[64,4,64]{2,0,1:T(8,128)S(1)}, u32[]{:S(2)}, u32[]{:S(2)}) collective-permute-start(f32[64,4,64]{2,0,1:T(8,128)S(1)} %select_select_fusion.12), channel_id=1, source_target_pairs={{0,2},{1,3},{2,0},{3,1},{4,6},{5,7},{6,4},{7,5},{8,10},{9,11},{10,... | collective-permute-start | bytes 196616 | tf_op jit(solution)/shard_map/ppermute | solution.py:125
  61.4 10.8 %collective-permute-start.17 = (f32[64,2,4,64]{3,0,2,1:T(8,128)S(1)}, f32[64,2,4,64]{3,0,2,1:T(8,128)S(1)}, u32[]{:S(2)}, u32[]{:S(2)}) collective-permute-start(f32[64,2,4,64]{3,0,2,1:T(8,128)S(1)} %pad_maximum_fusion.12), channel_id=1, source_target_pairs={{0,8},{1,9},{2,10},{3,11},{4,12},{5,13},{6,14},{7,15},{8,0},{9,1},... | collective-permute-start | bytes 393224 | tf_op jit(solution)/shard_map/ppermute | solution.py:125
  72.3 9.3 %collective-permute-start.18 = (f32[64,2,2,4,64]{4,0,3,2,1:T(8,128)S(1)}, f32[64,2,2,4,64]{4,0,3,2,1:T(8,128)S(1)}, u32[]{:S(2)}, u32[]{:S(2)}) collective-permute-start(f32[64,2,2,4,64]{4,0,3,2,1:T(8,128)S(1)} %pad_maximum_fusion.10), channel_id=1, source_target_pairs={{0,4},{1,5},{2,6},{3,7},{4,0},{5,1},{6,2},{7,3},{8,12},{9,13},{10,... | collective-permute-start | bytes 786440 | tf_op jit(solution)/shard_map/ppermute | solution.py:125
  75.9 6.9 copy-start.5
  82.8 27.1 %collective-permute-start.19 = (f32[64,2,2,2,4,64]{5,0,4,3,2,1:T(8,128)}, f32[64,2,2,2,4,64]{5,0,4,3,2,1:T(8,128)}, u32[]{:S(2)}, u32[]{:S(2)}) collective-permute-start(f32[64,2,2,2,4,64]{5,0,4,3,2,1:T(8,128)} %pad_maximum_fusion.8), channel_id=1, source_target_pairs={{0,1},{1,0},{2,3},{3,2},{4,5},{5,4},{6,7},{7,6},{8,9},{9,8},{10,11... | collective-permute-start | bytes 1572872 | tf_op jit(solution)/shard_map/ppermute | solution.py:125
  89.2 93.6 %collective-permute-start.10 = (f32[64,64,64]{2,0,1:T(8,128)}, f32[64,64,64]{2,0,1:T(8,128)}, u32[]{:S(2)}, u32[]{:S(2)}) collective-permute-start(f32[64,64,64]{2,0,1:T(8,128)} %bitcast.300), channel_id=1, source_target_pairs={{0,48},{16,0},{32,16},{48,32},{64,112},{80,64},{96,80},{112,96},{1... | collective-permute-start | bytes 3145736 | tf_op jit(solution)/shard_map/ppermute | solution.py:39
  92.8 90.0 %collective-permute-start.11 = (f32[64,64,64]{2,0,1:T(8,128)}, f32[64,64,64]{2,0,1:T(8,128)}, u32[]{:S(2)}, u32[]{:S(2)}) collective-permute-start(f32[64,64,64]{2,0,1:T(8,128)} %bitcast.301), channel_id=1, source_target_pairs={{0,32},{16,48},{32,0},{48,16},{64,96},{80,112},{96,64},{112,80},{1... | collective-permute-start | bytes 3145736 | tf_op jit(solution)/shard_map/ppermute | solution.py:39
  97.2 91.2 %collective-permute-start.12 = (f32[64,64,64]{2,0,1:T(8,128)}, f32[64,64,64]{2,0,1:T(8,128)}, u32[]{:S(2)}, u32[]{:S(2)}) collective-permute-start(f32[64,64,64]{2,0,1:T(8,128)} %bitcast.302), channel_id=1, source_target_pairs={{0,16},{16,32},{32,48},{48,0},{64,80},{80,96},{96,112},{112,64},{1... | collective-permute-start | bytes 3145736 | tf_op jit(solution)/shard_map/ppermute | solution.py:39
  120.4 84.7 %collective-permute-start.20 = (f32[64,64,3]{1,0,2:T(8,128)S(1)}, f32[64,64,3]{1,0,2:T(8,128)S(1)}, u32[]{:S(2)}, u32[]{:S(2)}) collective-permute-start(f32[64,64,3]{1,0,2:T(8,128)S(1)} %broadcast_select_fusion.23), channel_id=1, source_target_pairs={{0,16},{16,0},{32,48},{48,32},{64,80},{80,64},{96,112},{112,96},{1... | collective-permute-start | bytes 147464 | tf_op jit(solution)/shard_map/ppermute | solution.py:78
  198.0 147.4 %collective-permute-start.13 = (f32[64,64,64]{2,0,1:T(8,128)}, f32[64,64,64]{2,0,1:T(8,128)}, u32[]{:S(2)}, u32[]{:S(2)}) collective-permute-start(f32[64,64,64]{2,0,1:T(8,128)} %get-tuple-element.9), channel_id=1, source_target_pairs={{0,192},{16,208},{32,224},{48,240},{64,0},{80,16},{96,32},{112,48}... | collective-permute-start | bytes 3145736 | tf_op jit(solution)/shard_map/ppermute | solution.py:50
  199.1 182.6 %collective-permute-start.14 = (f32[64,64,64]{2,0,1:T(8,128)}, f32[64,64,64]{2,0,1:T(8,128)}, u32[]{:S(2)}, u32[]{:S(2)}) collective-permute-start(f32[64,64,64]{2,0,1:T(8,128)} %get-tuple-element.8), channel_id=1, source_target_pairs={{0,128},{16,144},{32,160},{48,176},{64,192},{80,208},{96,224},{112... | collective-permute-start | bytes 3145736 | tf_op jit(solution)/shard_map/ppermute | solution.py:50
  200.0 181.7 %collective-permute-start.15 = (f32[64,64,64]{2,0,1:T(8,128)}, f32[64,64,64]{2,0,1:T(8,128)}, u32[]{:S(2)}, u32[]{:S(2)}) collective-permute-start(f32[64,64,64]{2,0,1:T(8,128)} %get-tuple-element.7), channel_id=1, source_target_pairs={{0,64},{16,80},{32,96},{48,112},{64,128},{80,144},{96,160},{112,17... | collective-permute-start | bytes 3145736 | tf_op jit(solution)/shard_map/ppermute | solution.py:50
  205.8 4.1 copy-start.1
  219.5 5.1 collective-permute-start.21
  234.1 52.3 %collective-permute-start.23 = (f32[7,64,64]{1,2,0:T(8,128)}, f32[7,64,64]{1,2,0:T(8,128)}, u32[]{:S(2)}, u32[]{:S(2)}) collective-permute-start(f32[7,64,64]{1,2,0:T(8,128)} %get-tuple-element.29), channel_id=1, source_target_pairs={{64,0},{80,16},{96,32},{112,48},{128,64},{144,80},{160,96},{176,11... | collective-permute-start | bytes 344072 | tf_op jit(solution)/shard_map/ppermute | solution.py:91
  235.4 102.5 %collective-permute-start.22 = (f32[7,64,64]{1,2,0:T(8,128)S(1)}, f32[7,64,64]{1,2,0:T(8,128)}, u32[]{:S(2)}, u32[]{:S(2)}) collective-permute-start(f32[7,64,64]{1,2,0:T(8,128)S(1)} %get-tuple-element.28), channel_id=1, source_target_pairs={{0,64},{16,80},{32,96},{48,112},{64,128},{80,144},{96,160},{112,17... | collective-permute-start | bytes 344072 | tf_op jit(solution)/shard_map/ppermute | solution.py:90
  340.8 40.9 %copy-start.2 = (f32[1,1,64,4096]{2,3,1,0:T(8,128)S(1)}, f32[1,1,64,4096]{2,3,1,0:T(8,128)}, u32[]{:S(2)}) copy-start(f32[1,1,64,4096]{2,3,1,0:T(8,128)} %copy.245) | copy-start | bytes 3145732
  381.7 3.6 copy-start.3
  381.7 3.6 copy-start.6
  385.2 6.1 copy-start.4
  392.1 41.3 %collective-permute-start.25 = (f32[7,64,64]{2,0,1:T(8,128)}, f32[7,64,64]{2,0,1:T(8,128)S(1)}, u32[]{:S(2)}, u32[]{:S(2)}) collective-permute-start(f32[7,64,64]{2,0,1:T(8,128)} %get-tuple-element.27), channel_id=1, source_target_pairs={{64,0},{80,16},{96,32},{112,48},{128,64},{144,80},{160,96},{176,11... | collective-permute-start | bytes 344072 | tf_op jit(solution)/shard_map/ppermute | solution.py:91
  393.4 40.1 %collective-permute-start.24 = (f32[7,64,64]{2,0,1:T(8,128)S(1)}, f32[7,64,64]{2,0,1:T(8,128)S(1)}, u32[]{:S(2)}, u32[]{:S(2)}) collective-permute-start(f32[7,64,64]{2,0,1:T(8,128)S(1)} %get-tuple-element.26), channel_id=1, source_target_pairs={{0,64},{16,80},{32,96},{48,112},{64,128},{80,144},{96,160},{112,17... | collective-permute-start | bytes 344072 | tf_op jit(solution)/shard_map/ppermute | solution.py:90
  436.5 7.0 collective-permute-start.26
  456.2 6.3 collective-permute-start.27
  474.6 3.2 collective-permute-start.28
  479.0 14.3 %collective-permute-start.29 = (f32[64,2,2,4,64]{4,0,3,2,1:T(8,128)S(1)}, f32[64,2,2,4,64]{4,0,3,2,1:T(8,128)S(1)}, u32[]{:S(2)}, u32[]{:S(2)}) collective-permute-start(f32[64,2,2,4,64]{4,0,3,2,1:T(8,128)S(1)} %select_bitcast_fusion.9), channel_id=1, source_target_pairs={{0,4},{1,5},{2,6},{3,7},{4,0},{5,1},{6,2},{7,3},{8,12},{9,13},{10,... | collective-permute-start | bytes 786440 | tf_op jit(solution)/shard_map/ppermute | solution.py:115
  493.4 9.4 %collective-permute-start.30 = (f32[64,2,4,64]{3,0,2,1:T(8,128)S(1)}, f32[64,2,4,64]{3,0,2,1:T(8,128)S(1)}, u32[]{:S(2)}, u32[]{:S(2)}) collective-permute-start(f32[64,2,4,64]{3,0,2,1:T(8,128)S(1)} %select_bitcast_fusion.15), channel_id=1, source_target_pairs={{0,8},{1,9},{2,10},{3,11},{4,12},{5,13},{6,14},{7,15},{8,0},{9,1},... | collective-permute-start | bytes 393224 | tf_op jit(solution)/shard_map/ppermute | solution.py:115
  502.8 9.1 %collective-permute-start.31 = (f32[64,4,64]{2,0,1:T(8,128)S(1)}, f32[64,4,64]{2,0,1:T(8,128)S(1)}, u32[]{:S(2)}, u32[]{:S(2)}) collective-permute-start(f32[64,4,64]{2,0,1:T(8,128)S(1)} %select_bitcast_fusion.21), channel_id=1, source_target_pairs={{0,2},{1,3},{2,0},{3,1},{4,6},{5,7},{6,4},{7,5},{8,10},{9,11},{10,... | collective-permute-start | bytes 196616 | tf_op jit(solution)/shard_map/ppermute | solution.py:115
  512.6 11.4 %collective-permute-start.32 = (f32[64,4,64]{2,0,1:T(8,128)S(1)}, f32[64,4,64]{2,0,1:T(8,128)S(1)}, u32[]{:S(2)}, u32[]{:S(2)}) collective-permute-start(f32[64,4,64]{2,0,1:T(8,128)S(1)} %fusion.51), channel_id=1, source_target_pairs={{0,2},{1,3},{2,0},{3,1},{4,6},{5,7},{6,4},{7,5},{8,10},{9,11},{10,... | collective-permute-start | bytes 196616 | tf_op jit(solution)/shard_map/ppermute | solution.py:125
  524.0 10.5 %collective-permute-start.33 = (f32[64,2,4,64]{3,0,2,1:T(8,128)S(1)}, f32[64,2,4,64]{3,0,2,1:T(8,128)S(1)}, u32[]{:S(2)}, u32[]{:S(2)}) collective-permute-start(f32[64,2,4,64]{3,0,2,1:T(8,128)S(1)} %pad_maximum_fusion.13), channel_id=1, source_target_pairs={{0,8},{1,9},{2,10},{3,11},{4,12},{5,13},{6,14},{7,15},{8,0},{9,1},... | collective-permute-start | bytes 393224 | tf_op jit(solution)/shard_map/ppermute | solution.py:125
  534.6 9.3 %collective-permute-start.34 = (f32[64,2,2,4,64]{4,0,3,2,1:T(8,128)S(1)}, f32[64,2,2,4,64]{4,0,3,2,1:T(8,128)S(1)}, u32[]{:S(2)}, u32[]{:S(2)}) collective-permute-start(f32[64,2,2,4,64]{4,0,3,2,1:T(8,128)S(1)} %pad_maximum_fusion.11), channel_id=1, source_target_pairs={{0,4},{1,5},{2,6},{3,7},{4,0},{5,1},{6,2},{7,3},{8,12},{9,13},{10,... | collective-permute-start | bytes 786440 | tf_op jit(solution)/shard_map/ppermute | solution.py:125
  544.1 2.7 collective-permute-start.35
  556.5 5.4 collective-permute-start.36
  562.5 4.1 copy-start
  576.2 5.1 collective-permute-start.37
  590.2 9.1 %collective-permute-start.39 = (f32[7,64,64]{1,2,0:T(8,128)S(1)}, f32[7,64,64]{1,2,0:T(8,128)S(1)}, u32[]{:S(2)}, u32[]{:S(2)}) collective-permute-start(f32[7,64,64]{1,2,0:T(8,128)S(1)} %get-tuple-element.17), channel_id=1, source_target_pairs={{64,0},{80,16},{96,32},{112,48},{128,64},{144,80},{160,96},{176,11... | collective-permute-start | bytes 344072 | tf_op jit(solution)/shard_map/ppermute | solution.py:91
  591.5 9.0 %collective-permute-start.38 = (f32[7,64,64]{1,2,0:T(8,128)S(1)}, f32[7,64,64]{1,2,0:T(8,128)S(1)}, u32[]{:S(2)}, u32[]{:S(2)}) collective-permute-start(f32[7,64,64]{1,2,0:T(8,128)S(1)} %get-tuple-element.16), channel_id=1, source_target_pairs={{0,64},{16,80},{32,96},{48,112},{64,128},{80,144},{96,160},{112,17... | collective-permute-start | bytes 344072 | tf_op jit(solution)/shard_map/ppermute | solution.py:90
  612.5 8.7 %collective-permute-start.41 = (f32[7,64,64]{2,0,1:T(8,128)S(1)}, f32[7,64,64]{2,0,1:T(8,128)S(1)}, u32[]{:S(2)}, u32[]{:S(2)}) collective-permute-start(f32[7,64,64]{2,0,1:T(8,128)S(1)} %get-tuple-element.15), channel_id=1, source_target_pairs={{64,0},{80,16},{96,32},{112,48},{128,64},{144,80},{160,96},{176,11... | collective-permute-start | bytes 344072 | tf_op jit(solution)/shard_map/ppermute | solution.py:91
  613.8 8.9 %collective-permute-start.40 = (f32[7,64,64]{2,0,1:T(8,128)S(1)}, f32[7,64,64]{2,0,1:T(8,128)S(1)}, u32[]{:S(2)}, u32[]{:S(2)}) collective-permute-start(f32[7,64,64]{2,0,1:T(8,128)S(1)} %get-tuple-element.14), channel_id=1, source_target_pairs={{0,64},{16,80},{32,96},{48,112},{64,128},{80,144},{96,160},{112,17... | collective-permute-start | bytes 344072 | tf_op jit(solution)/shard_map/ppermute | solution.py:90
  625.7 5.1 collective-permute-start.42
  643.5 7.0 collective-permute-start.43
  662.5 2.7 collective-permute-start.44
  666.5 14.1 %collective-permute-start.45 = (f32[64,2,2,4,64]{4,0,3,2,1:T(8,128)S(1)}, f32[64,2,2,4,64]{4,0,3,2,1:T(8,128)S(1)}, u32[]{:S(2)}, u32[]{:S(2)}) collective-permute-start(f32[64,2,2,4,64]{4,0,3,2,1:T(8,128)S(1)} %select_bitcast_fusion.6), channel_id=1, source_target_pairs={{0,4},{1,5},{2,6},{3,7},{4,0},{5,1},{6,2},{7,3},{8,12},{9,13},{10,... | collective-permute-start | bytes 786440 | tf_op jit(solution)/shard_map/ppermute | solution.py:115
  680.7 9.1 %collective-permute-start.46 = (f32[64,2,4,64]{3,0,2,1:T(8,128)S(1)}, f32[64,2,4,64]{3,0,2,1:T(8,128)S(1)}, u32[]{:S(2)}, u32[]{:S(2)}) collective-permute-start(f32[64,2,4,64]{3,0,2,1:T(8,128)S(1)} %select_bitcast_fusion.12), channel_id=1, source_target_pairs={{0,8},{1,9},{2,10},{3,11},{4,12},{5,13},{6,14},{7,15},{8,0},{9,1},... | collective-permute-start | bytes 393224 | tf_op jit(solution)/shard_map/ppermute | solution.py:115
  689.9 10.6 %collective-permute-start.47 = (f32[64,4,64]{2,0,1:T(8,128)S(1)}, f32[64,4,64]{2,0,1:T(8,128)S(1)}, u32[]{:S(2)}, u32[]{:S(2)}) collective-permute-start(f32[64,4,64]{2,0,1:T(8,128)S(1)} %select_bitcast_fusion.18), channel_id=1, source_target_pairs={{0,2},{1,3},{2,0},{3,1},{4,6},{5,7},{6,4},{7,5},{8,10},{9,11},{10,... | collective-permute-start | bytes 196616 | tf_op jit(solution)/shard_map/ppermute | solution.py:115
  701.1 11.0 %collective-permute-start.48 = (f32[64,4,64]{2,0,1:T(8,128)S(1)}, f32[64,4,64]{2,0,1:T(8,128)S(1)}, u32[]{:S(2)}, u32[]{:S(2)}) collective-permute-start(f32[64,4,64]{2,0,1:T(8,128)S(1)} %get-tuple-element.60), channel_id=1, source_target_pairs={{0,48},{16,0},{32,16},{48,32},{64,112},{80,64},{96,80},{112,96},{1... | collective-permute-start | bytes 196616 | tf_op jit(solution)/shard_map/ppermute | solution.py:39
  703.2 8.9 %collective-permute-start.49 = (f32[64,4,64]{2,0,1:T(8,128)S(1)}, f32[64,4,64]{2,0,1:T(8,128)S(1)}, u32[]{:S(2)}, u32[]{:S(2)}) collective-permute-start(f32[64,4,64]{2,0,1:T(8,128)S(1)} %get-tuple-element.59), channel_id=1, source_target_pairs={{0,32},{16,48},{32,0},{48,16},{64,96},{80,112},{96,64},{112,80},{1... | collective-permute-start | bytes 196616 | tf_op jit(solution)/shard_map/ppermute | solution.py:39
  703.2 9.0 %collective-permute-start.50 = (f32[64,4,64]{2,0,1:T(8,128)S(1)}, f32[64,4,64]{2,0,1:T(8,128)S(1)}, u32[]{:S(2)}, u32[]{:S(2)}) collective-permute-start(f32[64,4,64]{2,0,1:T(8,128)S(1)} %get-tuple-element.5), channel_id=1, source_target_pairs={{0,16},{16,32},{32,48},{48,0},{64,80},{80,96},{96,112},{112,64},{1... | collective-permute-start | bytes 196616 | tf_op jit(solution)/shard_map/ppermute | solution.py:39
  712.2 9.2 %collective-permute-start.51 = (f32[64,4,64]{2,0,1:T(8,128)S(1)}, f32[64,4,64]{2,0,1:T(8,128)S(1)}, u32[]{:S(2)}, u32[]{:S(2)}) collective-permute-start(f32[64,4,64]{2,0,1:T(8,128)S(1)} %get-tuple-element.47), channel_id=1, source_target_pairs={{0,192},{16,208},{32,224},{48,240},{64,0},{80,16},{96,32},{112,48}... | collective-permute-start | bytes 196616 | tf_op jit(solution)/shard_map/ppermute | solution.py:50
  717.6 8.3 %collective-permute-start.52 = (f32[64,4,64]{2,0,1:T(8,128)S(1)}, f32[64,4,64]{2,0,1:T(8,128)S(1)}, u32[]{:S(2)}, u32[]{:S(2)}) collective-permute-start(f32[64,4,64]{2,0,1:T(8,128)S(1)} %get-tuple-element.46), channel_id=1, source_target_pairs={{0,128},{16,144},{32,160},{48,176},{64,192},{80,208},{96,224},{112... | collective-permute-start | bytes 196616 | tf_op jit(solution)/shard_map/ppermute | solution.py:50
  717.6 8.3 %collective-permute-start.53 = (f32[64,4,64]{2,0,1:T(8,128)S(1)}, f32[64,4,64]{2,0,1:T(8,128)S(1)}, u32[]{:S(2)}, u32[]{:S(2)}) collective-permute-start(f32[64,4,64]{2,0,1:T(8,128)S(1)} %get-tuple-element.45), channel_id=1, source_target_pairs={{0,64},{16,80},{32,96},{48,112},{64,128},{80,144},{96,160},{112,17... | collective-permute-start | bytes 196616 | tf_op jit(solution)/shard_map/ppermute | solution.py:50

commit v5 on v4

--- a/solution.py
+++ b/solution.py
@@ -53,14 +53,17 @@
     return result
 
 
-def convolve(extended, kernel, axis, flipped):
+def band_matrix(kernel, length, flipped):
     radius = (kernel.shape[0] - 1) // 2
-    length = extended.shape[axis] - 2 * radius
-    taps = kernel[::-1] if flipped else kernel
     offset = jnp.arange(length + 2 * radius)[None, :] - jnp.arange(length)[:, None]
-    band = jnp.where(
-        (offset >= 0) & (offset <= 2 * radius), taps[jnp.clip(offset, 0, 2 * radius)], 0.0
-    )
+    band = jnp.zeros(offset.shape, jnp.float32)
+    for position in range(2 * radius + 1):
+        weight = kernel[2 * radius - position] if flipped else kernel[position]
+        band = jnp.where(offset == position, weight, band)
+    return band
+
+
+def convolve(extended, band, axis):
     hi = lax.Precision.HIGHEST
     if axis == 0:
         return jnp.einsum("ot,tab->oab", band, extended, precision=hi)
@@ -170,15 +173,20 @@
     along_x = normalized(kernel_x[0])
     along_y = normalized(kernel_y[0])
     along_z = normalized(kernel_z[0])
+    bands = {
+        (axis, flipped): band_matrix(taps, side, flipped)
+        for axis, taps in ((2, along_x), (1, along_y), (0, along_z))
+        for flipped in (False, True)
+    }
     for sweep_no in range(ITERS):
         full = view_all_gather(share, nv)
-        blurred = convolve(pair_halo(full, 2, radius_x, 1, my_x == 1), along_x, 2, False)
-        blurred = convolve(pair_halo(blurred, 1, radius_y, 3, my_y == 1), along_y, 1, False)
-        blurred = convolve(z_halo(blurred, 0, radius_z), along_z, 0, False)
+        blurred = convolve(pair_halo(full, 2, radius_x, 1, my_x == 1), bands[2, False], 2)
+        blurred = convolve(pair_halo(blurred, 1, radius_y, 3, my_y == 1), bands[1, False], 1)
+        blurred = convolve(z_halo(blurred, 0, radius_z), bands[0, False], 0)
         quotient = recorded / blurred
-        spread = convolve(z_halo(quotient, 0, radius_z), along_z, 0, True)
-        spread = convolve(pair_halo(spread, 1, radius_y, 3, my_y == 1), along_y, 1, True)
-        spread = convolve(pair_halo(spread, 2, radius_x, 1, my_x == 1), along_x, 2, True)
+        spread = convolve(z_halo(quotient, 0, radius_z), bands[0, True], 0)
+        spread = convolve(pair_halo(spread, 1, radius_y, 3, my_y == 1), bands[1, True], 1)
+        spread = convolve(pair_halo(spread, 2, radius_x, 1, my_x == 1), bands[2, True], 2)
         summed = view_reduce_scatter(spread, nv)
         share = share * jnp.where(keep, summed / (nv * measured.shape[0]), 1.0)
     share = route(share, brick_at, place[me], nsp)

time: 739 us -> 768 us (1.039)
  local copies, waits for them, and re-layouts: 144 us -> 73.1 us
  waiting for transfers between devices: 285 us -> 353 us
  matrix products: 87.2 us -> 125 us
    gather x8 -> x0, local copies, waits for them, and re-layouts: 71.8 us -> none  [convolve(): taps[jnp.clip(offset, 0, 2 * radius)]]
    ppermute x18, waiting for transfers between devices: 110 us -> 42 us  [route(): part = lax.ppermute(part, 'space', pairs)]
    ppermute x8, waiting for transfers between devices: 20.1 us -> 82.2 us  [pair_halo(): recv = lax.ppermute(send, 'space', [(i, i ^ partner) for i in range(nsp)])]
    dot_general x4, matrix products: 18.9 us -> 56.3 us  [convolve(): return jnp.einsum('ot,tab->oab', band, extended, precision=hi)]
    ppermute x4, waiting for transfers between devices: 54.1 us -> 91.1 us  [z_halo(): low = lax.ppermute(last, 'space', [(i, i + ROW) for i in range(nsp - ROW)])]
    ppermute x4, waiting for transfers between devices: 4.73 us -> 38.2 us  [z_halo(): lax.ppermute(first, 'space', [(i + ROW, i) for i in range(nsp - ROW)])]
  transfers between devices with their start and end apart: 54 -> 54, of which waited for: 36 -> 37; matrix products, arithmetic and copies ran while one was open for 22% -> 12% of each run, Pallas kernels for 0% -> 0%
where the time goes in v5:
time: 768 us; the launch traced here: 756 us
  waiting for transfers between devices  353 us (46%)
  starting transfers between devices  129 us (17%)
  matrix products  125 us (16%)
  local copies, waits for them, and re-layouts  73.1 us (10%)
  other arithmetic  47.2 us (6%)
  between operations  28.1 us (4%)
    ppermute x4, waiting for transfers between devices, z_halo(): low = lax.ppermute(last, 'space', [(i, i + ROW) for i in range(nsp - ROW)])  91.1 us
    ppermute x8, waiting for transfers between devices, pair_halo(): recv = lax.ppermute(send, 'space', [(i, i ^ partner) for i in range(nsp)])  82.2 us
    dot_general x4, matrix products, convolve(): return jnp.einsum('ot,tab->oab', band, extended, precision=hi)  56.3 us
    ppermute x8, waiting for transfers between devices, view_reduce_scatter(): x = keep + lax.ppermute(send, 'view', xor_pairs(nv, m))  50.1 us
    ppermute x18, waiting for transfers between devices, route(): part = lax.ppermute(part, 'space', pairs)  42 us
    ppermute x8, waiting for transfers between devices, view_all_gather(): recv = lax.ppermute(x, 'view', xor_pairs(nv, m))  41.6 us
    ppermute x4, waiting for transfers between devices, z_halo(): lax.ppermute(first, 'space', [(i + ROW, i) for i in range(nsp - ROW)])  38.2 us
    dot_general x4, matrix products, convolve(): return jnp.einsum('abt,ot->abo', extended, band, precision=hi)  36.9 us
  transfers between devices with their start and end apart: 54, of which 37 were waited for; matrix products, arithmetic and copies ran while one was open for 12% of the time, Pallas kernels for 0%

profile of v5, /device:TPU:8, one launch (start us, length us, event | category | flops | bytes accessed | tf_op | source)
XLA Modules:
  0.0 755.9 jit_solution(16637052266182313736)
XLA Ops:
  7.4 3.0 collective-permute-done.1
  14.1 3.1 collective-permute-start.3
  38.3 4.4 collective-permute-start.7
  50.0 8.3 %collective-permute-start.16 = (f32[64,4,64]{2,0,1:T(8,128)S(1)}, f32[64,4,64]{2,0,1:T(8,128)S(1)}, u32[]{:S(2)}, u32[]{:S(2)}) collective-permute-start(f32[64,4,64]{2,0,1:T(8,128)S(1)} %select_select_fusion.12), channel_id=1, source_target_pairs={{0,2},{1,3},{2,0},{3,1},{4,6},{5,7},{6,4},{7,5},{8,10},{9,11},{10,... | collective-permute-start | bytes 196616 | tf_op jit(solution)/shard_map/ppermute | solution.py:128
  61.5 3.1 collective-permute-start.17
  65.1 7.2 collective-permute-done.17
  75.8 5.9 collective-permute-done.18
  82.9 3.0 select_select_fusion.4
  86.6 3.1 copy.239
  90.7 3.1 copy.240
  94.5 3.2 copy.241
  114.0 3.2 copy.244
  117.1 3.2 copy.243
  120.3 3.1 copy.242
  126.6 63.7 %collective-permute-done.20 = f32[64,64,3]{1,0,2:T(8,128)} collective-permute-done((f32[64,64,3]{1,0,2:T(8,128)}, f32[64,64,3]{1,0,2:T(8,128)}, u32[]{:S(2)}, u32[]{:S(2)}) %collective-permute-start.20) | collective-permute-done | bytes 49184 | tf_op jit(solution)/shard_map/ppermute | solution.py:81
  196.0 9.6 %fusion.28 = f32[64,64,64]{2,1,0:T(8,128)S(1)} fusion(f32[64,64,3]{2,1,0:T(8,128)} %copy.254, f32[64,64,64]{2,1,0:T(8,128)S(1)} %copy-done.3, f32[64,64,3]{2,1,0:T(8,128)} %copy.252, f32[]{:T(128)} %bitcast.81, f32[]{:T(128)} %bitcast.80, f32[]{:T(128)} %bitcast.79, f32[]{:T(128)} %bitcast.78, f32[]{:T(128)} %bitcast.77, f32[]{:T(128)} %bitcast.76, f32[]{:T(128)} %bitcast.75), kind=kOutput, calls=%fused_computation.38 | convolution fusion | flops 220841600 | bytes 2195484 | tf_op jit(solution)/shard_map/abt,ot->abo/dot_general | solution.py:72
  206.9 7.1 select_select_fusion.1
  218.7 8.1 %fusion.43 = f32[64,64,64]{1,2,0:T(8,128)S(1)} fusion(f32[64,3,64]{2,1,0:T(4,128)S(1)} %get-tuple-element.68, f32[64,64,64]{2,1,0:T(8,128)S(1)} %fusion.28, f32[64,3,64]{2,1,0:T(4,128)S(1)} %get-tuple-element.67, f32[]{:T(128)} %bitcast.89, f32[]{:T(128)} %bitcast.88, f32[]{:T(128)} %bitcast.87, f32[]{:T(128)} %bitcast.86, f32[]{:T(128)} %bitcast.85, ...), kind=kOutput, calls=%fused_computation.56 | convolution fusion | flops 220841600 | bytes 2195484 | tf_op jit(solution)/shard_map/ot,atb->aob/dot_general | solution.py:71
  228.9 5.4 collective-permute-start.22
  237.6 29.9 %collective-permute-done.23 = f32[7,64,64]{1,2,0:T(8,128)} collective-permute-done((f32[7,64,64]{1,2,0:T(8,128)}, f32[7,64,64]{1,2,0:T(8,128)}, u32[]{:S(2)}, u32[]{:S(2)}) %collective-permute-start.23) | collective-permute-done | bytes 114720 | tf_op jit(solution)/shard_map/ppermute | solution.py:94
  267.5 87.3 %collective-permute-done.22 = f32[7,64,64]{1,2,0:T(8,128)} collective-permute-done((f32[7,64,64]{1,2,0:T(8,128)S(1)}, f32[7,64,64]{1,2,0:T(8,128)}, u32[]{:S(2)}, u32[]{:S(2)}) %collective-permute-start.22) | collective-permute-done | bytes 114720 | tf_op jit(solution)/shard_map/ppermute | solution.py:93
  354.7 2.7 pad_maximum_fusion
  357.5 4.6 copy.256
  362.0 35.6 %collective-permute-done.14 = f32[64,64,64]{2,0,1:T(8,128)} collective-permute-done((f32[64,64,64]{2,0,1:T(8,128)}, f32[64,64,64]{2,0,1:T(8,128)}, u32[]{:S(2)}, u32[]{:S(2)}) %collective-permute-start.14) | collective-permute-done | bytes 1048608 | tf_op jit(solution)/shard_map/ppermute | solution.py:50
  397.7 3.5 select_select_fusion
  401.2 15.5 %convolution_divide_fusion.1 = f32[64,64,64]{2,0,1:T(8,128)S(1)} fusion(f32[64,64,64]{2,0,1:T(8,128)S(1)} %select_select_fusion, f32[78,64,64]{0,2,1:T(8,128)S(1)} %copy-done.6, f32[]{:T(128)} %bitcast.47, f32[]{:T(128)} %bitcast.46, f32[]{:T(128)} %bitcast.45, f32[]{:T(128)} %bitcast.44, f32[]{:T(128)} %bitcast.43, f32[]{:T(128)} %bitcast.42, ...), kind=kOutput, calls=%fused_computation.60 | convolution fusion | flops 245783680 | bytes 3375164 | tf_op jit(solution)/shard_map/ot,tab->oab/dot_general | solution.py:69
  418.1 14.0 %collective-permute-start.24 = (f32[7,64,64]{2,0,1:T(8,128)S(1)}, f32[7,64,64]{2,0,1:T(8,128)S(1)}, u32[]{:S(2)}, u32[]{:S(2)}) collective-permute-start(f32[7,64,64]{2,0,1:T(8,128)S(1)} %get-tuple-element.26), channel_id=1, source_target_pairs={{0,64},{16,80},{32,96},{48,112},{64,128},{80,144},{96,160},{112,17... | collective-permute-start | bytes 344072 | tf_op jit(solution)/shard_map/ppermute | solution.py:93
  432.1 3.8 collective-permute-done.25
  437.1 11.6 %fusion = f32[64,64,64]{2,0,1:T(8,128)S(1)} fusion(f32[7,64,64]{2,0,1:T(8,128)S(1)} %collective-permute-done.25, f32[64,64,64]{2,0,1:T(8,128)S(1)} %convolution_divide_fusion.1, f32[7,64,64]{2,0,1:T(8,128)S(1)} %collective-permute-done.24, f32[]{:T(128)} %bitcast.47, f32[]{:T(128)} %bitcast.46, f32[]{:T(128)} %bitcast.45, f32[]{:T(128)} %bitcast.44, ...), kind=kOutput, calls=%fused_computation.3 | convolution fusion | flops 246160512 | bytes 2326588 | tf_op jit(solution)/shard_map/ot,tab->oab/dot_general | solution.py:69
  451.5 3.3 collective-permute-done.26
  455.7 3.2 copy.288
  458.9 7.7 %convolution_bitcast_fusion.1 = f32[64,64,64]{1,0,2:T(8,128)S(1)} fusion(f32[64,70,64]{1,0,2:T(8,128)} %copy.288, f32[]{:T(128)} %bitcast.89, f32[]{:T(128)} %bitcast.88, f32[]{:T(128)} %bitcast.87, f32[]{:T(128)} %bitcast.86, f32[]{:T(128)} %bitcast.85, f32[]{:T(128)} %bitcast.84, f32[]{:T(128)} %bitcast.83), kind=kOutput, calls=%fused_computation.59 | convolution fusion | flops 220268160 | bytes 2195484 | tf_op jit(solution)/shard_map/ot,atb->aob/dot_general | solution.py:71
  467.2 3.4 collective-permute-start.27
  474.1 9.1 %fusion.26 = f32[64,64,64]{2,1,0:T(8,128)S(1)} fusion(f32[64,64,70]{1,0,2:T(8,128)S(1)} %pad_maximum_fusion.3, f32[]{:T(128)} %bitcast.81, f32[]{:T(128)} %bitcast.80, f32[]{:T(128)} %bitcast.79, f32[]{:T(128)} %bitcast.78, f32[]{:T(128)} %bitcast.77, f32[]{:T(128)} %bitcast.76, f32[]{:T(128)} %bitcast.75), kind=kOutput, calls=%fused_computation.31 | convolution fusion | flops 220268160 | bytes 2195484 | tf_op jit(solution)/shard_map/abt,ot->abo/dot_general | solution.py:72
  491.1 12.4 %collective-permute-done.29 = f32[64,2,2,4,64]{4,0,3,2,1:T(8,128)S(1)} collective-permute-done((f32[64,2,2,4,64]{4,0,3,2,1:T(8,128)S(1)}, f32[64,2,2,4,64]{4,0,3,2,1:T(8,128)S(1)}, u32[]{:S(2)}, u32[]{:S(2)}) %collective-permute-start.29) | collective-permute-done | bytes 262176 | tf_op jit(solution)/shard_map/ppermute | solution.py:118
  503.7 2.9 collective-permute-start.30
  506.5 6.3 collective-permute-done.30
  512.8 6.0 collective-permute-start.31
  519.5 4.5 collective-permute-done.31
  524.6 6.5 collective-permute-start.32
  531.1 3.9 collective-permute-done.32
  535.1 10.5 %collective-permute-done.33 = f32[64,2,4,64]{3,0,2,1:T(8,128)S(1)} collective-permute-done((f32[64,2,4,64]{3,0,2,1:T(8,128)S(1)}, f32[64,2,4,64]{3,0,2,1:T(8,128)S(1)}, u32[]{:S(2)}, u32[]{:S(2)}) %collective-permute-start.33) | collective-permute-done | bytes 131104 | tf_op jit(solution)/shard_map/ppermute | solution.py:128
  545.8 9.2 %collective-permute-done.34 = f32[64,2,2,4,64]{4,0,3,2,1:T(8,128)S(1)} collective-permute-done((f32[64,2,2,4,64]{4,0,3,2,1:T(8,128)S(1)}, f32[64,2,2,4,64]{4,0,3,2,1:T(8,128)S(1)}, u32[]{:S(2)}, u32[]{:S(2)}) %collective-permute-start.34) | collective-permute-done | bytes 262176 | tf_op jit(solution)/shard_map/ppermute | solution.py:128
  558.8 2.7 fusion.235
  577.5 9.0 %fusion.34 = f32[64,64,64]{2,1,0:T(8,128)S(1)} fusion(f32[64,64,3]{2,1,0:T(8,128)} %copy.272, f32[64,64,64]{2,1,0:T(8,128)S(1)} %copy-done.4, f32[64,64,3]{2,1,0:T(8,128)} %copy.270, f32[]{:T(128)} %bitcast.81, f32[]{:T(128)} %bitcast.80, f32[]{:T(128)} %bitcast.79, f32[]{:T(128)} %bitcast.78, f32[]{:T(128)} %bitcast.77, f32[]{:T(128)} %bitcast.76, f32[]{:T(128)} %bitcast.75), kind=kOutput, calls=%fused_computation.45 | convolution fusion | flops 220841600 | bytes 2195484 | tf_op jit(solution)/shard_map/abt,ot->abo/dot_general | solution.py:72
  587.4 4.9 collective-permute-done.37
  593.0 8.2 %fusion.40 = f32[64,64,64]{1,2,0:T(8,128)S(1)} fusion(f32[64,3,64]{2,1,0:T(4,128)S(1)} %get-tuple-element.64, f32[64,64,64]{2,1,0:T(8,128)S(1)} %fusion.34, f32[64,3,64]{2,1,0:T(4,128)S(1)} %get-tuple-element.63, f32[]{:T(128)} %bitcast.89, f32[]{:T(128)} %bitcast.88, f32[]{:T(128)} %bitcast.87, f32[]{:T(128)} %bitcast.86, f32[]{:T(128)} %bitcast.85, ...), kind=kOutput, calls=%fused_computation.55 | convolution fusion | flops 220841600 | bytes 2195484 | tf_op jit(solution)/shard_map/ot,atb->aob/dot_general | solution.py:71
  602.5 4.8 collective-permute-start.38
  610.8 3.3 copy.274
  614.1 17.7 %convolution_divide_fusion = f32[64,64,64]{2,0,1:T(8,128)S(1)} fusion(f32[64,64,64]{2,0,1:T(8,128)} %copy-done.7, f32[78,64,64]{0,2,1:T(8,128)} %copy.274, f32[]{:T(128)} %bitcast.47, f32[]{:T(128)} %bitcast.46, f32[]{:T(128)} %bitcast.45, f32[]{:T(128)} %bitcast.44, f32[]{:T(128)} %bitcast.43, f32[]{:T(128)} %bitcast.42, f32[]{:T(128)} %bitcast.41, ...), kind=kOutput, calls=%fused_computation.58 | convolution fusion | flops 245783680 | bytes 3375164 | tf_op jit(solution)/shard_map/ot,tab->oab/dot_general | solution.py:69
  633.2 5.0 collective-permute-start.40
  642.0 11.6 %fusion.6 = f32[64,64,64]{2,0,1:T(8,128)S(1)} fusion(f32[7,64,64]{2,0,1:T(8,128)S(1)} %collective-permute-done.41, f32[64,64,64]{2,0,1:T(8,128)S(1)} %convolution_divide_fusion, f32[7,64,64]{2,0,1:T(8,128)S(1)} %collective-permute-done.40, f32[]{:T(128)} %bitcast.47, f32[]{:T(128)} %bitcast.46, f32[]{:T(128)} %bitcast.45, f32[]{:T(128)} %bitcast.44, ...), kind=kOutput, calls=%fused_computation.9 | convolution fusion | flops 246160512 | bytes 2326588 | tf_op jit(solution)/shard_map/ot,tab->oab/dot_general | solution.py:69
  654.9 4.5 collective-permute-done.42
  660.4 3.2 copy.292
  663.6 7.7 %convolution_bitcast_fusion = f32[64,64,64]{1,0,2:T(8,128)S(1)} fusion(f32[64,70,64]{1,0,2:T(8,128)} %copy.292, f32[]{:T(128)} %bitcast.89, f32[]{:T(128)} %bitcast.88, f32[]{:T(128)} %bitcast.87, f32[]{:T(128)} %bitcast.86, f32[]{:T(128)} %bitcast.85, f32[]{:T(128)} %bitcast.84, f32[]{:T(128)} %bitcast.83), kind=kOutput, calls=%fused_computation.57 | convolution fusion | flops 220268160 | bytes 2195484 | tf_op jit(solution)/shard_map/ot,atb->aob/dot_general | solution.py:71
  671.9 4.6 collective-permute-start.43
  680.0 9.1 %fusion.24 = f32[64,64,64]{2,1,0:T(8,128)S(1)} fusion(f32[64,64,70]{1,0,2:T(8,128)S(1)} %pad_maximum_fusion.5, f32[]{:T(128)} %bitcast.81, f32[]{:T(128)} %bitcast.80, f32[]{:T(128)} %bitcast.79, f32[]{:T(128)} %bitcast.78, f32[]{:T(128)} %bitcast.77, f32[]{:T(128)} %bitcast.76, f32[]{:T(128)} %bitcast.75), kind=kOutput, calls=%fused_computation.29 | convolution fusion | flops 220268160 | bytes 2195484 | tf_op jit(solution)/shard_map/abt,ot->abo/dot_general | solution.py:72
  696.8 12.2 %collective-permute-done.45 = f32[64,2,2,4,64]{4,0,3,2,1:T(8,128)S(1)} collective-permute-done((f32[64,2,2,4,64]{4,0,3,2,1:T(8,128)S(1)}, f32[64,2,2,4,64]{4,0,3,2,1:T(8,128)S(1)}, u32[]{:S(2)}, u32[]{:S(2)}) %collective-permute-start.45) | collective-permute-done | bytes 262176 | tf_op jit(solution)/shard_map/ppermute | solution.py:118
  709.2 3.2 collective-permute-start.46
  712.4 6.1 collective-permute-done.46
  718.5 5.8 collective-permute-start.47
  724.3 3.3 collective-permute-done.47
  739.6 7.1 collective-permute-start.51
  750.5 4.4 collective-permute-done.52
  (216 shorter events, 141.2 us)
Async XLA Ops:
  1.5 3.8 collective-permute-start
  5.3 5.1 collective-permute-start.1
  10.5 3.6 collective-permute-start.2
  14.1 4.7 collective-permute-start.3
  26.2 32.2 %copy-start.9 = (f32[1,7]{1,0:T(1,128)S(1)}, f32[1,7]{1,0:T(1,128)}, u32[]{:S(2)}) copy-start(f32[1,7]{1,0:T(1,128)} %param.9) | copy-start | bytes 88
  27.1 11.1 %collective-permute-start.4 = (f32[64,4,64]{2,0,1:T(8,128)S(1)}, f32[64,4,64]{2,0,1:T(8,128)S(1)}, u32[]{:S(2)}, u32[]{:S(2)}) collective-permute-start(f32[64,4,64]{2,0,1:T(8,128)S(1)} %bitcast.269), channel_id=1, source_target_pairs={{0,48},{16,0},{32,16},{48,32},{64,112},{80,64},{96,80},{112,96},{1... | collective-permute-start | bytes 196616 | tf_op jit(solution)/shard_map/ppermute | solution.py:39
  29.2 9.0 %collective-permute-start.5 = (f32[64,4,64]{2,0,1:T(8,128)S(1)}, f32[64,4,64]{2,0,1:T(8,128)S(1)}, u32[]{:S(2)}, u32[]{:S(2)}) collective-permute-start(f32[64,4,64]{2,0,1:T(8,128)S(1)} %bitcast.270), channel_id=1, source_target_pairs={{0,32},{16,48},{32,0},{48,16},{64,96},{80,112},{96,64},{112,80},{1... | collective-permute-start | bytes 196616 | tf_op jit(solution)/shard_map/ppermute | solution.py:39
  30.5 7.7 %collective-permute-start.6 = (f32[64,4,64]{2,0,1:T(8,128)S(1)}, f32[64,4,64]{2,0,1:T(8,128)S(1)}, u32[]{:S(2)}, u32[]{:S(2)}) collective-permute-start(f32[64,4,64]{2,0,1:T(8,128)S(1)} %bitcast.271), channel_id=1, source_target_pairs={{0,16},{16,32},{32,48},{48,0},{64,80},{80,96},{96,112},{112,64},{1... | collective-permute-start | bytes 196616 | tf_op jit(solution)/shard_map/ppermute | solution.py:39
  38.3 9.7 %collective-permute-start.7 = (f32[64,4,64]{2,0,1:T(8,128)S(1)}, f32[64,4,64]{2,0,1:T(8,128)S(1)}, u32[]{:S(2)}, u32[]{:S(2)}) collective-permute-start(f32[64,4,64]{2,0,1:T(8,128)S(1)} %get-tuple-element.54), channel_id=1, source_target_pairs={{0,192},{16,208},{32,224},{48,240},{64,0},{80,16},{96,32},{112,48}... | collective-permute-start | bytes 196616 | tf_op jit(solution)/shard_map/ppermute | solution.py:50
  42.7 7.3 collective-permute-start.8
  42.7 7.3 collective-permute-start.9
  50.0 24.7 %copy-start.10 = (f32[1,7]{1,0:T(1,128)S(1)}, f32[1,7]{1,0:T(1,128)}, u32[]{:S(2)}) copy-start(f32[1,7]{1,0:T(1,128)} %param.10) | copy-start | bytes 88
  50.0 11.4 %collective-permute-start.16 = (f32[64,4,64]{2,0,1:T(8,128)S(1)}, f32[64,4,64]{2,0,1:T(8,128)S(1)}, u32[]{:S(2)}, u32[]{:S(2)}) collective-permute-start(f32[64,4,64]{2,0,1:T(8,128)S(1)} %select_select_fusion.12), channel_id=1, source_target_pairs={{0,2},{1,3},{2,0},{3,1},{4,6},{5,7},{6,4},{7,5},{8,10},{9,11},{10,... | collective-permute-start | bytes 196616 | tf_op jit(solution)/shard_map/ppermute | solution.py:128
  61.5 10.8 %collective-permute-start.17 = (f32[64,2,4,64]{3,0,2,1:T(8,128)S(1)}, f32[64,2,4,64]{3,0,2,1:T(8,128)S(1)}, u32[]{:S(2)}, u32[]{:S(2)}) collective-permute-start(f32[64,2,4,64]{3,0,2,1:T(8,128)S(1)} %pad_maximum_fusion.12), channel_id=1, source_target_pairs={{0,8},{1,9},{2,10},{3,11},{4,12},{5,13},{6,14},{7,15},{8,0},{9,1},... | collective-permute-start | bytes 393224 | tf_op jit(solution)/shard_map/ppermute | solution.py:128
  72.4 9.3 %collective-permute-start.18 = (f32[64,2,2,4,64]{4,0,3,2,1:T(8,128)S(1)}, f32[64,2,2,4,64]{4,0,3,2,1:T(8,128)S(1)}, u32[]{:S(2)}, u32[]{:S(2)}) collective-permute-start(f32[64,2,2,4,64]{4,0,3,2,1:T(8,128)S(1)} %pad_maximum_fusion.10), channel_id=1, source_target_pairs={{0,4},{1,5},{2,6},{3,7},{4,0},{5,1},{6,2},{7,3},{8,12},{9,13},{10,... | collective-permute-start | bytes 786440 | tf_op jit(solution)/shard_map/ppermute | solution.py:128
  75.8 7.1 copy-start.8
  82.9 18.6 %collective-permute-start.19 = (f32[64,2,2,2,4,64]{5,0,4,3,2,1:T(8,128)}, f32[64,2,2,2,4,64]{5,0,4,3,2,1:T(8,128)}, u32[]{:S(2)}, u32[]{:S(2)}) collective-permute-start(f32[64,2,2,2,4,64]{5,0,4,3,2,1:T(8,128)} %pad_maximum_fusion.8), channel_id=1, source_target_pairs={{0,1},{1,0},{2,3},{3,2},{4,5},{5,4},{6,7},{7,6},{8,9},{9,8},{10,11... | collective-permute-start | bytes 1572872 | tf_op jit(solution)/shard_map/ppermute | solution.py:128
  89.7 117.2 %collective-permute-start.10 = (f32[64,64,64]{2,0,1:T(8,128)}, f32[64,64,64]{2,0,1:T(8,128)}, u32[]{:S(2)}, u32[]{:S(2)}) collective-permute-start(f32[64,64,64]{2,0,1:T(8,128)} %bitcast.261), channel_id=1, source_target_pairs={{0,48},{16,0},{32,16},{48,32},{64,112},{80,64},{96,80},{112,96},{1... | collective-permute-start | bytes 3145736 | tf_op jit(solution)/shard_map/ppermute | solution.py:39
  93.8 113.0 %collective-permute-start.11 = (f32[64,64,64]{2,0,1:T(8,128)}, f32[64,64,64]{2,0,1:T(8,128)}, u32[]{:S(2)}, u32[]{:S(2)}) collective-permute-start(f32[64,64,64]{2,0,1:T(8,128)} %bitcast.262), channel_id=1, source_target_pairs={{0,32},{16,48},{32,0},{48,16},{64,96},{80,112},{96,64},{112,80},{1... | collective-permute-start | bytes 3145736 | tf_op jit(solution)/shard_map/ppermute | solution.py:39
  97.7 109.2 %collective-permute-start.12 = (f32[64,64,64]{2,0,1:T(8,128)}, f32[64,64,64]{2,0,1:T(8,128)}, u32[]{:S(2)}, u32[]{:S(2)}) collective-permute-start(f32[64,64,64]{2,0,1:T(8,128)} %bitcast.263), channel_id=1, source_target_pairs={{0,16},{16,32},{32,48},{48,0},{64,80},{80,96},{96,112},{112,64},{1... | collective-permute-start | bytes 3145736 | tf_op jit(solution)/shard_map/ppermute | solution.py:39
  105.9 7.4 copy-start.11
  112.4 77.9 %collective-permute-start.20 = (f32[64,64,3]{1,0,2:T(8,128)}, f32[64,64,3]{1,0,2:T(8,128)}, u32[]{:S(2)}, u32[]{:S(2)}) collective-permute-start(f32[64,64,3]{1,0,2:T(8,128)} %broadcast_select_fusion.23), channel_id=1, source_target_pairs={{0,16},{16,0},{32,48},{48,32},{64,80},{80,64},{96,112},{112,96},{1... | collective-permute-start | bytes 147464 | tf_op jit(solution)/shard_map/ppermute | solution.py:81
  195.9 11.0 %copy-start = (f32[1,1,64,4096]{2,3,1,0:T(8,128)S(1)}, f32[1,1,64,4096]{2,3,1,0:T(8,128)}, u32[]{:S(2)}) copy-start(f32[1,1,64,4096]{2,3,1,0:T(8,128)} %copy.244) | copy-start | bytes 3145732
  195.9 11.0 %copy-start.1 = (f32[1,1,64,4096]{2,3,1,0:T(8,128)S(1)}, f32[1,1,64,4096]{2,3,1,0:T(8,128)}, u32[]{:S(2)}) copy-start(f32[1,1,64,4096]{2,3,1,0:T(8,128)} %copy.243) | copy-start | bytes 3145732
  195.9 11.0 %copy-start.2 = (f32[1,1,64,4096]{2,3,1,0:T(8,128)S(1)}, f32[1,1,64,4096]{2,3,1,0:T(8,128)}, u32[]{:S(2)}) copy-start(f32[1,1,64,4096]{2,3,1,0:T(8,128)} %copy.242) | copy-start | bytes 3145732
  206.2 11.8 %collective-permute-start.21 = (f32[64,3,64]{2,1,0:T(4,128)S(1)}, f32[64,3,64]{2,1,0:T(4,128)S(1)}, u32[]{:S(2)}, u32[]{:S(2)}) collective-permute-start(f32[64,3,64]{2,1,0:T(4,128)S(1)} %slice_select_fusion.1), channel_id=1, source_target_pairs={{0,48},{16,32},{32,16},{48,0},{64,112},{80,96},{96,80},{112,64},{1... | collective-permute-start | bytes 147464 | tf_op jit(solution)/shard_map/ppermute | solution.py:81
  214.0 148.0 %collective-permute-start.13 = (f32[64,64,64]{2,0,1:T(8,128)}, f32[64,64,64]{2,0,1:T(8,128)}, u32[]{:S(2)}, u32[]{:S(2)}) collective-permute-start(f32[64,64,64]{2,0,1:T(8,128)} %get-tuple-element.9), channel_id=1, source_target_pairs={{0,192},{16,208},{32,224},{48,240},{64,0},{80,16},{96,32},{112,48}... | collective-permute-start | bytes 3145736 | tf_op jit(solution)/shard_map/ppermute | solution.py:50
  215.2 182.5 %collective-permute-start.14 = (f32[64,64,64]{2,0,1:T(8,128)}, f32[64,64,64]{2,0,1:T(8,128)}, u32[]{:S(2)}, u32[]{:S(2)}) collective-permute-start(f32[64,64,64]{2,0,1:T(8,128)} %get-tuple-element.8), channel_id=1, source_target_pairs={{0,128},{16,144},{32,160},{48,176},{64,192},{80,208},{96,224},{112... | collective-permute-start | bytes 3145736 | tf_op jit(solution)/shard_map/ppermute | solution.py:50
  216.0 181.7 %collective-permute-start.15 = (f32[64,64,64]{2,0,1:T(8,128)}, f32[64,64,64]{2,0,1:T(8,128)}, u32[]{:S(2)}, u32[]{:S(2)}) collective-permute-start(f32[64,64,64]{2,0,1:T(8,128)} %get-tuple-element.7), channel_id=1, source_target_pairs={{0,64},{16,80},{32,96},{48,112},{64,128},{80,144},{96,160},{112,17... | collective-permute-start | bytes 3145736 | tf_op jit(solution)/shard_map/ppermute | solution.py:50
  227.6 39.9 %collective-permute-start.23 = (f32[7,64,64]{1,2,0:T(8,128)}, f32[7,64,64]{1,2,0:T(8,128)}, u32[]{:S(2)}, u32[]{:S(2)}) collective-permute-start(f32[7,64,64]{1,2,0:T(8,128)} %get-tuple-element.29), channel_id=1, source_target_pairs={{64,0},{80,16},{96,32},{112,48},{128,64},{144,80},{160,96},{176,11... | collective-permute-start | bytes 344072 | tf_op jit(solution)/shard_map/ppermute | solution.py:94
  228.9 125.9 %collective-permute-start.22 = (f32[7,64,64]{1,2,0:T(8,128)S(1)}, f32[7,64,64]{1,2,0:T(8,128)}, u32[]{:S(2)}, u32[]{:S(2)}) collective-permute-start(f32[7,64,64]{1,2,0:T(8,128)S(1)} %get-tuple-element.28), channel_id=1, source_target_pairs={{0,64},{16,80},{32,96},{48,112},{64,128},{80,144},{96,160},{112,17... | collective-permute-start | bytes 344072 | tf_op jit(solution)/shard_map/ppermute | solution.py:93
  357.5 40.2 %copy-start.5 = (f32[1,1,64,4096]{2,3,1,0:T(8,128)S(1)}, f32[1,1,64,4096]{2,3,1,0:T(8,128)}, u32[]{:S(2)}) copy-start(f32[1,1,64,4096]{2,3,1,0:T(8,128)} %copy.245) | copy-start | bytes 3145732
  401.2 15.5 %copy-start.7 = (f32[64,64,64]{2,0,1:T(8,128)}, f32[64,64,64]{2,0,1:T(8,128)S(1)}, u32[]{:S(2)}) copy-start(f32[64,64,64]{2,0,1:T(8,128)S(1)} %select_select_fusion) | copy-start | bytes 3145732
  416.8 19.2 %collective-permute-start.25 = (f32[7,64,64]{2,0,1:T(8,128)S(1)}, f32[7,64,64]{2,0,1:T(8,128)S(1)}, u32[]{:S(2)}, u32[]{:S(2)}) collective-permute-start(f32[7,64,64]{2,0,1:T(8,128)S(1)} %get-tuple-element.27), channel_id=1, source_target_pairs={{64,0},{80,16},{96,32},{112,48},{128,64},{144,80},{160,96},{176,11... | collective-permute-start | bytes 344072 | tf_op jit(solution)/shard_map/ppermute | solution.py:94
  418.1 19.1 %collective-permute-start.24 = (f32[7,64,64]{2,0,1:T(8,128)S(1)}, f32[7,64,64]{2,0,1:T(8,128)S(1)}, u32[]{:S(2)}, u32[]{:S(2)}) collective-permute-start(f32[7,64,64]{2,0,1:T(8,128)S(1)} %get-tuple-element.26), channel_id=1, source_target_pairs={{0,64},{16,80},{32,96},{48,112},{64,128},{80,144},{96,160},{112,17... | collective-permute-start | bytes 344072 | tf_op jit(solution)/shard_map/ppermute | solution.py:93
  449.5 5.3 collective-permute-start.26
  467.2 6.0 collective-permute-start.27
  485.0 3.2 collective-permute-start.28
  489.4 14.1 %collective-permute-start.29 = (f32[64,2,2,4,64]{4,0,3,2,1:T(8,128)S(1)}, f32[64,2,2,4,64]{4,0,3,2,1:T(8,128)S(1)}, u32[]{:S(2)}, u32[]{:S(2)}) collective-permute-start(f32[64,2,2,4,64]{4,0,3,2,1:T(8,128)S(1)} %select_bitcast_fusion.9), channel_id=1, source_target_pairs={{0,4},{1,5},{2,6},{3,7},{4,0},{5,1},{6,2},{7,3},{8,12},{9,13},{10,... | collective-permute-start | bytes 786440 | tf_op jit(solution)/shard_map/ppermute | solution.py:118
  503.7 9.1 %collective-permute-start.30 = (f32[64,2,4,64]{3,0,2,1:T(8,128)S(1)}, f32[64,2,4,64]{3,0,2,1:T(8,128)S(1)}, u32[]{:S(2)}, u32[]{:S(2)}) collective-permute-start(f32[64,2,4,64]{3,0,2,1:T(8,128)S(1)} %select_bitcast_fusion.15), channel_id=1, source_target_pairs={{0,8},{1,9},{2,10},{3,11},{4,12},{5,13},{6,14},{7,15},{8,0},{9,1},... | collective-permute-start | bytes 393224 | tf_op jit(solution)/shard_map/ppermute | solution.py:118
  512.8 11.1 %collective-permute-start.31 = (f32[64,4,64]{2,0,1:T(8,128)S(1)}, f32[64,4,64]{2,0,1:T(8,128)S(1)}, u32[]{:S(2)}, u32[]{:S(2)}) collective-permute-start(f32[64,4,64]{2,0,1:T(8,128)S(1)} %select_bitcast_fusion.21), channel_id=1, source_target_pairs={{0,2},{1,3},{2,0},{3,1},{4,6},{5,7},{6,4},{7,5},{8,10},{9,11},{10,... | collective-permute-start | bytes 196616 | tf_op jit(solution)/shard_map/ppermute | solution.py:118
  524.6 10.4 %collective-permute-start.32 = (f32[64,4,64]{2,0,1:T(8,128)S(1)}, f32[64,4,64]{2,0,1:T(8,128)S(1)}, u32[]{:S(2)}, u32[]{:S(2)}) collective-permute-start(f32[64,4,64]{2,0,1:T(8,128)S(1)} %fusion.51), channel_id=1, source_target_pairs={{0,2},{1,3},{2,0},{3,1},{4,6},{5,7},{6,4},{7,5},{8,10},{9,11},{10,... | collective-permute-start | bytes 196616 | tf_op jit(solution)/shard_map/ppermute | solution.py:128
  535.0 10.6 %collective-permute-start.33 = (f32[64,2,4,64]{3,0,2,1:T(8,128)S(1)}, f32[64,2,4,64]{3,0,2,1:T(8,128)S(1)}, u32[]{:S(2)}, u32[]{:S(2)}) collective-permute-start(f32[64,2,4,64]{3,0,2,1:T(8,128)S(1)} %pad_maximum_fusion.13), channel_id=1, source_target_pairs={{0,8},{1,9},{2,10},{3,11},{4,12},{5,13},{6,14},{7,15},{8,0},{9,1},... | collective-permute-start | bytes 393224 | tf_op jit(solution)/shard_map/ppermute | solution.py:128
  545.7 9.3 %collective-permute-start.34 = (f32[64,2,2,4,64]{4,0,3,2,1:T(8,128)S(1)}, f32[64,2,2,4,64]{4,0,3,2,1:T(8,128)S(1)}, u32[]{:S(2)}, u32[]{:S(2)}) collective-permute-start(f32[64,2,2,4,64]{4,0,3,2,1:T(8,128)S(1)} %pad_maximum_fusion.11), channel_id=1, source_target_pairs={{0,4},{1,5},{2,6},{3,7},{4,0},{5,1},{6,2},{7,3},{8,12},{9,13},{10,... | collective-permute-start | bytes 786440 | tf_op jit(solution)/shard_map/ppermute | solution.py:128
  555.2 2.7 collective-permute-start.35
  567.4 5.4 collective-permute-start.36
  573.4 4.2 copy-start.4
  587.2 5.1 collective-permute-start.37
  601.2 8.1 %collective-permute-start.39 = (f32[7,64,64]{1,2,0:T(8,128)S(1)}, f32[7,64,64]{1,2,0:T(8,128)S(1)}, u32[]{:S(2)}, u32[]{:S(2)}) collective-permute-start(f32[7,64,64]{1,2,0:T(8,128)S(1)} %get-tuple-element.17), channel_id=1, source_target_pairs={{64,0},{80,16},{96,32},{112,48},{128,64},{144,80},{160,96},{176,11... | collective-permute-start | bytes 344072 | tf_op jit(solution)/shard_map/ppermute | solution.py:94
  602.5 8.1 %collective-permute-start.38 = (f32[7,64,64]{1,2,0:T(8,128)S(1)}, f32[7,64,64]{1,2,0:T(8,128)S(1)}, u32[]{:S(2)}, u32[]{:S(2)}) collective-permute-start(f32[7,64,64]{1,2,0:T(8,128)S(1)} %get-tuple-element.16), channel_id=1, source_target_pairs={{0,64},{16,80},{32,96},{48,112},{64,128},{80,144},{96,160},{112,17... | collective-permute-start | bytes 344072 | tf_op jit(solution)/shard_map/ppermute | solution.py:93
  631.9 8.7 %collective-permute-start.41 = (f32[7,64,64]{2,0,1:T(8,128)S(1)}, f32[7,64,64]{2,0,1:T(8,128)S(1)}, u32[]{:S(2)}, u32[]{:S(2)}) collective-permute-start(f32[7,64,64]{2,0,1:T(8,128)S(1)} %get-tuple-element.15), channel_id=1, source_target_pairs={{64,0},{80,16},{96,32},{112,48},{128,64},{144,80},{160,96},{176,11... | collective-permute-start | bytes 344072 | tf_op jit(solution)/shard_map/ppermute | solution.py:94
  633.2 8.9 %collective-permute-start.40 = (f32[7,64,64]{2,0,1:T(8,128)S(1)}, f32[7,64,64]{2,0,1:T(8,128)S(1)}, u32[]{:S(2)}, u32[]{:S(2)}) collective-permute-start(f32[7,64,64]{2,0,1:T(8,128)S(1)} %get-tuple-element.14), channel_id=1, source_target_pairs={{0,64},{16,80},{32,96},{48,112},{64,128},{80,144},{96,160},{112,17... | collective-permute-start | bytes 344072 | tf_op jit(solution)/shard_map/ppermute | solution.py:93
  654.4 5.1 collective-permute-start.42
  671.9 7.2 collective-permute-start.43
  690.9 2.7 collective-permute-start.44
  694.9 14.1 %collective-permute-start.45 = (f32[64,2,2,4,64]{4,0,3,2,1:T(8,128)S(1)}, f32[64,2,2,4,64]{4,0,3,2,1:T(8,128)S(1)}, u32[]{:S(2)}, u32[]{:S(2)}) collective-permute-start(f32[64,2,2,4,64]{4,0,3,2,1:T(8,128)S(1)} %select_bitcast_fusion.6), channel_id=1, source_target_pairs={{0,4},{1,5},{2,6},{3,7},{4,0},{5,1},{6,2},{7,3},{8,12},{9,13},{10,... | collective-permute-start | bytes 786440 | tf_op jit(solution)/shard_map/ppermute | solution.py:118
  709.2 9.3 %collective-permute-start.46 = (f32[64,2,4,64]{3,0,2,1:T(8,128)S(1)}, f32[64,2,4,64]{3,0,2,1:T(8,128)S(1)}, u32[]{:S(2)}, u32[]{:S(2)}) collective-permute-start(f32[64,2,4,64]{3,0,2,1:T(8,128)S(1)} %select_bitcast_fusion.12), channel_id=1, source_target_pairs={{0,8},{1,9},{2,10},{3,11},{4,12},{5,13},{6,14},{7,15},{8,0},{9,1},... | collective-permute-start | bytes 393224 | tf_op jit(solution)/shard_map/ppermute | solution.py:118
  718.5 9.1 %collective-permute-start.47 = (f32[64,4,64]{2,0,1:T(8,128)S(1)}, f32[64,4,64]{2,0,1:T(8,128)S(1)}, u32[]{:S(2)}, u32[]{:S(2)}) collective-permute-start(f32[64,4,64]{2,0,1:T(8,128)S(1)} %select_bitcast_fusion.18), channel_id=1, source_target_pairs={{0,2},{1,3},{2,0},{3,1},{4,6},{5,7},{6,4},{7,5},{8,10},{9,11},{10,... | collective-permute-start | bytes 196616 | tf_op jit(solution)/shard_map/ppermute | solution.py:118
  728.3 11.2 %collective-permute-start.48 = (f32[64,4,64]{2,0,1:T(8,128)S(1)}, f32[64,4,64]{2,0,1:T(8,128)S(1)}, u32[]{:S(2)}, u32[]{:S(2)}) collective-permute-start(f32[64,4,64]{2,0,1:T(8,128)S(1)} %get-tuple-element.60), channel_id=1, source_target_pairs={{0,48},{16,0},{32,16},{48,32},{64,112},{80,64},{96,80},{112,96},{1... | collective-permute-start | bytes 196616 | tf_op jit(solution)/shard_map/ppermute | solution.py:39
  730.4 9.1 %collective-permute-start.49 = (f32[64,4,64]{2,0,1:T(8,128)S(1)}, f32[64,4,64]{2,0,1:T(8,128)S(1)}, u32[]{:S(2)}, u32[]{:S(2)}) collective-permute-start(f32[64,4,64]{2,0,1:T(8,128)S(1)} %get-tuple-element.59), channel_id=1, source_target_pairs={{0,32},{16,48},{32,0},{48,16},{64,96},{80,112},{96,64},{112,80},{1... | collective-permute-start | bytes 196616 | tf_op jit(solution)/shard_map/ppermute | solution.py:39
  730.6 9.0 %collective-permute-start.50 = (f32[64,4,64]{2,0,1:T(8,128)S(1)}, f32[64,4,64]{2,0,1:T(8,128)S(1)}, u32[]{:S(2)}, u32[]{:S(2)}) collective-permute-start(f32[64,4,64]{2,0,1:T(8,128)S(1)} %get-tuple-element.5), channel_id=1, source_target_pairs={{0,16},{16,32},{32,48},{48,0},{64,80},{80,96},{96,112},{112,64},{1... | collective-permute-start | bytes 196616 | tf_op jit(solution)/shard_map/ppermute | solution.py:39
  739.6 10.9 %collective-permute-start.51 = (f32[64,4,64]{2,0,1:T(8,128)S(1)}, f32[64,4,64]{2,0,1:T(8,128)S(1)}, u32[]{:S(2)}, u32[]{:S(2)}) collective-permute-start(f32[64,4,64]{2,0,1:T(8,128)S(1)} %get-tuple-element.47), channel_id=1, source_target_pairs={{0,192},{16,208},{32,224},{48,240},{64,0},{80,16},{96,32},{112,48}... | collective-permute-start | bytes 196616 | tf_op jit(solution)/shard_map/ppermute | solution.py:50
  746.7 8.2 %collective-permute-start.52 = (f32[64,4,64]{2,0,1:T(8,128)S(1)}, f32[64,4,64]{2,0,1:T(8,128)S(1)}, u32[]{:S(2)}, u32[]{:S(2)}) collective-permute-start(f32[64,4,64]{2,0,1:T(8,128)S(1)} %get-tuple-element.46), channel_id=1, source_target_pairs={{0,128},{16,144},{32,160},{48,176},{64,192},{80,208},{96,224},{112... | collective-permute-start | bytes 196616 | tf_op jit(solution)/shard_map/ppermute | solution.py:50
  746.7 8.2 %collective-permute-start.53 = (f32[64,4,64]{2,0,1:T(8,128)S(1)}, f32[64,4,64]{2,0,1:T(8,128)S(1)}, u32[]{:S(2)}, u32[]{:S(2)}) collective-permute-start(f32[64,4,64]{2,0,1:T(8,128)S(1)} %get-tuple-element.45), channel_id=1, source_target_pairs={{0,64},{16,80},{32,96},{48,112},{64,128},{80,144},{96,160},{112,17... | collective-permute-start | bytes 196616 | tf_op jit(solution)/shard_map/ppermute | solution.py:50
  (2 other events, 7.7 us)

commit v6 on v5

--- a/solution.py
+++ b/solution.py
@@ -178,6 +178,7 @@
         for axis, taps in ((2, along_x), (1, along_y), (0, along_z))
         for flipped in (False, True)
     }
+    bands = lax.optimization_barrier(bands)
     for sweep_no in range(ITERS):
         full = view_all_gather(share, nv)
         blurred = convolve(pair_halo(full, 2, radius_x, 1, my_x == 1), bands[2, False], 2)

time: 768 us -> 703 us (0.915)
  matrix products: 125 us -> 52.8 us
  other arithmetic: 47.2 us -> 66.8 us
  waiting for transfers between devices: 353 us -> 336 us
    dot_general x4, matrix products: 56.3 us -> 18.9 us  [convolve(): return jnp.einsum('ot,tab->oab', band, extended, precision=hi)]
    select_n x0 -> x3, other arithmetic: none -> 20.2 us  [band_matrix(): band = jnp.where(offset == position, weight, band)]
    dot_general x4, matrix products: 36.9 us -> 19.2 us  [convolve(): return jnp.einsum('abt,ot->abo', extended, band, precision=hi)]
    dot_general x4, matrix products: 31.7 us -> 14.7 us  [convolve(): return jnp.einsum('ot,atb->aob', band, extended, precision=hi)]
    ppermute x8, waiting for transfers between devices: 41.6 us -> 27.2 us  [view_all_gather(): recv = lax.ppermute(x, 'view', xor_pairs(nv, m))]
    ppermute x8, waiting for transfers between devices: 82.2 us -> 73.3 us  [pair_halo(): recv = lax.ppermute(send, 'space', [(i, i ^ partner) for i in range(nsp)])]
    ppermute x8, starting transfers between devices: 19.7 us -> 28.1 us  [view_all_gather(): recv = lax.ppermute(x, 'view', xor_pairs(nv, m))]
  transfers between devices with their start and end apart: 54 -> 54, of which waited for: 37 -> 36; matrix products, arithmetic and copies ran while one was open for 12% -> 14% of each run, Pallas kernels for 0% -> 0%
where the time goes in v6:
time: 703 us; the launch traced here: 692 us
  waiting for transfers between devices  336 us (48%)
  starting transfers between devices  135 us (19%)
  local copies, waits for them, and re-layouts  73.3 us (10%)
  other arithmetic  66.8 us (10%)
  matrix products  52.8 us (8%)
  between operations  28.5 us (4%)
    ppermute x4, waiting for transfers between devices, z_halo(): low = lax.ppermute(last, 'space', [(i, i + ROW) for i in range(nsp - ROW)])  91.1 us
    ppermute x8, waiting for transfers between devices, pair_halo(): recv = lax.ppermute(send, 'space', [(i, i ^ partner) for i in range(nsp)])  73.3 us
    ppermute x8, waiting for transfers between devices, view_reduce_scatter(): x = keep + lax.ppermute(send, 'view', xor_pairs(nv, m))  52.9 us
    ppermute x4, waiting for transfers between devices, z_halo(): lax.ppermute(first, 'space', [(i + ROW, i) for i in range(nsp - ROW)])  43.1 us
    ppermute x18, waiting for transfers between devices, route(): part = lax.ppermute(part, 'space', pairs)  41.6 us
    ppermute x4, starting transfers between devices, z_halo(): low = lax.ppermute(last, 'space', [(i, i + ROW) for i in range(nsp - ROW)])  32.1 us
    ppermute x18, starting transfers between devices, route(): part = lax.ppermute(part, 'space', pairs)  30.3 us
    ppermute x8, starting transfers between devices, view_all_gather(): recv = lax.ppermute(x, 'view', xor_pairs(nv, m))  28.1 us
  transfers between devices with their start and end apart: 54, of which 36 were waited for; matrix products, arithmetic and copies ran while one was open for 14% of the time, Pallas kernels for 0%

profile of v6, /device:TPU:8, one launch (start us, length us, event | category | flops | bytes accessed | tf_op | source)
XLA Modules:
  0.0 692.2 jit_solution(14040490805730154603)
XLA Ops:
  7.5 3.0 collective-permute-done.1
  14.1 3.1 collective-permute-start.3
  39.8 4.4 collective-permute-start.7
  51.5 8.4 %collective-permute-start.16 = (f32[64,4,64]{2,0,1:T(8,128)S(1)}, f32[64,4,64]{2,0,1:T(8,128)S(1)}, u32[]{:S(2)}, u32[]{:S(2)}) collective-permute-start(f32[64,4,64]{2,0,1:T(8,128)S(1)} %select_select_fusion.12), channel_id=1, source_target_pairs={{0,2},{1,3},{2,0},{3,1},{4,6},{5,7},{6,4},{7,5},{8,10},{9,11},{10,... | collective-permute-start | bytes 196616 | tf_op jit(solution)/shard_map/ppermute | solution.py:128
  63.0 3.1 collective-permute-start.17
  67.5 6.3 collective-permute-done.17
  76.1 5.0 select_select_fusion.22
  81.1 5.1 select_select_fusion.20
  87.5 3.0 select_select_fusion.4
  91.1 3.1 copy.239
  94.6 3.1 copy.240
  98.9 3.2 copy.241
  117.0 10.2 %select_select_fusion.24 = (f32[64,78]{1,0:T(8,128)}, f32[64,78]{1,0:T(8,128)}) fusion(f32[]{:T(128)} %bitcast.47, f32[]{:T(128)} %bitcast.46, f32[]{:T(128)} %bitcast.45, f32[]{:T(128)} %bitcast.44, f32[]{:T(128)} %bitcast.43, f32[]{:T(128)} %bitcast.42, f32[]{:T(128)} %bitcast.41, f32[]{:T(128)} %bitcast.40, f32[]{:T(128)} %bitcast.39, f32[]{:T(128)} %bitcast.38, ...), kind=kLoop, calls=%fused_computation.175 | loop fusion | flops 229632 | bytes 39996 | tf_op jit(solution)/shard_map/jit(_where)/select_n | solution.py:62
  127.2 3.2 copy.244
  130.4 3.2 copy.243
  133.5 3.1 copy.242
  139.8 54.8 %collective-permute-done.20 = f32[64,64,3]{1,0,2:T(8,128)} collective-permute-done((f32[64,64,3]{1,0,2:T(8,128)}, f32[64,64,3]{1,0,2:T(8,128)}, u32[]{:S(2)}, u32[]{:S(2)}) %collective-permute-start.20) | collective-permute-done | bytes 49184 | tf_op jit(solution)/shard_map/ppermute | solution.py:81
  200.3 4.8 fusion.28
  206.3 7.0 %select_select_fusion.1 = (f32[64,64,64]{2,0,1:T(8,128)}, f32[64,64,64]{2,0,1:T(8,128)}, f32[64,64,64]{2,0,1:T(8,128)}) fusion(f32[64,64,64]{2,0,1:T(8,128)} %collective-permute-done.10, f32[64,64,64]{2,0,1:T(8,128)} %collective-permute-done.11, f32[64,64,64]{2,0,1:T(8,128)} %collective-permute-done.12, f32[64,64,64]{2,0,1:T(8,128)S(1)} %bitcast.255, ...), kind=kLoop, calls=%fused_computation.52 | loop fusion | flops 2359296 | bytes 9437193 | tf_op jit(solution)/shard_map/jit(_where)/select_n | solution.py:47
  218.5 3.9 fusion.43
  224.4 5.4 collective-permute-start.22
  231.8 34.9 %collective-permute-done.23 = f32[7,64,64]{1,2,0:T(8,128)} collective-permute-done((f32[7,64,64]{1,2,0:T(8,128)}, f32[7,64,64]{1,2,0:T(8,128)}, u32[]{:S(2)}, u32[]{:S(2)}) %collective-permute-start.23) | collective-permute-done | bytes 114720 | tf_op jit(solution)/shard_map/ppermute | solution.py:94
  266.7 87.3 %collective-permute-done.22 = f32[7,64,64]{1,2,0:T(8,128)} collective-permute-done((f32[7,64,64]{1,2,0:T(8,128)}, f32[7,64,64]{1,2,0:T(8,128)}, u32[]{:S(2)}, u32[]{:S(2)}) %collective-permute-start.22) | collective-permute-done | bytes 114720 | tf_op jit(solution)/shard_map/ppermute | solution.py:93
  354.0 2.7 pad_maximum_fusion
  356.7 4.6 copy.256
  361.3 36.2 %collective-permute-done.14 = f32[64,64,64]{2,0,1:T(8,128)} collective-permute-done((f32[64,64,64]{2,0,1:T(8,128)}, f32[64,64,64]{2,0,1:T(8,128)}, u32[]{:S(2)}, u32[]{:S(2)}) %collective-permute-start.14) | collective-permute-done | bytes 1048608 | tf_op jit(solution)/shard_map/ppermute | solution.py:50
  399.4 6.1 convolution_divide_fusion.1
  406.9 15.5 %collective-permute-start.24 = (f32[7,64,64]{2,0,1:T(8,128)S(1)}, f32[7,64,64]{2,0,1:T(8,128)S(1)}, u32[]{:S(2)}, u32[]{:S(2)}) collective-permute-start(f32[7,64,64]{2,0,1:T(8,128)S(1)} %get-tuple-element.38), channel_id=1, source_target_pairs={{0,64},{16,80},{32,96},{48,112},{64,128},{80,144},{96,160},{112,17... | collective-permute-start | bytes 344072 | tf_op jit(solution)/shard_map/ppermute | solution.py:93
  422.4 3.5 collective-permute-done.25
  432.0 3.3 collective-permute-done.26
  436.2 3.2 copy.288
  439.4 3.5 convolution_bitcast_fusion.1
  443.5 3.4 collective-permute-start.27
  450.5 4.8 fusion.26
  462.0 13.6 %collective-permute-done.29 = f32[64,2,2,4,64]{4,0,3,2,1:T(8,128)S(1)} collective-permute-done((f32[64,2,2,4,64]{4,0,3,2,1:T(8,128)S(1)}, f32[64,2,2,4,64]{4,0,3,2,1:T(8,128)S(1)}, u32[]{:S(2)}, u32[]{:S(2)}) %collective-permute-start.29) | collective-permute-done | bytes 262176 | tf_op jit(solution)/shard_map/ppermute | solution.py:118
  475.7 2.8 collective-permute-start.30
  478.5 6.3 collective-permute-done.30
  484.9 4.9 collective-permute-start.31
  490.4 3.6 collective-permute-done.31
  494.6 5.6 collective-permute-start.32
  500.2 3.5 collective-permute-done.32
  503.7 2.8 collective-permute-start.33
  506.6 5.2 collective-permute-done.33
  511.8 6.6 collective-permute-start.34
  518.5 7.2 %collective-permute-done.34 = f32[64,2,2,4,64]{4,0,3,2,1:T(8,128)S(1)} collective-permute-done((f32[64,2,2,4,64]{4,0,3,2,1:T(8,128)S(1)}, f32[64,2,2,4,64]{4,0,3,2,1:T(8,128)S(1)}, u32[]{:S(2)}, u32[]{:S(2)}) %collective-permute-start.34) | collective-permute-done | bytes 262176 | tf_op jit(solution)/shard_map/ppermute | solution.py:128
  529.4 2.7 fusion.107
  548.3 4.7 fusion.34
  553.8 4.9 collective-permute-done.37
  559.3 4.0 fusion.40
  564.6 6.2 collective-permute-start.38
  574.5 3.3 copy.274
  577.8 8.3 %convolution_divide_fusion = f32[64,64,64]{2,0,1:T(8,128)S(1)} fusion(f32[64,64,64]{2,0,1:T(8,128)} %copy-done.7, f32[78,64,64]{0,2,1:T(8,128)} %copy.274, f32[64,78]{1,0:T(8,128)S(1)} %copy-done.13), kind=kOutput, calls=%fused_computation.58 | convolution fusion | flops 245628928 | bytes 3395072 | tf_op jit(solution)/shard_map/ot,tab->oab/dot_general | solution.py:69
  587.5 5.0 collective-permute-start.40
  599.8 4.5 collective-permute-done.42
  605.3 3.2 copy.292
  608.5 3.5 convolution_bitcast_fusion
  612.6 4.2 collective-permute-start.43
  620.4 4.8 fusion.24
  631.7 13.3 %collective-permute-done.45 = f32[64,2,2,4,64]{4,0,3,2,1:T(8,128)S(1)} collective-permute-done((f32[64,2,2,4,64]{4,0,3,2,1:T(8,128)S(1)}, f32[64,2,2,4,64]{4,0,3,2,1:T(8,128)S(1)}, u32[]{:S(2)}, u32[]{:S(2)}) %collective-permute-start.45) | collective-permute-done | bytes 262176 | tf_op jit(solution)/shard_map/ppermute | solution.py:118
  647.4 7.0 %collective-permute-done.46 = f32[64,2,4,64]{3,0,2,1:T(8,128)S(1)} collective-permute-done((f32[64,2,4,64]{3,0,2,1:T(8,128)S(1)}, f32[64,2,4,64]{3,0,2,1:T(8,128)S(1)}, u32[]{:S(2)}, u32[]{:S(2)}) %collective-permute-start.46) | collective-permute-done | bytes 131104 | tf_op jit(solution)/shard_map/ppermute | solution.py:118
  654.4 5.2 collective-permute-start.47
  659.6 3.9 collective-permute-done.47
  676.0 6.6 collective-permute-start.51
  686.4 4.5 collective-permute-done.52
  (229 shorter events, 146.7 us)
Async XLA Ops:
  0.0 32.3 %copy-start.14 = (f32[1,15]{1,0:T(1,128)S(1)}, f32[1,15]{1,0:T(1,128)}, u32[]{:S(2)}) copy-start(f32[1,15]{1,0:T(1,128)} %param.11) | copy-start | bytes 184
  0.0 33.0 %copy-start.15 = (f32[1,7]{1,0:T(1,128)S(1)}, f32[1,7]{1,0:T(1,128)}, u32[]{:S(2)}) copy-start(f32[1,7]{1,0:T(1,128)} %param.10) | copy-start | bytes 88
  1.5 3.8 collective-permute-start
  5.3 5.1 collective-permute-start.1
  7.5 38.0 %copy-start.16 = (f32[1,7]{1,0:T(1,128)S(1)}, f32[1,7]{1,0:T(1,128)}, u32[]{:S(2)}) copy-start(f32[1,7]{1,0:T(1,128)} %param.9) | copy-start | bytes 88
  10.5 3.6 collective-permute-start.2
  14.1 4.7 collective-permute-start.3
  26.9 12.8 %collective-permute-start.4 = (f32[64,4,64]{2,0,1:T(8,128)S(1)}, f32[64,4,64]{2,0,1:T(8,128)S(1)}, u32[]{:S(2)}, u32[]{:S(2)}) collective-permute-start(f32[64,4,64]{2,0,1:T(8,128)S(1)} %bitcast.269), channel_id=1, source_target_pairs={{0,48},{16,0},{32,16},{48,32},{64,112},{80,64},{96,80},{112,96},{1... | collective-permute-start | bytes 196616 | tf_op jit(solution)/shard_map/ppermute | solution.py:39
  29.0 10.7 %collective-permute-start.5 = (f32[64,4,64]{2,0,1:T(8,128)S(1)}, f32[64,4,64]{2,0,1:T(8,128)S(1)}, u32[]{:S(2)}, u32[]{:S(2)}) collective-permute-start(f32[64,4,64]{2,0,1:T(8,128)S(1)} %bitcast.270), channel_id=1, source_target_pairs={{0,32},{16,48},{32,0},{48,16},{64,96},{80,112},{96,64},{112,80},{1... | collective-permute-start | bytes 196616 | tf_op jit(solution)/shard_map/ppermute | solution.py:39
  30.3 9.4 %collective-permute-start.6 = (f32[64,4,64]{2,0,1:T(8,128)S(1)}, f32[64,4,64]{2,0,1:T(8,128)S(1)}, u32[]{:S(2)}, u32[]{:S(2)}) collective-permute-start(f32[64,4,64]{2,0,1:T(8,128)S(1)} %bitcast.271), channel_id=1, source_target_pairs={{0,16},{16,32},{32,48},{48,0},{64,80},{80,96},{96,112},{112,64},{1... | collective-permute-start | bytes 196616 | tf_op jit(solution)/shard_map/ppermute | solution.py:39
  39.8 10.8 %collective-permute-start.7 = (f32[64,4,64]{2,0,1:T(8,128)S(1)}, f32[64,4,64]{2,0,1:T(8,128)S(1)}, u32[]{:S(2)}, u32[]{:S(2)}) collective-permute-start(f32[64,4,64]{2,0,1:T(8,128)S(1)} %get-tuple-element.66), channel_id=1, source_target_pairs={{0,192},{16,208},{32,224},{48,240},{64,0},{80,16},{96,32},{112,48}... | collective-permute-start | bytes 196616 | tf_op jit(solution)/shard_map/ppermute | solution.py:50
  44.2 7.3 %collective-permute-start.8 = (f32[64,4,64]{2,0,1:T(8,128)S(1)}, f32[64,4,64]{2,0,1:T(8,128)S(1)}, u32[]{:S(2)}, u32[]{:S(2)}) collective-permute-start(f32[64,4,64]{2,0,1:T(8,128)S(1)} %get-tuple-element.65), channel_id=1, source_target_pairs={{0,128},{16,144},{32,160},{48,176},{64,192},{80,208},{96,224},{112... | collective-permute-start | bytes 196616 | tf_op jit(solution)/shard_map/ppermute | solution.py:50
  44.2 7.3 %collective-permute-start.9 = (f32[64,4,64]{2,0,1:T(8,128)S(1)}, f32[64,4,64]{2,0,1:T(8,128)S(1)}, u32[]{:S(2)}, u32[]{:S(2)}) collective-permute-start(f32[64,4,64]{2,0,1:T(8,128)S(1)} %get-tuple-element.64), channel_id=1, source_target_pairs={{0,64},{16,80},{32,96},{48,112},{64,128},{80,144},{96,160},{112,17... | collective-permute-start | bytes 196616 | tf_op jit(solution)/shard_map/ppermute | solution.py:50
  51.5 11.4 %collective-permute-start.16 = (f32[64,4,64]{2,0,1:T(8,128)S(1)}, f32[64,4,64]{2,0,1:T(8,128)S(1)}, u32[]{:S(2)}, u32[]{:S(2)}) collective-permute-start(f32[64,4,64]{2,0,1:T(8,128)S(1)} %select_select_fusion.12), channel_id=1, source_target_pairs={{0,2},{1,3},{2,0},{3,1},{4,6},{5,7},{6,4},{7,5},{8,10},{9,11},{10,... | collective-permute-start | bytes 196616 | tf_op jit(solution)/shard_map/ppermute | solution.py:128
  63.0 10.8 %collective-permute-start.17 = (f32[64,2,4,64]{3,0,2,1:T(8,128)S(1)}, f32[64,2,4,64]{3,0,2,1:T(8,128)S(1)}, u32[]{:S(2)}, u32[]{:S(2)}) collective-permute-start(f32[64,2,4,64]{3,0,2,1:T(8,128)S(1)} %pad_maximum_fusion.12), channel_id=1, source_target_pairs={{0,8},{1,9},{2,10},{3,11},{4,12},{5,13},{6,14},{7,15},{8,0},{9,1},... | collective-permute-start | bytes 393224 | tf_op jit(solution)/shard_map/ppermute | solution.py:128
  73.9 12.2 %collective-permute-start.18 = (f32[64,2,2,4,64]{4,0,3,2,1:T(8,128)S(1)}, f32[64,2,2,4,64]{4,0,3,2,1:T(8,128)S(1)}, u32[]{:S(2)}, u32[]{:S(2)}) collective-permute-start(f32[64,2,2,4,64]{4,0,3,2,1:T(8,128)S(1)} %pad_maximum_fusion.10), channel_id=1, source_target_pairs={{0,4},{1,5},{2,6},{3,7},{4,0},{5,1},{6,2},{7,3},{8,12},{9,13},{10,... | collective-permute-start | bytes 786440 | tf_op jit(solution)/shard_map/ppermute | solution.py:128
  87.4 18.4 %collective-permute-start.19 = (f32[64,2,2,2,4,64]{5,0,4,3,2,1:T(8,128)}, f32[64,2,2,2,4,64]{5,0,4,3,2,1:T(8,128)}, u32[]{:S(2)}, u32[]{:S(2)}) collective-permute-start(f32[64,2,2,2,4,64]{5,0,4,3,2,1:T(8,128)} %pad_maximum_fusion.8), channel_id=1, source_target_pairs={{0,1},{1,0},{2,3},{3,2},{4,5},{5,4},{6,7},{7,6},{8,9},{9,8},{10,11... | collective-permute-start | bytes 1572872 | tf_op jit(solution)/shard_map/ppermute | solution.py:128
  94.2 112.0 %collective-permute-start.10 = (f32[64,64,64]{2,0,1:T(8,128)}, f32[64,64,64]{2,0,1:T(8,128)}, u32[]{:S(2)}, u32[]{:S(2)}) collective-permute-start(f32[64,64,64]{2,0,1:T(8,128)} %bitcast.261), channel_id=1, source_target_pairs={{0,48},{16,0},{32,16},{48,32},{64,112},{80,64},{96,80},{112,96},{1... | collective-permute-start | bytes 3145736 | tf_op jit(solution)/shard_map/ppermute | solution.py:39
  97.7 108.6 %collective-permute-start.11 = (f32[64,64,64]{2,0,1:T(8,128)}, f32[64,64,64]{2,0,1:T(8,128)}, u32[]{:S(2)}, u32[]{:S(2)}) collective-permute-start(f32[64,64,64]{2,0,1:T(8,128)} %bitcast.262), channel_id=1, source_target_pairs={{0,32},{16,48},{32,0},{48,16},{64,96},{80,112},{96,64},{112,80},{1... | collective-permute-start | bytes 3145736 | tf_op jit(solution)/shard_map/ppermute | solution.py:39
  102.1 104.2 %collective-permute-start.12 = (f32[64,64,64]{2,0,1:T(8,128)}, f32[64,64,64]{2,0,1:T(8,128)}, u32[]{:S(2)}, u32[]{:S(2)}) collective-permute-start(f32[64,64,64]{2,0,1:T(8,128)} %bitcast.263), channel_id=1, source_target_pairs={{0,16},{16,32},{32,48},{48,0},{64,80},{80,96},{96,112},{112,64},{1... | collective-permute-start | bytes 3145736 | tf_op jit(solution)/shard_map/ppermute | solution.py:39
  116.8 77.8 %collective-permute-start.20 = (f32[64,64,3]{1,0,2:T(8,128)}, f32[64,64,3]{1,0,2:T(8,128)}, u32[]{:S(2)}, u32[]{:S(2)}) collective-permute-start(f32[64,64,3]{1,0,2:T(8,128)} %broadcast_select_fusion.23), channel_id=1, source_target_pairs={{0,16},{16,0},{32,48},{48,32},{64,80},{80,64},{96,112},{112,96},{1... | collective-permute-start | bytes 147464 | tf_op jit(solution)/shard_map/ppermute | solution.py:81
  200.3 6.0 copy-start
  200.3 6.0 copy-start.1
  200.3 6.0 copy-start.2
  205.7 12.1 %collective-permute-start.21 = (f32[64,3,64]{2,1,0:T(4,128)S(1)}, f32[64,3,64]{2,1,0:T(4,128)S(1)}, u32[]{:S(2)}, u32[]{:S(2)}) collective-permute-start(f32[64,3,64]{2,1,0:T(4,128)S(1)} %slice_select_fusion.1), channel_id=1, source_target_pairs={{0,48},{16,32},{32,16},{48,0},{64,112},{80,96},{96,80},{112,64},{1... | collective-permute-start | bytes 147464 | tf_op jit(solution)/shard_map/ppermute | solution.py:81
  206.3 12.2 %copy-start.9 = (f32[64,70]{1,0:T(8,128)S(1)}, f32[64,70]{1,0:T(8,128)}, u32[]{:S(2)}) copy-start(f32[64,70]{1,0:T(8,128)} %get-tuple-element.14) | copy-start | bytes 53764
  213.3 148.0 %collective-permute-start.13 = (f32[64,64,64]{2,0,1:T(8,128)}, f32[64,64,64]{2,0,1:T(8,128)}, u32[]{:S(2)}, u32[]{:S(2)}) collective-permute-start(f32[64,64,64]{2,0,1:T(8,128)} %get-tuple-element.21), channel_id=1, source_target_pairs={{0,192},{16,208},{32,224},{48,240},{64,0},{80,16},{96,32},{112,48}... | collective-permute-start | bytes 3145736 | tf_op jit(solution)/shard_map/ppermute | solution.py:50
  214.5 183.0 %collective-permute-start.14 = (f32[64,64,64]{2,0,1:T(8,128)}, f32[64,64,64]{2,0,1:T(8,128)}, u32[]{:S(2)}, u32[]{:S(2)}) collective-permute-start(f32[64,64,64]{2,0,1:T(8,128)} %get-tuple-element.20), channel_id=1, source_target_pairs={{0,128},{16,144},{32,160},{48,176},{64,192},{80,208},{96,224},{112... | collective-permute-start | bytes 3145736 | tf_op jit(solution)/shard_map/ppermute | solution.py:50
  215.8 181.7 %collective-permute-start.15 = (f32[64,64,64]{2,0,1:T(8,128)}, f32[64,64,64]{2,0,1:T(8,128)}, u32[]{:S(2)}, u32[]{:S(2)}) collective-permute-start(f32[64,64,64]{2,0,1:T(8,128)} %get-tuple-element.19), channel_id=1, source_target_pairs={{0,64},{16,80},{32,96},{48,112},{64,128},{80,144},{96,160},{112,17... | collective-permute-start | bytes 3145736 | tf_op jit(solution)/shard_map/ppermute | solution.py:50
  223.2 43.5 %collective-permute-start.23 = (f32[7,64,64]{1,2,0:T(8,128)}, f32[7,64,64]{1,2,0:T(8,128)}, u32[]{:S(2)}, u32[]{:S(2)}) collective-permute-start(f32[7,64,64]{1,2,0:T(8,128)} %get-tuple-element.41), channel_id=1, source_target_pairs={{64,0},{80,16},{96,32},{112,48},{128,64},{144,80},{160,96},{176,11... | collective-permute-start | bytes 344072 | tf_op jit(solution)/shard_map/ppermute | solution.py:94
  224.4 129.6 %collective-permute-start.22 = (f32[7,64,64]{1,2,0:T(8,128)}, f32[7,64,64]{1,2,0:T(8,128)}, u32[]{:S(2)}, u32[]{:S(2)}) collective-permute-start(f32[7,64,64]{1,2,0:T(8,128)} %get-tuple-element.40), channel_id=1, source_target_pairs={{0,64},{16,80},{32,96},{48,112},{64,128},{80,144},{96,160},{112,17... | collective-permute-start | bytes 344072 | tf_op jit(solution)/shard_map/ppermute | solution.py:93
  356.7 40.8 %copy-start.5 = (f32[1,1,64,4096]{2,3,1,0:T(8,128)S(1)}, f32[1,1,64,4096]{2,3,1,0:T(8,128)}, u32[]{:S(2)}) copy-start(f32[1,1,64,4096]{2,3,1,0:T(8,128)} %copy.245) | copy-start | bytes 3145732
  399.4 6.1 copy-start.7
  399.4 27.7 %copy-start.11 = (f32[64,78]{1,0:T(8,128)S(1)}, f32[64,78]{1,0:T(8,128)}, u32[]{:S(2)}) copy-start(f32[64,78]{1,0:T(8,128)} %get-tuple-element.11) | copy-start | bytes 59908
  405.6 20.3 %collective-permute-start.25 = (f32[7,64,64]{2,0,1:T(8,128)S(1)}, f32[7,64,64]{2,0,1:T(8,128)S(1)}, u32[]{:S(2)}, u32[]{:S(2)}) collective-permute-start(f32[7,64,64]{2,0,1:T(8,128)S(1)} %get-tuple-element.39), channel_id=1, source_target_pairs={{64,0},{80,16},{96,32},{112,48},{128,64},{144,80},{160,96},{176,11... | collective-permute-start | bytes 344072 | tf_op jit(solution)/shard_map/ppermute | solution.py:94
  406.9 20.2 %collective-permute-start.24 = (f32[7,64,64]{2,0,1:T(8,128)S(1)}, f32[7,64,64]{2,0,1:T(8,128)S(1)}, u32[]{:S(2)}, u32[]{:S(2)}) collective-permute-start(f32[7,64,64]{2,0,1:T(8,128)S(1)} %get-tuple-element.38), channel_id=1, source_target_pairs={{0,64},{16,80},{32,96},{48,112},{64,128},{80,144},{96,160},{112,17... | collective-permute-start | bytes 344072 | tf_op jit(solution)/shard_map/ppermute | solution.py:93
  430.0 5.3 collective-permute-start.26
  443.5 6.0 collective-permute-start.27
  457.1 3.2 collective-permute-start.28
  461.5 14.1 %collective-permute-start.29 = (f32[64,2,2,4,64]{4,0,3,2,1:T(8,128)S(1)}, f32[64,2,2,4,64]{4,0,3,2,1:T(8,128)S(1)}, u32[]{:S(2)}, u32[]{:S(2)}) collective-permute-start(f32[64,2,2,4,64]{4,0,3,2,1:T(8,128)S(1)} %select_bitcast_fusion.9), channel_id=1, source_target_pairs={{0,4},{1,5},{2,6},{3,7},{4,0},{5,1},{6,2},{7,3},{8,12},{9,13},{10,... | collective-permute-start | bytes 786440 | tf_op jit(solution)/shard_map/ppermute | solution.py:118
  475.7 9.1 %collective-permute-start.30 = (f32[64,2,4,64]{3,0,2,1:T(8,128)S(1)}, f32[64,2,4,64]{3,0,2,1:T(8,128)S(1)}, u32[]{:S(2)}, u32[]{:S(2)}) collective-permute-start(f32[64,2,4,64]{3,0,2,1:T(8,128)S(1)} %select_bitcast_fusion.15), channel_id=1, source_target_pairs={{0,8},{1,9},{2,10},{3,11},{4,12},{5,13},{6,14},{7,15},{8,0},{9,1},... | collective-permute-start | bytes 393224 | tf_op jit(solution)/shard_map/ppermute | solution.py:118
  484.9 9.1 %collective-permute-start.31 = (f32[64,4,64]{2,0,1:T(8,128)S(1)}, f32[64,4,64]{2,0,1:T(8,128)S(1)}, u32[]{:S(2)}, u32[]{:S(2)}) collective-permute-start(f32[64,4,64]{2,0,1:T(8,128)S(1)} %select_bitcast_fusion.21), channel_id=1, source_target_pairs={{0,2},{1,3},{2,0},{3,1},{4,6},{5,7},{6,4},{7,5},{8,10},{9,11},{10,... | collective-permute-start | bytes 196616 | tf_op jit(solution)/shard_map/ppermute | solution.py:118
  494.6 9.1 %collective-permute-start.32 = (f32[64,4,64]{2,0,1:T(8,128)S(1)}, f32[64,4,64]{2,0,1:T(8,128)S(1)}, u32[]{:S(2)}, u32[]{:S(2)}) collective-permute-start(f32[64,4,64]{2,0,1:T(8,128)S(1)} %fusion.51), channel_id=1, source_target_pairs={{0,2},{1,3},{2,0},{3,1},{4,6},{5,7},{6,4},{7,5},{8,10},{9,11},{10,... | collective-permute-start | bytes 196616 | tf_op jit(solution)/shard_map/ppermute | solution.py:128
  503.7 8.0 %collective-permute-start.33 = (f32[64,2,4,64]{3,0,2,1:T(8,128)S(1)}, f32[64,2,4,64]{3,0,2,1:T(8,128)S(1)}, u32[]{:S(2)}, u32[]{:S(2)}) collective-permute-start(f32[64,2,4,64]{3,0,2,1:T(8,128)S(1)} %pad_maximum_fusion.13), channel_id=1, source_target_pairs={{0,8},{1,9},{2,10},{3,11},{4,12},{5,13},{6,14},{7,15},{8,0},{9,1},... | collective-permute-start | bytes 393224 | tf_op jit(solution)/shard_map/ppermute | solution.py:128
  511.8 13.8 %collective-permute-start.34 = (f32[64,2,2,4,64]{4,0,3,2,1:T(8,128)S(1)}, f32[64,2,2,4,64]{4,0,3,2,1:T(8,128)S(1)}, u32[]{:S(2)}, u32[]{:S(2)}) collective-permute-start(f32[64,2,2,4,64]{4,0,3,2,1:T(8,128)S(1)} %pad_maximum_fusion.11), channel_id=1, source_target_pairs={{0,4},{1,5},{2,6},{3,7},{4,0},{5,1},{6,2},{7,3},{8,12},{9,13},{10,... | collective-permute-start | bytes 786440 | tf_op jit(solution)/shard_map/ppermute | solution.py:128
  525.8 2.7 collective-permute-start.35
  538.1 5.4 collective-permute-start.36
  553.5 5.1 collective-permute-start.37
  563.3 9.8 %collective-permute-start.39 = (f32[7,64,64]{1,2,0:T(8,128)S(1)}, f32[7,64,64]{1,2,0:T(8,128)S(1)}, u32[]{:S(2)}, u32[]{:S(2)}) collective-permute-start(f32[7,64,64]{1,2,0:T(8,128)S(1)} %get-tuple-element.29), channel_id=1, source_target_pairs={{64,0},{80,16},{96,32},{112,48},{128,64},{144,80},{160,96},{176,11... | collective-permute-start | bytes 344072 | tf_op jit(solution)/shard_map/ppermute | solution.py:94
  564.6 9.7 %collective-permute-start.38 = (f32[7,64,64]{1,2,0:T(8,128)S(1)}, f32[7,64,64]{1,2,0:T(8,128)S(1)}, u32[]{:S(2)}, u32[]{:S(2)}) collective-permute-start(f32[7,64,64]{1,2,0:T(8,128)S(1)} %get-tuple-element.28), channel_id=1, source_target_pairs={{0,64},{16,80},{32,96},{48,112},{64,128},{80,144},{96,160},{112,17... | collective-permute-start | bytes 344072 | tf_op jit(solution)/shard_map/ppermute | solution.py:93
  586.2 8.7 %collective-permute-start.41 = (f32[7,64,64]{2,0,1:T(8,128)S(1)}, f32[7,64,64]{2,0,1:T(8,128)S(1)}, u32[]{:S(2)}, u32[]{:S(2)}) collective-permute-start(f32[7,64,64]{2,0,1:T(8,128)S(1)} %get-tuple-element.27), channel_id=1, source_target_pairs={{64,0},{80,16},{96,32},{112,48},{128,64},{144,80},{160,96},{176,11... | collective-permute-start | bytes 344072 | tf_op jit(solution)/shard_map/ppermute | solution.py:94
  587.5 8.9 %collective-permute-start.40 = (f32[7,64,64]{2,0,1:T(8,128)S(1)}, f32[7,64,64]{2,0,1:T(8,128)S(1)}, u32[]{:S(2)}, u32[]{:S(2)}) collective-permute-start(f32[7,64,64]{2,0,1:T(8,128)S(1)} %get-tuple-element.26), channel_id=1, source_target_pairs={{0,64},{16,80},{32,96},{48,112},{64,128},{80,144},{96,160},{112,17... | collective-permute-start | bytes 344072 | tf_op jit(solution)/shard_map/ppermute | solution.py:93
  599.3 5.1 collective-permute-start.42
  612.6 6.8 collective-permute-start.43
  627.0 2.7 collective-permute-start.44
  631.0 14.1 %collective-permute-start.45 = (f32[64,2,2,4,64]{4,0,3,2,1:T(8,128)S(1)}, f32[64,2,2,4,64]{4,0,3,2,1:T(8,128)S(1)}, u32[]{:S(2)}, u32[]{:S(2)}) collective-permute-start(f32[64,2,2,4,64]{4,0,3,2,1:T(8,128)S(1)} %select_bitcast_fusion.6), channel_id=1, source_target_pairs={{0,4},{1,5},{2,6},{3,7},{4,0},{5,1},{6,2},{7,3},{8,12},{9,13},{10,... | collective-permute-start | bytes 786440 | tf_op jit(solution)/shard_map/ppermute | solution.py:118
  645.2 9.1 %collective-permute-start.46 = (f32[64,2,4,64]{3,0,2,1:T(8,128)S(1)}, f32[64,2,4,64]{3,0,2,1:T(8,128)S(1)}, u32[]{:S(2)}, u32[]{:S(2)}) collective-permute-start(f32[64,2,4,64]{3,0,2,1:T(8,128)S(1)} %select_bitcast_fusion.12), channel_id=1, source_target_pairs={{0,8},{1,9},{2,10},{3,11},{4,12},{5,13},{6,14},{7,15},{8,0},{9,1},... | collective-permute-start | bytes 393224 | tf_op jit(solution)/shard_map/ppermute | solution.py:118
  654.4 9.1 %collective-permute-start.47 = (f32[64,4,64]{2,0,1:T(8,128)S(1)}, f32[64,4,64]{2,0,1:T(8,128)S(1)}, u32[]{:S(2)}, u32[]{:S(2)}) collective-permute-start(f32[64,4,64]{2,0,1:T(8,128)S(1)} %select_bitcast_fusion.18), channel_id=1, source_target_pairs={{0,2},{1,3},{2,0},{3,1},{4,6},{5,7},{6,4},{7,5},{8,10},{9,11},{10,... | collective-permute-start | bytes 196616 | tf_op jit(solution)/shard_map/ppermute | solution.py:118
  664.2 11.7 %collective-permute-start.48 = (f32[64,4,64]{2,0,1:T(8,128)S(1)}, f32[64,4,64]{2,0,1:T(8,128)S(1)}, u32[]{:S(2)}, u32[]{:S(2)}) collective-permute-start(f32[64,4,64]{2,0,1:T(8,128)S(1)} %get-tuple-element.72), channel_id=1, source_target_pairs={{0,48},{16,0},{32,16},{48,32},{64,112},{80,64},{96,80},{112,96},{1... | collective-permute-start | bytes 196616 | tf_op jit(solution)/shard_map/ppermute | solution.py:39
  666.3 9.6 %collective-permute-start.49 = (f32[64,4,64]{2,0,1:T(8,128)S(1)}, f32[64,4,64]{2,0,1:T(8,128)S(1)}, u32[]{:S(2)}, u32[]{:S(2)}) collective-permute-start(f32[64,4,64]{2,0,1:T(8,128)S(1)} %get-tuple-element.71), channel_id=1, source_target_pairs={{0,32},{16,48},{32,0},{48,16},{64,96},{80,112},{96,64},{112,80},{1... | collective-permute-start | bytes 196616 | tf_op jit(solution)/shard_map/ppermute | solution.py:39
  666.3 9.7 %collective-permute-start.50 = (f32[64,4,64]{2,0,1:T(8,128)S(1)}, f32[64,4,64]{2,0,1:T(8,128)S(1)}, u32[]{:S(2)}, u32[]{:S(2)}) collective-permute-start(f32[64,4,64]{2,0,1:T(8,128)S(1)} %get-tuple-element.17), channel_id=1, source_target_pairs={{0,16},{16,32},{32,48},{48,0},{64,80},{80,96},{96,112},{112,64},{1... | collective-permute-start | bytes 196616 | tf_op jit(solution)/shard_map/ppermute | solution.py:39
  676.0 10.4 %collective-permute-start.51 = (f32[64,4,64]{2,0,1:T(8,128)S(1)}, f32[64,4,64]{2,0,1:T(8,128)S(1)}, u32[]{:S(2)}, u32[]{:S(2)}) collective-permute-start(f32[64,4,64]{2,0,1:T(8,128)S(1)} %get-tuple-element.59), channel_id=1, source_target_pairs={{0,192},{16,208},{32,224},{48,240},{64,0},{80,16},{96,32},{112,48}... | collective-permute-start | bytes 196616 | tf_op jit(solution)/shard_map/ppermute | solution.py:50
  682.6 8.3 %collective-permute-start.52 = (f32[64,4,64]{2,0,1:T(8,128)S(1)}, f32[64,4,64]{2,0,1:T(8,128)S(1)}, u32[]{:S(2)}, u32[]{:S(2)}) collective-permute-start(f32[64,4,64]{2,0,1:T(8,128)S(1)} %get-tuple-element.58), channel_id=1, source_target_pairs={{0,128},{16,144},{32,160},{48,176},{64,192},{80,208},{96,224},{112... | collective-permute-start | bytes 196616 | tf_op jit(solution)/shard_map/ppermute | solution.py:50
  682.6 8.3 %collective-permute-start.53 = (f32[64,4,64]{2,0,1:T(8,128)S(1)}, f32[64,4,64]{2,0,1:T(8,128)S(1)}, u32[]{:S(2)}, u32[]{:S(2)}) collective-permute-start(f32[64,4,64]{2,0,1:T(8,128)S(1)} %get-tuple-element.57), channel_id=1, source_target_pairs={{0,64},{16,80},{32,96},{48,112},{64,128},{80,144},{96,160},{112,17... | collective-permute-start | bytes 196616 | tf_op jit(solution)/shard_map/ppermute | solution.py:50
  (7 other events, 18.9 us)

commit v7 on v6

--- a/solution.py
+++ b/solution.py
@@ -25,31 +25,37 @@
     return buf
 
 
-def route(x, dest, src_of_me, nsp):
+def route(x, dest, src_of_me, nsp, columns_first=False):
     me = lax.axis_index("space")
     rows = nsp // ROW
-    my_row, my_col = me // ROW, me % ROW
-    dest_col = dest[me] % ROW
+    if columns_first:
+        n1, n2 = rows, ROW
+        first, second = (lambda s: s // ROW), (lambda s: s % ROW)
+        put = lambda s2, s1: s1 * ROW + s2
+    else:
+        n1, n2 = ROW, rows
+        first, second = (lambda s: s % ROW), (lambda s: s // ROW)
+        put = lambda s2, s1: s2 * ROW + s1
+    my1, my2 = first(me), second(me)
+    dest1 = first(dest[me])
     zero = jnp.zeros_like(x)
     received = []
-    for k in range(ROW):
-        part = jnp.where((dest_col - my_col) % ROW == k, x, zero)
+    for k in range(n1):
+        part = jnp.where((dest1 - my1) % n1 == k, x, zero)
         if k:
-            pairs = [(a * ROW + b, a * ROW + (b + k) % ROW) for a in range(rows) for b in range(ROW)]
+            pairs = [(put(q2, q1), put(q2, (q1 + k) % n1)) for q2 in range(n2) for q1 in range(n1)]
             part = lax.ppermute(part, "space", pairs)
-        src = my_row * ROW + (my_col - k) % ROW
-        received.append((part, dest[src]))
+        received.append((part, dest[put(my2, (my1 - k) % n1)]))
     result = zero
-    for j in range(rows):
-        target = ((my_row + j) % rows) * ROW + my_col
+    for j in range(n2):
+        target = put((my2 + j) % n2, my1)
         part = zero
         for data, d in received:
             part = jnp.where(d == target, data, part)
         if j:
-            pairs = [(a * ROW + c, ((a + j) % rows) * ROW + c) for a in range(rows) for c in range(ROW)]
+            pairs = [(put(q2, q1), put((q2 + j) % n2, q1)) for q2 in range(n2) for q1 in range(n1)]
             part = lax.ppermute(part, "space", pairs)
-        src_row = src_of_me // ROW
-        result = jnp.where((my_row - src_row) % rows == j, part, result)
+        result = jnp.where((my2 - second(src_of_me)) % n2 == j, part, result)
     return result
 
 
@@ -165,7 +171,14 @@
     share = jnp.transpose(estimate[0].reshape(side, estimate.shape[2] // side, side), (2, 1, 0))
     share = route(share, place, my_brick, nsp)
     recorded = jnp.transpose(measured[0, 0].reshape(side, side, side), (2, 1, 0))
-    recorded = route(recorded, place, my_brick, nsp)
+    half = side // 2
+    recorded = jnp.concatenate(
+        [
+            route(recorded[:half], place, my_brick, nsp),
+            route(recorded[half:], place, my_brick, nsp, columns_first=True),
+        ],
+        axis=0,
+    )
 
     radius_x = (kernel_x.shape[1] - 1) // 2
     radius_y = (kernel_y.shape[1] - 1) // 2

time: 703 us -> 647 us (0.920)
  waiting for transfers between devices: 336 us -> 289 us
  local copies, waits for them, and re-layouts: 73.3 us -> 54.8 us
  between operations: 28.5 us -> 38.7 us
  starting transfers between devices: 135 us -> 125 us
  other arithmetic: 66.8 us -> 74.4 us
    ppermute x18 -> x24, waiting for transfers between devices: 41.6 us -> 171 us  [route(): part = lax.ppermute(part, 'space', pairs)]
    ppermute x4, waiting for transfers between devices: 91.1 us -> 4.22 us  [z_halo(): low = lax.ppermute(last, 'space', [(i, i + ROW) for i in range(nsp - ROW)])]
    ppermute x8, waiting for transfers between devices: 73.3 us -> 18.1 us  [pair_halo(): recv = lax.ppermute(send, 'space', [(i, i ^ partner) for i in range(nsp)])]
    ppermute x4, waiting for transfers between devices: 43.1 us -> 7.93 us  [z_halo(): lax.ppermute(first, 'space', [(i + ROW, i) for i in range(nsp - ROW)])]
    ppermute x4, starting transfers between devices: 32.1 us -> 19.5 us  [z_halo(): low = lax.ppermute(last, 'space', [(i, i + ROW) for i in range(nsp - ROW)])]
    select_n x8 -> x4, local copies, waits for them, and re-layouts: 11.8 us -> 0.37 us  [route(): part = jnp.where(d == target, data, part)]
    select_n x6 -> x3, local copies, waits for them, and re-layouts: 9.72 us -> 0.27 us  [route(): part = jnp.where((dest1 - my1) % n1 == k, x, zero)]
    ppermute x18 -> x24, starting transfers between devices: 30.3 us -> 37.5 us  [route(): part = lax.ppermute(part, 'space', pairs)]
  transfers between devices with their start and end apart: 54 -> 60, of which waited for: 36 -> 41; matrix products, arithmetic and copies ran while one was open for 14% -> 13% of each run, Pallas kernels for 0% -> 0%
where the time goes in v7:
time: 647 us; the launch traced here: 637 us
  waiting for transfers between devices  289 us (45%)
  starting transfers between devices  125 us (19%)
  other arithmetic  74.4 us (11%)
  local copies, waits for them, and re-layouts  54.8 us (8%)
  matrix products  54.4 us (8%)
  between operations  38.7 us (6%)
    ppermute x24, waiting for transfers between devices, route(): part = lax.ppermute(part, 'space', pairs)  171 us
    ppermute x8, waiting for transfers between devices, view_reduce_scatter(): x = keep + lax.ppermute(send, 'view', xor_pairs(nv, m))  52.3 us
    ppermute x24, starting transfers between devices, route(): part = lax.ppermute(part, 'space', pairs)  37.5 us
    ppermute x8, waiting for transfers between devices, view_all_gather(): recv = lax.ppermute(x, 'view', xor_pairs(nv, m))  26.5 us
    ppermute x8, starting transfers between devices, view_all_gather(): recv = lax.ppermute(x, 'view', xor_pairs(nv, m))  22.4 us
    ppermute x8, starting transfers between devices, view_reduce_scatter(): x = keep + lax.ppermute(send, 'view', xor_pairs(nv, m))  21.5 us
    select_n x3, other arithmetic, band_matrix(): band = jnp.where(offset == position, weight, band)  20 us
    ppermute x4, starting transfers between devices, z_halo(): low = lax.ppermute(last, 'space', [(i, i + ROW) for i in range(nsp - ROW)])  19.5 us
  transfers between devices with their start and end apart: 60, of which 41 were waited for; matrix products, arithmetic and copies ran while one was open for 13% of the time, Pallas kernels for 0%

profile of v7, /device:TPU:8, one launch (start us, length us, event | category | flops | bytes accessed | tf_op | source)
XLA Modules:
  0.0 636.9 jit_solution(9929774256675469596)
XLA Ops:
  9.8 4.3 collective-permute-done.1
  14.3 3.4 collective-permute-done.2
  40.8 4.3 collective-permute-start.7
  52.6 6.9 %collective-permute-start.22 = (f32[64,4,64]{2,0,1:T(8,128)S(1)}, f32[64,4,64]{2,0,1:T(8,128)S(1)}, u32[]{:S(2)}, u32[]{:S(2)}) collective-permute-start(f32[64,4,64]{2,0,1:T(8,128)S(1)} %select_select_fusion.12), channel_id=1, source_target_pairs={{0,2},{1,3},{2,0},{3,1},{4,6},{5,7},{6,4},{7,5},{8,10},{9,11},{10,... | collective-permute-start | bytes 196616 | tf_op jit(solution)/shard_map/ppermute | solution.py:134
  60.2 3.2 collective-permute-done.22
  63.5 3.1 collective-permute-start.23
  67.3 5.0 select_select_fusion.22
  78.0 5.0 select_select_fusion.20
  83.0 10.0 %select_select_fusion.24 = (f32[64,78]{1,0:T(8,128)}, f32[64,78]{1,0:T(8,128)}) fusion(f32[]{:T(128)} %bitcast.47, f32[]{:T(128)} %bitcast.46, f32[]{:T(128)} %bitcast.45, f32[]{:T(128)} %bitcast.44, f32[]{:T(128)} %bitcast.43, f32[]{:T(128)} %bitcast.42, f32[]{:T(128)} %bitcast.41, f32[]{:T(128)} %bitcast.40, f32[]{:T(128)} %bitcast.39, f32[]{:T(128)} %bitcast.38, ...), kind=kLoop, calls=%fused_computation.181 | loop fusion | flops 229632 | bytes 39996 | tf_op jit(solution)/shard_map/jit(_where)/select_n | solution.py:68
  108.5 2.7 fusion.114
  117.1 30.9 %collective-permute-done.10 = f32[32,64,64]{2,0,1:T(8,128)} collective-permute-done((f32[32,64,64]{2,0,1:T(8,128)}, f32[32,64,64]{2,0,1:T(8,128)}, u32[]{:S(2)}, u32[]{:S(2)}) %collective-permute-start.10) | collective-permute-done | bytes 524320 | tf_op jit(solution)/shard_map/ppermute | solution.py:47
  151.5 4.1 select_select_fusion.5
  155.7 2.7 collective-permute-start.13
  166.7 4.9 fusion.28
  173.5 8.8 %collective-permute-done.13 = f32[32,64,64]{2,0,1:T(8,128)S(1)} collective-permute-done((f32[32,64,64]{2,0,1:T(8,128)}, f32[32,64,64]{2,0,1:T(8,128)S(1)}, u32[]{:S(2)}, u32[]{:S(2)}) %collective-permute-start.13) | collective-permute-done | bytes 524320 | tf_op jit(solution)/shard_map/ppermute | solution.py:57
  182.7 64.0 %collective-permute-done.14 = f32[32,64,64]{2,0,1:T(8,128)} collective-permute-done((f32[32,64,64]{2,0,1:T(8,128)}, f32[32,64,64]{2,0,1:T(8,128)}, u32[]{:S(2)}, u32[]{:S(2)}) %collective-permute-start.14) | collective-permute-done | bytes 524320 | tf_op jit(solution)/shard_map/ppermute | solution.py:57
  249.2 4.2 collective-permute-start.17
  262.3 5.5 fusion.45
  267.8 29.9 %collective-permute-done.17 = f32[32,64,64]{2,0,1:T(8,128)S(1)} collective-permute-done((f32[32,64,64]{2,0,1:T(8,128)}, f32[32,64,64]{2,0,1:T(8,128)S(1)}, u32[]{:S(2)}, u32[]{:S(2)}) %collective-permute-start.17) | collective-permute-done | bytes 524320 | tf_op jit(solution)/shard_map/ppermute | solution.py:47
  297.7 3.8 select_select_fusion.1
  301.6 3.5 collective-permute-start.19
  308.8 5.4 collective-permute-start.28
  317.1 3.6 pad_maximum_fusion
  320.7 4.4 copy.226
  325.1 3.8 collective-permute-done.19
  328.9 22.6 %collective-permute-done.20 = f32[32,64,64]{2,0,1:T(8,128)} collective-permute-done((f32[32,64,64]{2,0,1:T(8,128)}, f32[32,64,64]{2,0,1:T(8,128)}, u32[]{:S(2)}, u32[]{:S(2)}) %collective-permute-start.20) | collective-permute-done | bytes 524320 | tf_op jit(solution)/shard_map/ppermute | solution.py:57
  354.4 6.1 fusion.41
  361.8 4.6 collective-permute-start.30
  366.4 3.2 collective-permute-done.31
  376.3 2.9 collective-permute-done.32
  380.1 3.3 copy.258
  383.4 3.5 convolution_bitcast_fusion.1
  387.6 4.2 collective-permute-start.33
  395.8 4.8 fusion.26
  406.5 14.0 %collective-permute-done.35 = f32[64,2,2,4,64]{4,0,3,2,1:T(8,128)S(1)} collective-permute-done((f32[64,2,2,4,64]{4,0,3,2,1:T(8,128)S(1)}, f32[64,2,2,4,64]{4,0,3,2,1:T(8,128)S(1)}, u32[]{:S(2)}, u32[]{:S(2)}) %collective-permute-start.35) | collective-permute-done | bytes 262176 | tf_op jit(solution)/shard_map/ppermute | solution.py:124
  423.0 6.7 %collective-permute-done.36 = f32[64,2,4,64]{3,0,2,1:T(8,128)S(1)} collective-permute-done((f32[64,2,4,64]{3,0,2,1:T(8,128)S(1)}, f32[64,2,4,64]{3,0,2,1:T(8,128)S(1)}, u32[]{:S(2)}, u32[]{:S(2)}) %collective-permute-start.36) | collective-permute-done | bytes 131104 | tf_op jit(solution)/shard_map/ppermute | solution.py:124
  429.8 6.2 collective-permute-start.37
  436.6 3.6 collective-permute-done.37
  440.9 6.4 %collective-permute-start.38 = (f32[64,4,64]{2,0,1:T(8,128)S(1)}, f32[64,4,64]{2,0,1:T(8,128)S(1)}, u32[]{:S(2)}, u32[]{:S(2)}) collective-permute-start(f32[64,4,64]{2,0,1:T(8,128)S(1)} %fusion.53), channel_id=1, source_target_pairs={{0,2},{1,3},{2,0},{3,1},{4,6},{5,7},{6,4},{7,5},{8,10},{9,11},{10,... | collective-permute-start | bytes 196616 | tf_op jit(solution)/shard_map/ppermute | solution.py:134
  447.3 3.9 collective-permute-done.38
  451.3 2.8 collective-permute-start.39
  454.1 6.6 %collective-permute-done.39 = f32[64,2,4,64]{3,0,2,1:T(8,128)S(1)} collective-permute-done((f32[64,2,4,64]{3,0,2,1:T(8,128)S(1)}, f32[64,2,4,64]{3,0,2,1:T(8,128)S(1)}, u32[]{:S(2)}, u32[]{:S(2)}) %collective-permute-start.39) | collective-permute-done | bytes 131104 | tf_op jit(solution)/shard_map/ppermute | solution.py:134
  461.3 9.2 %collective-permute-done.40 = f32[64,2,2,4,64]{4,0,3,2,1:T(8,128)S(1)} collective-permute-done((f32[64,2,2,4,64]{4,0,3,2,1:T(8,128)S(1)}, f32[64,2,2,4,64]{4,0,3,2,1:T(8,128)S(1)}, u32[]{:S(2)}, u32[]{:S(2)}) %collective-permute-start.40) | collective-permute-done | bytes 262176 | tf_op jit(solution)/shard_map/ppermute | solution.py:134
  474.3 2.8 fusion.109
  493.1 4.7 fusion.34
  498.6 5.0 collective-permute-done.43
  504.3 4.0 fusion.42
  509.6 4.6 collective-permute-start.44
  517.9 3.3 copy.244
  521.2 8.3 %fusion.40 = f32[64,64,64]{2,0,1:T(8,128)S(1)} fusion(f32[32,64,64]{2,0,1:T(8,128)} %copy-done.9, f32[32,64,64]{2,0,1:T(8,128)} %get-tuple-element.49, f32[78,64,64]{0,2,1:T(8,128)} %copy.244, f32[64,78]{1,0:T(8,128)S(1)} %copy-done.16), kind=kOutput, calls=%fused_computation.52 | convolution fusion | flops 245891072 | bytes 3395072 | tf_op jit(solution)/shard_map/ot,tab->oab/dot_general | solution.py:75
  530.8 5.0 collective-permute-start.46
  543.6 4.4 collective-permute-done.48
  548.9 3.3 copy.262
  552.1 3.5 convolution_bitcast_fusion
  556.3 4.2 collective-permute-start.49
  564.1 4.8 fusion.24
  571.1 2.6 collective-permute-done.50
  576.5 12.5 %collective-permute-done.51 = f32[64,2,2,4,64]{4,0,3,2,1:T(8,128)S(1)} collective-permute-done((f32[64,2,2,4,64]{4,0,3,2,1:T(8,128)S(1)}, f32[64,2,2,4,64]{4,0,3,2,1:T(8,128)S(1)}, u32[]{:S(2)}, u32[]{:S(2)}) %collective-permute-start.51) | collective-permute-done | bytes 262176 | tf_op jit(solution)/shard_map/ppermute | solution.py:124
  589.2 4.1 collective-permute-start.52
  593.2 5.8 collective-permute-done.52
  599.1 6.7 %collective-permute-start.53 = (f32[64,4,64]{2,0,1:T(8,128)S(1)}, f32[64,4,64]{2,0,1:T(8,128)S(1)}, u32[]{:S(2)}, u32[]{:S(2)}) collective-permute-start(f32[64,4,64]{2,0,1:T(8,128)S(1)} %select_bitcast_fusion.18), channel_id=1, source_target_pairs={{0,2},{1,3},{2,0},{3,1},{4,6},{5,7},{6,4},{7,5},{8,10},{9,11},{10,... | collective-permute-start | bytes 196616 | tf_op jit(solution)/shard_map/ppermute | solution.py:124
  605.8 4.5 collective-permute-done.53
  622.3 4.4 collective-permute-start.57
  629.9 5.8 collective-permute-done.58
  (239 shorter events, 152.2 us)
Async XLA Ops:
  0.0 34.2 %copy-start.17 = (f32[1,7]{1,0:T(1,128)S(1)}, f32[1,7]{1,0:T(1,128)}, u32[]{:S(2)}) copy-start(f32[1,7]{1,0:T(1,128)} %param.9) | copy-start | bytes 88
  1.5 7.3 %collective-permute-start = (s32[16,7]{0,1:T(8,128)S(1)}, s32[16,7]{0,1:T(8,128)S(1)}, u32[]{:S(2)}, u32[]{:S(2)}) collective-permute-start(s32[16,7]{0,1:T(8,128)S(1)} %broadcast_select_fusion.24), channel_id=1, source_target_pairs={{0,16},{16,0},{32,48},{48,32},{64,80},{80,64},{96,112},{112,96},{1... | collective-permute-start | bytes 1352 | tf_op jit(solution)/shard_map/ppermute | solution.py:23
  8.9 5.1 collective-permute-start.1
  14.1 3.6 collective-permute-start.2
  17.7 4.5 collective-permute-start.3
  29.9 10.8 %collective-permute-start.4 = (f32[64,4,64]{2,0,1:T(8,128)S(1)}, f32[64,4,64]{2,0,1:T(8,128)S(1)}, u32[]{:S(2)}, u32[]{:S(2)}) collective-permute-start(f32[64,4,64]{2,0,1:T(8,128)S(1)} %bitcast.253), channel_id=1, source_target_pairs={{0,48},{16,0},{32,16},{48,32},{64,112},{80,64},{96,80},{112,96},{1... | collective-permute-start | bytes 196616 | tf_op jit(solution)/shard_map/ppermute | solution.py:47
  30.3 10.4 %collective-permute-start.5 = (f32[64,4,64]{2,0,1:T(8,128)S(1)}, f32[64,4,64]{2,0,1:T(8,128)S(1)}, u32[]{:S(2)}, u32[]{:S(2)}) collective-permute-start(f32[64,4,64]{2,0,1:T(8,128)S(1)} %bitcast.254), channel_id=1, source_target_pairs={{0,32},{16,48},{32,0},{48,16},{64,96},{80,112},{96,64},{112,80},{1... | collective-permute-start | bytes 196616 | tf_op jit(solution)/shard_map/ppermute | solution.py:47
  32.8 8.0 %collective-permute-start.6 = (f32[64,4,64]{2,0,1:T(8,128)S(1)}, f32[64,4,64]{2,0,1:T(8,128)S(1)}, u32[]{:S(2)}, u32[]{:S(2)}) collective-permute-start(f32[64,4,64]{2,0,1:T(8,128)S(1)} %bitcast.255), channel_id=1, source_target_pairs={{0,16},{16,32},{32,48},{48,0},{64,80},{80,96},{96,112},{112,64},{1... | collective-permute-start | bytes 196616 | tf_op jit(solution)/shard_map/ppermute | solution.py:47
  40.8 10.9 %collective-permute-start.7 = (f32[64,4,64]{2,0,1:T(8,128)S(1)}, f32[64,4,64]{2,0,1:T(8,128)S(1)}, u32[]{:S(2)}, u32[]{:S(2)}) collective-permute-start(f32[64,4,64]{2,0,1:T(8,128)S(1)} %get-tuple-element.69), channel_id=1, source_target_pairs={{0,192},{16,208},{32,224},{48,240},{64,0},{80,16},{96,32},{112,48}... | collective-permute-start | bytes 196616 | tf_op jit(solution)/shard_map/ppermute | solution.py:57
  45.1 7.4 %collective-permute-start.8 = (f32[64,4,64]{2,0,1:T(8,128)S(1)}, f32[64,4,64]{2,0,1:T(8,128)S(1)}, u32[]{:S(2)}, u32[]{:S(2)}) collective-permute-start(f32[64,4,64]{2,0,1:T(8,128)S(1)} %get-tuple-element.68), channel_id=1, source_target_pairs={{0,128},{16,144},{32,160},{48,176},{64,192},{80,208},{96,224},{112... | collective-permute-start | bytes 196616 | tf_op jit(solution)/shard_map/ppermute | solution.py:57
  45.2 7.4 %collective-permute-start.9 = (f32[64,4,64]{2,0,1:T(8,128)S(1)}, f32[64,4,64]{2,0,1:T(8,128)S(1)}, u32[]{:S(2)}, u32[]{:S(2)}) collective-permute-start(f32[64,4,64]{2,0,1:T(8,128)S(1)} %get-tuple-element.67), channel_id=1, source_target_pairs={{0,64},{16,80},{32,96},{48,112},{64,128},{80,144},{96,160},{112,17... | collective-permute-start | bytes 196616 | tf_op jit(solution)/shard_map/ppermute | solution.py:57
  52.6 10.9 %collective-permute-start.22 = (f32[64,4,64]{2,0,1:T(8,128)S(1)}, f32[64,4,64]{2,0,1:T(8,128)S(1)}, u32[]{:S(2)}, u32[]{:S(2)}) collective-permute-start(f32[64,4,64]{2,0,1:T(8,128)S(1)} %select_select_fusion.12), channel_id=1, source_target_pairs={{0,2},{1,3},{2,0},{3,1},{4,6},{5,7},{6,4},{7,5},{8,10},{9,11},{10,... | collective-permute-start | bytes 196616 | tf_op jit(solution)/shard_map/ppermute | solution.py:134
  63.5 9.7 %collective-permute-start.23 = (f32[64,2,4,64]{3,0,2,1:T(8,128)S(1)}, f32[64,2,4,64]{3,0,2,1:T(8,128)S(1)}, u32[]{:S(2)}, u32[]{:S(2)}) collective-permute-start(f32[64,2,4,64]{3,0,2,1:T(8,128)S(1)} %pad_maximum_fusion.13), channel_id=1, source_target_pairs={{0,8},{1,9},{2,10},{3,11},{4,12},{5,13},{6,14},{7,15},{8,0},{9,1},... | collective-permute-start | bytes 393224 | tf_op jit(solution)/shard_map/ppermute | solution.py:134
  74.2 20.1 %collective-permute-start.24 = (f32[64,2,2,4,64]{4,0,3,2,1:T(8,128)}, f32[64,2,2,4,64]{4,0,3,2,1:T(8,128)}, u32[]{:S(2)}, u32[]{:S(2)}) collective-permute-start(f32[64,2,2,4,64]{4,0,3,2,1:T(8,128)} %pad_maximum_fusion.11), channel_id=1, source_target_pairs={{0,4},{1,5},{2,6},{3,7},{4,0},{5,1},{6,2},{7,3},{8,12},{9,13},{10,... | collective-permute-start | bytes 786440 | tf_op jit(solution)/shard_map/ppermute | solution.py:134
  96.6 9.2 %collective-permute-start.25 = (f32[64,2,2,2,4,64]{5,0,4,3,2,1:T(8,128)}, f32[64,2,2,2,4,64]{5,0,4,3,2,1:T(8,128)}, u32[]{:S(2)}, u32[]{:S(2)}) collective-permute-start(f32[64,2,2,2,4,64]{5,0,4,3,2,1:T(8,128)} %pad_maximum_fusion.9), channel_id=1, source_target_pairs={{0,1},{1,0},{2,3},{3,2},{4,5},{5,4},{6,7},{7,6},{8,9},{9,8},{10,11... | collective-permute-start | bytes 1572872 | tf_op jit(solution)/shard_map/ppermute | solution.py:134
  99.1 168.7 %collective-permute-start.16 = (f32[32,64,64]{2,0,1:T(8,128)}, f32[32,64,64]{2,0,1:T(8,128)}, u32[]{:S(2)}, u32[]{:S(2)}) collective-permute-start(f32[32,64,64]{2,0,1:T(8,128)} %get-tuple-element.54), channel_id=1, source_target_pairs={{0,192},{64,0},{128,64},{192,128},{16,208},{80,16},{144,80},{208,1... | collective-permute-start | bytes 1572872 | tf_op jit(solution)/shard_map/ppermute | solution.py:47
  100.6 47.4 %collective-permute-start.10 = (f32[32,64,64]{2,0,1:T(8,128)}, f32[32,64,64]{2,0,1:T(8,128)}, u32[]{:S(2)}, u32[]{:S(2)}) collective-permute-start(f32[32,64,64]{2,0,1:T(8,128)} %get-tuple-element.55), channel_id=1, source_target_pairs={{0,48},{16,0},{32,16},{48,32},{64,112},{80,64},{96,80},{112,96},{1... | collective-permute-start | bytes 1572872 | tf_op jit(solution)/shard_map/ppermute | solution.py:47
  101.3 48.0 %collective-permute-start.11 = (f32[32,64,64]{2,0,1:T(8,128)}, f32[32,64,64]{2,0,1:T(8,128)}, u32[]{:S(2)}, u32[]{:S(2)}) collective-permute-start(f32[32,64,64]{2,0,1:T(8,128)} %get-tuple-element.52), channel_id=1, source_target_pairs={{0,32},{16,48},{32,0},{48,16},{64,96},{80,112},{96,64},{112,80},{1... | collective-permute-start | bytes 1572872 | tf_op jit(solution)/shard_map/ppermute | solution.py:47
  102.5 49.0 %collective-permute-start.12 = (f32[32,64,64]{2,0,1:T(8,128)}, f32[32,64,64]{2,0,1:T(8,128)}, u32[]{:S(2)}, u32[]{:S(2)}) collective-permute-start(f32[32,64,64]{2,0,1:T(8,128)} %get-tuple-element.51), channel_id=1, source_target_pairs={{0,16},{16,32},{32,48},{48,0},{64,80},{80,96},{96,112},{112,64},{1... | collective-permute-start | bytes 1572872 | tf_op jit(solution)/shard_map/ppermute | solution.py:47
  105.8 162.1 %collective-permute-start.18 = (f32[32,64,64]{2,0,1:T(8,128)}, f32[32,64,64]{2,0,1:T(8,128)}, u32[]{:S(2)}, u32[]{:S(2)}) collective-permute-start(f32[32,64,64]{2,0,1:T(8,128)} %get-tuple-element.53), channel_id=1, source_target_pairs={{0,64},{64,128},{128,192},{192,0},{16,80},{80,144},{144,208},{208,... | collective-permute-start | bytes 1572872 | tf_op jit(solution)/shard_map/ppermute | solution.py:47
  117.1 41.3 %copy-start.1 = (f32[64,2,2,2,2,4,64]{6,0,5,4,3,2,1:T(8,128)S(1)}, f32[64,2,2,2,2,4,64]{6,0,5,4,3,2,1:T(8,128)}, u32[]{:S(2)}) copy-start(f32[64,2,2,2,2,4,64]{6,0,5,4,3,2,1:T(8,128)} %copy-done) | copy-start | bytes 3145732
  148.1 12.9 %collective-permute-start.26 = (f32[64,64,3]{1,0,2:T(8,128)S(1)}, f32[64,64,3]{1,0,2:T(8,128)S(1)}, u32[]{:S(2)}, u32[]{:S(2)}) collective-permute-start(f32[64,64,3]{1,0,2:T(8,128)S(1)} %broadcast_select_fusion.20), channel_id=1, source_target_pairs={{0,16},{16,0},{32,48},{48,32},{64,80},{80,64},{96,112},{112,96},{1... | collective-permute-start | bytes 147464 | tf_op jit(solution)/shard_map/ppermute | solution.py:87
  155.7 26.7 %collective-permute-start.13 = (f32[32,64,64]{2,0,1:T(8,128)}, f32[32,64,64]{2,0,1:T(8,128)S(1)}, u32[]{:S(2)}, u32[]{:S(2)}) collective-permute-start(f32[32,64,64]{2,0,1:T(8,128)} %get-tuple-element.21), channel_id=1, source_target_pairs={{0,192},{16,208},{32,224},{48,240},{64,0},{80,16},{96,32},{112,48}... | collective-permute-start | bytes 1572872 | tf_op jit(solution)/shard_map/ppermute | solution.py:57
  158.4 88.3 %collective-permute-start.14 = (f32[32,64,64]{2,0,1:T(8,128)}, f32[32,64,64]{2,0,1:T(8,128)}, u32[]{:S(2)}, u32[]{:S(2)}) collective-permute-start(f32[32,64,64]{2,0,1:T(8,128)} %get-tuple-element.20), channel_id=1, source_target_pairs={{0,128},{16,144},{32,160},{48,176},{64,192},{80,208},{96,224},{112... | collective-permute-start | bytes 1572872 | tf_op jit(solution)/shard_map/ppermute | solution.py:57
  160.9 85.8 %collective-permute-start.15 = (f32[32,64,64]{2,0,1:T(8,128)}, f32[32,64,64]{2,0,1:T(8,128)}, u32[]{:S(2)}, u32[]{:S(2)}) collective-permute-start(f32[32,64,64]{2,0,1:T(8,128)} %get-tuple-element.19), channel_id=1, source_target_pairs={{0,64},{16,80},{32,96},{48,112},{64,128},{80,144},{96,160},{112,17... | collective-permute-start | bytes 1572872 | tf_op jit(solution)/shard_map/ppermute | solution.py:57
  182.4 78.4 %collective-permute-start.27 = (f32[64,3,64]{2,1,0:T(4,128)S(1)}, f32[64,3,64]{2,1,0:T(4,128)}, u32[]{:S(2)}, u32[]{:S(2)}) collective-permute-start(f32[64,3,64]{2,1,0:T(4,128)S(1)} %slice_select_fusion.9), channel_id=1, source_target_pairs={{0,48},{16,32},{32,16},{48,0},{64,112},{80,96},{96,80},{112,64},{1... | collective-permute-start | bytes 147464 | tf_op jit(solution)/shard_map/ppermute | solution.py:87
  249.2 48.6 %collective-permute-start.17 = (f32[32,64,64]{2,0,1:T(8,128)}, f32[32,64,64]{2,0,1:T(8,128)S(1)}, u32[]{:S(2)}, u32[]{:S(2)}) collective-permute-start(f32[32,64,64]{2,0,1:T(8,128)} %get-tuple-element.50), channel_id=1, source_target_pairs={{0,128},{64,192},{128,0},{192,64},{16,144},{80,208},{144,16},{208,... | collective-permute-start | bytes 1572872 | tf_op jit(solution)/shard_map/ppermute | solution.py:47
  267.8 39.0 %copy-start.2 = (f32[64,64,64]{1,2,0:T(8,128)}, f32[64,64,64]{1,2,0:T(8,128)S(1)}, u32[]{:S(2)}) copy-start(f32[64,64,64]{1,2,0:T(8,128)S(1)} %fusion.45) | copy-start | bytes 3145732
  301.6 27.3 %collective-permute-start.19 = (f32[32,64,64]{2,0,1:T(8,128)}, f32[32,64,64]{2,0,1:T(8,128)}, u32[]{:S(2)}, u32[]{:S(2)}) collective-permute-start(f32[32,64,64]{2,0,1:T(8,128)} %get-tuple-element.24), channel_id=1, source_target_pairs={{0,48},{64,112},{128,176},{192,240},{16,0},{80,64},{144,128},{208,... | collective-permute-start | bytes 1572872 | tf_op jit(solution)/shard_map/ppermute | solution.py:57
  305.0 46.5 %collective-permute-start.20 = (f32[32,64,64]{2,0,1:T(8,128)}, f32[32,64,64]{2,0,1:T(8,128)}, u32[]{:S(2)}, u32[]{:S(2)}) collective-permute-start(f32[32,64,64]{2,0,1:T(8,128)} %get-tuple-element.23), channel_id=1, source_target_pairs={{0,32},{64,96},{128,160},{192,224},{16,48},{80,112},{144,176},{208... | collective-permute-start | bytes 1572872 | tf_op jit(solution)/shard_map/ppermute | solution.py:57
  305.8 46.3 %collective-permute-start.21 = (f32[32,64,64]{2,0,1:T(8,128)}, f32[32,64,64]{2,0,1:T(8,128)}, u32[]{:S(2)}, u32[]{:S(2)}) collective-permute-start(f32[32,64,64]{2,0,1:T(8,128)} %get-tuple-element.22), channel_id=1, source_target_pairs={{0,16},{64,80},{128,144},{192,208},{16,32},{80,96},{144,160},{208,... | collective-permute-start | bytes 1572872 | tf_op jit(solution)/shard_map/ppermute | solution.py:57
  307.5 9.2 %collective-permute-start.29 = (f32[7,64,64]{1,2,0:T(8,128)}, f32[7,64,64]{1,2,0:T(8,128)}, u32[]{:S(2)}, u32[]{:S(2)}) collective-permute-start(f32[7,64,64]{1,2,0:T(8,128)} %get-tuple-element.44), channel_id=1, source_target_pairs={{64,0},{80,16},{96,32},{112,48},{128,64},{144,80},{160,96},{176,11... | collective-permute-start | bytes 344072 | tf_op jit(solution)/shard_map/ppermute | solution.py:100
  308.8 8.3 %collective-permute-start.28 = (f32[7,64,64]{1,2,0:T(8,128)S(1)}, f32[7,64,64]{1,2,0:T(8,128)}, u32[]{:S(2)}, u32[]{:S(2)}) collective-permute-start(f32[7,64,64]{1,2,0:T(8,128)S(1)} %get-tuple-element.43), channel_id=1, source_target_pairs={{0,64},{16,80},{32,96},{48,112},{64,128},{80,144},{96,160},{112,17... | collective-permute-start | bytes 344072 | tf_op jit(solution)/shard_map/ppermute | solution.py:99
  325.1 29.2 %copy-start.16 = (f32[64,78]{1,0:T(8,128)S(1)}, f32[64,78]{1,0:T(8,128)}, u32[]{:S(2)}) copy-start(f32[64,78]{1,0:T(8,128)} %get-tuple-element.12) | copy-start | bytes 59908
  360.5 9.1 %collective-permute-start.31 = (f32[7,64,64]{2,0,1:T(8,128)S(1)}, f32[7,64,64]{2,0,1:T(8,128)S(1)}, u32[]{:S(2)}, u32[]{:S(2)}) collective-permute-start(f32[7,64,64]{2,0,1:T(8,128)S(1)} %get-tuple-element.42), channel_id=1, source_target_pairs={{64,0},{80,16},{96,32},{112,48},{128,64},{144,80},{160,96},{176,11... | collective-permute-start | bytes 344072 | tf_op jit(solution)/shard_map/ppermute | solution.py:100
  361.8 9.0 %collective-permute-start.30 = (f32[7,64,64]{2,0,1:T(8,128)S(1)}, f32[7,64,64]{2,0,1:T(8,128)S(1)}, u32[]{:S(2)}, u32[]{:S(2)}) collective-permute-start(f32[7,64,64]{2,0,1:T(8,128)S(1)} %get-tuple-element.41), channel_id=1, source_target_pairs={{0,64},{16,80},{32,96},{48,112},{64,128},{80,144},{96,160},{112,17... | collective-permute-start | bytes 344072 | tf_op jit(solution)/shard_map/ppermute | solution.py:99
  373.7 5.5 collective-permute-start.32
  387.6 6.8 %collective-permute-start.33 = (f32[64,64,3]{1,0,2:T(8,128)S(1)}, f32[64,64,3]{1,0,2:T(8,128)S(1)}, u32[]{:S(2)}, u32[]{:S(2)}) collective-permute-start(f32[64,64,3]{1,0,2:T(8,128)S(1)} %slice_select_fusion.11), channel_id=1, source_target_pairs={{0,16},{16,0},{32,48},{48,32},{64,80},{80,64},{96,112},{112,96},{1... | collective-permute-start | bytes 147464 | tf_op jit(solution)/shard_map/ppermute | solution.py:87
  402.4 2.7 collective-permute-start.34
  406.4 14.1 %collective-permute-start.35 = (f32[64,2,2,4,64]{4,0,3,2,1:T(8,128)S(1)}, f32[64,2,2,4,64]{4,0,3,2,1:T(8,128)S(1)}, u32[]{:S(2)}, u32[]{:S(2)}) collective-permute-start(f32[64,2,2,4,64]{4,0,3,2,1:T(8,128)S(1)} %select_bitcast_fusion.9), channel_id=1, source_target_pairs={{0,4},{1,5},{2,6},{3,7},{4,0},{5,1},{6,2},{7,3},{8,12},{9,13},{10,... | collective-permute-start | bytes 786440 | tf_op jit(solution)/shard_map/ppermute | solution.py:124
  420.6 9.1 %collective-permute-start.36 = (f32[64,2,4,64]{3,0,2,1:T(8,128)S(1)}, f32[64,2,4,64]{3,0,2,1:T(8,128)S(1)}, u32[]{:S(2)}, u32[]{:S(2)}) collective-permute-start(f32[64,2,4,64]{3,0,2,1:T(8,128)S(1)} %select_bitcast_fusion.15), channel_id=1, source_target_pairs={{0,8},{1,9},{2,10},{3,11},{4,12},{5,13},{6,14},{7,15},{8,0},{9,1},... | collective-permute-start | bytes 393224 | tf_op jit(solution)/shard_map/ppermute | solution.py:124
  429.8 10.4 %collective-permute-start.37 = (f32[64,4,64]{2,0,1:T(8,128)S(1)}, f32[64,4,64]{2,0,1:T(8,128)S(1)}, u32[]{:S(2)}, u32[]{:S(2)}) collective-permute-start(f32[64,4,64]{2,0,1:T(8,128)S(1)} %select_bitcast_fusion.21), channel_id=1, source_target_pairs={{0,2},{1,3},{2,0},{3,1},{4,6},{5,7},{6,4},{7,5},{8,10},{9,11},{10,... | collective-permute-start | bytes 196616 | tf_op jit(solution)/shard_map/ppermute | solution.py:124
  440.9 10.3 %collective-permute-start.38 = (f32[64,4,64]{2,0,1:T(8,128)S(1)}, f32[64,4,64]{2,0,1:T(8,128)S(1)}, u32[]{:S(2)}, u32[]{:S(2)}) collective-permute-start(f32[64,4,64]{2,0,1:T(8,128)S(1)} %fusion.53), channel_id=1, source_target_pairs={{0,2},{1,3},{2,0},{3,1},{4,6},{5,7},{6,4},{7,5},{8,10},{9,11},{10,... | collective-permute-start | bytes 196616 | tf_op jit(solution)/shard_map/ppermute | solution.py:134
  451.3 9.4 %collective-permute-start.39 = (f32[64,2,4,64]{3,0,2,1:T(8,128)S(1)}, f32[64,2,4,64]{3,0,2,1:T(8,128)S(1)}, u32[]{:S(2)}, u32[]{:S(2)}) collective-permute-start(f32[64,2,4,64]{3,0,2,1:T(8,128)S(1)} %pad_maximum_fusion.14), channel_id=1, source_target_pairs={{0,8},{1,9},{2,10},{3,11},{4,12},{5,13},{6,14},{7,15},{8,0},{9,1},... | collective-permute-start | bytes 393224 | tf_op jit(solution)/shard_map/ppermute | solution.py:134
  460.8 9.7 %collective-permute-start.40 = (f32[64,2,2,4,64]{4,0,3,2,1:T(8,128)S(1)}, f32[64,2,2,4,64]{4,0,3,2,1:T(8,128)S(1)}, u32[]{:S(2)}, u32[]{:S(2)}) collective-permute-start(f32[64,2,2,4,64]{4,0,3,2,1:T(8,128)S(1)} %pad_maximum_fusion.12), channel_id=1, source_target_pairs={{0,4},{1,5},{2,6},{3,7},{4,0},{5,1},{6,2},{7,3},{8,12},{9,13},{10,... | collective-permute-start | bytes 786440 | tf_op jit(solution)/shard_map/ppermute | solution.py:134
  470.6 2.7 collective-permute-start.41
  483.1 5.2 collective-permute-start.42
  498.4 5.3 collective-permute-start.43
  508.3 8.2 %collective-permute-start.45 = (f32[7,64,64]{1,2,0:T(8,128)S(1)}, f32[7,64,64]{1,2,0:T(8,128)S(1)}, u32[]{:S(2)}, u32[]{:S(2)}) collective-permute-start(f32[7,64,64]{1,2,0:T(8,128)S(1)} %get-tuple-element.32), channel_id=1, source_target_pairs={{64,0},{80,16},{96,32},{112,48},{128,64},{144,80},{160,96},{176,11... | collective-permute-start | bytes 344072 | tf_op jit(solution)/shard_map/ppermute | solution.py:100
  509.6 8.1 %collective-permute-start.44 = (f32[7,64,64]{1,2,0:T(8,128)S(1)}, f32[7,64,64]{1,2,0:T(8,128)S(1)}, u32[]{:S(2)}, u32[]{:S(2)}) collective-permute-start(f32[7,64,64]{1,2,0:T(8,128)S(1)} %get-tuple-element.31), channel_id=1, source_target_pairs={{0,64},{16,80},{32,96},{48,112},{64,128},{80,144},{96,160},{112,17... | collective-permute-start | bytes 344072 | tf_op jit(solution)/shard_map/ppermute | solution.py:99
  529.5 8.7 %collective-permute-start.47 = (f32[7,64,64]{2,0,1:T(8,128)S(1)}, f32[7,64,64]{2,0,1:T(8,128)S(1)}, u32[]{:S(2)}, u32[]{:S(2)}) collective-permute-start(f32[7,64,64]{2,0,1:T(8,128)S(1)} %get-tuple-element.30), channel_id=1, source_target_pairs={{64,0},{80,16},{96,32},{112,48},{128,64},{144,80},{160,96},{176,11... | collective-permute-start | bytes 344072 | tf_op jit(solution)/shard_map/ppermute | solution.py:100
  530.8 8.9 %collective-permute-start.46 = (f32[7,64,64]{2,0,1:T(8,128)S(1)}, f32[7,64,64]{2,0,1:T(8,128)S(1)}, u32[]{:S(2)}, u32[]{:S(2)}) collective-permute-start(f32[7,64,64]{2,0,1:T(8,128)S(1)} %get-tuple-element.29), channel_id=1, source_target_pairs={{0,64},{16,80},{32,96},{48,112},{64,128},{80,144},{96,160},{112,17... | collective-permute-start | bytes 344072 | tf_op jit(solution)/shard_map/ppermute | solution.py:99
  542.7 5.3 collective-permute-start.48
  556.3 6.8 %collective-permute-start.49 = (f32[64,64,3]{1,0,2:T(8,128)S(1)}, f32[64,64,3]{1,0,2:T(8,128)S(1)}, u32[]{:S(2)}, u32[]{:S(2)}) collective-permute-start(f32[64,64,3]{1,0,2:T(8,128)S(1)} %slice_select_fusion.10), channel_id=1, source_target_pairs={{0,16},{16,0},{32,48},{48,32},{64,80},{80,64},{96,112},{112,96},{1... | collective-permute-start | bytes 147464 | tf_op jit(solution)/shard_map/ppermute | solution.py:87
  570.7 3.0 collective-permute-start.50
  575.0 14.1 %collective-permute-start.51 = (f32[64,2,2,4,64]{4,0,3,2,1:T(8,128)S(1)}, f32[64,2,2,4,64]{4,0,3,2,1:T(8,128)S(1)}, u32[]{:S(2)}, u32[]{:S(2)}) collective-permute-start(f32[64,2,2,4,64]{4,0,3,2,1:T(8,128)S(1)} %select_bitcast_fusion.6), channel_id=1, source_target_pairs={{0,4},{1,5},{2,6},{3,7},{4,0},{5,1},{6,2},{7,3},{8,12},{9,13},{10,... | collective-permute-start | bytes 786440 | tf_op jit(solution)/shard_map/ppermute | solution.py:124
  589.2 9.9 %collective-permute-start.52 = (f32[64,2,4,64]{3,0,2,1:T(8,128)S(1)}, f32[64,2,4,64]{3,0,2,1:T(8,128)S(1)}, u32[]{:S(2)}, u32[]{:S(2)}) collective-permute-start(f32[64,2,4,64]{3,0,2,1:T(8,128)S(1)} %select_bitcast_fusion.12), channel_id=1, source_target_pairs={{0,8},{1,9},{2,10},{3,11},{4,12},{5,13},{6,14},{7,15},{8,0},{9,1},... | collective-permute-start | bytes 393224 | tf_op jit(solution)/shard_map/ppermute | solution.py:124
  599.1 11.2 %collective-permute-start.53 = (f32[64,4,64]{2,0,1:T(8,128)S(1)}, f32[64,4,64]{2,0,1:T(8,128)S(1)}, u32[]{:S(2)}, u32[]{:S(2)}) collective-permute-start(f32[64,4,64]{2,0,1:T(8,128)S(1)} %select_bitcast_fusion.18), channel_id=1, source_target_pairs={{0,2},{1,3},{2,0},{3,1},{4,6},{5,7},{6,4},{7,5},{8,10},{9,11},{10,... | collective-permute-start | bytes 196616 | tf_op jit(solution)/shard_map/ppermute | solution.py:124
  611.0 11.2 %collective-permute-start.54 = (f32[64,4,64]{2,0,1:T(8,128)S(1)}, f32[64,4,64]{2,0,1:T(8,128)S(1)}, u32[]{:S(2)}, u32[]{:S(2)}) collective-permute-start(f32[64,4,64]{2,0,1:T(8,128)S(1)} %get-tuple-element.75), channel_id=1, source_target_pairs={{0,48},{16,0},{32,16},{48,32},{64,112},{80,64},{96,80},{112,96},{1... | collective-permute-start | bytes 196616 | tf_op jit(solution)/shard_map/ppermute | solution.py:47
  613.1 9.1 %collective-permute-start.55 = (f32[64,4,64]{2,0,1:T(8,128)S(1)}, f32[64,4,64]{2,0,1:T(8,128)S(1)}, u32[]{:S(2)}, u32[]{:S(2)}) collective-permute-start(f32[64,4,64]{2,0,1:T(8,128)S(1)} %get-tuple-element.74), channel_id=1, source_target_pairs={{0,32},{16,48},{32,0},{48,16},{64,96},{80,112},{96,64},{112,80},{1... | collective-permute-start | bytes 196616 | tf_op jit(solution)/shard_map/ppermute | solution.py:47
  613.1 9.2 %collective-permute-start.56 = (f32[64,4,64]{2,0,1:T(8,128)S(1)}, f32[64,4,64]{2,0,1:T(8,128)S(1)}, u32[]{:S(2)}, u32[]{:S(2)}) collective-permute-start(f32[64,4,64]{2,0,1:T(8,128)S(1)} %get-tuple-element.17), channel_id=1, source_target_pairs={{0,16},{16,32},{32,48},{48,0},{64,80},{80,96},{96,112},{112,64},{1... | collective-permute-start | bytes 196616 | tf_op jit(solution)/shard_map/ppermute | solution.py:47
  622.3 7.6 %collective-permute-start.57 = (f32[64,4,64]{2,0,1:T(8,128)S(1)}, f32[64,4,64]{2,0,1:T(8,128)S(1)}, u32[]{:S(2)}, u32[]{:S(2)}) collective-permute-start(f32[64,4,64]{2,0,1:T(8,128)S(1)} %get-tuple-element.62), channel_id=1, source_target_pairs={{0,192},{16,208},{32,224},{48,240},{64,0},{80,16},{96,32},{112,48}... | collective-permute-start | bytes 196616 | tf_op jit(solution)/shard_map/ppermute | solution.py:57
  626.7 9.0 %collective-permute-start.58 = (f32[64,4,64]{2,0,1:T(8,128)S(1)}, f32[64,4,64]{2,0,1:T(8,128)S(1)}, u32[]{:S(2)}, u32[]{:S(2)}) collective-permute-start(f32[64,4,64]{2,0,1:T(8,128)S(1)} %get-tuple-element.61), channel_id=1, source_target_pairs={{0,128},{16,144},{32,160},{48,176},{64,192},{80,208},{96,224},{112... | collective-permute-start | bytes 196616 | tf_op jit(solution)/shard_map/ppermute | solution.py:57
  626.9 8.9 %collective-permute-start.59 = (f32[64,4,64]{2,0,1:T(8,128)S(1)}, f32[64,4,64]{2,0,1:T(8,128)S(1)}, u32[]{:S(2)}, u32[]{:S(2)}) collective-permute-start(f32[64,4,64]{2,0,1:T(8,128)S(1)} %get-tuple-element.60), channel_id=1, source_target_pairs={{0,64},{16,80},{32,96},{48,112},{64,128},{80,144},{96,160},{112,17... | collective-permute-start | bytes 196616 | tf_op jit(solution)/shard_map/ppermute | solution.py:57
  (14 other events, 141.5 us)

commit v8 on v7

--- a/solution.py
+++ b/solution.py
@@ -101,43 +101,37 @@
     return jnp.concatenate([low, volume, high], axis=axis)
 
 
-RS_BITS = (1, 4, 8, 2)
-
-
-def bit_axis(present, m):
-    order = [8, 4, 2, 1]
-    return 1 + sum(1 for b in order if b in present and order.index(b) < order.index(m))
+GROUPS = (2, 0)
 
 
 def view_reduce_scatter(full, nv):
     me = lax.axis_index("view")
     s0, s1, s2 = full.shape
-    x = full.reshape(s0, 2, 2, 2, 2, s1 // nv, s2)
-    present = {8, 4, 2, 1}
-    for m in RS_BITS:
-        ax = bit_axis(present, m)
-        x0 = lax.index_in_dim(x, 0, axis=ax, keepdims=False)
-        x1 = lax.index_in_dim(x, 1, axis=ax, keepdims=False)
-        mine = (me & m) != 0
-        keep = jnp.where(mine, x1, x0)
-        send = jnp.where(mine, x0, x1)
-        x = keep + lax.ppermute(send, "view", xor_pairs(nv, m))
-        present.discard(m)
+    x = full.reshape(s0, 4, 4, s1 // nv, s2)
+    for shift in GROUPS:
+        digit = (me >> shift) & 3
+        total = lax.dynamic_index_in_dim(x, digit, axis=1, keepdims=False)
+        for t in (1, 2, 3):
+            piece = lax.dynamic_index_in_dim(x, digit ^ t, axis=1, keepdims=False)
+            total = total + lax.ppermute(piece, "view", xor_pairs(nv, t << shift))
+        x = total
     return x
 
 
 def view_all_gather(share, nv):
     me = lax.axis_index("view")
     x = share
-    present = set()
-    for m in reversed(RS_BITS):
-        recv = lax.ppermute(x, "view", xor_pairs(nv, m))
-        mine = (me & m) != 0
-        lo = jnp.where(mine, recv, x)
-        hi = jnp.where(mine, x, recv)
-        ax = bit_axis(present | {m}, m)
-        x = jnp.stack([lo, hi], axis=ax)
-        present.add(m)
+    for shift in reversed(GROUPS):
+        digit = (me >> shift) & 3
+        pieces = [x] + [lax.ppermute(x, "view", xor_pairs(nv, t << shift)) for t in (1, 2, 3)]
+        slots = []
+        for q in range(4):
+            offset = digit ^ q
+            slot = pieces[3]
+            for t in (2, 1, 0):
+                slot = jnp.where(offset == t, pieces[t], slot)
+            slots.append(slot)
+        x = jnp.stack(slots, axis=1)
     s0 = x.shape[0]
     return x.reshape(s0, -1, x.shape[-1])
 

time: 647 us -> 657 us (1.015)
  starting transfers between devices: 125 us -> 137 us
    ppermute x24, waiting for transfers between devices: 171 us -> 150 us  [route(): part = lax.ppermute(part, 'space', pairs)]
    ppermute x16 -> x24, waiting for transfers between devices: 78.7 us -> 98.8 us  [the longest x12 52.9 us: view_all_gather(): lax.ppermute(x, 'view', xor_pairs(nv, t << shift))]
    ppermute x24, starting transfers between devices: 37.5 us -> 44.9 us  [route(): part = lax.ppermute(part, 'space', pairs)]
    unnamed x41 -> x47, local copies, waits for them, and re-layouts: 12.9 us -> 16.6 us
    ppermute x16 -> x24, starting transfers between devices: 43.9 us -> 42.7 us  [the longest x12 22.2 us: view_all_gather(): lax.ppermute(x, 'view', xor_pairs(nv, t << shift))]
  transfers between devices with their start and end apart: 60 -> 68, of which waited for: 41 -> 45; matrix products, arithmetic and copies ran while one was open for 13% -> 14% of each run, Pallas kernels for 0% -> 0%
where the time goes in v8:
time: 657 us; the launch traced here: 645 us
  waiting for transfers between devices  288 us (44%)
  starting transfers between devices  137 us (21%)
  other arithmetic  68.7 us (10%)
  local copies, waits for them, and re-layouts  58.3 us (9%)
  matrix products  54.4 us (8%)
  between operations  38.7 us (6%)
    ppermute x24, waiting for transfers between devices, route(): part = lax.ppermute(part, 'space', pairs)  150 us
    ppermute x12, waiting for transfers between devices, view_all_gather(): lax.ppermute(x, 'view', xor_pairs(nv, t << shift))  52.9 us
    ppermute x12, waiting for transfers between devices, view_reduce_scatter(): total = total + lax.ppermute(piece, 'view', xor_pairs(nv, t << shift))  45.9 us
    ppermute x24, starting transfers between devices, route(): part = lax.ppermute(part, 'space', pairs)  44.9 us
    ppermute x4, starting transfers between devices, z_halo(): low = lax.ppermute(last, 'space', [(i, i + ROW) for i in range(nsp - ROW)])  24.9 us
    ppermute x12, starting transfers between devices, view_all_gather(): lax.ppermute(x, 'view', xor_pairs(nv, t << shift))  22.2 us
    ppermute x12, starting transfers between devices, view_reduce_scatter(): total = total + lax.ppermute(piece, 'view', xor_pairs(nv, t << shift))  20.5 us
    select_n x3, other arithmetic, band_matrix(): band = jnp.where(offset == position, weight, band)  19.8 us
  transfers between devices with their start and end apart: 68, of which 45 were waited for; matrix products, arithmetic and copies ran while one was open for 14% of the time, Pallas kernels for 0%

profile of v8, /device:TPU:8, one launch (start us, length us, event | category | flops | bytes accessed | tf_op | source)
XLA Modules:
  0.0 645.2 jit_solution(17559029450676917623)
XLA Ops:
  12.7 4.8 select_select_fusion.22
  17.5 5.0 select_select_fusion.20
  23.5 4.3 collective-permute-done.1
  28.0 3.4 collective-permute-done.2
  53.8 4.0 collective-permute-start.7
  66.0 5.4 collective-permute-start.23
  71.8 9.9 %select_select_fusion.24 = (f32[64,78]{1,0:T(8,128)}, f32[64,78]{1,0:T(8,128)}) fusion(f32[]{:T(128)} %bitcast.47, f32[]{:T(128)} %bitcast.46, f32[]{:T(128)} %bitcast.45, f32[]{:T(128)} %bitcast.44, f32[]{:T(128)} %bitcast.43, f32[]{:T(128)} %bitcast.42, f32[]{:T(128)} %bitcast.41, f32[]{:T(128)} %bitcast.40, f32[]{:T(128)} %bitcast.39, f32[]{:T(128)} %bitcast.38, ...), kind=kLoop, calls=%fused_computation.187 | loop fusion | flops 229632 | bytes 39996 | tf_op jit(solution)/shard_map/jit(_where)/select_n | solution.py:68
  95.8 3.8 collective-permute-done.25
  100.9 11.4 %collective-permute-done.26 = f32[64,4,4,64]{3,0,2,1:T(8,128)} collective-permute-done((f32[64,4,4,64]{3,0,2,1:T(8,128)}, f32[64,4,4,64]{3,0,2,1:T(8,128)}, u32[]{:S(2)}, u32[]{:S(2)}) %collective-permute-start.26) | collective-permute-done | bytes 262176 | tf_op jit(solution)/shard_map/ppermute | solution.py:126
  112.4 2.8 collective-permute-done.27
  115.2 2.9 collective-permute-start.18
  132.7 6.9 %collective-permute-done.10 = f32[32,64,64]{2,0,1:T(8,128)S(1)} collective-permute-done((f32[32,64,64]{2,0,1:T(8,128)}, f32[32,64,64]{2,0,1:T(8,128)S(1)}, u32[]{:S(2)}, u32[]{:S(2)}) %collective-permute-start.10) | collective-permute-done | bytes 524320 | tf_op jit(solution)/shard_map/ppermute | solution.py:47
  141.9 5.6 collective-permute-done.12
  147.5 3.9 select_select_fusion.5
  155.4 9.1 %collective-permute-start.15 = (f32[32,64,64]{2,0,1:T(8,128)}, f32[32,64,64]{2,0,1:T(8,128)}, u32[]{:S(2)}, u32[]{:S(2)}) collective-permute-start(f32[32,64,64]{2,0,1:T(8,128)} %get-tuple-element.19), channel_id=1, source_target_pairs={{0,64},{16,80},{32,96},{48,112},{64,128},{80,144},{96,160},{112,17... | collective-permute-start | bytes 1572872 | tf_op jit(solution)/shard_map/ppermute | solution.py:57
  169.2 4.9 fusion.28
  177.9 66.1 %collective-permute-done.14 = f32[32,64,64]{2,0,1:T(8,128)} collective-permute-done((f32[32,64,64]{2,0,1:T(8,128)}, f32[32,64,64]{2,0,1:T(8,128)}, u32[]{:S(2)}, u32[]{:S(2)}) %collective-permute-start.14) | collective-permute-done | bytes 524320 | tf_op jit(solution)/shard_map/ppermute | solution.py:57
  244.0 3.6 select_select_fusion.4
  256.9 5.5 fusion.45
  262.4 32.2 %collective-permute-done.17 = f32[32,64,64]{2,0,1:T(8,128)S(1)} collective-permute-done((f32[32,64,64]{2,0,1:T(8,128)}, f32[32,64,64]{2,0,1:T(8,128)S(1)}, u32[]{:S(2)}, u32[]{:S(2)}) %collective-permute-start.17) | collective-permute-done | bytes 524320 | tf_op jit(solution)/shard_map/ppermute | solution.py:47
  294.6 3.8 select_select_fusion.1
  298.5 3.0 collective-permute-start.19
  305.1 5.6 collective-permute-start.30
  314.1 3.6 pad_maximum_fusion
  317.7 4.4 copy.249
  322.1 3.2 collective-permute-done.19
  325.3 22.7 %collective-permute-done.20 = f32[32,64,64]{2,0,1:T(8,128)} collective-permute-done((f32[32,64,64]{2,0,1:T(8,128)}, f32[32,64,64]{2,0,1:T(8,128)}, u32[]{:S(2)}, u32[]{:S(2)}) %collective-permute-start.20) | collective-permute-done | bytes 524320 | tf_op jit(solution)/shard_map/ppermute | solution.py:57
  350.9 6.1 fusion.41
  358.3 4.6 collective-permute-start.32
  362.9 3.4 collective-permute-done.33
  372.9 2.9 collective-permute-done.34
  376.8 3.3 copy.284
  380.1 3.4 convolution_bitcast_fusion.1
  384.1 4.2 collective-permute-start.35
  392.4 4.9 fusion.26
  397.9 2.8 collective-permute-start.38
  403.3 17.8 %collective-permute-done.38 = f32[64,4,4,64]{3,0,2,1:T(8,128)S(1)} collective-permute-done((f32[64,4,4,64]{3,0,2,1:T(8,128)S(1)}, f32[64,4,4,64]{3,0,2,1:T(8,128)S(1)}, u32[]{:S(2)}, u32[]{:S(2)}) %collective-permute-start.38) | collective-permute-done | bytes 262176 | tf_op jit(solution)/shard_map/ppermute | solution.py:116
  423.9 3.1 collective-permute-start.40
  431.4 2.9 collective-permute-done.40
  436.0 4.0 collective-permute-start.43
  441.3 4.0 collective-permute-done.43
  445.4 4.3 collective-permute-done.44
  454.9 10.1 %collective-permute-done.45 = f32[64,4,4,64]{3,0,2,1:T(8,128)S(1)} collective-permute-done((f32[64,4,4,64]{3,0,2,1:T(8,128)S(1)}, f32[64,4,4,64]{3,0,2,1:T(8,128)S(1)}, u32[]{:S(2)}, u32[]{:S(2)}) %collective-permute-start.45) | collective-permute-done | bytes 262176 | tf_op jit(solution)/shard_map/ppermute | solution.py:126
  465.0 12.5 %collective-permute-done.46 = f32[64,4,4,64]{3,0,2,1:T(8,128)S(1)} collective-permute-done((f32[64,4,4,64]{3,0,2,1:T(8,128)S(1)}, f32[64,4,4,64]{3,0,2,1:T(8,128)S(1)}, u32[]{:S(2)}, u32[]{:S(2)}) %collective-permute-start.46) | collective-permute-done | bytes 262176 | tf_op jit(solution)/shard_map/ppermute | solution.py:126
  480.7 2.8 fusion.118
  498.9 4.7 fusion.34
  504.7 5.0 collective-permute-done.49
  510.4 4.0 fusion.42
  515.7 9.7 %collective-permute-start.50 = (f32[7,64,64]{1,2,0:T(8,128)S(1)}, f32[7,64,64]{1,2,0:T(8,128)S(1)}, u32[]{:S(2)}, u32[]{:S(2)}) collective-permute-start(f32[7,64,64]{1,2,0:T(8,128)S(1)} %get-tuple-element.33), channel_id=1, source_target_pairs={{0,64},{16,80},{32,96},{48,112},{64,128},{80,144},{96,160},{112,17... | collective-permute-start | bytes 344072 | tf_op jit(solution)/shard_map/ppermute | solution.py:99
  529.1 3.3 copy.268
  532.4 8.3 %fusion.40 = f32[64,64,64]{2,0,1:T(8,128)S(1)} fusion(f32[32,64,64]{2,0,1:T(8,128)} %copy-done.9, f32[32,64,64]{2,0,1:T(8,128)} %get-tuple-element.57, f32[78,64,64]{0,2,1:T(8,128)} %copy.268, f32[64,78]{1,0:T(8,128)S(1)} %copy-done.17), kind=kOutput, calls=%fused_computation.52 | convolution fusion | flops 245891072 | bytes 3395072 | tf_op jit(solution)/shard_map/ot,tab->oab/dot_general | solution.py:75
  542.1 5.0 collective-permute-start.52
  554.2 5.0 collective-permute-done.54
  560.2 3.3 copy.288
  563.4 3.5 convolution_bitcast_fusion
  567.6 4.2 collective-permute-start.55
  575.4 4.9 fusion.24
  582.9 2.7 collective-permute-start.56
  585.7 14.0 %collective-permute-done.58 = f32[64,4,4,64]{3,0,2,1:T(8,128)S(1)} collective-permute-done((f32[64,4,4,64]{3,0,2,1:T(8,128)S(1)}, f32[64,4,4,64]{3,0,2,1:T(8,128)S(1)}, u32[]{:S(2)}, u32[]{:S(2)}) %collective-permute-start.58) | collective-permute-done | bytes 262176 | tf_op jit(solution)/shard_map/ppermute | solution.py:116
  603.9 3.1 collective-permute-start.59
  607.1 4.0 collective-permute-done.61
  611.1 2.7 collective-permute-done.60
  626.0 6.8 %collective-permute-start.65 = (f32[64,4,64]{2,0,1:T(8,128)S(1)}, f32[64,4,64]{2,0,1:T(8,128)S(1)}, u32[]{:S(2)}, u32[]{:S(2)}) collective-permute-start(f32[64,4,64]{2,0,1:T(8,128)S(1)} %get-tuple-element.66), channel_id=1, source_target_pairs={{0,192},{16,208},{32,224},{48,240},{64,0},{80,16},{96,32},{112,48}... | collective-permute-start | bytes 196616 | tf_op jit(solution)/shard_map/ppermute | solution.py:57
  636.7 7.5 %collective-permute-done.66 = f32[64,4,64]{2,0,1:T(8,128)S(1)} collective-permute-done((f32[64,4,64]{2,0,1:T(8,128)S(1)}, f32[64,4,64]{2,0,1:T(8,128)S(1)}, u32[]{:S(2)}, u32[]{:S(2)}) %collective-permute-start.66) | collective-permute-done | bytes 65568 | tf_op jit(solution)/shard_map/ppermute | solution.py:57
  (244 shorter events, 165.7 us)
Async XLA Ops:
  1.5 21.1 %collective-permute-start = (s32[16,7]{0,1:T(8,128)S(1)}, s32[16,7]{0,1:T(8,128)S(1)}, u32[]{:S(2)}, u32[]{:S(2)}) collective-permute-start(s32[16,7]{0,1:T(8,128)S(1)} %broadcast_select_fusion.24), channel_id=1, source_target_pairs={{0,16},{16,0},{32,48},{48,32},{64,80},{80,64},{96,112},{112,96},{1... | collective-permute-start | bytes 1352 | tf_op jit(solution)/shard_map/ppermute | solution.py:23
  42.6 11.1 %collective-permute-start.4 = (f32[64,4,64]{2,0,1:T(8,128)S(1)}, f32[64,4,64]{2,0,1:T(8,128)S(1)}, u32[]{:S(2)}, u32[]{:S(2)}) collective-permute-start(f32[64,4,64]{2,0,1:T(8,128)S(1)} %bitcast.280), channel_id=1, source_target_pairs={{0,48},{16,0},{32,16},{48,32},{64,112},{80,64},{96,80},{112,96},{1... | collective-permute-start | bytes 196616 | tf_op jit(solution)/shard_map/ppermute | solution.py:47
  43.2 10.5 %collective-permute-start.5 = (f32[64,4,64]{2,0,1:T(8,128)S(1)}, f32[64,4,64]{2,0,1:T(8,128)S(1)}, u32[]{:S(2)}, u32[]{:S(2)}) collective-permute-start(f32[64,4,64]{2,0,1:T(8,128)S(1)} %bitcast.281), channel_id=1, source_target_pairs={{0,32},{16,48},{32,0},{48,16},{64,96},{80,112},{96,64},{112,80},{1... | collective-permute-start | bytes 196616 | tf_op jit(solution)/shard_map/ppermute | solution.py:47
  45.7 8.0 %collective-permute-start.6 = (f32[64,4,64]{2,0,1:T(8,128)S(1)}, f32[64,4,64]{2,0,1:T(8,128)S(1)}, u32[]{:S(2)}, u32[]{:S(2)}) collective-permute-start(f32[64,4,64]{2,0,1:T(8,128)S(1)} %bitcast.282), channel_id=1, source_target_pairs={{0,16},{16,32},{32,48},{48,0},{64,80},{80,96},{96,112},{112,64},{1... | collective-permute-start | bytes 196616 | tf_op jit(solution)/shard_map/ppermute | solution.py:47
  53.8 10.6 %collective-permute-start.7 = (f32[64,4,64]{2,0,1:T(8,128)S(1)}, f32[64,4,64]{2,0,1:T(8,128)S(1)}, u32[]{:S(2)}, u32[]{:S(2)}) collective-permute-start(f32[64,4,64]{2,0,1:T(8,128)S(1)} %get-tuple-element.83), channel_id=1, source_target_pairs={{0,192},{16,208},{32,224},{48,240},{64,0},{80,16},{96,32},{112,48}... | collective-permute-start | bytes 196616 | tf_op jit(solution)/shard_map/ppermute | solution.py:57
  57.8 7.4 %collective-permute-start.8 = (f32[64,4,64]{2,0,1:T(8,128)S(1)}, f32[64,4,64]{2,0,1:T(8,128)S(1)}, u32[]{:S(2)}, u32[]{:S(2)}) collective-permute-start(f32[64,4,64]{2,0,1:T(8,128)S(1)} %get-tuple-element.82), channel_id=1, source_target_pairs={{0,128},{16,144},{32,160},{48,176},{64,192},{80,208},{96,224},{112... | collective-permute-start | bytes 196616 | tf_op jit(solution)/shard_map/ppermute | solution.py:57
  57.8 7.4 %collective-permute-start.9 = (f32[64,4,64]{2,0,1:T(8,128)S(1)}, f32[64,4,64]{2,0,1:T(8,128)S(1)}, u32[]{:S(2)}, u32[]{:S(2)}) collective-permute-start(f32[64,4,64]{2,0,1:T(8,128)S(1)} %get-tuple-element.81), channel_id=1, source_target_pairs={{0,64},{16,80},{32,96},{48,112},{64,128},{80,144},{96,160},{112,17... | collective-permute-start | bytes 196616 | tf_op jit(solution)/shard_map/ppermute | solution.py:57
  65.9 16.5 %collective-permute-start.22 = (f32[64,4,64]{2,0,1:T(8,128)S(1)}, f32[64,4,64]{2,0,1:T(8,128)S(1)}, u32[]{:S(2)}, u32[]{:S(2)}) collective-permute-start(f32[64,4,64]{2,0,1:T(8,128)S(1)} %select_select_fusion.12), channel_id=1, source_target_pairs={{0,1},{1,0},{2,3},{3,2},{4,5},{5,4},{6,7},{7,6},{8,9},{9,8},{10,11... | collective-permute-start | bytes 196616 | tf_op jit(solution)/shard_map/ppermute | solution.py:126
  66.0 16.4 %collective-permute-start.23 = (f32[64,4,64]{2,0,1:T(8,128)S(1)}, f32[64,4,64]{2,0,1:T(8,128)S(1)}, u32[]{:S(2)}, u32[]{:S(2)}) collective-permute-start(f32[64,4,64]{2,0,1:T(8,128)S(1)} %select_select_fusion.12), channel_id=1, source_target_pairs={{0,2},{1,3},{2,0},{3,1},{4,6},{5,7},{6,4},{7,5},{8,10},{9,11},{10,... | collective-permute-start | bytes 196616 | tf_op jit(solution)/shard_map/ppermute | solution.py:126
  71.4 12.2 %collective-permute-start.24 = (f32[64,4,64]{2,0,1:T(8,128)S(1)}, f32[64,4,64]{2,0,1:T(8,128)S(1)}, u32[]{:S(2)}, u32[]{:S(2)}) collective-permute-start(f32[64,4,64]{2,0,1:T(8,128)S(1)} %select_select_fusion.12), channel_id=1, source_target_pairs={{0,3},{1,2},{2,1},{3,0},{4,7},{5,6},{6,5},{7,4},{8,11},{9,10},{10,... | collective-permute-start | bytes 196616 | tf_op jit(solution)/shard_map/ppermute | solution.py:126
  84.6 15.1 %collective-permute-start.25 = (f32[64,4,4,64]{3,0,2,1:T(8,128)}, f32[64,4,4,64]{3,0,2,1:T(8,128)}, u32[]{:S(2)}, u32[]{:S(2)}) collective-permute-start(f32[64,4,4,64]{3,0,2,1:T(8,128)} %pad_maximum_fusion.9), channel_id=1, source_target_pairs={{0,4},{1,5},{2,6},{3,7},{4,0},{5,1},{6,2},{7,3},{8,12},{9,13},{10,... | collective-permute-start | bytes 786440 | tf_op jit(solution)/shard_map/ppermute | solution.py:126
  86.0 26.3 %collective-permute-start.26 = (f32[64,4,4,64]{3,0,2,1:T(8,128)}, f32[64,4,4,64]{3,0,2,1:T(8,128)}, u32[]{:S(2)}, u32[]{:S(2)}) collective-permute-start(f32[64,4,4,64]{3,0,2,1:T(8,128)} %pad_maximum_fusion.9), channel_id=1, source_target_pairs={{0,8},{1,9},{2,10},{3,11},{4,12},{5,13},{6,14},{7,15},{8,0},{9,1},... | collective-permute-start | bytes 786440 | tf_op jit(solution)/shard_map/ppermute | solution.py:126
  88.8 26.4 %collective-permute-start.27 = (f32[64,4,4,64]{3,0,2,1:T(8,128)}, f32[64,4,4,64]{3,0,2,1:T(8,128)}, u32[]{:S(2)}, u32[]{:S(2)}) collective-permute-start(f32[64,4,4,64]{3,0,2,1:T(8,128)} %pad_maximum_fusion.9), channel_id=1, source_target_pairs={{0,12},{1,13},{2,14},{3,15},{4,8},{5,9},{6,10},{7,11},{8,4},{9,5},... | collective-permute-start | bytes 786440 | tf_op jit(solution)/shard_map/ppermute | solution.py:126
  92.6 169.8 %collective-permute-start.16 = (f32[32,64,64]{2,0,1:T(8,128)}, f32[32,64,64]{2,0,1:T(8,128)}, u32[]{:S(2)}, u32[]{:S(2)}) collective-permute-start(f32[32,64,64]{2,0,1:T(8,128)} %get-tuple-element.62), channel_id=1, source_target_pairs={{0,192},{64,0},{128,64},{192,128},{16,208},{80,16},{144,80},{208,1... | collective-permute-start | bytes 1572872 | tf_op jit(solution)/shard_map/ppermute | solution.py:47
  93.8 45.8 %collective-permute-start.10 = (f32[32,64,64]{2,0,1:T(8,128)}, f32[32,64,64]{2,0,1:T(8,128)S(1)}, u32[]{:S(2)}, u32[]{:S(2)}) collective-permute-start(f32[32,64,64]{2,0,1:T(8,128)} %get-tuple-element.63), channel_id=1, source_target_pairs={{0,48},{16,0},{32,16},{48,32},{64,112},{80,64},{96,80},{112,96},{1... | collective-permute-start | bytes 1572872 | tf_op jit(solution)/shard_map/ppermute | solution.py:47
  99.6 42.3 %collective-permute-start.11 = (f32[32,64,64]{2,0,1:T(8,128)}, f32[32,64,64]{2,0,1:T(8,128)}, u32[]{:S(2)}, u32[]{:S(2)}) collective-permute-start(f32[32,64,64]{2,0,1:T(8,128)} %get-tuple-element.60), channel_id=1, source_target_pairs={{0,32},{16,48},{32,0},{48,16},{64,96},{80,112},{96,64},{112,80},{1... | collective-permute-start | bytes 1572872 | tf_op jit(solution)/shard_map/ppermute | solution.py:47
  112.4 35.1 %collective-permute-start.12 = (f32[32,64,64]{2,0,1:T(8,128)}, f32[32,64,64]{2,0,1:T(8,128)}, u32[]{:S(2)}, u32[]{:S(2)}) collective-permute-start(f32[32,64,64]{2,0,1:T(8,128)} %get-tuple-element.59), channel_id=1, source_target_pairs={{0,16},{16,32},{32,48},{48,0},{64,80},{80,96},{96,112},{112,64},{1... | collective-permute-start | bytes 1572872 | tf_op jit(solution)/shard_map/ppermute | solution.py:47
  115.2 147.3 %collective-permute-start.18 = (f32[32,64,64]{2,0,1:T(8,128)}, f32[32,64,64]{2,0,1:T(8,128)}, u32[]{:S(2)}, u32[]{:S(2)}) collective-permute-start(f32[32,64,64]{2,0,1:T(8,128)} %get-tuple-element.61), channel_id=1, source_target_pairs={{0,64},{64,128},{128,192},{192,0},{16,80},{80,144},{144,208},{208,... | collective-permute-start | bytes 1572872 | tf_op jit(solution)/shard_map/ppermute | solution.py:47
  139.6 15.7 %collective-permute-start.28 = (f32[64,64,3]{1,0,2:T(8,128)S(1)}, f32[64,64,3]{1,0,2:T(8,128)S(1)}, u32[]{:S(2)}, u32[]{:S(2)}) collective-permute-start(f32[64,64,3]{1,0,2:T(8,128)S(1)} %broadcast_select_fusion.20), channel_id=1, source_target_pairs={{0,16},{16,0},{32,48},{48,32},{64,80},{80,64},{96,112},{112,96},{1... | collective-permute-start | bytes 147464 | tf_op jit(solution)/shard_map/ppermute | solution.py:87
  151.3 26.0 %collective-permute-start.13 = (f32[32,64,64]{2,0,1:T(8,128)}, f32[32,64,64]{2,0,1:T(8,128)}, u32[]{:S(2)}, u32[]{:S(2)}) collective-permute-start(f32[32,64,64]{2,0,1:T(8,128)} %get-tuple-element.21), channel_id=1, source_target_pairs={{0,192},{16,208},{32,224},{48,240},{64,0},{80,16},{96,32},{112,48}... | collective-permute-start | bytes 1572872 | tf_op jit(solution)/shard_map/ppermute | solution.py:57
  153.0 91.0 %collective-permute-start.14 = (f32[32,64,64]{2,0,1:T(8,128)}, f32[32,64,64]{2,0,1:T(8,128)}, u32[]{:S(2)}, u32[]{:S(2)}) collective-permute-start(f32[32,64,64]{2,0,1:T(8,128)} %get-tuple-element.20), channel_id=1, source_target_pairs={{0,128},{16,144},{32,160},{48,176},{64,192},{80,208},{96,224},{112... | collective-permute-start | bytes 1572872 | tf_op jit(solution)/shard_map/ppermute | solution.py:57
  155.4 88.7 %collective-permute-start.15 = (f32[32,64,64]{2,0,1:T(8,128)}, f32[32,64,64]{2,0,1:T(8,128)}, u32[]{:S(2)}, u32[]{:S(2)}) collective-permute-start(f32[32,64,64]{2,0,1:T(8,128)} %get-tuple-element.19), channel_id=1, source_target_pairs={{0,64},{16,80},{32,96},{48,112},{64,128},{80,144},{96,160},{112,17... | collective-permute-start | bytes 1572872 | tf_op jit(solution)/shard_map/ppermute | solution.py:57
  177.4 78.8 %collective-permute-start.29 = (f32[64,3,64]{2,1,0:T(4,128)S(1)}, f32[64,3,64]{2,1,0:T(4,128)S(1)}, u32[]{:S(2)}, u32[]{:S(2)}) collective-permute-start(f32[64,3,64]{2,1,0:T(4,128)S(1)} %slice_select_fusion.9), channel_id=1, source_target_pairs={{0,48},{16,32},{32,16},{48,0},{64,112},{80,96},{96,80},{112,64},{1... | collective-permute-start | bytes 147464 | tf_op jit(solution)/shard_map/ppermute | solution.py:87
  247.6 47.0 %collective-permute-start.17 = (f32[32,64,64]{2,0,1:T(8,128)}, f32[32,64,64]{2,0,1:T(8,128)S(1)}, u32[]{:S(2)}, u32[]{:S(2)}) collective-permute-start(f32[32,64,64]{2,0,1:T(8,128)} %get-tuple-element.58), channel_id=1, source_target_pairs={{0,128},{64,192},{128,0},{192,64},{16,144},{80,208},{144,16},{208,... | collective-permute-start | bytes 1572872 | tf_op jit(solution)/shard_map/ppermute | solution.py:47
  298.5 26.9 %collective-permute-start.19 = (f32[32,64,64]{2,0,1:T(8,128)}, f32[32,64,64]{2,0,1:T(8,128)}, u32[]{:S(2)}, u32[]{:S(2)}) collective-permute-start(f32[32,64,64]{2,0,1:T(8,128)} %get-tuple-element.24), channel_id=1, source_target_pairs={{0,48},{64,112},{128,176},{192,240},{16,0},{80,64},{144,128},{208,... | collective-permute-start | bytes 1572872 | tf_op jit(solution)/shard_map/ppermute | solution.py:57
  301.5 46.6 %collective-permute-start.20 = (f32[32,64,64]{2,0,1:T(8,128)}, f32[32,64,64]{2,0,1:T(8,128)}, u32[]{:S(2)}, u32[]{:S(2)}) collective-permute-start(f32[32,64,64]{2,0,1:T(8,128)} %get-tuple-element.23), channel_id=1, source_target_pairs={{0,32},{64,96},{128,160},{192,224},{16,48},{80,112},{144,176},{208... | collective-permute-start | bytes 1572872 | tf_op jit(solution)/shard_map/ppermute | solution.py:57
  302.2 46.5 %collective-permute-start.21 = (f32[32,64,64]{2,0,1:T(8,128)}, f32[32,64,64]{2,0,1:T(8,128)}, u32[]{:S(2)}, u32[]{:S(2)}) collective-permute-start(f32[32,64,64]{2,0,1:T(8,128)} %get-tuple-element.22), channel_id=1, source_target_pairs={{0,16},{64,80},{128,144},{192,208},{16,32},{80,96},{144,160},{208,... | collective-permute-start | bytes 1572872 | tf_op jit(solution)/shard_map/ppermute | solution.py:57
  303.8 9.5 %collective-permute-start.31 = (f32[7,64,64]{1,2,0:T(8,128)}, f32[7,64,64]{1,2,0:T(8,128)}, u32[]{:S(2)}, u32[]{:S(2)}) collective-permute-start(f32[7,64,64]{1,2,0:T(8,128)} %get-tuple-element.50), channel_id=1, source_target_pairs={{64,0},{80,16},{96,32},{112,48},{128,64},{144,80},{160,96},{176,11... | collective-permute-start | bytes 344072 | tf_op jit(solution)/shard_map/ppermute | solution.py:100
  305.1 9.1 %collective-permute-start.30 = (f32[7,64,64]{1,2,0:T(8,128)}, f32[7,64,64]{1,2,0:T(8,128)}, u32[]{:S(2)}, u32[]{:S(2)}) collective-permute-start(f32[7,64,64]{1,2,0:T(8,128)} %get-tuple-element.49), channel_id=1, source_target_pairs={{0,64},{16,80},{32,96},{48,112},{64,128},{80,144},{96,160},{112,17... | collective-permute-start | bytes 344072 | tf_op jit(solution)/shard_map/ppermute | solution.py:99
  357.0 9.3 %collective-permute-start.33 = (f32[7,64,64]{2,0,1:T(8,128)S(1)}, f32[7,64,64]{2,0,1:T(8,128)S(1)}, u32[]{:S(2)}, u32[]{:S(2)}) collective-permute-start(f32[7,64,64]{2,0,1:T(8,128)S(1)} %get-tuple-element.48), channel_id=1, source_target_pairs={{64,0},{80,16},{96,32},{112,48},{128,64},{144,80},{160,96},{176,11... | collective-permute-start | bytes 344072 | tf_op jit(solution)/shard_map/ppermute | solution.py:100
  358.3 9.2 %collective-permute-start.32 = (f32[7,64,64]{2,0,1:T(8,128)S(1)}, f32[7,64,64]{2,0,1:T(8,128)S(1)}, u32[]{:S(2)}, u32[]{:S(2)}) collective-permute-start(f32[7,64,64]{2,0,1:T(8,128)S(1)} %get-tuple-element.47), channel_id=1, source_target_pairs={{0,64},{16,80},{32,96},{48,112},{64,128},{80,144},{96,160},{112,17... | collective-permute-start | bytes 344072 | tf_op jit(solution)/shard_map/ppermute | solution.py:99
  370.5 5.3 collective-permute-start.34
  384.1 6.8 %collective-permute-start.35 = (f32[64,64,3]{1,0,2:T(8,128)S(1)}, f32[64,64,3]{1,0,2:T(8,128)S(1)}, u32[]{:S(2)}, u32[]{:S(2)}) collective-permute-start(f32[64,64,3]{1,0,2:T(8,128)S(1)} %slice_select_fusion.11), channel_id=1, source_target_pairs={{0,16},{16,0},{32,48},{48,32},{64,80},{80,64},{96,112},{112,96},{1... | collective-permute-start | bytes 147464 | tf_op jit(solution)/shard_map/ppermute | solution.py:87
  397.9 23.2 %collective-permute-start.38 = (f32[64,4,4,64]{3,0,2,1:T(8,128)S(1)}, f32[64,4,4,64]{3,0,2,1:T(8,128)S(1)}, u32[]{:S(2)}, u32[]{:S(2)}) collective-permute-start(f32[64,4,4,64]{3,0,2,1:T(8,128)S(1)} %bitcast.274), channel_id=1, source_target_pairs={{0,12},{1,13},{2,14},{3,15},{4,8},{5,9},{6,10},{7,11},{8,4},{9,5},... | collective-permute-start | bytes 786440 | tf_op jit(solution)/shard_map/ppermute | solution.py:116
  400.9 20.2 %collective-permute-start.37 = (f32[64,4,4,64]{3,0,2,1:T(8,128)S(1)}, f32[64,4,4,64]{3,0,2,1:T(8,128)S(1)}, u32[]{:S(2)}, u32[]{:S(2)}) collective-permute-start(f32[64,4,4,64]{3,0,2,1:T(8,128)S(1)} %bitcast.275), channel_id=1, source_target_pairs={{0,8},{1,9},{2,10},{3,11},{4,12},{5,13},{6,14},{7,15},{8,0},{9,1},... | collective-permute-start | bytes 786440 | tf_op jit(solution)/shard_map/ppermute | solution.py:116
  402.8 19.2 %collective-permute-start.36 = (f32[64,4,4,64]{3,0,2,1:T(8,128)}, f32[64,4,4,64]{3,0,2,1:T(8,128)S(1)}, u32[]{:S(2)}, u32[]{:S(2)}) collective-permute-start(f32[64,4,4,64]{3,0,2,1:T(8,128)} %bitcast.255), channel_id=1, source_target_pairs={{0,4},{1,5},{2,6},{3,7},{4,0},{5,1},{6,2},{7,3},{8,12},{9,13},{10,... | collective-permute-start | bytes 786440 | tf_op jit(solution)/shard_map/ppermute | solution.py:116
  422.3 9.1 %collective-permute-start.41 = (f32[64,4,64]{2,0,1:T(8,128)S(1)}, f32[64,4,64]{2,0,1:T(8,128)S(1)}, u32[]{:S(2)}, u32[]{:S(2)}) collective-permute-start(f32[64,4,64]{2,0,1:T(8,128)S(1)} %get-tuple-element.75), channel_id=1, source_target_pairs={{0,3},{1,2},{2,1},{3,0},{4,7},{5,6},{6,5},{7,4},{8,11},{9,10},{10,... | collective-permute-start | bytes 196616 | tf_op jit(solution)/shard_map/ppermute | solution.py:116
  423.9 10.3 %collective-permute-start.40 = (f32[64,4,64]{2,0,1:T(8,128)S(1)}, f32[64,4,64]{2,0,1:T(8,128)S(1)}, u32[]{:S(2)}, u32[]{:S(2)}) collective-permute-start(f32[64,4,64]{2,0,1:T(8,128)S(1)} %get-tuple-element.76), channel_id=1, source_target_pairs={{0,2},{1,3},{2,0},{3,1},{4,6},{5,7},{6,4},{7,5},{8,10},{9,11},{10,... | collective-permute-start | bytes 196616 | tf_op jit(solution)/shard_map/ppermute | solution.py:116
  427.0 7.2 %collective-permute-start.39 = (f32[64,4,64]{2,0,1:T(8,128)S(1)}, f32[64,4,64]{2,0,1:T(8,128)S(1)}, u32[]{:S(2)}, u32[]{:S(2)}) collective-permute-start(f32[64,4,64]{2,0,1:T(8,128)S(1)} %get-tuple-element.74), channel_id=1, source_target_pairs={{0,1},{1,0},{2,3},{3,2},{4,5},{5,4},{6,7},{7,6},{8,9},{9,8},{10,11... | collective-permute-start | bytes 196616 | tf_op jit(solution)/shard_map/ppermute | solution.py:116
  434.9 6.4 collective-permute-start.42
  436.0 9.4 %collective-permute-start.43 = (f32[64,4,64]{2,0,1:T(8,128)S(1)}, f32[64,4,64]{2,0,1:T(8,128)S(1)}, u32[]{:S(2)}, u32[]{:S(2)}) collective-permute-start(f32[64,4,64]{2,0,1:T(8,128)S(1)} %fusion.63), channel_id=1, source_target_pairs={{0,2},{1,3},{2,0},{3,1},{4,6},{5,7},{6,4},{7,5},{8,10},{9,11},{10,... | collective-permute-start | bytes 196616 | tf_op jit(solution)/shard_map/ppermute | solution.py:126
  439.9 9.8 %collective-permute-start.44 = (f32[64,4,64]{2,0,1:T(8,128)S(1)}, f32[64,4,64]{2,0,1:T(8,128)S(1)}, u32[]{:S(2)}, u32[]{:S(2)}) collective-permute-start(f32[64,4,64]{2,0,1:T(8,128)S(1)} %fusion.63), channel_id=1, source_target_pairs={{0,3},{1,2},{2,1},{3,0},{4,7},{5,6},{6,5},{7,4},{8,11},{9,10},{10,... | collective-permute-start | bytes 196616 | tf_op jit(solution)/shard_map/ppermute | solution.py:126
  449.9 15.1 %collective-permute-start.45 = (f32[64,4,4,64]{3,0,2,1:T(8,128)S(1)}, f32[64,4,4,64]{3,0,2,1:T(8,128)S(1)}, u32[]{:S(2)}, u32[]{:S(2)}) collective-permute-start(f32[64,4,4,64]{3,0,2,1:T(8,128)S(1)} %pad_maximum_fusion.10), channel_id=1, source_target_pairs={{0,4},{1,5},{2,6},{3,7},{4,0},{5,1},{6,2},{7,3},{8,12},{9,13},{10,... | collective-permute-start | bytes 786440 | tf_op jit(solution)/shard_map/ppermute | solution.py:126
  451.9 25.6 %collective-permute-start.46 = (f32[64,4,4,64]{3,0,2,1:T(8,128)S(1)}, f32[64,4,4,64]{3,0,2,1:T(8,128)S(1)}, u32[]{:S(2)}, u32[]{:S(2)}) collective-permute-start(f32[64,4,4,64]{3,0,2,1:T(8,128)S(1)} %pad_maximum_fusion.10), channel_id=1, source_target_pairs={{0,8},{1,9},{2,10},{3,11},{4,12},{5,13},{6,14},{7,15},{8,0},{9,1},... | collective-permute-start | bytes 786440 | tf_op jit(solution)/shard_map/ppermute | solution.py:126
  454.3 25.7 %collective-permute-start.47 = (f32[64,4,4,64]{3,0,2,1:T(8,128)S(1)}, f32[64,4,4,64]{3,0,2,1:T(8,128)S(1)}, u32[]{:S(2)}, u32[]{:S(2)}) collective-permute-start(f32[64,4,4,64]{3,0,2,1:T(8,128)S(1)} %pad_maximum_fusion.10), channel_id=1, source_target_pairs={{0,12},{1,13},{2,14},{3,15},{4,8},{5,9},{6,10},{7,11},{8,4},{9,5},... | collective-permute-start | bytes 786440 | tf_op jit(solution)/shard_map/ppermute | solution.py:126
  504.2 5.5 collective-permute-start.49
  514.4 13.0 %collective-permute-start.51 = (f32[7,64,64]{1,2,0:T(8,128)S(1)}, f32[7,64,64]{1,2,0:T(8,128)S(1)}, u32[]{:S(2)}, u32[]{:S(2)}) collective-permute-start(f32[7,64,64]{1,2,0:T(8,128)S(1)} %get-tuple-element.34), channel_id=1, source_target_pairs={{64,0},{80,16},{96,32},{112,48},{128,64},{144,80},{160,96},{176,11... | collective-permute-start | bytes 344072 | tf_op jit(solution)/shard_map/ppermute | solution.py:100
  515.7 13.2 %collective-permute-start.50 = (f32[7,64,64]{1,2,0:T(8,128)S(1)}, f32[7,64,64]{1,2,0:T(8,128)S(1)}, u32[]{:S(2)}, u32[]{:S(2)}) collective-permute-start(f32[7,64,64]{1,2,0:T(8,128)S(1)} %get-tuple-element.33), channel_id=1, source_target_pairs={{0,64},{16,80},{32,96},{48,112},{64,128},{80,144},{96,160},{112,17... | collective-permute-start | bytes 344072 | tf_op jit(solution)/shard_map/ppermute | solution.py:99
  540.8 8.7 %collective-permute-start.53 = (f32[7,64,64]{2,0,1:T(8,128)S(1)}, f32[7,64,64]{2,0,1:T(8,128)S(1)}, u32[]{:S(2)}, u32[]{:S(2)}) collective-permute-start(f32[7,64,64]{2,0,1:T(8,128)S(1)} %get-tuple-element.32), channel_id=1, source_target_pairs={{64,0},{80,16},{96,32},{112,48},{128,64},{144,80},{160,96},{176,11... | collective-permute-start | bytes 344072 | tf_op jit(solution)/shard_map/ppermute | solution.py:100
  542.1 8.9 %collective-permute-start.52 = (f32[7,64,64]{2,0,1:T(8,128)S(1)}, f32[7,64,64]{2,0,1:T(8,128)S(1)}, u32[]{:S(2)}, u32[]{:S(2)}) collective-permute-start(f32[7,64,64]{2,0,1:T(8,128)S(1)} %get-tuple-element.31), channel_id=1, source_target_pairs={{0,64},{16,80},{32,96},{48,112},{64,128},{80,144},{96,160},{112,17... | collective-permute-start | bytes 344072 | tf_op jit(solution)/shard_map/ppermute | solution.py:99
  554.0 5.2 collective-permute-start.54
  567.6 6.8 %collective-permute-start.55 = (f32[64,64,3]{1,0,2:T(8,128)S(1)}, f32[64,64,3]{1,0,2:T(8,128)S(1)}, u32[]{:S(2)}, u32[]{:S(2)}) collective-permute-start(f32[64,64,3]{1,0,2:T(8,128)S(1)} %slice_select_fusion.10), channel_id=1, source_target_pairs={{0,16},{16,0},{32,48},{48,32},{64,80},{80,64},{96,112},{112,96},{1... | collective-permute-start | bytes 147464 | tf_op jit(solution)/shard_map/ppermute | solution.py:87
  580.9 18.7 %collective-permute-start.58 = (f32[64,4,4,64]{3,0,2,1:T(8,128)S(1)}, f32[64,4,4,64]{3,0,2,1:T(8,128)S(1)}, u32[]{:S(2)}, u32[]{:S(2)}) collective-permute-start(f32[64,4,4,64]{3,0,2,1:T(8,128)S(1)} %bitcast.276), channel_id=1, source_target_pairs={{0,12},{1,13},{2,14},{3,15},{4,8},{5,9},{6,10},{7,11},{8,4},{9,5},... | collective-permute-start | bytes 786440 | tf_op jit(solution)/shard_map/ppermute | solution.py:116
  581.9 17.8 %collective-permute-start.57 = (f32[64,4,4,64]{3,0,2,1:T(8,128)S(1)}, f32[64,4,4,64]{3,0,2,1:T(8,128)S(1)}, u32[]{:S(2)}, u32[]{:S(2)}) collective-permute-start(f32[64,4,4,64]{3,0,2,1:T(8,128)S(1)} %bitcast.277), channel_id=1, source_target_pairs={{0,8},{1,9},{2,10},{3,11},{4,12},{5,13},{6,14},{7,15},{8,0},{9,1},... | collective-permute-start | bytes 786440 | tf_op jit(solution)/shard_map/ppermute | solution.py:116
  582.9 17.7 %collective-permute-start.56 = (f32[64,4,4,64]{3,0,2,1:T(8,128)S(1)}, f32[64,4,4,64]{3,0,2,1:T(8,128)S(1)}, u32[]{:S(2)}, u32[]{:S(2)}) collective-permute-start(f32[64,4,4,64]{3,0,2,1:T(8,128)S(1)} %bitcast.278), channel_id=1, source_target_pairs={{0,4},{1,5},{2,6},{3,7},{4,0},{5,1},{6,2},{7,3},{8,12},{9,13},{10,... | collective-permute-start | bytes 786440 | tf_op jit(solution)/shard_map/ppermute | solution.py:116
  601.0 10.1 %collective-permute-start.61 = (f32[64,4,64]{2,0,1:T(8,128)S(1)}, f32[64,4,64]{2,0,1:T(8,128)S(1)}, u32[]{:S(2)}, u32[]{:S(2)}) collective-permute-start(f32[64,4,64]{2,0,1:T(8,128)S(1)} %get-tuple-element.68), channel_id=1, source_target_pairs={{0,3},{1,2},{2,1},{3,0},{4,7},{5,6},{6,5},{7,4},{8,11},{9,10},{10,... | collective-permute-start | bytes 196616 | tf_op jit(solution)/shard_map/ppermute | solution.py:116
  601.3 12.6 %collective-permute-start.60 = (f32[64,4,64]{2,0,1:T(8,128)S(1)}, f32[64,4,64]{2,0,1:T(8,128)S(1)}, u32[]{:S(2)}, u32[]{:S(2)}) collective-permute-start(f32[64,4,64]{2,0,1:T(8,128)S(1)} %get-tuple-element.69), channel_id=1, source_target_pairs={{0,2},{1,3},{2,0},{3,1},{4,6},{5,7},{6,4},{7,5},{8,10},{9,11},{10,... | collective-permute-start | bytes 196616 | tf_op jit(solution)/shard_map/ppermute | solution.py:116
  603.9 9.9 %collective-permute-start.59 = (f32[64,4,64]{2,0,1:T(8,128)S(1)}, f32[64,4,64]{2,0,1:T(8,128)S(1)}, u32[]{:S(2)}, u32[]{:S(2)}) collective-permute-start(f32[64,4,64]{2,0,1:T(8,128)S(1)} %get-tuple-element.67), channel_id=1, source_target_pairs={{0,1},{1,0},{2,3},{3,2},{4,5},{5,4},{6,7},{7,6},{8,9},{9,8},{10,11... | collective-permute-start | bytes 196616 | tf_op jit(solution)/shard_map/ppermute | solution.py:116
  614.6 11.3 %collective-permute-start.62 = (f32[64,4,64]{2,0,1:T(8,128)S(1)}, f32[64,4,64]{2,0,1:T(8,128)S(1)}, u32[]{:S(2)}, u32[]{:S(2)}) collective-permute-start(f32[64,4,64]{2,0,1:T(8,128)S(1)} %get-tuple-element.85), channel_id=1, source_target_pairs={{0,48},{16,0},{32,16},{48,32},{64,112},{80,64},{96,80},{112,96},{1... | collective-permute-start | bytes 196616 | tf_op jit(solution)/shard_map/ppermute | solution.py:47
  616.4 9.5 %collective-permute-start.63 = (f32[64,4,64]{2,0,1:T(8,128)S(1)}, f32[64,4,64]{2,0,1:T(8,128)S(1)}, u32[]{:S(2)}, u32[]{:S(2)}) collective-permute-start(f32[64,4,64]{2,0,1:T(8,128)S(1)} %get-tuple-element.84), channel_id=1, source_target_pairs={{0,32},{16,48},{32,0},{48,16},{64,96},{80,112},{96,64},{112,80},{1... | collective-permute-start | bytes 196616 | tf_op jit(solution)/shard_map/ppermute | solution.py:47
  616.4 9.5 %collective-permute-start.64 = (f32[64,4,64]{2,0,1:T(8,128)S(1)}, f32[64,4,64]{2,0,1:T(8,128)S(1)}, u32[]{:S(2)}, u32[]{:S(2)}) collective-permute-start(f32[64,4,64]{2,0,1:T(8,128)S(1)} %get-tuple-element.17), channel_id=1, source_target_pairs={{0,16},{16,32},{32,48},{48,0},{64,80},{80,96},{96,112},{112,64},{1... | collective-permute-start | bytes 196616 | tf_op jit(solution)/shard_map/ppermute | solution.py:47
  626.0 10.8 %collective-permute-start.65 = (f32[64,4,64]{2,0,1:T(8,128)S(1)}, f32[64,4,64]{2,0,1:T(8,128)S(1)}, u32[]{:S(2)}, u32[]{:S(2)}) collective-permute-start(f32[64,4,64]{2,0,1:T(8,128)S(1)} %get-tuple-element.66), channel_id=1, source_target_pairs={{0,192},{16,208},{32,224},{48,240},{64,0},{80,16},{96,32},{112,48}... | collective-permute-start | bytes 196616 | tf_op jit(solution)/shard_map/ppermute | solution.py:57
  632.8 11.4 %collective-permute-start.66 = (f32[64,4,64]{2,0,1:T(8,128)S(1)}, f32[64,4,64]{2,0,1:T(8,128)S(1)}, u32[]{:S(2)}, u32[]{:S(2)}) collective-permute-start(f32[64,4,64]{2,0,1:T(8,128)S(1)} %get-tuple-element.65), channel_id=1, source_target_pairs={{0,128},{16,144},{32,160},{48,176},{64,192},{80,208},{96,224},{112... | collective-permute-start | bytes 196616 | tf_op jit(solution)/shard_map/ppermute | solution.py:57
  632.8 11.4 %collective-permute-start.67 = (f32[64,4,64]{2,0,1:T(8,128)S(1)}, f32[64,4,64]{2,0,1:T(8,128)S(1)}, u32[]{:S(2)}, u32[]{:S(2)}) collective-permute-start(f32[64,4,64]{2,0,1:T(8,128)S(1)} %get-tuple-element.64), channel_id=1, source_target_pairs={{0,64},{16,80},{32,96},{48,112},{64,128},{80,144},{96,160},{112,17... | collective-permute-start | bytes 196616 | tf_op jit(solution)/shard_map/ppermute | solution.py:57
  (22 other events, 364.8 us)

commit v9 on v7

--- a/solution.py
+++ b/solution.py
@@ -171,11 +171,11 @@
     share = jnp.transpose(estimate[0].reshape(side, estimate.shape[2] // side, side), (2, 1, 0))
     share = route(share, place, my_brick, nsp)
     recorded = jnp.transpose(measured[0, 0].reshape(side, side, side), (2, 1, 0))
-    half = side // 2
+    chunk = side // 4
     recorded = jnp.concatenate(
         [
-            route(recorded[:half], place, my_brick, nsp),
-            route(recorded[half:], place, my_brick, nsp, columns_first=True),
+            route(recorded[c * chunk:(c + 1) * chunk], place, my_brick, nsp, columns_first=c % 2 == 1)
+            for c in range(4)
         ],
         axis=0,
     )

time: 647 us -> 643 us (level)
  waiting for transfers between devices: 289 us -> 303 us
  other arithmetic: 74.4 us -> 66.6 us
    ppermute x24 -> x36, starting transfers between devices: 37.5 us -> 59.1 us  [route(): part = lax.ppermute(part, 'space', pairs)]
    ppermute x8, starting transfers between devices: 21.5 us -> 4.98 us  [view_reduce_scatter(): x = keep + lax.ppermute(send, 'view', xor_pairs(nv, m))]
    ppermute x8, waiting for transfers between devices: 52.3 us -> 64.7 us  [view_reduce_scatter(): x = keep + lax.ppermute(send, 'view', xor_pairs(nv, m))]
    ppermute x24 -> x36, waiting for transfers between devices: 171 us -> 159 us  [route(): part = lax.ppermute(part, 'space', pairs)]
    ppermute x8, starting transfers between devices: 22.4 us -> 14.8 us  [view_all_gather(): recv = lax.ppermute(x, 'view', xor_pairs(nv, m))]
  transfers between devices with their start and end apart: 60 -> 72, of which waited for: 41 -> 44; matrix products, arithmetic and copies ran while one was open for 13% -> 13% of each run, Pallas kernels for 0% -> 0%
where the time goes in v9:
time: 643 us; the launch traced here: 637 us
  waiting for transfers between devices  303 us (47%)
  starting transfers between devices  122 us (19%)
  other arithmetic  66.6 us (10%)
  local copies, waits for them, and re-layouts  54.4 us (8%)
  matrix products  52.8 us (8%)
  between operations  38.6 us (6%)
    ppermute x36, waiting for transfers between devices, route(): part = lax.ppermute(part, 'space', pairs)  159 us
    ppermute x8, waiting for transfers between devices, view_reduce_scatter(): x = keep + lax.ppermute(send, 'view', xor_pairs(nv, m))  64.7 us
    ppermute x36, starting transfers between devices, route(): part = lax.ppermute(part, 'space', pairs)  59.1 us
    ppermute x8, waiting for transfers between devices, view_all_gather(): recv = lax.ppermute(x, 'view', xor_pairs(nv, m))  27.2 us
    ppermute x8, waiting for transfers between devices, pair_halo(): recv = lax.ppermute(send, 'space', [(i, i ^ partner) for i in range(nsp)])  19.9 us
    select_n x3, other arithmetic, band_matrix(): band = jnp.where(offset == position, weight, band)  19.8 us
    dot_general x4, matrix products, convolve(): return jnp.einsum('abt,ot->abo', extended, band, precision=hi)  19.3 us
    dot_general x4, matrix products, convolve(): return jnp.einsum('ot,tab->oab', band, extended, precision=hi)  18.7 us
  transfers between devices with their start and end apart: 72, of which 44 were waited for; matrix products, arithmetic and copies ran while one was open for 13% of the time, Pallas kernels for 0%

profile of v9, /device:TPU:8, one launch (start us, length us, event | category | flops | bytes accessed | tf_op | source)
XLA Modules:
  0.0 636.6 jit_solution(10525845777627409702)
XLA Ops:
  12.7 4.9 select_select_fusion.30
  17.6 4.9 select_select_fusion.28
  25.4 4.3 collective-permute-done.1
  29.9 3.4 collective-permute-done.2
  34.8 3.0 collective-permute-done.3
  55.4 4.3 collective-permute-start.7
  67.2 6.9 %collective-permute-start.34 = (f32[64,4,64]{2,0,1:T(8,128)S(1)}, f32[64,4,64]{2,0,1:T(8,128)S(1)}, u32[]{:S(2)}, u32[]{:S(2)}) collective-permute-start(f32[64,4,64]{2,0,1:T(8,128)S(1)} %select_select_fusion.20), channel_id=1, source_target_pairs={{0,2},{1,3},{2,0},{3,1},{4,6},{5,7},{6,4},{7,5},{8,10},{9,11},{10,... | collective-permute-start | bytes 196616 | tf_op jit(solution)/shard_map/ppermute | solution.py:134
  74.1 9.9 %select_select_fusion.32 = (f32[64,78]{1,0:T(8,128)}, f32[64,78]{1,0:T(8,128)}) fusion(f32[]{:T(128)} %bitcast.47, f32[]{:T(128)} %bitcast.46, f32[]{:T(128)} %bitcast.45, f32[]{:T(128)} %bitcast.44, f32[]{:T(128)} %bitcast.43, f32[]{:T(128)} %bitcast.42, f32[]{:T(128)} %bitcast.41, f32[]{:T(128)} %bitcast.40, f32[]{:T(128)} %bitcast.39, f32[]{:T(128)} %bitcast.38, ...), kind=kLoop, calls=%fused_computation.197 | loop fusion | flops 229632 | bytes 39996 | tf_op jit(solution)/shard_map/jit(_where)/select_n | solution.py:68
  85.5 3.0 collective-permute-start.35
  108.4 13.4 %collective-permute-done.22 = f32[16,64,64]{2,0,1:T(8,128)S(1)} collective-permute-done((f32[16,64,64]{2,0,1:T(8,128)}, f32[16,64,64]{2,0,1:T(8,128)S(1)}, u32[]{:S(2)}, u32[]{:S(2)}) %collective-permute-start.22) | collective-permute-done | bytes 262176 | tf_op jit(solution)/shard_map/ppermute | solution.py:47
  121.8 3.3 collective-permute-done.23
  131.2 12.6 %collective-permute-done.25 = f32[16,64,64]{2,0,1:T(8,128)S(1)} collective-permute-done((f32[16,64,64]{2,0,1:T(8,128)S(1)}, f32[16,64,64]{2,0,1:T(8,128)S(1)}, u32[]{:S(2)}, u32[]{:S(2)}) %collective-permute-start.25) | collective-permute-done | bytes 262176 | tf_op jit(solution)/shard_map/ppermute | solution.py:57
  146.2 29.8 %collective-permute-done.26 = f32[16,64,64]{2,0,1:T(8,128)S(1)} collective-permute-done((f32[16,64,64]{2,0,1:T(8,128)S(1)}, f32[16,64,64]{2,0,1:T(8,128)S(1)}, u32[]{:S(2)}, u32[]{:S(2)}) %collective-permute-start.26) | collective-permute-done | bytes 262176 | tf_op jit(solution)/shard_map/ppermute | solution.py:57
  181.8 2.7 fusion.112
  191.6 2.7 select_select_fusion.13
  194.2 10.4 %collective-permute-start.13 = (f32[16,64,64]{2,0,1:T(8,128)}, f32[16,64,64]{2,0,1:T(8,128)}, u32[]{:S(2)}, u32[]{:S(2)}) collective-permute-start(f32[16,64,64]{2,0,1:T(8,128)} %get-tuple-element.21), channel_id=1, source_target_pairs={{0,192},{16,208},{32,224},{48,240},{64,0},{80,16},{96,32},{112,48}... | collective-permute-start | bytes 786440 | tf_op jit(solution)/shard_map/ppermute | solution.py:57
  212.7 5.0 fusion.28
  218.3 3.4 collective-permute-start.28
  221.7 34.1 %collective-permute-done.14 = f32[16,64,64]{2,0,1:T(8,128)} collective-permute-done((f32[16,64,64]{2,0,1:T(8,128)}, f32[16,64,64]{2,0,1:T(8,128)}, u32[]{:S(2)}, u32[]{:S(2)}) %collective-permute-start.14) | collective-permute-done | bytes 262176 | tf_op jit(solution)/shard_map/ppermute | solution.py:57
  261.9 4.0 fusion.43
  266.0 3.2 collective-permute-start.29
  269.2 3.3 collective-permute-start.40
  272.5 28.7 %collective-permute-done.17 = f32[16,64,64]{2,0,1:T(8,128)S(1)} collective-permute-done((f32[16,64,64]{2,0,1:T(8,128)S(1)}, f32[16,64,64]{2,0,1:T(8,128)S(1)}, u32[]{:S(2)}, u32[]{:S(2)}) %collective-permute-start.17) | collective-permute-done | bytes 262176 | tf_op jit(solution)/shard_map/ppermute | solution.py:47
  304.7 3.8 collective-permute-start.20
  308.5 4.0 collective-permute-done.29
  312.5 3.2 collective-permute-start.21
  320.8 4.4 copy.226
  326.2 6.7 %collective-permute-done.20 = f32[16,64,64]{2,0,1:T(8,128)} collective-permute-done((f32[16,64,64]{2,0,1:T(8,128)}, f32[16,64,64]{2,0,1:T(8,128)}, u32[]{:S(2)}, u32[]{:S(2)}) %collective-permute-start.20) | collective-permute-done | bytes 262176 | tf_op jit(solution)/shard_map/ppermute | solution.py:57
  332.9 6.2 collective-permute-done.21
  339.5 2.7 collective-permute-done.31
  342.2 9.8 %collective-permute-done.32 = f32[16,64,64]{2,0,1:T(8,128)} collective-permute-done((f32[16,64,64]{2,0,1:T(8,128)}, f32[16,64,64]{2,0,1:T(8,128)}, u32[]{:S(2)}, u32[]{:S(2)}) %collective-permute-start.32) | collective-permute-done | bytes 262176 | tf_op jit(solution)/shard_map/ppermute | solution.py:57
  353.1 6.1 convolution_divide_fusion.1
  359.2 5.4 collective-permute-start.42
  366.3 3.0 collective-permute-done.42
  369.3 4.1 collective-permute-done.43
  378.9 2.9 collective-permute-done.44
  382.8 3.3 copy.258
  386.1 3.5 convolution_bitcast_fusion.1
  390.3 4.8 collective-permute-start.45
  399.2 4.8 fusion.26
  410.5 13.4 %collective-permute-done.47 = f32[64,2,2,4,64]{4,0,3,2,1:T(8,128)S(1)} collective-permute-done((f32[64,2,2,4,64]{4,0,3,2,1:T(8,128)S(1)}, f32[64,2,2,4,64]{4,0,3,2,1:T(8,128)S(1)}, u32[]{:S(2)}, u32[]{:S(2)}) %collective-permute-start.47) | collective-permute-done | bytes 262176 | tf_op jit(solution)/shard_map/ppermute | solution.py:124
  424.9 8.2 %collective-permute-done.48 = f32[64,2,4,64]{3,0,2,1:T(8,128)S(1)} collective-permute-done((f32[64,2,4,64]{3,0,2,1:T(8,128)S(1)}, f32[64,2,4,64]{3,0,2,1:T(8,128)S(1)}, u32[]{:S(2)}, u32[]{:S(2)}) %collective-permute-start.48) | collective-permute-done | bytes 131104 | tf_op jit(solution)/shard_map/ppermute | solution.py:124
  434.0 8.2 %collective-permute-done.49 = f32[64,4,64]{2,0,1:T(8,128)S(1)} collective-permute-done((f32[64,4,64]{2,0,1:T(8,128)S(1)}, f32[64,4,64]{2,0,1:T(8,128)S(1)}, u32[]{:S(2)}, u32[]{:S(2)}) %collective-permute-start.49) | collective-permute-done | bytes 65568 | tf_op jit(solution)/shard_map/ppermute | solution.py:124
  444.6 7.2 %collective-permute-done.50 = f32[64,4,64]{2,0,1:T(8,128)S(1)} collective-permute-done((f32[64,4,64]{2,0,1:T(8,128)S(1)}, f32[64,4,64]{2,0,1:T(8,128)S(1)}, u32[]{:S(2)}, u32[]{:S(2)}) %collective-permute-start.50) | collective-permute-done | bytes 65568 | tf_op jit(solution)/shard_map/ppermute | solution.py:134
  453.1 6.8 %collective-permute-done.51 = f32[64,2,4,64]{3,0,2,1:T(8,128)S(1)} collective-permute-done((f32[64,2,4,64]{3,0,2,1:T(8,128)S(1)}, f32[64,2,4,64]{3,0,2,1:T(8,128)S(1)}, u32[]{:S(2)}, u32[]{:S(2)}) %collective-permute-start.51) | collective-permute-done | bytes 131104 | tf_op jit(solution)/shard_map/ppermute | solution.py:134
  460.9 10.6 %collective-permute-done.52 = f32[64,2,2,4,64]{4,0,3,2,1:T(8,128)S(1)} collective-permute-done((f32[64,2,2,4,64]{4,0,3,2,1:T(8,128)S(1)}, f32[64,2,2,4,64]{4,0,3,2,1:T(8,128)S(1)}, u32[]{:S(2)}, u32[]{:S(2)}) %collective-permute-start.52) | collective-permute-done | bytes 262176 | tf_op jit(solution)/shard_map/ppermute | solution.py:134
  475.4 2.8 fusion.107
  494.1 4.7 fusion.34
  500.0 5.0 collective-permute-done.55
  505.7 4.0 fusion.40
  515.6 4.2 collective-permute-done.57
  520.1 3.3 copy.244
  523.4 8.1 %convolution_divide_fusion = f32[64,64,64]{2,0,1:T(8,128)S(1)} fusion(f32[78,64,64]{0,2,1:T(8,128)} %copy.244, f32[16,64,64]{2,0,1:T(8,128)} %copy-done.21, f32[16,64,64]{2,0,1:T(8,128)S(1)} %copy-done.16, f32[16,64,64]{2,0,1:T(8,128)} %copy-done.20, f32[16,64,64]{2,0,1:T(8,128)} %get-tuple-element.49, f32[64,78]{1,0:T(8,128)S(1)} %copy-done.28), kind=kOutput, calls=%fused_computation.55 | convolution fusion | flops 246415360 | bytes 3395072 | tf_op jit(solution)/shard_map/ot,tab->oab/dot_general | solution.py:75
  531.5 3.4 collective-permute-start.58
  538.8 4.4 collective-permute-done.59
  547.0 4.4 collective-permute-done.60
  552.4 3.3 copy.262
  555.7 3.5 convolution_bitcast_fusion
  559.9 4.2 collective-permute-start.61
  567.7 4.8 fusion.24
  579.3 13.3 %collective-permute-done.63 = f32[64,2,2,4,64]{4,0,3,2,1:T(8,128)S(1)} collective-permute-done((f32[64,2,2,4,64]{4,0,3,2,1:T(8,128)S(1)}, f32[64,2,2,4,64]{4,0,3,2,1:T(8,128)S(1)}, u32[]{:S(2)}, u32[]{:S(2)}) %collective-permute-start.63) | collective-permute-done | bytes 262176 | tf_op jit(solution)/shard_map/ppermute | solution.py:124
  594.0 7.8 %collective-permute-done.64 = f32[64,2,4,64]{3,0,2,1:T(8,128)S(1)} collective-permute-done((f32[64,2,4,64]{3,0,2,1:T(8,128)S(1)}, f32[64,2,4,64]{3,0,2,1:T(8,128)S(1)}, u32[]{:S(2)}, u32[]{:S(2)}) %collective-permute-start.64) | collective-permute-done | bytes 131104 | tf_op jit(solution)/shard_map/ppermute | solution.py:124
  602.6 8.5 %collective-permute-done.65 = f32[64,4,64]{2,0,1:T(8,128)S(1)} collective-permute-done((f32[64,4,64]{2,0,1:T(8,128)S(1)}, f32[64,4,64]{2,0,1:T(8,128)S(1)}, u32[]{:S(2)}, u32[]{:S(2)}) %collective-permute-start.65) | collective-permute-done | bytes 65568 | tf_op jit(solution)/shard_map/ppermute | solution.py:124
  631.0 4.6 collective-permute-done.70
  (289 shorter events, 169.4 us)
Async XLA Ops:
  1.5 22.9 %collective-permute-start = (s32[16,7]{0,1:T(8,128)S(1)}, s32[16,7]{0,1:T(8,128)S(1)}, u32[]{:S(2)}, u32[]{:S(2)}) collective-permute-start(s32[16,7]{0,1:T(8,128)S(1)} %broadcast_select_fusion.24), channel_id=1, source_target_pairs={{0,16},{16,0},{32,48},{48,32},{64,80},{80,64},{96,112},{112,96},{1... | collective-permute-start | bytes 1352 | tf_op jit(solution)/shard_map/ppermute | solution.py:23
  44.8 10.5 %collective-permute-start.4 = (f32[64,4,64]{2,0,1:T(8,128)S(1)}, f32[64,4,64]{2,0,1:T(8,128)S(1)}, u32[]{:S(2)}, u32[]{:S(2)}) collective-permute-start(f32[64,4,64]{2,0,1:T(8,128)S(1)} %bitcast.257), channel_id=1, source_target_pairs={{0,48},{16,0},{32,16},{48,32},{64,112},{80,64},{96,80},{112,96},{1... | collective-permute-start | bytes 196616 | tf_op jit(solution)/shard_map/ppermute | solution.py:47
  45.2 10.1 %collective-permute-start.5 = (f32[64,4,64]{2,0,1:T(8,128)S(1)}, f32[64,4,64]{2,0,1:T(8,128)S(1)}, u32[]{:S(2)}, u32[]{:S(2)}) collective-permute-start(f32[64,4,64]{2,0,1:T(8,128)S(1)} %bitcast.258), channel_id=1, source_target_pairs={{0,32},{16,48},{32,0},{48,16},{64,96},{80,112},{96,64},{112,80},{1... | collective-permute-start | bytes 196616 | tf_op jit(solution)/shard_map/ppermute | solution.py:47
  47.6 7.7 %collective-permute-start.6 = (f32[64,4,64]{2,0,1:T(8,128)S(1)}, f32[64,4,64]{2,0,1:T(8,128)S(1)}, u32[]{:S(2)}, u32[]{:S(2)}) collective-permute-start(f32[64,4,64]{2,0,1:T(8,128)S(1)} %bitcast.259), channel_id=1, source_target_pairs={{0,16},{16,32},{32,48},{48,0},{64,80},{80,96},{96,112},{112,64},{1... | collective-permute-start | bytes 196616 | tf_op jit(solution)/shard_map/ppermute | solution.py:47
  55.4 10.8 %collective-permute-start.7 = (f32[64,4,64]{2,0,1:T(8,128)S(1)}, f32[64,4,64]{2,0,1:T(8,128)S(1)}, u32[]{:S(2)}, u32[]{:S(2)}) collective-permute-start(f32[64,4,64]{2,0,1:T(8,128)S(1)} %get-tuple-element.82), channel_id=1, source_target_pairs={{0,192},{16,208},{32,224},{48,240},{64,0},{80,16},{96,32},{112,48}... | collective-permute-start | bytes 196616 | tf_op jit(solution)/shard_map/ppermute | solution.py:57
  59.7 7.4 %collective-permute-start.8 = (f32[64,4,64]{2,0,1:T(8,128)S(1)}, f32[64,4,64]{2,0,1:T(8,128)S(1)}, u32[]{:S(2)}, u32[]{:S(2)}) collective-permute-start(f32[64,4,64]{2,0,1:T(8,128)S(1)} %get-tuple-element.81), channel_id=1, source_target_pairs={{0,128},{16,144},{32,160},{48,176},{64,192},{80,208},{96,224},{112... | collective-permute-start | bytes 196616 | tf_op jit(solution)/shard_map/ppermute | solution.py:57
  59.8 7.4 %collective-permute-start.9 = (f32[64,4,64]{2,0,1:T(8,128)S(1)}, f32[64,4,64]{2,0,1:T(8,128)S(1)}, u32[]{:S(2)}, u32[]{:S(2)}) collective-permute-start(f32[64,4,64]{2,0,1:T(8,128)S(1)} %get-tuple-element.80), channel_id=1, source_target_pairs={{0,64},{16,80},{32,96},{48,112},{64,128},{80,144},{96,160},{112,17... | collective-permute-start | bytes 196616 | tf_op jit(solution)/shard_map/ppermute | solution.py:57
  67.2 17.6 %collective-permute-start.34 = (f32[64,4,64]{2,0,1:T(8,128)S(1)}, f32[64,4,64]{2,0,1:T(8,128)S(1)}, u32[]{:S(2)}, u32[]{:S(2)}) collective-permute-start(f32[64,4,64]{2,0,1:T(8,128)S(1)} %select_select_fusion.20), channel_id=1, source_target_pairs={{0,2},{1,3},{2,0},{3,1},{4,6},{5,7},{6,4},{7,5},{8,10},{9,11},{10,... | collective-permute-start | bytes 196616 | tf_op jit(solution)/shard_map/ppermute | solution.py:134
  85.5 21.1 %collective-permute-start.35 = (f32[64,2,4,64]{3,0,2,1:T(8,128)}, f32[64,2,4,64]{3,0,2,1:T(8,128)}, u32[]{:S(2)}, u32[]{:S(2)}) collective-permute-start(f32[64,2,4,64]{3,0,2,1:T(8,128)} %pad_maximum_fusion.13), channel_id=1, source_target_pairs={{0,8},{1,9},{2,10},{3,11},{4,12},{5,13},{6,14},{7,15},{8,0},{9,1},... | collective-permute-start | bytes 393224 | tf_op jit(solution)/shard_map/ppermute | solution.py:134
  101.5 20.3 %collective-permute-start.22 = (f32[16,64,64]{2,0,1:T(8,128)}, f32[16,64,64]{2,0,1:T(8,128)S(1)}, u32[]{:S(2)}, u32[]{:S(2)}) collective-permute-start(f32[16,64,64]{2,0,1:T(8,128)} %get-tuple-element.60), channel_id=1, source_target_pairs={{0,48},{16,0},{32,16},{48,32},{64,112},{80,64},{96,80},{112,96},{1... | collective-permute-start | bytes 786440 | tf_op jit(solution)/shard_map/ppermute | solution.py:47
  102.3 22.8 %collective-permute-start.23 = (f32[16,64,64]{2,0,1:T(8,128)}, f32[16,64,64]{2,0,1:T(8,128)S(1)}, u32[]{:S(2)}, u32[]{:S(2)}) collective-permute-start(f32[16,64,64]{2,0,1:T(8,128)} %get-tuple-element.56), channel_id=1, source_target_pairs={{0,32},{16,48},{32,0},{48,16},{64,96},{80,112},{96,64},{112,80},{1... | collective-permute-start | bytes 786440 | tf_op jit(solution)/shard_map/ppermute | solution.py:47
  103.5 21.6 %collective-permute-start.24 = (f32[16,64,64]{2,0,1:T(8,128)}, f32[16,64,64]{2,0,1:T(8,128)}, u32[]{:S(2)}, u32[]{:S(2)}) collective-permute-start(f32[16,64,64]{2,0,1:T(8,128)} %get-tuple-element.57), channel_id=1, source_target_pairs={{0,16},{16,32},{32,48},{48,0},{64,80},{80,96},{96,112},{112,64},{1... | collective-permute-start | bytes 786440 | tf_op jit(solution)/shard_map/ppermute | solution.py:47
  105.9 84.8 %collective-permute-start.10 = (f32[16,64,64]{2,0,1:T(8,128)}, f32[16,64,64]{2,0,1:T(8,128)}, u32[]{:S(2)}, u32[]{:S(2)}) collective-permute-start(f32[16,64,64]{2,0,1:T(8,128)} %get-tuple-element.62), channel_id=1, source_target_pairs={{0,48},{16,0},{32,16},{48,32},{64,112},{80,64},{96,80},{112,96},{1... | collective-permute-start | bytes 786440 | tf_op jit(solution)/shard_map/ppermute | solution.py:47
  107.7 22.4 %collective-permute-start.36 = (f32[64,2,2,4,64]{4,0,3,2,1:T(8,128)S(1)}, f32[64,2,2,4,64]{4,0,3,2,1:T(8,128)S(1)}, u32[]{:S(2)}, u32[]{:S(2)}) collective-permute-start(f32[64,2,2,4,64]{4,0,3,2,1:T(8,128)S(1)} %pad_maximum_fusion.11), channel_id=1, source_target_pairs={{0,4},{1,5},{2,6},{3,7},{4,0},{5,1},{6,2},{7,3},{8,12},{9,13},{10,... | collective-permute-start | bytes 786440 | tf_op jit(solution)/shard_map/ppermute | solution.py:134
  126.6 17.2 %collective-permute-start.25 = (f32[16,64,64]{2,0,1:T(8,128)S(1)}, f32[16,64,64]{2,0,1:T(8,128)S(1)}, u32[]{:S(2)}, u32[]{:S(2)}) collective-permute-start(f32[16,64,64]{2,0,1:T(8,128)S(1)} %get-tuple-element.27), channel_id=1, source_target_pairs={{0,192},{16,208},{32,224},{48,240},{64,0},{80,16},{96,32},{112,48}... | collective-permute-start | bytes 786440 | tf_op jit(solution)/shard_map/ppermute | solution.py:57
  128.4 47.7 %collective-permute-start.26 = (f32[16,64,64]{2,0,1:T(8,128)S(1)}, f32[16,64,64]{2,0,1:T(8,128)S(1)}, u32[]{:S(2)}, u32[]{:S(2)}) collective-permute-start(f32[16,64,64]{2,0,1:T(8,128)S(1)} %get-tuple-element.26), channel_id=1, source_target_pairs={{0,128},{16,144},{32,160},{48,176},{64,192},{80,208},{96,224},{112... | collective-permute-start | bytes 786440 | tf_op jit(solution)/shard_map/ppermute | solution.py:57
  129.0 47.1 %collective-permute-start.27 = (f32[16,64,64]{2,0,1:T(8,128)S(1)}, f32[16,64,64]{2,0,1:T(8,128)S(1)}, u32[]{:S(2)}, u32[]{:S(2)}) collective-permute-start(f32[16,64,64]{2,0,1:T(8,128)S(1)} %get-tuple-element.25), channel_id=1, source_target_pairs={{0,64},{16,80},{32,96},{48,112},{64,128},{80,144},{96,160},{112,17... | collective-permute-start | bytes 786440 | tf_op jit(solution)/shard_map/ppermute | solution.py:57
  130.4 49.2 %collective-permute-start.37 = (f32[64,2,2,2,4,64]{5,0,4,3,2,1:T(8,128)S(1)}, f32[64,2,2,2,4,64]{5,0,4,3,2,1:T(8,128)S(1)}, u32[]{:S(2)}, u32[]{:S(2)}) collective-permute-start(f32[64,2,2,2,4,64]{5,0,4,3,2,1:T(8,128)S(1)} %pad_maximum_fusion.9), channel_id=1, source_target_pairs={{0,1},{1,0},{2,3},{3,2},{4,5},{5,4},{6,7},{7,6},{8,9},{9,8},{10,11... | collective-permute-start | bytes 1572872 | tf_op jit(solution)/shard_map/ppermute | solution.py:134
  143.8 47.8 %collective-permute-start.11 = (f32[16,64,64]{2,0,1:T(8,128)}, f32[16,64,64]{2,0,1:T(8,128)}, u32[]{:S(2)}, u32[]{:S(2)}) collective-permute-start(f32[16,64,64]{2,0,1:T(8,128)} %get-tuple-element.54), channel_id=1, source_target_pairs={{0,32},{16,48},{32,0},{48,16},{64,96},{80,112},{96,64},{112,80},{1... | collective-permute-start | bytes 786440 | tf_op jit(solution)/shard_map/ppermute | solution.py:47
  176.1 89.9 %collective-permute-start.16 = (f32[16,64,64]{2,0,1:T(8,128)}, f32[16,64,64]{2,0,1:T(8,128)S(1)}, u32[]{:S(2)}, u32[]{:S(2)}) collective-permute-start(f32[16,64,64]{2,0,1:T(8,128)} %get-tuple-element.61), channel_id=1, source_target_pairs={{0,192},{64,0},{128,64},{192,128},{16,208},{80,16},{144,80},{208,1... | collective-permute-start | bytes 786440 | tf_op jit(solution)/shard_map/ppermute | solution.py:47
  176.1 93.1 %collective-permute-start.18 = (f32[16,64,64]{2,0,1:T(8,128)}, f32[16,64,64]{2,0,1:T(8,128)S(1)}, u32[]{:S(2)}, u32[]{:S(2)}) collective-permute-start(f32[16,64,64]{2,0,1:T(8,128)} %get-tuple-element.55), channel_id=1, source_target_pairs={{0,64},{64,128},{128,192},{192,0},{16,80},{80,144},{144,208},{208,... | collective-permute-start | bytes 786440 | tf_op jit(solution)/shard_map/ppermute | solution.py:47
  179.6 12.0 %collective-permute-start.12 = (f32[16,64,64]{2,0,1:T(8,128)}, f32[16,64,64]{2,0,1:T(8,128)}, u32[]{:S(2)}, u32[]{:S(2)}) collective-permute-start(f32[16,64,64]{2,0,1:T(8,128)} %get-tuple-element.52), channel_id=1, source_target_pairs={{0,16},{16,32},{32,48},{48,0},{64,80},{80,96},{96,112},{112,64},{1... | collective-permute-start | bytes 786440 | tf_op jit(solution)/shard_map/ppermute | solution.py:47
  190.7 16.5 %collective-permute-start.38 = (f32[64,64,3]{1,0,2:T(8,128)S(1)}, f32[64,64,3]{1,0,2:T(8,128)S(1)}, u32[]{:S(2)}, u32[]{:S(2)}) collective-permute-start(f32[64,64,3]{1,0,2:T(8,128)S(1)} %broadcast_select_fusion.20), channel_id=1, source_target_pairs={{0,16},{16,0},{32,48},{48,32},{64,80},{80,64},{96,112},{112,96},{1... | collective-permute-start | bytes 147464 | tf_op jit(solution)/shard_map/ppermute | solution.py:87
  194.2 24.1 %collective-permute-start.13 = (f32[16,64,64]{2,0,1:T(8,128)}, f32[16,64,64]{2,0,1:T(8,128)}, u32[]{:S(2)}, u32[]{:S(2)}) collective-permute-start(f32[16,64,64]{2,0,1:T(8,128)} %get-tuple-element.21), channel_id=1, source_target_pairs={{0,192},{16,208},{32,224},{48,240},{64,0},{80,16},{96,32},{112,48}... | collective-permute-start | bytes 786440 | tf_op jit(solution)/shard_map/ppermute | solution.py:57
  204.7 51.2 %collective-permute-start.14 = (f32[16,64,64]{2,0,1:T(8,128)}, f32[16,64,64]{2,0,1:T(8,128)}, u32[]{:S(2)}, u32[]{:S(2)}) collective-permute-start(f32[16,64,64]{2,0,1:T(8,128)} %get-tuple-element.20), channel_id=1, source_target_pairs={{0,128},{16,144},{32,160},{48,176},{64,192},{80,208},{96,224},{112... | collective-permute-start | bytes 786440 | tf_op jit(solution)/shard_map/ppermute | solution.py:57
  207.2 48.6 %collective-permute-start.15 = (f32[16,64,64]{2,0,1:T(8,128)}, f32[16,64,64]{2,0,1:T(8,128)}, u32[]{:S(2)}, u32[]{:S(2)}) collective-permute-start(f32[16,64,64]{2,0,1:T(8,128)} %get-tuple-element.19), channel_id=1, source_target_pairs={{0,64},{16,80},{32,96},{48,112},{64,128},{80,144},{96,160},{112,17... | collective-permute-start | bytes 786440 | tf_op jit(solution)/shard_map/ppermute | solution.py:57
  218.3 85.5 %collective-permute-start.28 = (f32[16,64,64]{2,0,1:T(8,128)S(1)}, f32[16,64,64]{2,0,1:T(8,128)S(1)}, u32[]{:S(2)}, u32[]{:S(2)}) collective-permute-start(f32[16,64,64]{2,0,1:T(8,128)S(1)} %copy-done.19), channel_id=1, source_target_pairs={{0,192},{64,0},{128,64},{192,128},{16,208},{80,16},{144,80},{208,1... | collective-permute-start | bytes 786440 | tf_op jit(solution)/shard_map/ppermute | solution.py:47
  255.8 48.8 %collective-permute-start.30 = (f32[16,64,64]{2,0,1:T(8,128)S(1)}, f32[16,64,64]{2,0,1:T(8,128)S(1)}, u32[]{:S(2)}, u32[]{:S(2)}) collective-permute-start(f32[16,64,64]{2,0,1:T(8,128)S(1)} %copy-done.18), channel_id=1, source_target_pairs={{0,64},{64,128},{128,192},{192,0},{16,80},{80,144},{144,208},{208,... | collective-permute-start | bytes 786440 | tf_op jit(solution)/shard_map/ppermute | solution.py:47
  255.9 5.4 collective-permute-start.39
  261.2 40.0 %collective-permute-start.17 = (f32[16,64,64]{2,0,1:T(8,128)S(1)}, f32[16,64,64]{2,0,1:T(8,128)S(1)}, u32[]{:S(2)}, u32[]{:S(2)}) collective-permute-start(f32[16,64,64]{2,0,1:T(8,128)S(1)} %get-tuple-element.50), channel_id=1, source_target_pairs={{0,128},{64,192},{128,0},{192,64},{16,144},{80,208},{144,16},{208,... | collective-permute-start | bytes 786440 | tf_op jit(solution)/shard_map/ppermute | solution.py:47
  266.0 46.5 %collective-permute-start.29 = (f32[16,64,64]{2,0,1:T(8,128)S(1)}, f32[16,64,64]{2,0,1:T(8,128)S(1)}, u32[]{:S(2)}, u32[]{:S(2)}) collective-permute-start(f32[16,64,64]{2,0,1:T(8,128)S(1)} %get-tuple-element.51), channel_id=1, source_target_pairs={{0,128},{64,192},{128,0},{192,64},{16,144},{80,208},{144,16},{208,... | collective-permute-start | bytes 786440 | tf_op jit(solution)/shard_map/ppermute | solution.py:47
  269.2 47.8 %collective-permute-start.40 = (f32[7,64,64]{1,2,0:T(8,128)S(1)}, f32[7,64,64]{1,2,0:T(8,128)S(1)}, u32[]{:S(2)}, u32[]{:S(2)}) collective-permute-start(f32[7,64,64]{1,2,0:T(8,128)S(1)} %get-tuple-element.63), channel_id=1, source_target_pairs={{0,64},{16,80},{32,96},{48,112},{64,128},{80,144},{96,160},{112,17... | collective-permute-start | bytes 344072 | tf_op jit(solution)/shard_map/ppermute | solution.py:99
  301.2 15.9 %collective-permute-start.41 = (f32[7,64,64]{1,2,0:T(8,128)S(1)}, f32[7,64,64]{1,2,0:T(8,128)S(1)}, u32[]{:S(2)}, u32[]{:S(2)}) collective-permute-start(f32[7,64,64]{1,2,0:T(8,128)S(1)} %get-tuple-element.64), channel_id=1, source_target_pairs={{64,0},{80,16},{96,32},{112,48},{128,64},{144,80},{160,96},{176,11... | collective-permute-start | bytes 344072 | tf_op jit(solution)/shard_map/ppermute | solution.py:100
  303.8 22.3 %collective-permute-start.19 = (f32[16,64,64]{2,0,1:T(8,128)}, f32[16,64,64]{2,0,1:T(8,128)}, u32[]{:S(2)}, u32[]{:S(2)}) collective-permute-start(f32[16,64,64]{2,0,1:T(8,128)} %get-tuple-element.24), channel_id=1, source_target_pairs={{0,48},{64,112},{128,176},{192,240},{16,0},{80,64},{144,128},{208,... | collective-permute-start | bytes 786440 | tf_op jit(solution)/shard_map/ppermute | solution.py:57
  304.7 28.3 %collective-permute-start.20 = (f32[16,64,64]{2,0,1:T(8,128)}, f32[16,64,64]{2,0,1:T(8,128)}, u32[]{:S(2)}, u32[]{:S(2)}) collective-permute-start(f32[16,64,64]{2,0,1:T(8,128)} %get-tuple-element.23), channel_id=1, source_target_pairs={{0,32},{64,96},{128,160},{192,224},{16,48},{80,112},{144,176},{208... | collective-permute-start | bytes 786440 | tf_op jit(solution)/shard_map/ppermute | solution.py:57
  312.5 26.6 %collective-permute-start.21 = (f32[16,64,64]{2,0,1:T(8,128)}, f32[16,64,64]{2,0,1:T(8,128)}, u32[]{:S(2)}, u32[]{:S(2)}) collective-permute-start(f32[16,64,64]{2,0,1:T(8,128)} %get-tuple-element.22), channel_id=1, source_target_pairs={{0,16},{64,80},{128,144},{192,208},{16,32},{80,96},{144,160},{208,... | collective-permute-start | bytes 786440 | tf_op jit(solution)/shard_map/ppermute | solution.py:57
  317.0 25.1 %collective-permute-start.31 = (f32[16,64,64]{2,0,1:T(8,128)}, f32[16,64,64]{2,0,1:T(8,128)}, u32[]{:S(2)}, u32[]{:S(2)}) collective-permute-start(f32[16,64,64]{2,0,1:T(8,128)} %get-tuple-element.30), channel_id=1, source_target_pairs={{0,48},{64,112},{128,176},{192,240},{16,0},{80,64},{144,128},{208,... | collective-permute-start | bytes 786440 | tf_op jit(solution)/shard_map/ppermute | solution.py:57
  317.1 34.8 %collective-permute-start.32 = (f32[16,64,64]{2,0,1:T(8,128)}, f32[16,64,64]{2,0,1:T(8,128)}, u32[]{:S(2)}, u32[]{:S(2)}) collective-permute-start(f32[16,64,64]{2,0,1:T(8,128)} %get-tuple-element.29), channel_id=1, source_target_pairs={{0,32},{64,96},{128,160},{192,224},{16,48},{80,112},{144,176},{208... | collective-permute-start | bytes 786440 | tf_op jit(solution)/shard_map/ppermute | solution.py:57
  326.2 26.5 %collective-permute-start.33 = (f32[16,64,64]{2,0,1:T(8,128)}, f32[16,64,64]{2,0,1:T(8,128)S(1)}, u32[]{:S(2)}, u32[]{:S(2)}) collective-permute-start(f32[16,64,64]{2,0,1:T(8,128)} %get-tuple-element.28), channel_id=1, source_target_pairs={{0,16},{64,80},{128,144},{192,208},{16,32},{80,96},{144,160},{208,... | collective-permute-start | bytes 786440 | tf_op jit(solution)/shard_map/ppermute | solution.py:57
  359.2 10.1 %collective-permute-start.42 = (f32[7,64,64]{2,0,1:T(8,128)S(1)}, f32[7,64,64]{2,0,1:T(8,128)S(1)}, u32[]{:S(2)}, u32[]{:S(2)}) collective-permute-start(f32[7,64,64]{2,0,1:T(8,128)S(1)} %get-tuple-element.47), channel_id=1, source_target_pairs={{0,64},{16,80},{32,96},{48,112},{64,128},{80,144},{96,160},{112,17... | collective-permute-start | bytes 344072 | tf_op jit(solution)/shard_map/ppermute | solution.py:99
  364.6 8.8 %collective-permute-start.43 = (f32[7,64,64]{2,0,1:T(8,128)S(1)}, f32[7,64,64]{2,0,1:T(8,128)S(1)}, u32[]{:S(2)}, u32[]{:S(2)}) collective-permute-start(f32[7,64,64]{2,0,1:T(8,128)S(1)} %get-tuple-element.48), channel_id=1, source_target_pairs={{64,0},{80,16},{96,32},{112,48},{128,64},{144,80},{160,96},{176,11... | collective-permute-start | bytes 344072 | tf_op jit(solution)/shard_map/ppermute | solution.py:100
  376.4 5.4 collective-permute-start.44
  390.3 7.4 %collective-permute-start.45 = (f32[64,64,3]{1,0,2:T(8,128)S(1)}, f32[64,64,3]{1,0,2:T(8,128)S(1)}, u32[]{:S(2)}, u32[]{:S(2)}) collective-permute-start(f32[64,64,3]{1,0,2:T(8,128)S(1)} %slice_select_fusion.19), channel_id=1, source_target_pairs={{0,16},{16,0},{32,48},{48,32},{64,80},{80,64},{96,112},{112,96},{1... | collective-permute-start | bytes 147464 | tf_op jit(solution)/shard_map/ppermute | solution.py:87
  409.8 14.1 %collective-permute-start.47 = (f32[64,2,2,4,64]{4,0,3,2,1:T(8,128)S(1)}, f32[64,2,2,4,64]{4,0,3,2,1:T(8,128)S(1)}, u32[]{:S(2)}, u32[]{:S(2)}) collective-permute-start(f32[64,2,2,4,64]{4,0,3,2,1:T(8,128)S(1)} %select_bitcast_fusion.9), channel_id=1, source_target_pairs={{0,4},{1,5},{2,6},{3,7},{4,0},{5,1},{6,2},{7,3},{8,12},{9,13},{10,... | collective-permute-start | bytes 786440 | tf_op jit(solution)/shard_map/ppermute | solution.py:124
  424.0 9.1 %collective-permute-start.48 = (f32[64,2,4,64]{3,0,2,1:T(8,128)S(1)}, f32[64,2,4,64]{3,0,2,1:T(8,128)S(1)}, u32[]{:S(2)}, u32[]{:S(2)}) collective-permute-start(f32[64,2,4,64]{3,0,2,1:T(8,128)S(1)} %select_bitcast_fusion.15), channel_id=1, source_target_pairs={{0,8},{1,9},{2,10},{3,11},{4,12},{5,13},{6,14},{7,15},{8,0},{9,1},... | collective-permute-start | bytes 393224 | tf_op jit(solution)/shard_map/ppermute | solution.py:124
  433.2 9.0 %collective-permute-start.49 = (f32[64,4,64]{2,0,1:T(8,128)S(1)}, f32[64,4,64]{2,0,1:T(8,128)S(1)}, u32[]{:S(2)}, u32[]{:S(2)}) collective-permute-start(f32[64,4,64]{2,0,1:T(8,128)S(1)} %select_bitcast_fusion.21), channel_id=1, source_target_pairs={{0,2},{1,3},{2,0},{3,1},{4,6},{5,7},{6,4},{7,5},{8,10},{9,11},{10,... | collective-permute-start | bytes 196616 | tf_op jit(solution)/shard_map/ppermute | solution.py:124
  442.8 9.0 %collective-permute-start.50 = (f32[64,4,64]{2,0,1:T(8,128)S(1)}, f32[64,4,64]{2,0,1:T(8,128)S(1)}, u32[]{:S(2)}, u32[]{:S(2)}) collective-permute-start(f32[64,4,64]{2,0,1:T(8,128)S(1)} %fusion.51), channel_id=1, source_target_pairs={{0,2},{1,3},{2,0},{3,1},{4,6},{5,7},{6,4},{7,5},{8,10},{9,11},{10,... | collective-permute-start | bytes 196616 | tf_op jit(solution)/shard_map/ppermute | solution.py:134
  451.8 8.1 %collective-permute-start.51 = (f32[64,2,4,64]{3,0,2,1:T(8,128)S(1)}, f32[64,2,4,64]{3,0,2,1:T(8,128)S(1)}, u32[]{:S(2)}, u32[]{:S(2)}) collective-permute-start(f32[64,2,4,64]{3,0,2,1:T(8,128)S(1)} %pad_maximum_fusion.14), channel_id=1, source_target_pairs={{0,8},{1,9},{2,10},{3,11},{4,12},{5,13},{6,14},{7,15},{8,0},{9,1},... | collective-permute-start | bytes 393224 | tf_op jit(solution)/shard_map/ppermute | solution.py:134
  460.0 11.5 %collective-permute-start.52 = (f32[64,2,2,4,64]{4,0,3,2,1:T(8,128)S(1)}, f32[64,2,2,4,64]{4,0,3,2,1:T(8,128)S(1)}, u32[]{:S(2)}, u32[]{:S(2)}) collective-permute-start(f32[64,2,2,4,64]{4,0,3,2,1:T(8,128)S(1)} %pad_maximum_fusion.12), channel_id=1, source_target_pairs={{0,4},{1,5},{2,6},{3,7},{4,0},{5,1},{6,2},{7,3},{8,12},{9,13},{10,... | collective-permute-start | bytes 786440 | tf_op jit(solution)/shard_map/ppermute | solution.py:134
  499.5 5.5 collective-permute-start.55
  509.7 5.9 collective-permute-start.56
  511.9 7.9 %collective-permute-start.57 = (f32[7,64,64]{1,2,0:T(8,128)S(1)}, f32[7,64,64]{1,2,0:T(8,128)S(1)}, u32[]{:S(2)}, u32[]{:S(2)}) collective-permute-start(f32[7,64,64]{1,2,0:T(8,128)S(1)} %get-tuple-element.38), channel_id=1, source_target_pairs={{64,0},{80,16},{96,32},{112,48},{128,64},{144,80},{160,96},{176,11... | collective-permute-start | bytes 344072 | tf_op jit(solution)/shard_map/ppermute | solution.py:100
  531.5 7.3 %collective-permute-start.58 = (f32[7,64,64]{2,0,1:T(8,128)S(1)}, f32[7,64,64]{2,0,1:T(8,128)S(1)}, u32[]{:S(2)}, u32[]{:S(2)}) collective-permute-start(f32[7,64,64]{2,0,1:T(8,128)S(1)} %get-tuple-element.35), channel_id=1, source_target_pairs={{0,64},{16,80},{32,96},{48,112},{64,128},{80,144},{96,160},{112,17... | collective-permute-start | bytes 344072 | tf_op jit(solution)/shard_map/ppermute | solution.py:99
  535.0 8.3 %collective-permute-start.59 = (f32[7,64,64]{2,0,1:T(8,128)S(1)}, f32[7,64,64]{2,0,1:T(8,128)S(1)}, u32[]{:S(2)}, u32[]{:S(2)}) collective-permute-start(f32[7,64,64]{2,0,1:T(8,128)S(1)} %get-tuple-element.36), channel_id=1, source_target_pairs={{64,0},{80,16},{96,32},{112,48},{128,64},{144,80},{160,96},{176,11... | collective-permute-start | bytes 344072 | tf_op jit(solution)/shard_map/ppermute | solution.py:100
  559.9 6.8 %collective-permute-start.61 = (f32[64,64,3]{1,0,2:T(8,128)S(1)}, f32[64,64,3]{1,0,2:T(8,128)S(1)}, u32[]{:S(2)}, u32[]{:S(2)}) collective-permute-start(f32[64,64,3]{1,0,2:T(8,128)S(1)} %slice_select_fusion.18), channel_id=1, source_target_pairs={{0,16},{16,0},{32,48},{48,32},{64,80},{80,64},{96,112},{112,96},{1... | collective-permute-start | bytes 147464 | tf_op jit(solution)/shard_map/ppermute | solution.py:87
  578.5 14.1 %collective-permute-start.63 = (f32[64,2,2,4,64]{4,0,3,2,1:T(8,128)S(1)}, f32[64,2,2,4,64]{4,0,3,2,1:T(8,128)S(1)}, u32[]{:S(2)}, u32[]{:S(2)}) collective-permute-start(f32[64,2,2,4,64]{4,0,3,2,1:T(8,128)S(1)} %select_bitcast_fusion.6), channel_id=1, source_target_pairs={{0,4},{1,5},{2,6},{3,7},{4,0},{5,1},{6,2},{7,3},{8,12},{9,13},{10,... | collective-permute-start | bytes 786440 | tf_op jit(solution)/shard_map/ppermute | solution.py:124
  592.7 9.1 %collective-permute-start.64 = (f32[64,2,4,64]{3,0,2,1:T(8,128)S(1)}, f32[64,2,4,64]{3,0,2,1:T(8,128)S(1)}, u32[]{:S(2)}, u32[]{:S(2)}) collective-permute-start(f32[64,2,4,64]{3,0,2,1:T(8,128)S(1)} %select_bitcast_fusion.12), channel_id=1, source_target_pairs={{0,8},{1,9},{2,10},{3,11},{4,12},{5,13},{6,14},{7,15},{8,0},{9,1},... | collective-permute-start | bytes 393224 | tf_op jit(solution)/shard_map/ppermute | solution.py:124
  601.9 9.2 %collective-permute-start.65 = (f32[64,4,64]{2,0,1:T(8,128)S(1)}, f32[64,4,64]{2,0,1:T(8,128)S(1)}, u32[]{:S(2)}, u32[]{:S(2)}) collective-permute-start(f32[64,4,64]{2,0,1:T(8,128)S(1)} %select_bitcast_fusion.18), channel_id=1, source_target_pairs={{0,2},{1,3},{2,0},{3,1},{4,6},{5,7},{6,4},{7,5},{8,10},{9,11},{10,... | collective-permute-start | bytes 196616 | tf_op jit(solution)/shard_map/ppermute | solution.py:124
  611.9 11.3 %collective-permute-start.66 = (f32[64,4,64]{2,0,1:T(8,128)S(1)}, f32[64,4,64]{2,0,1:T(8,128)S(1)}, u32[]{:S(2)}, u32[]{:S(2)}) collective-permute-start(f32[64,4,64]{2,0,1:T(8,128)S(1)} %get-tuple-element.88), channel_id=1, source_target_pairs={{0,48},{16,0},{32,16},{48,32},{64,112},{80,64},{96,80},{112,96},{1... | collective-permute-start | bytes 196616 | tf_op jit(solution)/shard_map/ppermute | solution.py:47
  614.0 9.3 %collective-permute-start.67 = (f32[64,4,64]{2,0,1:T(8,128)S(1)}, f32[64,4,64]{2,0,1:T(8,128)S(1)}, u32[]{:S(2)}, u32[]{:S(2)}) collective-permute-start(f32[64,4,64]{2,0,1:T(8,128)S(1)} %get-tuple-element.87), channel_id=1, source_target_pairs={{0,32},{16,48},{32,0},{48,16},{64,96},{80,112},{96,64},{112,80},{1... | collective-permute-start | bytes 196616 | tf_op jit(solution)/shard_map/ppermute | solution.py:47
  614.0 9.3 %collective-permute-start.68 = (f32[64,4,64]{2,0,1:T(8,128)S(1)}, f32[64,4,64]{2,0,1:T(8,128)S(1)}, u32[]{:S(2)}, u32[]{:S(2)}) collective-permute-start(f32[64,4,64]{2,0,1:T(8,128)S(1)} %get-tuple-element.17), channel_id=1, source_target_pairs={{0,16},{16,32},{32,48},{48,0},{64,80},{80,96},{96,112},{112,64},{1... | collective-permute-start | bytes 196616 | tf_op jit(solution)/shard_map/ppermute | solution.py:47
  623.3 7.7 %collective-permute-start.69 = (f32[64,4,64]{2,0,1:T(8,128)S(1)}, f32[64,4,64]{2,0,1:T(8,128)S(1)}, u32[]{:S(2)}, u32[]{:S(2)}) collective-permute-start(f32[64,4,64]{2,0,1:T(8,128)S(1)} %get-tuple-element.75), channel_id=1, source_target_pairs={{0,192},{16,208},{32,224},{48,240},{64,0},{80,16},{96,32},{112,48}... | collective-permute-start | bytes 196616 | tf_op jit(solution)/shard_map/ppermute | solution.py:57
  625.0 10.6 %collective-permute-start.70 = (f32[64,4,64]{2,0,1:T(8,128)S(1)}, f32[64,4,64]{2,0,1:T(8,128)S(1)}, u32[]{:S(2)}, u32[]{:S(2)}) collective-permute-start(f32[64,4,64]{2,0,1:T(8,128)S(1)} %get-tuple-element.74), channel_id=1, source_target_pairs={{0,128},{16,144},{32,160},{48,176},{64,192},{80,208},{96,224},{112... | collective-permute-start | bytes 196616 | tf_op jit(solution)/shard_map/ppermute | solution.py:57
  626.0 9.5 %collective-permute-start.71 = (f32[64,4,64]{2,0,1:T(8,128)S(1)}, f32[64,4,64]{2,0,1:T(8,128)S(1)}, u32[]{:S(2)}, u32[]{:S(2)}) collective-permute-start(f32[64,4,64]{2,0,1:T(8,128)S(1)} %get-tuple-element.73), channel_id=1, source_target_pairs={{0,64},{16,80},{32,96},{48,112},{64,128},{80,144},{96,160},{112,17... | collective-permute-start | bytes 196616 | tf_op jit(solution)/shard_map/ppermute | solution.py:57
  (37 other events, 470.1 us)

commit v10 on v9

--- a/solution.py
+++ b/solution.py
@@ -91,6 +91,33 @@
     return jnp.concatenate([low, volume, high], axis=axis)
 
 
+def xy_halo(volume, radius_i, radius_j, high_x, high_y):
+    nsp = lax.axis_size("space")
+    length = volume.shape[1]
+
+    def toward(slab, axis, is_high):
+        radius = radius_i if axis == 2 else radius_j
+        first = lax.slice_in_dim(slab, 0, radius, axis=axis)
+        last = lax.slice_in_dim(slab, length - radius, length, axis=axis)
+        return jnp.where(is_high, first, last)
+
+    def swap(x, partner):
+        return lax.ppermute(x, "space", [(i, i ^ partner) for i in range(nsp)])
+
+    def place(inner, halo, axis, is_high):
+        zero = jnp.zeros_like(halo)
+        low = jnp.where(is_high, halo, zero)
+        high = jnp.where(is_high, zero, halo)
+        return jnp.concatenate([low, inner, high], axis=axis)
+
+    x_slab = swap(toward(volume, 2, high_x), 1)
+    y_slab = swap(toward(volume, 1, high_y), 3)
+    corner = swap(toward(toward(volume, 2, high_x), 1, high_y), 2)
+    rows = place(volume, x_slab, 2, high_x)
+    edge = place(y_slab, corner, 2, high_x)
+    return place(rows, edge, 1, high_y)
+
+
 def z_halo(volume, axis, radius):
     length = volume.shape[axis]
     nsp = lax.axis_size("space")
@@ -194,13 +221,13 @@
     bands = lax.optimization_barrier(bands)
     for sweep_no in range(ITERS):
         full = view_all_gather(share, nv)
-        blurred = convolve(pair_halo(full, 2, radius_x, 1, my_x == 1), bands[2, False], 2)
-        blurred = convolve(pair_halo(blurred, 1, radius_y, 3, my_y == 1), bands[1, False], 1)
+        blurred = convolve(xy_halo(full, radius_x, radius_y, my_x == 1, my_y == 1), bands[2, False], 2)
+        blurred = convolve(blurred, bands[1, False], 1)
         blurred = convolve(z_halo(blurred, 0, radius_z), bands[0, False], 0)
         quotient = recorded / blurred
         spread = convolve(z_halo(quotient, 0, radius_z), bands[0, True], 0)
-        spread = convolve(pair_halo(spread, 1, radius_y, 3, my_y == 1), bands[1, True], 1)
-        spread = convolve(pair_halo(spread, 2, radius_x, 1, my_x == 1), bands[2, True], 2)
+        spread = convolve(xy_halo(spread, radius_x, radius_y, my_x == 1, my_y == 1), bands[1, True], 1)
+        spread = convolve(spread, bands[2, True], 2)
         summed = view_reduce_scatter(spread, nv)
         share = share * jnp.where(keep, summed / (nv * measured.shape[0]), 1.0)
     share = route(share, brick_at, place[me], nsp)

time: 643 us -> 624 us (0.970)
  waiting for transfers between devices: 303 us -> 257 us
  starting transfers between devices: 122 us -> 147 us
  local copies, waits for them, and re-layouts: 54.4 us -> 39.5 us
  matrix products: 52.8 us -> 60.2 us
    ppermute x36, waiting for transfers between devices: 159 us -> 123 us  [route(): part = lax.ppermute(part, 'space', pairs)]
    ppermute x36, starting transfers between devices: 59.1 us -> 70.2 us  [route(): part = lax.ppermute(part, 'space', pairs)]
    ppermute x8, starting transfers between devices: 4.98 us -> 15.7 us  [view_reduce_scatter(): x = keep + lax.ppermute(send, 'view', xor_pairs(nv, m))]
    ppermute x8, waiting for transfers between devices: 64.7 us -> 56.4 us  [view_reduce_scatter(): x = keep + lax.ppermute(send, 'view', xor_pairs(nv, m))]
    select_n x8 -> x0, local copies, waits for them, and re-layouts: 8.19 us -> none  [the longest x4 4.12 us: pair_halo(): low = jnp.where(is_high, recv, zero)]
    unnamed x0 -> x2, matrix products: none -> 6.75 us
    unnamed x63 -> x43, local copies, waits for them, and re-layouts: 12.9 us -> 7.4 us
    dot_general x4 -> x2, matrix products: 18.7 us -> 14.2 us  [convolve(): return jnp.einsum('ot,tab->oab', band, extended, precision=hi)]
  transfers between devices with their start and end apart: 72 -> 76, of which waited for: 44 -> 42; matrix products, arithmetic and copies ran while one was open for 13% -> 14% of each run, Pallas kernels for 0% -> 0%
where the time goes in v10:
time: 624 us; the launch traced here: 614 us
  waiting for transfers between devices  257 us (41%)
  starting transfers between devices  147 us (24%)
  other arithmetic  71.5 us (11%)
  matrix products  60.2 us (10%)
  local copies, waits for them, and re-layouts  39.5 us (6%)
  between operations  39.4 us (6%)
    ppermute x36, waiting for transfers between devices, route(): part = lax.ppermute(part, 'space', pairs)  123 us
    ppermute x36, starting transfers between devices, route(): part = lax.ppermute(part, 'space', pairs)  70.2 us
    ppermute x8, waiting for transfers between devices, view_reduce_scatter(): x = keep + lax.ppermute(send, 'view', xor_pairs(nv, m))  56.4 us
    ppermute x8, waiting for transfers between devices, view_all_gather(): recv = lax.ppermute(x, 'view', xor_pairs(nv, m))  30.5 us
    ppermute x12, starting transfers between devices, swap(): return lax.ppermute(x, 'space', [(i, i ^ partner) for i in range(nsp)])  20.1 us
    dot_general x4, matrix products, convolve(): return jnp.einsum('abt,ot->abo', extended, band, precision=hi)  19.6 us
    dot_general x4, matrix products, convolve(): return jnp.einsum('ot,atb->aob', band, extended, precision=hi)  19.6 us
    select_n x3, other arithmetic, band_matrix(): band = jnp.where(offset == position, weight, band)  18.9 us
  transfers between devices with their start and end apart: 76, of which 42 were waited for; matrix products, arithmetic and copies ran while one was open for 14% of the time, Pallas kernels for 0%

profile of v10, /device:TPU:8, one launch (start us, length us, event | category | flops | bytes accessed | tf_op | source)
XLA Modules:
  0.0 614.5 jit_solution(2005467714621641180)
XLA Ops:
  13.4 4.4 select_select_fusion.25
  17.8 4.5 select_select_fusion.23
  27.8 3.4 collective-permute-done.2
  32.8 3.0 collective-permute-done.3
  47.4 10.0 %select_select_fusion.27 = (f32[64,78]{1,0:T(8,128)S(1)}, f32[64,78]{1,0:T(8,128)}) fusion(f32[]{:T(128)} %bitcast.40, f32[]{:T(128)} %bitcast.39, f32[]{:T(128)} %bitcast.38, f32[]{:T(128)} %bitcast.37, f32[]{:T(128)} %bitcast.36, f32[]{:T(128)} %bitcast.35, f32[]{:T(128)} %bitcast.34, f32[]{:T(128)} %bitcast.33, f32[]{:T(128)} %bitcast.32, f32[]{:T(128)} %bitcast.31, ...), kind=kLoop, calls=%fused_computation.182 | loop fusion | flops 229632 | bytes 39996 | tf_op jit(solution)/shard_map/jit(_where)/select_n | solution.py:68
  63.5 4.3 collective-permute-start.7
  76.2 6.9 %collective-permute-start.34 = (f32[64,4,64]{0,2,1:T(8,128)S(1)}, f32[64,4,64]{0,2,1:T(8,128)}, u32[]{:S(2)}, u32[]{:S(2)}) collective-permute-start(f32[64,4,64]{0,2,1:T(8,128)S(1)} %fusion.15), channel_id=1, source_target_pairs={{0,2},{1,3},{2,0},{3,1},{4,6},{5,7},{6,4},{7,5},{8,10},{9,11},{10,... | collective-permute-start | bytes 196616 | tf_op jit(solution)/shard_map/ppermute | solution.py:161
  94.2 13.1 %collective-permute-done.22 = f32[16,64,64]{2,0,1:T(8,128)S(1)} collective-permute-done((f32[16,64,64]{2,0,1:T(8,128)}, f32[16,64,64]{2,0,1:T(8,128)S(1)}, u32[]{:S(2)}, u32[]{:S(2)}) %collective-permute-start.22) | collective-permute-done | bytes 262176 | tf_op jit(solution)/shard_map/ppermute | solution.py:47
  107.4 3.0 collective-permute-start.35
  118.2 9.2 %collective-permute-done.25 = f32[16,64,64]{2,0,1:T(8,128)S(1)} collective-permute-done((f32[16,64,64]{2,0,1:T(8,128)S(1)}, f32[16,64,64]{2,0,1:T(8,128)S(1)}, u32[]{:S(2)}, u32[]{:S(2)}) %collective-permute-start.25) | collective-permute-done | bytes 262176 | tf_op jit(solution)/shard_map/ppermute | solution.py:57
  127.4 4.3 collective-permute-start.16
  131.7 30.9 %collective-permute-done.26 = f32[16,64,64]{2,0,1:T(8,128)S(1)} collective-permute-done((f32[16,64,64]{2,0,1:T(8,128)S(1)}, f32[16,64,64]{2,0,1:T(8,128)S(1)}, u32[]{:S(2)}, u32[]{:S(2)}) %collective-permute-start.26) | collective-permute-done | bytes 262176 | tf_op jit(solution)/shard_map/ppermute | solution.py:57
  166.3 5.5 collective-permute-done.36
  174.5 2.6 select_select_fusion.13
  177.1 3.0 collective-permute-start.13
  180.1 8.4 %collective-permute-start.14 = (f32[16,64,64]{2,0,1:T(8,128)}, f32[16,64,64]{2,0,1:T(8,128)}, u32[]{:S(2)}, u32[]{:S(2)}) collective-permute-start(f32[16,64,64]{2,0,1:T(8,128)} %get-tuple-element.20), channel_id=1, source_target_pairs={{0,128},{16,144},{32,160},{48,176},{64,192},{80,208},{96,224},{112... | collective-permute-start | bytes 786440 | tf_op jit(solution)/shard_map/ppermute | solution.py:57
  192.8 3.2 collective-permute-done.38
  195.9 3.0 collective-permute-start.40
  202.8 3.6 collective-permute-done.39
  206.4 10.3 %collective-permute-start.15 = (f32[16,64,64]{2,0,1:T(8,128)}, f32[16,64,64]{2,0,1:T(8,128)}, u32[]{:S(2)}, u32[]{:S(2)}) collective-permute-start(f32[16,64,64]{2,0,1:T(8,128)} %get-tuple-element.19), channel_id=1, source_target_pairs={{0,64},{16,80},{32,96},{48,112},{64,128},{80,144},{96,160},{112,17... | collective-permute-start | bytes 786440 | tf_op jit(solution)/shard_map/ppermute | solution.py:57
  219.2 3.4 copy.52
  222.6 7.9 %fusion.40 = f32[64,70,64]{1,2,0:T(8,128)S(1)} fusion(f32[64,70,70]{2,1,0:T(8,128)} %copy.52, f32[64,70]{1,0:T(8,128)S(1)} %get-tuple-element.13), kind=kOutput, calls=%fused_computation.166 | convolution fusion | flops 240844800 | bytes 2419200 | tf_op jit(solution)/shard_map/abt,ot->abo/dot_general | solution.py:78
  253.0 3.3 collective-permute-start.28
  258.5 3.6 pad_maximum_fusion.6
  262.1 4.4 copy.39
  266.5 26.6 %collective-permute-done.17 = f32[16,64,64]{2,0,1:T(8,128)} collective-permute-done((f32[16,64,64]{2,0,1:T(8,128)}, f32[16,64,64]{2,0,1:T(8,128)}, u32[]{:S(2)}, u32[]{:S(2)}) %collective-permute-start.17) | collective-permute-done | bytes 262176 | tf_op jit(solution)/shard_map/ppermute | solution.py:47
  298.2 13.7 %collective-permute-done.29 = f32[16,64,64]{2,0,1:T(8,128)S(1)} collective-permute-done((f32[16,64,64]{2,0,1:T(8,128)}, f32[16,64,64]{2,0,1:T(8,128)S(1)}, u32[]{:S(2)}, u32[]{:S(2)}) %collective-permute-start.29) | collective-permute-done | bytes 262176 | tf_op jit(solution)/shard_map/ppermute | solution.py:47
  316.2 11.0 %collective-permute-done.31 = f32[16,64,64]{2,0,1:T(8,128)S(1)} collective-permute-done((f32[16,64,64]{2,0,1:T(8,128)S(1)}, f32[16,64,64]{2,0,1:T(8,128)S(1)}, u32[]{:S(2)}, u32[]{:S(2)}) %collective-permute-start.31) | collective-permute-done | bytes 262176 | tf_op jit(solution)/shard_map/ppermute | solution.py:57
  327.2 8.3 %collective-permute-done.32 = f32[16,64,64]{2,0,1:T(8,128)S(1)} collective-permute-done((f32[16,64,64]{2,0,1:T(8,128)S(1)}, f32[16,64,64]{2,0,1:T(8,128)S(1)}, u32[]{:S(2)}, u32[]{:S(2)}) %collective-permute-start.32) | collective-permute-done | bytes 262176 | tf_op jit(solution)/shard_map/ppermute | solution.py:57
  337.1 6.1 convolution_divide_fusion.1
  346.3 3.0 collective-permute-done.43
  349.3 4.7 collective-permute-done.44
  356.5 3.4 fusion.92
  360.5 3.2 collective-permute-start.47
  366.8 2.8 collective-permute-done.45
  374.1 7.9 %fusion.34 = f32[64,70,64]{1,2,0:T(8,128)S(1)} fusion(f32[64,70,70]{1,2,0:T(8,128)} %copy.53, f32[64,70]{1,0:T(8,128)S(1)} %get-tuple-element.15), kind=kOutput, calls=%fused_computation.160 | convolution fusion | flops 240844800 | bytes 2419200 | tf_op jit(solution)/shard_map/ot,atb->aob/dot_general | solution.py:77
  386.5 2.6 collective-permute-done.48
  391.1 12.5 %collective-permute-done.49 = f32[64,2,2,4,64]{0,4,3,2,1:T(8,128)S(1)} collective-permute-done((f32[64,2,2,4,64]{0,4,3,2,1:T(8,128)S(1)}, f32[64,2,2,4,64]{0,4,3,2,1:T(8,128)S(1)}, u32[]{:S(2)}, u32[]{:S(2)}) %collective-permute-start.49) | collective-permute-done | bytes 262176 | tf_op jit(solution)/shard_map/ppermute | solution.py:151
  403.7 3.1 collective-permute-start.50
  406.8 6.0 collective-permute-done.50
  415.7 7.5 %collective-permute-done.51 = f32[64,4,64]{0,2,1:T(8,128)S(1)} collective-permute-done((f32[64,4,64]{0,2,1:T(8,128)S(1)}, f32[64,4,64]{0,2,1:T(8,128)S(1)}, u32[]{:S(2)}, u32[]{:S(2)}) %collective-permute-start.51) | collective-permute-done | bytes 65568 | tf_op jit(solution)/shard_map/ppermute | solution.py:151
  425.0 8.5 %collective-permute-done.52 = f32[64,4,64]{0,2,1:T(8,128)S(1)} collective-permute-done((f32[64,4,64]{0,2,1:T(8,128)S(1)}, f32[64,4,64]{0,2,1:T(8,128)S(1)}, u32[]{:S(2)}, u32[]{:S(2)}) %collective-permute-start.52) | collective-permute-done | bytes 65568 | tf_op jit(solution)/shard_map/ppermute | solution.py:161
  433.5 3.1 collective-permute-start.53
  436.6 6.7 %collective-permute-done.53 = f32[64,2,4,64]{0,3,2,1:T(8,128)S(1)} collective-permute-done((f32[64,2,4,64]{0,3,2,1:T(8,128)S(1)}, f32[64,2,4,64]{0,3,2,1:T(8,128)S(1)}, u32[]{:S(2)}, u32[]{:S(2)}) %collective-permute-start.53) | collective-permute-done | bytes 131104 | tf_op jit(solution)/shard_map/ppermute | solution.py:161
  446.0 7.2 %collective-permute-done.54 = f32[64,2,2,4,64]{0,4,3,2,1:T(8,128)S(1)} collective-permute-done((f32[64,2,2,4,64]{0,4,3,2,1:T(8,128)S(1)}, f32[64,2,2,4,64]{0,4,3,2,1:T(8,128)S(1)}, u32[]{:S(2)}, u32[]{:S(2)}) %collective-permute-start.54) | collective-permute-done | bytes 262176 | tf_op jit(solution)/shard_map/ppermute | solution.py:161
  453.5 2.6 collective-permute-done.55
  470.9 7.9 %fusion.38 = f32[64,70,64]{1,2,0:T(8,128)S(1)} fusion(f32[64,70,70]{2,1,0:T(8,128)} %copy.54, f32[64,70]{1,0:T(8,128)S(1)} %get-tuple-element.13), kind=kOutput, calls=%fused_computation.164 | convolution fusion | flops 240844800 | bytes 2419200 | tf_op jit(solution)/shard_map/abt,ot->abo/dot_general | solution.py:78
  480.7 4.5 collective-permute-start.59
  489.0 4.2 collective-permute-done.60
  493.5 3.3 copy.47
  496.8 8.1 %convolution_divide_fusion = f32[64,64,64]{2,0,1:T(8,128)S(1)} fusion(f32[78,64,64]{0,2,1:T(8,128)} %copy.47, f32[16,64,64]{2,0,1:T(8,128)} %copy-done.13, f32[16,64,64]{2,0,1:T(8,128)S(1)} %copy-done.10, f32[16,64,64]{2,0,1:T(8,128)} %copy-done.12, f32[16,64,64]{2,0,1:T(8,128)} %get-tuple-element.43, f32[64,78]{1,0:T(8,128)S(1)} %copy-done.18), kind=kOutput, calls=%fused_computation.18 | convolution fusion | flops 246415360 | bytes 3395072 | tf_op jit(solution)/shard_map/ot,tab->oab/dot_general | solution.py:75
  504.9 3.1 collective-permute-start.61
  511.9 4.4 collective-permute-done.62
  518.8 3.4 fusion.93
  522.8 3.9 collective-permute-start.65
  529.8 2.9 collective-permute-done.63
  537.1 7.9 %fusion.32 = f32[64,70,64]{1,2,0:T(8,128)S(1)} fusion(f32[64,70,70]{1,2,0:T(8,128)} %copy.55, f32[64,70]{1,0:T(8,128)S(1)} %get-tuple-element.15), kind=kOutput, calls=%fused_computation.158 | convolution fusion | flops 240844800 | bytes 2419200 | tf_op jit(solution)/shard_map/ot,atb->aob/dot_general | solution.py:77
  549.5 2.6 collective-permute-done.66
  554.6 12.2 %collective-permute-done.67 = f32[64,2,2,4,64]{0,4,3,2,1:T(8,128)S(1)} collective-permute-done((f32[64,2,2,4,64]{0,4,3,2,1:T(8,128)S(1)}, f32[64,2,2,4,64]{0,4,3,2,1:T(8,128)S(1)}, u32[]{:S(2)}, u32[]{:S(2)}) %collective-permute-start.67) | collective-permute-done | bytes 262176 | tf_op jit(solution)/shard_map/ppermute | solution.py:151
  567.0 3.7 collective-permute-start.68
  570.7 5.8 collective-permute-done.68
  576.5 2.9 collective-permute-start.69
  579.4 7.1 %collective-permute-done.69 = f32[64,4,64]{0,2,1:T(8,128)S(1)} collective-permute-done((f32[64,4,64]{0,2,1:T(8,128)S(1)}, f32[64,4,64]{0,2,1:T(8,128)S(1)}, u32[]{:S(2)}, u32[]{:S(2)}) %collective-permute-start.69) | collective-permute-done | bytes 65568 | tf_op jit(solution)/shard_map/ppermute | solution.py:151
  607.2 6.1 collective-permute-done.74
  (281 shorter events, 171.1 us)
Async XLA Ops:
  1.5 20.9 %collective-permute-start = (s32[16,7]{0,1:T(8,128)S(1)}, s32[16,7]{0,1:T(8,128)S(1)}, u32[]{:S(2)}, u32[]{:S(2)}) collective-permute-start(s32[16,7]{0,1:T(8,128)S(1)} %broadcast_select_fusion.22), channel_id=1, source_target_pairs={{0,16},{16,0},{32,48},{48,32},{64,80},{80,64},{96,112},{112,96},{1... | collective-permute-start | bytes 1352 | tf_op jit(solution)/shard_map/ppermute | solution.py:23
  42.5 20.9 %collective-permute-start.4 = (f32[64,4,64]{0,2,1:T(8,128)S(1)}, f32[64,4,64]{0,2,1:T(8,128)S(1)}, u32[]{:S(2)}, u32[]{:S(2)}) collective-permute-start(f32[64,4,64]{0,2,1:T(8,128)S(1)} %bitcast.290), channel_id=1, source_target_pairs={{0,48},{16,0},{32,16},{48,32},{64,112},{80,64},{96,80},{112,96},{1... | collective-permute-start | bytes 196616 | tf_op jit(solution)/shard_map/ppermute | solution.py:47
  42.9 20.5 %collective-permute-start.5 = (f32[64,4,64]{0,2,1:T(8,128)S(1)}, f32[64,4,64]{0,2,1:T(8,128)S(1)}, u32[]{:S(2)}, u32[]{:S(2)}) collective-permute-start(f32[64,4,64]{0,2,1:T(8,128)S(1)} %bitcast.291), channel_id=1, source_target_pairs={{0,32},{16,48},{32,0},{48,16},{64,96},{80,112},{96,64},{112,80},{1... | collective-permute-start | bytes 196616 | tf_op jit(solution)/shard_map/ppermute | solution.py:47
  46.1 17.4 %collective-permute-start.6 = (f32[64,4,64]{0,2,1:T(8,128)}, f32[64,4,64]{0,2,1:T(8,128)S(1)}, u32[]{:S(2)}, u32[]{:S(2)}) collective-permute-start(f32[64,4,64]{0,2,1:T(8,128)} %bitcast.259), channel_id=1, source_target_pairs={{0,16},{16,32},{32,48},{48,0},{64,80},{80,96},{96,112},{112,64},{1... | collective-permute-start | bytes 196616 | tf_op jit(solution)/shard_map/ppermute | solution.py:47
  63.5 11.6 %collective-permute-start.7 = (f32[64,4,64]{0,2,1:T(8,128)S(1)}, f32[64,4,64]{0,2,1:T(8,128)S(1)}, u32[]{:S(2)}, u32[]{:S(2)}) collective-permute-start(f32[64,4,64]{0,2,1:T(8,128)S(1)} %get-tuple-element.74), channel_id=1, source_target_pairs={{0,192},{16,208},{32,224},{48,240},{64,0},{80,16},{96,32},{112,48}... | collective-permute-start | bytes 196616 | tf_op jit(solution)/shard_map/ppermute | solution.py:57
  67.9 7.4 %collective-permute-start.8 = (f32[64,4,64]{0,2,1:T(8,128)S(1)}, f32[64,4,64]{0,2,1:T(8,128)S(1)}, u32[]{:S(2)}, u32[]{:S(2)}) collective-permute-start(f32[64,4,64]{0,2,1:T(8,128)S(1)} %get-tuple-element.73), channel_id=1, source_target_pairs={{0,128},{16,144},{32,160},{48,176},{64,192},{80,208},{96,224},{112... | collective-permute-start | bytes 196616 | tf_op jit(solution)/shard_map/ppermute | solution.py:57
  67.9 7.4 %collective-permute-start.9 = (f32[64,4,64]{0,2,1:T(8,128)S(1)}, f32[64,4,64]{0,2,1:T(8,128)}, u32[]{:S(2)}, u32[]{:S(2)}) collective-permute-start(f32[64,4,64]{0,2,1:T(8,128)S(1)} %get-tuple-element.72), channel_id=1, source_target_pairs={{0,64},{16,80},{32,96},{48,112},{64,128},{80,144},{96,160},{112,17... | collective-permute-start | bytes 196616 | tf_op jit(solution)/shard_map/ppermute | solution.py:57
  76.2 14.9 %collective-permute-start.34 = (f32[64,4,64]{0,2,1:T(8,128)S(1)}, f32[64,4,64]{0,2,1:T(8,128)}, u32[]{:S(2)}, u32[]{:S(2)}) collective-permute-start(f32[64,4,64]{0,2,1:T(8,128)S(1)} %fusion.15), channel_id=1, source_target_pairs={{0,2},{1,3},{2,0},{3,1},{4,6},{5,7},{6,4},{7,5},{8,10},{9,11},{10,... | collective-permute-start | bytes 196616 | tf_op jit(solution)/shard_map/ppermute | solution.py:161
  86.0 21.3 %collective-permute-start.22 = (f32[16,64,64]{2,0,1:T(8,128)}, f32[16,64,64]{2,0,1:T(8,128)S(1)}, u32[]{:S(2)}, u32[]{:S(2)}) collective-permute-start(f32[16,64,64]{2,0,1:T(8,128)} %get-tuple-element.54), channel_id=1, source_target_pairs={{0,48},{16,0},{32,16},{48,32},{64,112},{80,64},{96,80},{112,96},{1... | collective-permute-start | bytes 786440 | tf_op jit(solution)/shard_map/ppermute | solution.py:47
  86.1 25.9 %collective-permute-start.23 = (f32[16,64,64]{2,0,1:T(8,128)}, f32[16,64,64]{2,0,1:T(8,128)}, u32[]{:S(2)}, u32[]{:S(2)}) collective-permute-start(f32[16,64,64]{2,0,1:T(8,128)} %get-tuple-element.50), channel_id=1, source_target_pairs={{0,32},{16,48},{32,0},{48,16},{64,96},{80,112},{96,64},{112,80},{1... | collective-permute-start | bytes 786440 | tf_op jit(solution)/shard_map/ppermute | solution.py:47
  87.5 24.5 %collective-permute-start.24 = (f32[16,64,64]{2,0,1:T(8,128)}, f32[16,64,64]{2,0,1:T(8,128)}, u32[]{:S(2)}, u32[]{:S(2)}) collective-permute-start(f32[16,64,64]{2,0,1:T(8,128)} %get-tuple-element.51), channel_id=1, source_target_pairs={{0,16},{16,32},{32,48},{48,0},{64,80},{80,96},{96,112},{112,64},{1... | collective-permute-start | bytes 786440 | tf_op jit(solution)/shard_map/ppermute | solution.py:47
  89.3 83.4 %collective-permute-start.10 = (f32[16,64,64]{2,0,1:T(8,128)}, f32[16,64,64]{2,0,1:T(8,128)S(1)}, u32[]{:S(2)}, u32[]{:S(2)}) collective-permute-start(f32[16,64,64]{2,0,1:T(8,128)} %get-tuple-element.56), channel_id=1, source_target_pairs={{0,48},{16,0},{32,16},{48,32},{64,112},{80,64},{96,80},{112,96},{1... | collective-permute-start | bytes 786440 | tf_op jit(solution)/shard_map/ppermute | solution.py:47
  91.1 83.0 %collective-permute-start.11 = (f32[16,64,64]{2,0,1:T(8,128)}, f32[16,64,64]{2,0,1:T(8,128)S(1)}, u32[]{:S(2)}, u32[]{:S(2)}) collective-permute-start(f32[16,64,64]{2,0,1:T(8,128)} %get-tuple-element.48), channel_id=1, source_target_pairs={{0,32},{16,48},{32,0},{48,16},{64,96},{80,112},{96,64},{112,80},{1... | collective-permute-start | bytes 786440 | tf_op jit(solution)/shard_map/ppermute | solution.py:47
  107.4 8.8 %collective-permute-start.35 = (f32[64,2,4,64]{0,3,2,1:T(8,128)S(1)}, f32[64,2,4,64]{0,3,2,1:T(8,128)S(1)}, u32[]{:S(2)}, u32[]{:S(2)}) collective-permute-start(f32[64,2,4,64]{0,3,2,1:T(8,128)S(1)} %pad_maximum_fusion.15), channel_id=1, source_target_pairs={{0,8},{1,9},{2,10},{3,11},{4,12},{5,13},{6,14},{7,15},{8,0},{9,1},... | collective-permute-start | bytes 393224 | tf_op jit(solution)/shard_map/ppermute | solution.py:161
  113.5 13.9 %collective-permute-start.25 = (f32[16,64,64]{2,0,1:T(8,128)S(1)}, f32[16,64,64]{2,0,1:T(8,128)S(1)}, u32[]{:S(2)}, u32[]{:S(2)}) collective-permute-start(f32[16,64,64]{2,0,1:T(8,128)S(1)} %get-tuple-element.27), channel_id=1, source_target_pairs={{0,192},{16,208},{32,224},{48,240},{64,0},{80,16},{96,32},{112,48}... | collective-permute-start | bytes 786440 | tf_op jit(solution)/shard_map/ppermute | solution.py:57
  115.0 47.6 %collective-permute-start.26 = (f32[16,64,64]{2,0,1:T(8,128)S(1)}, f32[16,64,64]{2,0,1:T(8,128)S(1)}, u32[]{:S(2)}, u32[]{:S(2)}) collective-permute-start(f32[16,64,64]{2,0,1:T(8,128)S(1)} %get-tuple-element.26), channel_id=1, source_target_pairs={{0,128},{16,144},{32,160},{48,176},{64,192},{80,208},{96,224},{112... | collective-permute-start | bytes 786440 | tf_op jit(solution)/shard_map/ppermute | solution.py:57
  116.1 47.9 %collective-permute-start.27 = (f32[16,64,64]{2,0,1:T(8,128)S(1)}, f32[16,64,64]{2,0,1:T(8,128)S(1)}, u32[]{:S(2)}, u32[]{:S(2)}) collective-permute-start(f32[16,64,64]{2,0,1:T(8,128)S(1)} %get-tuple-element.25), channel_id=1, source_target_pairs={{0,64},{16,80},{32,96},{48,112},{64,128},{80,144},{96,160},{112,17... | collective-permute-start | bytes 786440 | tf_op jit(solution)/shard_map/ppermute | solution.py:57
  127.4 139.2 %collective-permute-start.16 = (f32[16,64,64]{2,0,1:T(8,128)}, f32[16,64,64]{2,0,1:T(8,128)S(1)}, u32[]{:S(2)}, u32[]{:S(2)}) collective-permute-start(f32[16,64,64]{2,0,1:T(8,128)} %get-tuple-element.55), channel_id=1, source_target_pairs={{0,192},{64,0},{128,64},{192,128},{16,208},{80,16},{144,80},{208,1... | collective-permute-start | bytes 786440 | tf_op jit(solution)/shard_map/ppermute | solution.py:47
  162.6 9.2 %collective-permute-start.36 = (f32[64,2,2,4,64]{0,4,3,2,1:T(8,128)S(1)}, f32[64,2,2,4,64]{0,4,3,2,1:T(8,128)S(1)}, u32[]{:S(2)}, u32[]{:S(2)}) collective-permute-start(f32[64,2,2,4,64]{0,4,3,2,1:T(8,128)S(1)} %pad_maximum_fusion.13), channel_id=1, source_target_pairs={{0,4},{1,5},{2,6},{3,7},{4,0},{5,1},{6,2},{7,3},{8,12},{9,13},{10,... | collective-permute-start | bytes 786440 | tf_op jit(solution)/shard_map/ppermute | solution.py:161
  165.3 9.2 %collective-permute-start.12 = (f32[16,64,64]{2,0,1:T(8,128)S(1)}, f32[16,64,64]{2,0,1:T(8,128)S(1)}, u32[]{:S(2)}, u32[]{:S(2)}) collective-permute-start(f32[16,64,64]{2,0,1:T(8,128)S(1)} %get-tuple-element.46), channel_id=1, source_target_pairs={{0,16},{16,32},{32,48},{48,0},{64,80},{80,96},{96,112},{112,64},{1... | collective-permute-start | bytes 786440 | tf_op jit(solution)/shard_map/ppermute | solution.py:47
  172.0 16.6 %collective-permute-start.37 = (f32[64,2,2,2,4,64]{0,5,4,3,1,2:T(8,128)S(1)}, f32[64,2,2,2,4,64]{0,5,4,3,1,2:T(8,128)S(1)}, u32[]{:S(2)}, u32[]{:S(2)}) collective-permute-start(f32[64,2,2,2,4,64]{0,5,4,3,1,2:T(8,128)S(1)} %pad_maximum_fusion.11), channel_id=1, source_target_pairs={{0,1},{1,0},{2,3},{3,2},{4,5},{5,4},{6,7},{7,6},{8,9},{9,8},{10,11... | collective-permute-start | bytes 1572872 | tf_op jit(solution)/shard_map/ppermute | solution.py:161
  173.5 93.0 %collective-permute-start.18 = (f32[16,64,64]{2,0,1:T(8,128)}, f32[16,64,64]{2,0,1:T(8,128)S(1)}, u32[]{:S(2)}, u32[]{:S(2)}) collective-permute-start(f32[16,64,64]{2,0,1:T(8,128)} %get-tuple-element.49), channel_id=1, source_target_pairs={{0,64},{64,128},{128,192},{192,0},{16,80},{80,144},{144,208},{208,... | collective-permute-start | bytes 786440 | tf_op jit(solution)/shard_map/ppermute | solution.py:47
  177.1 57.6 %collective-permute-start.13 = (f32[16,64,64]{2,0,1:T(8,128)}, f32[16,64,64]{2,0,1:T(8,128)}, u32[]{:S(2)}, u32[]{:S(2)}) collective-permute-start(f32[16,64,64]{2,0,1:T(8,128)} %get-tuple-element.21), channel_id=1, source_target_pairs={{0,192},{16,208},{32,224},{48,240},{64,0},{80,16},{96,32},{112,48}... | collective-permute-start | bytes 786440 | tf_op jit(solution)/shard_map/ppermute | solution.py:57
  180.1 57.1 %collective-permute-start.14 = (f32[16,64,64]{2,0,1:T(8,128)}, f32[16,64,64]{2,0,1:T(8,128)}, u32[]{:S(2)}, u32[]{:S(2)}) collective-permute-start(f32[16,64,64]{2,0,1:T(8,128)} %get-tuple-element.20), channel_id=1, source_target_pairs={{0,128},{16,144},{32,160},{48,176},{64,192},{80,208},{96,224},{112... | collective-permute-start | bytes 786440 | tf_op jit(solution)/shard_map/ppermute | solution.py:57
  195.9 5.9 collective-permute-start.40
  206.4 32.1 %collective-permute-start.15 = (f32[16,64,64]{2,0,1:T(8,128)}, f32[16,64,64]{2,0,1:T(8,128)}, u32[]{:S(2)}, u32[]{:S(2)}) collective-permute-start(f32[16,64,64]{2,0,1:T(8,128)} %get-tuple-element.19), channel_id=1, source_target_pairs={{0,64},{16,80},{32,96},{48,112},{64,128},{80,144},{96,160},{112,17... | collective-permute-start | bytes 786440 | tf_op jit(solution)/shard_map/ppermute | solution.py:57
  234.7 18.3 %collective-permute-start.41 = (f32[7,64,64]{1,2,0:T(8,128)}, f32[7,64,64]{1,2,0:T(8,128)}, u32[]{:S(2)}, u32[]{:S(2)}) collective-permute-start(f32[7,64,64]{1,2,0:T(8,128)} %get-tuple-element.57), channel_id=1, source_target_pairs={{0,64},{16,80},{32,96},{48,112},{64,128},{80,144},{96,160},{112,17... | collective-permute-start | bytes 344072 | tf_op jit(solution)/shard_map/ppermute | solution.py:126
  237.3 19.0 %collective-permute-start.42 = (f32[7,64,64]{1,2,0:T(8,128)}, f32[7,64,64]{1,2,0:T(8,128)}, u32[]{:S(2)}, u32[]{:S(2)}) collective-permute-start(f32[7,64,64]{1,2,0:T(8,128)} %get-tuple-element.58), channel_id=1, source_target_pairs={{64,0},{80,16},{96,32},{112,48},{128,64},{144,80},{160,96},{176,11... | collective-permute-start | bytes 344072 | tf_op jit(solution)/shard_map/ppermute | solution.py:127
  241.1 52.0 %collective-permute-start.17 = (f32[16,64,64]{2,0,1:T(8,128)}, f32[16,64,64]{2,0,1:T(8,128)}, u32[]{:S(2)}, u32[]{:S(2)}) collective-permute-start(f32[16,64,64]{2,0,1:T(8,128)} %get-tuple-element.44), channel_id=1, source_target_pairs={{0,128},{64,192},{128,0},{192,64},{16,144},{80,208},{144,16},{208,... | collective-permute-start | bytes 786440 | tf_op jit(solution)/shard_map/ppermute | solution.py:47
  253.0 43.7 %collective-permute-start.28 = (f32[16,64,64]{2,0,1:T(8,128)}, f32[16,64,64]{2,0,1:T(8,128)}, u32[]{:S(2)}, u32[]{:S(2)}) collective-permute-start(f32[16,64,64]{2,0,1:T(8,128)} %get-tuple-element.53), channel_id=1, source_target_pairs={{0,192},{64,0},{128,64},{192,128},{16,208},{80,16},{144,80},{208,1... | collective-permute-start | bytes 786440 | tf_op jit(solution)/shard_map/ppermute | solution.py:47
  256.3 41.8 %collective-permute-start.30 = (f32[16,64,64]{2,0,1:T(8,128)}, f32[16,64,64]{2,0,1:T(8,128)}, u32[]{:S(2)}, u32[]{:S(2)}) collective-permute-start(f32[16,64,64]{2,0,1:T(8,128)} %get-tuple-element.52), channel_id=1, source_target_pairs={{0,64},{64,128},{128,192},{192,0},{16,80},{80,144},{144,208},{208,... | collective-permute-start | bytes 786440 | tf_op jit(solution)/shard_map/ppermute | solution.py:47
  266.5 45.3 %collective-permute-start.29 = (f32[16,64,64]{2,0,1:T(8,128)}, f32[16,64,64]{2,0,1:T(8,128)S(1)}, u32[]{:S(2)}, u32[]{:S(2)}) collective-permute-start(f32[16,64,64]{2,0,1:T(8,128)} %get-tuple-element.45), channel_id=1, source_target_pairs={{0,128},{64,192},{128,0},{192,64},{16,144},{80,208},{144,16},{208,... | collective-permute-start | bytes 786440 | tf_op jit(solution)/shard_map/ppermute | solution.py:47
  294.4 21.2 %collective-permute-start.19 = (f32[16,64,64]{2,0,1:T(8,128)S(1)}, f32[16,64,64]{2,0,1:T(8,128)S(1)}, u32[]{:S(2)}, u32[]{:S(2)}) collective-permute-start(f32[16,64,64]{2,0,1:T(8,128)S(1)} %get-tuple-element.24), channel_id=1, source_target_pairs={{0,48},{64,112},{128,176},{192,240},{16,0},{80,64},{144,128},{208,... | collective-permute-start | bytes 786440 | tf_op jit(solution)/shard_map/ppermute | solution.py:57
  296.0 19.9 %collective-permute-start.20 = (f32[16,64,64]{2,0,1:T(8,128)S(1)}, f32[16,64,64]{2,0,1:T(8,128)S(1)}, u32[]{:S(2)}, u32[]{:S(2)}) collective-permute-start(f32[16,64,64]{2,0,1:T(8,128)S(1)} %get-tuple-element.23), channel_id=1, source_target_pairs={{0,32},{64,96},{128,160},{192,224},{16,48},{80,112},{144,176},{208... | collective-permute-start | bytes 786440 | tf_op jit(solution)/shard_map/ppermute | solution.py:57
  296.7 19.2 %collective-permute-start.21 = (f32[16,64,64]{2,0,1:T(8,128)S(1)}, f32[16,64,64]{2,0,1:T(8,128)S(1)}, u32[]{:S(2)}, u32[]{:S(2)}) collective-permute-start(f32[16,64,64]{2,0,1:T(8,128)S(1)} %get-tuple-element.22), channel_id=1, source_target_pairs={{0,16},{64,80},{128,144},{192,208},{16,32},{80,96},{144,160},{208,... | collective-permute-start | bytes 786440 | tf_op jit(solution)/shard_map/ppermute | solution.py:57
  313.3 13.9 %collective-permute-start.31 = (f32[16,64,64]{2,0,1:T(8,128)S(1)}, f32[16,64,64]{2,0,1:T(8,128)S(1)}, u32[]{:S(2)}, u32[]{:S(2)}) collective-permute-start(f32[16,64,64]{2,0,1:T(8,128)S(1)} %get-tuple-element.30), channel_id=1, source_target_pairs={{0,48},{64,112},{128,176},{192,240},{16,0},{80,64},{144,128},{208,... | collective-permute-start | bytes 786440 | tf_op jit(solution)/shard_map/ppermute | solution.py:57
  313.7 21.8 %collective-permute-start.32 = (f32[16,64,64]{2,0,1:T(8,128)S(1)}, f32[16,64,64]{2,0,1:T(8,128)S(1)}, u32[]{:S(2)}, u32[]{:S(2)}) collective-permute-start(f32[16,64,64]{2,0,1:T(8,128)S(1)} %get-tuple-element.29), channel_id=1, source_target_pairs={{0,32},{64,96},{128,160},{192,224},{16,48},{80,112},{144,176},{208... | collective-permute-start | bytes 786440 | tf_op jit(solution)/shard_map/ppermute | solution.py:57
  315.6 21.2 %collective-permute-start.33 = (f32[16,64,64]{2,0,1:T(8,128)S(1)}, f32[16,64,64]{2,0,1:T(8,128)S(1)}, u32[]{:S(2)}, u32[]{:S(2)}) collective-permute-start(f32[16,64,64]{2,0,1:T(8,128)S(1)} %get-tuple-element.28), channel_id=1, source_target_pairs={{0,16},{64,80},{128,144},{192,208},{16,32},{80,96},{144,160},{208,... | collective-permute-start | bytes 786440 | tf_op jit(solution)/shard_map/ppermute | solution.py:57
  343.3 6.1 collective-permute-start.43
  345.0 9.0 %collective-permute-start.44 = (f32[7,64,64]{2,0,1:T(8,128)S(1)}, f32[7,64,64]{2,0,1:T(8,128)S(1)}, u32[]{:S(2)}, u32[]{:S(2)}) collective-permute-start(f32[7,64,64]{2,0,1:T(8,128)S(1)} %get-tuple-element.42), channel_id=1, source_target_pairs={{64,0},{80,16},{96,32},{112,48},{128,64},{144,80},{160,96},{176,11... | collective-permute-start | bytes 344072 | tf_op jit(solution)/shard_map/ppermute | solution.py:127
  360.5 9.7 %collective-permute-start.47 = (f32[64,64,3]{0,2,1:T(4,128)S(1)}, f32[64,64,3]{0,2,1:T(4,128)S(1)}, u32[]{:S(2)}, u32[]{:S(2)}) collective-permute-start(f32[64,64,3]{0,2,1:T(4,128)S(1)} %slice_select_fusion.18), channel_id=1, source_target_pairs={{0,16},{16,0},{32,48},{48,32},{64,80},{80,64},{96,112},{112,96},{1... | collective-permute-start | bytes 147464 | tf_op jit(solution)/shard_map/ppermute | solution.py:105
  365.1 5.7 collective-permute-start.46
  389.5 14.1 %collective-permute-start.49 = (f32[64,2,2,4,64]{0,4,3,2,1:T(8,128)S(1)}, f32[64,2,2,4,64]{0,4,3,2,1:T(8,128)S(1)}, u32[]{:S(2)}, u32[]{:S(2)}) collective-permute-start(f32[64,2,2,4,64]{0,4,3,2,1:T(8,128)S(1)} %select_bitcast_fusion.9), channel_id=1, source_target_pairs={{0,4},{1,5},{2,6},{3,7},{4,0},{5,1},{6,2},{7,3},{8,12},{9,13},{10,... | collective-permute-start | bytes 786440 | tf_op jit(solution)/shard_map/ppermute | solution.py:151
  403.7 9.1 %collective-permute-start.50 = (f32[64,2,4,64]{0,3,2,1:T(8,128)S(1)}, f32[64,2,4,64]{0,3,2,1:T(8,128)S(1)}, u32[]{:S(2)}, u32[]{:S(2)}) collective-permute-start(f32[64,2,4,64]{0,3,2,1:T(8,128)S(1)} %select_bitcast_fusion.15), channel_id=1, source_target_pairs={{0,8},{1,9},{2,10},{3,11},{4,12},{5,13},{6,14},{7,15},{8,0},{9,1},... | collective-permute-start | bytes 393224 | tf_op jit(solution)/shard_map/ppermute | solution.py:151
  412.9 10.3 %collective-permute-start.51 = (f32[64,4,64]{0,2,1:T(8,128)S(1)}, f32[64,4,64]{0,2,1:T(8,128)S(1)}, u32[]{:S(2)}, u32[]{:S(2)}) collective-permute-start(f32[64,4,64]{0,2,1:T(8,128)S(1)} %select_bitcast_fusion.22), channel_id=1, source_target_pairs={{0,2},{1,3},{2,0},{3,1},{4,6},{5,7},{6,4},{7,5},{8,10},{9,11},{10,... | collective-permute-start | bytes 196616 | tf_op jit(solution)/shard_map/ppermute | solution.py:151
  423.8 9.6 %collective-permute-start.52 = (f32[64,4,64]{0,2,1:T(8,128)S(1)}, f32[64,4,64]{0,2,1:T(8,128)S(1)}, u32[]{:S(2)}, u32[]{:S(2)}) collective-permute-start(f32[64,4,64]{0,2,1:T(8,128)S(1)} %fusion.9), channel_id=1, source_target_pairs={{0,2},{1,3},{2,0},{3,1},{4,6},{5,7},{6,4},{7,5},{8,10},{9,11},{10,... | collective-permute-start | bytes 196616 | tf_op jit(solution)/shard_map/ppermute | solution.py:161
  433.5 9.8 %collective-permute-start.53 = (f32[64,2,4,64]{0,3,2,1:T(8,128)S(1)}, f32[64,2,4,64]{0,3,2,1:T(8,128)S(1)}, u32[]{:S(2)}, u32[]{:S(2)}) collective-permute-start(f32[64,2,4,64]{0,3,2,1:T(8,128)S(1)} %pad_maximum_fusion.16), channel_id=1, source_target_pairs={{0,8},{1,9},{2,10},{3,11},{4,12},{5,13},{6,14},{7,15},{8,0},{9,1},... | collective-permute-start | bytes 393224 | tf_op jit(solution)/shard_map/ppermute | solution.py:161
  443.5 9.7 %collective-permute-start.54 = (f32[64,2,2,4,64]{0,4,3,2,1:T(8,128)S(1)}, f32[64,2,2,4,64]{0,4,3,2,1:T(8,128)S(1)}, u32[]{:S(2)}, u32[]{:S(2)}) collective-permute-start(f32[64,2,2,4,64]{0,4,3,2,1:T(8,128)S(1)} %pad_maximum_fusion.14), channel_id=1, source_target_pairs={{0,4},{1,5},{2,6},{3,7},{4,0},{5,1},{6,2},{7,3},{8,12},{9,13},{10,... | collective-permute-start | bytes 786440 | tf_op jit(solution)/shard_map/ppermute | solution.py:161
  457.4 8.4 %collective-permute-start.58 = (f32[64,64,3]{0,2,1:T(4,128)S(1)}, f32[64,64,3]{0,2,1:T(4,128)S(1)}, u32[]{:S(2)}, u32[]{:S(2)}) collective-permute-start(f32[64,64,3]{0,2,1:T(4,128)S(1)} %slice_select_fusion.17), channel_id=1, source_target_pairs={{0,16},{16,0},{32,48},{48,32},{64,80},{80,64},{96,112},{112,96},{1... | collective-permute-start | bytes 147464 | tf_op jit(solution)/shard_map/ppermute | solution.py:105
  459.8 5.3 collective-permute-start.56
  480.7 8.3 %collective-permute-start.59 = (f32[7,64,64]{1,2,0:T(8,128)S(1)}, f32[7,64,64]{1,2,0:T(8,128)S(1)}, u32[]{:S(2)}, u32[]{:S(2)}) collective-permute-start(f32[7,64,64]{1,2,0:T(8,128)S(1)} %get-tuple-element.35), channel_id=1, source_target_pairs={{0,64},{16,80},{32,96},{48,112},{64,128},{80,144},{96,160},{112,17... | collective-permute-start | bytes 344072 | tf_op jit(solution)/shard_map/ppermute | solution.py:126
  485.3 7.9 %collective-permute-start.60 = (f32[7,64,64]{1,2,0:T(8,128)S(1)}, f32[7,64,64]{1,2,0:T(8,128)S(1)}, u32[]{:S(2)}, u32[]{:S(2)}) collective-permute-start(f32[7,64,64]{1,2,0:T(8,128)S(1)} %get-tuple-element.36), channel_id=1, source_target_pairs={{64,0},{80,16},{96,32},{112,48},{128,64},{144,80},{160,96},{176,11... | collective-permute-start | bytes 344072 | tf_op jit(solution)/shard_map/ppermute | solution.py:127
  504.9 6.9 %collective-permute-start.61 = (f32[7,64,64]{2,0,1:T(8,128)S(1)}, f32[7,64,64]{2,0,1:T(8,128)S(1)}, u32[]{:S(2)}, u32[]{:S(2)}) collective-permute-start(f32[7,64,64]{2,0,1:T(8,128)S(1)} %get-tuple-element.33), channel_id=1, source_target_pairs={{0,64},{16,80},{32,96},{48,112},{64,128},{80,144},{96,160},{112,17... | collective-permute-start | bytes 344072 | tf_op jit(solution)/shard_map/ppermute | solution.py:126
  508.0 8.3 %collective-permute-start.62 = (f32[7,64,64]{2,0,1:T(8,128)S(1)}, f32[7,64,64]{2,0,1:T(8,128)S(1)}, u32[]{:S(2)}, u32[]{:S(2)}) collective-permute-start(f32[7,64,64]{2,0,1:T(8,128)S(1)} %get-tuple-element.34), channel_id=1, source_target_pairs={{64,0},{80,16},{96,32},{112,48},{128,64},{144,80},{160,96},{176,11... | collective-permute-start | bytes 344072 | tf_op jit(solution)/shard_map/ppermute | solution.py:127
  522.8 10.5 %collective-permute-start.65 = (f32[64,64,3]{0,2,1:T(4,128)S(1)}, f32[64,64,3]{0,2,1:T(4,128)S(1)}, u32[]{:S(2)}, u32[]{:S(2)}) collective-permute-start(f32[64,64,3]{0,2,1:T(4,128)S(1)} %slice_select_fusion.16), channel_id=1, source_target_pairs={{0,16},{16,0},{32,48},{48,32},{64,80},{80,64},{96,112},{112,96},{1... | collective-permute-start | bytes 147464 | tf_op jit(solution)/shard_map/ppermute | solution.py:105
  528.1 5.8 collective-permute-start.64
  552.5 14.3 %collective-permute-start.67 = (f32[64,2,2,4,64]{0,4,3,2,1:T(8,128)S(1)}, f32[64,2,2,4,64]{0,4,3,2,1:T(8,128)S(1)}, u32[]{:S(2)}, u32[]{:S(2)}) collective-permute-start(f32[64,2,2,4,64]{0,4,3,2,1:T(8,128)S(1)} %select_bitcast_fusion.6), channel_id=1, source_target_pairs={{0,4},{1,5},{2,6},{3,7},{4,0},{5,1},{6,2},{7,3},{8,12},{9,13},{10,... | collective-permute-start | bytes 786440 | tf_op jit(solution)/shard_map/ppermute | solution.py:151
  567.0 9.4 %collective-permute-start.68 = (f32[64,2,4,64]{0,3,2,1:T(8,128)S(1)}, f32[64,2,4,64]{0,3,2,1:T(8,128)S(1)}, u32[]{:S(2)}, u32[]{:S(2)}) collective-permute-start(f32[64,2,4,64]{0,3,2,1:T(8,128)S(1)} %select_bitcast_fusion.12), channel_id=1, source_target_pairs={{0,8},{1,9},{2,10},{3,11},{4,12},{5,13},{6,14},{7,15},{8,0},{9,1},... | collective-permute-start | bytes 393224 | tf_op jit(solution)/shard_map/ppermute | solution.py:151
  576.5 9.9 %collective-permute-start.69 = (f32[64,4,64]{0,2,1:T(8,128)S(1)}, f32[64,4,64]{0,2,1:T(8,128)S(1)}, u32[]{:S(2)}, u32[]{:S(2)}) collective-permute-start(f32[64,4,64]{0,2,1:T(8,128)S(1)} %select_bitcast_fusion.19), channel_id=1, source_target_pairs={{0,2},{1,3},{2,0},{3,1},{4,6},{5,7},{6,4},{7,5},{8,10},{9,11},{10,... | collective-permute-start | bytes 196616 | tf_op jit(solution)/shard_map/ppermute | solution.py:151
  587.1 14.7 %collective-permute-start.70 = (f32[64,4,64]{0,2,1:T(8,128)S(1)}, f32[64,4,64]{0,2,1:T(8,128)S(1)}, u32[]{:S(2)}, u32[]{:S(2)}) collective-permute-start(f32[64,4,64]{0,2,1:T(8,128)S(1)} %get-tuple-element.80), channel_id=1, source_target_pairs={{0,48},{16,0},{32,16},{48,32},{64,112},{80,64},{96,80},{112,96},{1... | collective-permute-start | bytes 196616 | tf_op jit(solution)/shard_map/ppermute | solution.py:47
  589.4 12.4 %collective-permute-start.71 = (f32[64,4,64]{0,2,1:T(8,128)S(1)}, f32[64,4,64]{0,2,1:T(8,128)S(1)}, u32[]{:S(2)}, u32[]{:S(2)}) collective-permute-start(f32[64,4,64]{0,2,1:T(8,128)S(1)} %get-tuple-element.79), channel_id=1, source_target_pairs={{0,32},{16,48},{32,0},{48,16},{64,96},{80,112},{96,64},{112,80},{1... | collective-permute-start | bytes 196616 | tf_op jit(solution)/shard_map/ppermute | solution.py:47
  591.4 10.5 %collective-permute-start.72 = (f32[64,4,64]{0,2,1:T(8,128)S(1)}, f32[64,4,64]{0,2,1:T(8,128)S(1)}, u32[]{:S(2)}, u32[]{:S(2)}) collective-permute-start(f32[64,4,64]{0,2,1:T(8,128)S(1)} %get-tuple-element.17), channel_id=1, source_target_pairs={{0,16},{16,32},{32,48},{48,0},{64,80},{80,96},{96,112},{112,64},{1... | collective-permute-start | bytes 196616 | tf_op jit(solution)/shard_map/ppermute | solution.py:47
  602.0 11.3 %collective-permute-start.74 = (f32[64,4,64]{0,2,1:T(8,128)S(1)}, f32[64,4,64]{0,2,1:T(8,128)S(1)}, u32[]{:S(2)}, u32[]{:S(2)}) collective-permute-start(f32[64,4,64]{0,2,1:T(8,128)S(1)} %get-tuple-element.66), channel_id=1, source_target_pairs={{0,128},{16,144},{32,160},{48,176},{64,192},{80,208},{96,224},{112... | collective-permute-start | bytes 196616 | tf_op jit(solution)/shard_map/ppermute | solution.py:57
  603.0 10.3 %collective-permute-start.75 = (f32[64,4,64]{0,2,1:T(8,128)S(1)}, f32[64,4,64]{0,2,1:T(8,128)S(1)}, u32[]{:S(2)}, u32[]{:S(2)}) collective-permute-start(f32[64,4,64]{0,2,1:T(8,128)S(1)} %get-tuple-element.65), channel_id=1, source_target_pairs={{0,64},{16,80},{32,96},{48,112},{64,128},{80,144},{96,160},{112,17... | collective-permute-start | bytes 196616 | tf_op jit(solution)/shard_map/ppermute | solution.py:57
  (31 other events, 556.2 us)

commit v11 on v10

--- a/solution.py
+++ b/solution.py
@@ -136,12 +136,9 @@
     return 1 + sum(1 for b in order if b in present and order.index(b) < order.index(m))
 
 
-def view_reduce_scatter(full, nv):
+def view_reduce_scatter(x, nv, bits, present):
     me = lax.axis_index("view")
-    s0, s1, s2 = full.shape
-    x = full.reshape(s0, 2, 2, 2, 2, s1 // nv, s2)
-    present = {8, 4, 2, 1}
-    for m in RS_BITS:
+    for m in bits:
         ax = bit_axis(present, m)
         x0 = lax.index_in_dim(x, 0, axis=ax, keepdims=False)
         x1 = lax.index_in_dim(x, 1, axis=ax, keepdims=False)
@@ -149,24 +146,28 @@
         keep = jnp.where(mine, x1, x0)
         send = jnp.where(mine, x0, x1)
         x = keep + lax.ppermute(send, "view", xor_pairs(nv, m))
-        present.discard(m)
-    return x
-
-
-def view_all_gather(share, nv):
+        present = present - {m}
+    return x, present
+
+
+def view_all_gather(x, nv, bits, present):
     me = lax.axis_index("view")
-    x = share
-    present = set()
-    for m in reversed(RS_BITS):
+    for m in bits:
         recv = lax.ppermute(x, "view", xor_pairs(nv, m))
         mine = (me & m) != 0
         lo = jnp.where(mine, recv, x)
         hi = jnp.where(mine, x, recv)
-        ax = bit_axis(present | {m}, m)
-        x = jnp.stack([lo, hi], axis=ax)
-        present.add(m)
-    s0 = x.shape[0]
-    return x.reshape(s0, -1, x.shape[-1])
+        present = present | {m}
+        x = jnp.stack([lo, hi], axis=bit_axis(present, m))
+    return x, present
+
+
+def own_rows(x, bits, present):
+    me = lax.axis_index("view")
+    for m in bits:
+        x = lax.dynamic_index_in_dim(x, (me & m) // m, axis=bit_axis(present, m), keepdims=False)
+        present = present - {m}
+    return x
 
 
 def shards(estimate, measured, kernel_x, kernel_y, kernel_z, neighbors, inside):
@@ -219,8 +220,13 @@
         for flipped in (False, True)
     }
     bands = lax.optimization_barrier(bands)
+    views = nv * measured.shape[0]
+    all_bits = {8, 4, 2, 1}
+    split = lambda a: a.reshape(a.shape[0], 2, 2, 2, 2, a.shape[1] // nv, a.shape[2])
+    joined = lambda a: a.reshape(a.shape[0], -1, a.shape[-1])
+    full, _ = view_all_gather(share, nv, tuple(reversed(RS_BITS)), set())
+    full = joined(full)
     for sweep_no in range(ITERS):
-        full = view_all_gather(share, nv)
         blurred = convolve(xy_halo(full, radius_x, radius_y, my_x == 1, my_y == 1), bands[2, False], 2)
         blurred = convolve(blurred, bands[1, False], 1)
         blurred = convolve(z_halo(blurred, 0, radius_z), bands[0, False], 0)
@@ -228,8 +234,18 @@
         spread = convolve(z_halo(quotient, 0, radius_z), bands[0, True], 0)
         spread = convolve(xy_halo(spread, radius_x, radius_y, my_x == 1, my_y == 1), bands[1, True], 1)
         spread = convolve(spread, bands[2, True], 2)
-        summed = view_reduce_scatter(spread, nv)
-        share = share * jnp.where(keep, summed / (nv * measured.shape[0]), 1.0)
+        if sweep_no == ITERS - 1:
+            summed, _ = view_reduce_scatter(split(spread), nv, RS_BITS, all_bits)
+            share = share * jnp.where(keep, summed / views, 1.0)
+        else:
+            summed, present = view_reduce_scatter(split(spread), nv, RS_BITS[:2], all_bits)
+            for m in RS_BITS[2:]:
+                summed = summed + lax.ppermute(summed, "view", xor_pairs(nv, m))
+            quarter = own_rows(split(full), RS_BITS[:2], all_bits)
+            quarter = quarter * jnp.where(keep, summed / views, 1.0)
+            share = own_rows(quarter, RS_BITS[2:], present)
+            full, _ = view_all_gather(quarter, nv, tuple(reversed(RS_BITS[:2])), present)
+            full = joined(full)
     share = route(share, brick_at, place[me], nsp)
     return jnp.transpose(share, (2, 1, 0)).reshape(1, side, estimate.shape[2])
 

time: 624 us -> 632 us (1.013)
  starting transfers between devices: 147 us -> 161 us
  waiting for transfers between devices: 257 us -> 248 us
    ppermute x0 -> x2, waiting for transfers between devices: none -> 23 us  [shards(): summed = summed + lax.ppermute(summed, 'view', xor_pairs(nv, m))]
    ppermute x8 -> x6, waiting for transfers between devices: 56.4 us -> 41.5 us  [view_reduce_scatter(): x = keep + lax.ppermute(send, 'view', xor_pairs(nv, m))]
    ppermute x4, starting transfers between devices: 12 us -> 25.1 us  [z_halo(): low = lax.ppermute(last, 'space', [(i, i + ROW) for i in range(nsp - ROW)])]
    ppermute x8 -> x6, waiting for transfers between devices: 30.5 us -> 17.6 us  [view_all_gather(): recv = lax.ppermute(x, 'view', xor_pairs(nv, m))]
    ppermute x0 -> x2, starting transfers between devices: none -> 7.48 us  [shards(): summed = summed + lax.ppermute(summed, 'view', xor_pairs(nv, m))]
    ppermute x8 -> x6, starting transfers between devices: 18.4 us -> 13.4 us  [view_all_gather(): recv = lax.ppermute(x, 'view', xor_pairs(nv, m))]
    ppermute x8 -> x6, starting transfers between devices: 15.7 us -> 10.8 us  [view_reduce_scatter(): x = keep + lax.ppermute(send, 'view', xor_pairs(nv, m))]
  transfers between devices with their start and end apart: 76 -> 74, of which waited for: 42 -> 38; matrix products, arithmetic and copies ran while one was open for 14% -> 14% of each run, Pallas kernels for 0% -> 0%
where the time goes in v11:
time: 632 us; the launch traced here: 622 us
  waiting for transfers between devices  248 us (39%)
  starting transfers between devices  161 us (25%)
  other arithmetic  73 us (12%)
  matrix products  60.1 us (10%)
  local copies, waits for them, and re-layouts  40.6 us (6%)
  between operations  39.1 us (6%)
    ppermute x36, waiting for transfers between devices, route(): part = lax.ppermute(part, 'space', pairs)  121 us
    ppermute x36, starting transfers between devices, route(): part = lax.ppermute(part, 'space', pairs)  71.1 us
    ppermute x6, waiting for transfers between devices, view_reduce_scatter(): x = keep + lax.ppermute(send, 'view', xor_pairs(nv, m))  41.5 us
    ppermute x4, starting transfers between devices, z_halo(): low = lax.ppermute(last, 'space', [(i, i + ROW) for i in range(nsp - ROW)])  25.1 us
    ppermute x2, waiting for transfers between devices, shards(): summed = summed + lax.ppermute(summed, 'view', xor_pairs(nv, m))  23 us
    ppermute x12, starting transfers between devices, swap(): return lax.ppermute(x, 'space', [(i, i ^ partner) for i in range(nsp)])  22.8 us
    dot_general x4, matrix products, convolve(): return jnp.einsum('abt,ot->abo', extended, band, precision=hi)  19.6 us
    dot_general x4, matrix products, convolve(): return jnp.einsum('ot,atb->aob', band, extended, precision=hi)  19.6 us
  transfers between devices with their start and end apart: 74, of which 38 were waited for; matrix products, arithmetic and copies ran while one was open for 14% of the time, Pallas kernels for 0%

profile of v11, /device:TPU:8, one launch (start us, length us, event | category | flops | bytes accessed | tf_op | source)
XLA Modules:
  0.0 622.3 jit_solution(4419231992825409231)
XLA Ops:
  13.3 4.4 select_select_fusion.25
  17.7 4.4 select_select_fusion.23
  27.6 3.4 collective-permute-done.2
  32.5 3.0 collective-permute-done.3
  46.7 9.4 %select_select_fusion.27 = (f32[64,78]{1,0:T(8,128)S(1)}, f32[64,78]{1,0:T(8,128)S(1)}) fusion(f32[]{:T(128)} %bitcast.49, f32[]{:T(128)} %bitcast.48, f32[]{:T(128)} %bitcast.47, f32[]{:T(128)} %bitcast.46, f32[]{:T(128)} %bitcast.45, f32[]{:T(128)} %bitcast.44, f32[]{:T(128)} %bitcast.43, f32[]{:T(128)} %bitcast.42, f32[]{:T(128)} %bitcast.41, ...), kind=kLoop, calls=%fused_computation.174 | loop fusion | flops 229632 | bytes 39996 | tf_op jit(solution)/shard_map/jit(_where)/select_n | solution.py:68
  63.1 4.3 collective-permute-start.7
  75.0 6.9 %collective-permute-start.10 = (f32[64,4,64]{0,2,1:T(8,128)S(1)}, f32[64,4,64]{0,2,1:T(8,128)}, u32[]{:S(2)}, u32[]{:S(2)}) collective-permute-start(f32[64,4,64]{0,2,1:T(8,128)S(1)} %fusion.15), channel_id=1, source_target_pairs={{0,2},{1,3},{2,0},{3,1},{4,6},{5,7},{6,4},{7,5},{8,10},{9,11},{10,... | collective-permute-start | bytes 196616 | tf_op jit(solution)/shard_map/ppermute | solution.py:156
  93.1 12.2 %collective-permute-done.26 = f32[16,64,64]{2,0,1:T(8,128)S(1)} collective-permute-done((f32[16,64,64]{2,0,1:T(8,128)}, f32[16,64,64]{2,0,1:T(8,128)S(1)}, u32[]{:S(2)}, u32[]{:S(2)}) %collective-permute-start.26) | collective-permute-done | bytes 262176 | tf_op jit(solution)/shard_map/ppermute | solution.py:47
  105.3 3.0 collective-permute-start.11
  108.3 3.3 collective-permute-done.27
  117.7 9.6 %collective-permute-done.29 = f32[16,64,64]{2,0,1:T(8,128)S(1)} collective-permute-done((f32[16,64,64]{2,0,1:T(8,128)S(1)}, f32[16,64,64]{2,0,1:T(8,128)S(1)}, u32[]{:S(2)}, u32[]{:S(2)}) %collective-permute-start.29) | collective-permute-done | bytes 262176 | tf_op jit(solution)/shard_map/ppermute | solution.py:57
  127.3 4.0 collective-permute-start.20
  131.3 30.6 %collective-permute-done.30 = f32[16,64,64]{2,0,1:T(8,128)S(1)} collective-permute-done((f32[16,64,64]{2,0,1:T(8,128)S(1)}, f32[16,64,64]{2,0,1:T(8,128)S(1)}, u32[]{:S(2)}, u32[]{:S(2)}) %collective-permute-start.30) | collective-permute-done | bytes 262176 | tf_op jit(solution)/shard_map/ppermute | solution.py:57
  165.8 5.2 collective-permute-done.12
  174.1 2.7 select_select_fusion.13
  176.8 2.7 collective-permute-start.17
  179.5 7.9 %collective-permute-start.18 = (f32[16,64,64]{2,0,1:T(8,128)}, f32[16,64,64]{2,0,1:T(8,128)}, u32[]{:S(2)}, u32[]{:S(2)}) collective-permute-start(f32[16,64,64]{2,0,1:T(8,128)} %get-tuple-element.20), channel_id=1, source_target_pairs={{0,128},{16,144},{32,160},{48,176},{64,192},{80,208},{96,224},{112... | collective-permute-start | bytes 786440 | tf_op jit(solution)/shard_map/ppermute | solution.py:57
  195.9 3.0 collective-permute-start.40
  206.4 10.8 %collective-permute-start.19 = (f32[16,64,64]{2,0,1:T(8,128)}, f32[16,64,64]{2,0,1:T(8,128)}, u32[]{:S(2)}, u32[]{:S(2)}) collective-permute-start(f32[16,64,64]{2,0,1:T(8,128)} %get-tuple-element.19), channel_id=1, source_target_pairs={{0,64},{16,80},{32,96},{48,112},{64,128},{80,144},{96,160},{112,17... | collective-permute-start | bytes 786440 | tf_op jit(solution)/shard_map/ppermute | solution.py:57
  219.7 3.4 copy.52
  223.1 7.9 %fusion.40 = f32[64,70,64]{1,2,0:T(8,128)S(1)} fusion(f32[64,70,70]{2,1,0:T(8,128)} %copy.52, f32[64,70]{1,0:T(8,128)S(1)} %get-tuple-element.13), kind=kOutput, calls=%fused_computation.158 | convolution fusion | flops 240844800 | bytes 2419200 | tf_op jit(solution)/shard_map/abt,ot->abo/dot_general | solution.py:78
  235.2 2.6 collective-permute-start.41
  239.1 2.5 select_select_fusion.12
  253.0 3.8 collective-permute-start.32
  258.5 3.6 pad_maximum_fusion.6
  262.1 4.4 copy.39
  266.5 26.6 %collective-permute-done.21 = f32[16,64,64]{2,0,1:T(8,128)} collective-permute-done((f32[16,64,64]{2,0,1:T(8,128)}, f32[16,64,64]{2,0,1:T(8,128)}, u32[]{:S(2)}, u32[]{:S(2)}) %collective-permute-start.21) | collective-permute-done | bytes 262176 | tf_op jit(solution)/shard_map/ppermute | solution.py:47
  298.9 12.8 %collective-permute-done.33 = f32[16,64,64]{2,0,1:T(8,128)S(1)} collective-permute-done((f32[16,64,64]{2,0,1:T(8,128)}, f32[16,64,64]{2,0,1:T(8,128)S(1)}, u32[]{:S(2)}, u32[]{:S(2)}) %collective-permute-start.33) | collective-permute-done | bytes 262176 | tf_op jit(solution)/shard_map/ppermute | solution.py:47
  317.0 17.7 %collective-permute-done.35 = f32[16,64,64]{2,0,1:T(8,128)S(1)} collective-permute-done((f32[16,64,64]{2,0,1:T(8,128)S(1)}, f32[16,64,64]{2,0,1:T(8,128)S(1)}, u32[]{:S(2)}, u32[]{:S(2)}) %collective-permute-start.35) | collective-permute-done | bytes 262176 | tf_op jit(solution)/shard_map/ppermute | solution.py:57
  336.8 6.1 convolution_divide_fusion.1
  346.3 3.4 collective-permute-done.43
  349.7 4.1 collective-permute-done.44
  356.3 3.4 fusion.92
  360.4 4.3 collective-permute-start.47
  367.7 2.9 collective-permute-done.45
  375.3 7.9 %fusion.34 = f32[64,70,64]{1,2,0:T(8,128)S(1)} fusion(f32[64,70,70]{1,2,0:T(8,128)} %copy.53, f32[64,70]{1,0:T(8,128)S(1)} %get-tuple-element.15), kind=kOutput, calls=%fused_computation.152 | convolution fusion | flops 240844800 | bytes 2419200 | tf_op jit(solution)/shard_map/ot,atb->aob/dot_general | solution.py:77
  387.7 2.6 collective-permute-done.48
  392.3 12.5 %collective-permute-done.49 = f32[64,2,2,4,64]{0,4,3,2,1:T(8,128)S(1)} collective-permute-done((f32[64,2,2,4,64]{0,4,3,2,1:T(8,128)S(1)}, f32[64,2,2,4,64]{0,4,3,2,1:T(8,128)S(1)}, u32[]{:S(2)}, u32[]{:S(2)}) %collective-permute-start.49) | collective-permute-done | bytes 262176 | tf_op jit(solution)/shard_map/ppermute | solution.py:148
  404.9 3.1 collective-permute-start.50
  408.0 11.6 %collective-permute-done.50 = f32[64,2,2,4,64]{0,4,3,2,1:T(8,128)S(1)} collective-permute-done((f32[64,2,2,4,64]{0,4,3,2,1:T(8,128)S(1)}, f32[64,2,2,4,64]{0,4,3,2,1:T(8,128)S(1)}, u32[]{:S(2)}, u32[]{:S(2)}) %collective-permute-start.50) | collective-permute-done | bytes 262176 | tf_op jit(solution)/shard_map/ppermute | solution.py:243
  419.7 4.4 collective-permute-start.51
  424.8 11.3 %collective-permute-done.51 = f32[64,2,2,4,64]{0,4,3,2,1:T(8,128)S(1)} collective-permute-done((f32[64,2,2,4,64]{0,4,3,2,1:T(8,128)S(1)}, f32[64,2,2,4,64]{0,4,3,2,1:T(8,128)S(1)}, u32[]{:S(2)}, u32[]{:S(2)}) %collective-permute-start.51) | collective-permute-done | bytes 262176 | tf_op jit(solution)/shard_map/ppermute | solution.py:243
  438.8 9.7 %collective-permute-done.52 = f32[64,2,2,4,64]{0,4,3,2,1:T(8,128)S(1)} collective-permute-done((f32[64,2,2,4,64]{0,4,3,2,1:T(8,128)S(1)}, f32[64,2,2,4,64]{0,4,3,2,1:T(8,128)S(1)}, u32[]{:S(2)}, u32[]{:S(2)}) %collective-permute-start.52) | collective-permute-done | bytes 262176 | tf_op jit(solution)/shard_map/ppermute | solution.py:156
  448.8 2.6 collective-permute-done.53
  463.7 2.5 copy.54
  466.2 7.9 %fusion.38 = f32[64,70,64]{1,2,0:T(8,128)S(1)} fusion(f32[64,70,70]{2,1,0:T(8,128)} %copy.54, f32[64,70]{1,0:T(8,128)S(1)} %get-tuple-element.13), kind=kOutput, calls=%fused_computation.156 | convolution fusion | flops 240844800 | bytes 2419200 | tf_op jit(solution)/shard_map/abt,ot->abo/dot_general | solution.py:78
  476.0 18.3 %collective-permute-start.57 = (f32[7,64,64]{1,2,0:T(8,128)S(1)}, f32[7,64,64]{1,2,0:T(8,128)S(1)}, u32[]{:S(2)}, u32[]{:S(2)}) collective-permute-start(f32[7,64,64]{1,2,0:T(8,128)S(1)} %get-tuple-element.35), channel_id=1, source_target_pairs={{0,64},{16,80},{32,96},{48,112},{64,128},{80,144},{96,160},{112,17... | collective-permute-start | bytes 344072 | tf_op jit(solution)/shard_map/ppermute | solution.py:126
  498.1 4.2 collective-permute-done.58
  502.5 3.3 copy.47
  505.8 8.1 %convolution_divide_fusion = f32[64,64,64]{2,0,1:T(8,128)S(1)} fusion(f32[78,64,64]{0,2,1:T(8,128)} %copy.47, f32[16,64,64]{2,0,1:T(8,128)} %copy-done.18, f32[16,64,64]{2,0,1:T(8,128)S(1)} %copy-done.15, f32[16,64,64]{2,0,1:T(8,128)} %copy-done.17, f32[16,64,64]{2,0,1:T(8,128)} %get-tuple-element.43, f32[64,78]{1,0:T(8,128)S(1)} %get-tuple-element.12), kind=kOutput, calls=%fused_computation.20 | convolution fusion | flops 246415360 | bytes 3395072 | tf_op jit(solution)/shard_map/ot,tab->oab/dot_general | solution.py:75
  517.4 2.6 collective-permute-done.59
  520.0 4.4 collective-permute-done.60
  526.8 3.4 fusion.93
  530.9 3.9 collective-permute-start.63
  538.0 2.9 collective-permute-done.61
  545.5 7.9 %fusion.32 = f32[64,70,64]{1,2,0:T(8,128)S(1)} fusion(f32[64,70,70]{1,2,0:T(8,128)} %copy.55, f32[64,70]{1,0:T(8,128)S(1)} %get-tuple-element.15), kind=kOutput, calls=%fused_computation.150 | convolution fusion | flops 240844800 | bytes 2419200 | tf_op jit(solution)/shard_map/ot,atb->aob/dot_general | solution.py:77
  557.9 2.6 collective-permute-done.64
  562.5 12.5 %collective-permute-done.65 = f32[64,2,2,4,64]{0,4,3,2,1:T(8,128)S(1)} collective-permute-done((f32[64,2,2,4,64]{0,4,3,2,1:T(8,128)S(1)}, f32[64,2,2,4,64]{0,4,3,2,1:T(8,128)S(1)}, u32[]{:S(2)}, u32[]{:S(2)}) %collective-permute-start.65) | collective-permute-done | bytes 262176 | tf_op jit(solution)/shard_map/ppermute | solution.py:148
  575.2 3.1 collective-permute-start.66
  578.3 6.0 collective-permute-done.66
  584.4 4.4 collective-permute-start.67
  588.8 5.2 collective-permute-done.67
  599.6 2.5 collective-permute-start.70
  615.6 5.6 collective-permute-done.72
  (273 shorter events, 165.8 us)
Async XLA Ops:
  1.5 20.6 %collective-permute-start = (s32[16,7]{0,1:T(8,128)S(1)}, s32[16,7]{0,1:T(8,128)S(1)}, u32[]{:S(2)}, u32[]{:S(2)}) collective-permute-start(s32[16,7]{0,1:T(8,128)S(1)} %broadcast_select_fusion.22), channel_id=1, source_target_pairs={{0,16},{16,0},{32,48},{48,32},{64,80},{80,64},{96,112},{112,96},{1... | collective-permute-start | bytes 1352 | tf_op jit(solution)/shard_map/ppermute | solution.py:23
  41.8 20.5 %collective-permute-start.4 = (f32[64,4,64]{0,2,1:T(8,128)S(1)}, f32[64,4,64]{0,2,1:T(8,128)S(1)}, u32[]{:S(2)}, u32[]{:S(2)}) collective-permute-start(f32[64,4,64]{0,2,1:T(8,128)S(1)} %bitcast.275), channel_id=1, source_target_pairs={{0,48},{16,0},{32,16},{48,32},{64,112},{80,64},{96,80},{112,96},{1... | collective-permute-start | bytes 196616 | tf_op jit(solution)/shard_map/ppermute | solution.py:47
  42.2 20.1 %collective-permute-start.5 = (f32[64,4,64]{0,2,1:T(8,128)S(1)}, f32[64,4,64]{0,2,1:T(8,128)S(1)}, u32[]{:S(2)}, u32[]{:S(2)}) collective-permute-start(f32[64,4,64]{0,2,1:T(8,128)S(1)} %bitcast.276), channel_id=1, source_target_pairs={{0,32},{16,48},{32,0},{48,16},{64,96},{80,112},{96,64},{112,80},{1... | collective-permute-start | bytes 196616 | tf_op jit(solution)/shard_map/ppermute | solution.py:47
  45.4 17.0 %collective-permute-start.6 = (f32[64,4,64]{0,2,1:T(8,128)}, f32[64,4,64]{0,2,1:T(8,128)S(1)}, u32[]{:S(2)}, u32[]{:S(2)}) collective-permute-start(f32[64,4,64]{0,2,1:T(8,128)} %bitcast.244), channel_id=1, source_target_pairs={{0,16},{16,32},{32,48},{48,0},{64,80},{80,96},{96,112},{112,64},{1... | collective-permute-start | bytes 196616 | tf_op jit(solution)/shard_map/ppermute | solution.py:47
  63.1 11.6 %collective-permute-start.7 = (f32[64,4,64]{0,2,1:T(8,128)}, f32[64,4,64]{0,2,1:T(8,128)S(1)}, u32[]{:S(2)}, u32[]{:S(2)}) collective-permute-start(f32[64,4,64]{0,2,1:T(8,128)} %get-tuple-element.72), channel_id=1, source_target_pairs={{0,192},{16,208},{32,224},{48,240},{64,0},{80,16},{96,32},{112,48}... | collective-permute-start | bytes 196616 | tf_op jit(solution)/shard_map/ppermute | solution.py:57
  67.4 7.6 %collective-permute-start.8 = (f32[64,4,64]{0,2,1:T(8,128)}, f32[64,4,64]{0,2,1:T(8,128)S(1)}, u32[]{:S(2)}, u32[]{:S(2)}) collective-permute-start(f32[64,4,64]{0,2,1:T(8,128)} %get-tuple-element.71), channel_id=1, source_target_pairs={{0,128},{16,144},{32,160},{48,176},{64,192},{80,208},{96,224},{112... | collective-permute-start | bytes 196616 | tf_op jit(solution)/shard_map/ppermute | solution.py:57
  67.4 7.6 %collective-permute-start.9 = (f32[64,4,64]{0,2,1:T(8,128)S(1)}, f32[64,4,64]{0,2,1:T(8,128)S(1)}, u32[]{:S(2)}, u32[]{:S(2)}) collective-permute-start(f32[64,4,64]{0,2,1:T(8,128)S(1)} %get-tuple-element.70), channel_id=1, source_target_pairs={{0,64},{16,80},{32,96},{48,112},{64,128},{80,144},{96,160},{112,17... | collective-permute-start | bytes 196616 | tf_op jit(solution)/shard_map/ppermute | solution.py:57
  75.0 15.0 %collective-permute-start.10 = (f32[64,4,64]{0,2,1:T(8,128)S(1)}, f32[64,4,64]{0,2,1:T(8,128)}, u32[]{:S(2)}, u32[]{:S(2)}) collective-permute-start(f32[64,4,64]{0,2,1:T(8,128)S(1)} %fusion.15), channel_id=1, source_target_pairs={{0,2},{1,3},{2,0},{3,1},{4,6},{5,7},{6,4},{7,5},{8,10},{9,11},{10,... | collective-permute-start | bytes 196616 | tf_op jit(solution)/shard_map/ppermute | solution.py:156
  84.8 20.5 %collective-permute-start.26 = (f32[16,64,64]{2,0,1:T(8,128)}, f32[16,64,64]{2,0,1:T(8,128)S(1)}, u32[]{:S(2)}, u32[]{:S(2)}) collective-permute-start(f32[16,64,64]{2,0,1:T(8,128)} %get-tuple-element.54), channel_id=1, source_target_pairs={{0,48},{16,0},{32,16},{48,32},{64,112},{80,64},{96,80},{112,96},{1... | collective-permute-start | bytes 786440 | tf_op jit(solution)/shard_map/ppermute | solution.py:47
  85.6 26.1 %collective-permute-start.27 = (f32[16,64,64]{2,0,1:T(8,128)}, f32[16,64,64]{2,0,1:T(8,128)}, u32[]{:S(2)}, u32[]{:S(2)}) collective-permute-start(f32[16,64,64]{2,0,1:T(8,128)} %get-tuple-element.50), channel_id=1, source_target_pairs={{0,32},{16,48},{32,0},{48,16},{64,96},{80,112},{96,64},{112,80},{1... | collective-permute-start | bytes 786440 | tf_op jit(solution)/shard_map/ppermute | solution.py:47
  87.2 24.5 %collective-permute-start.28 = (f32[16,64,64]{2,0,1:T(8,128)}, f32[16,64,64]{2,0,1:T(8,128)}, u32[]{:S(2)}, u32[]{:S(2)}) collective-permute-start(f32[16,64,64]{2,0,1:T(8,128)} %get-tuple-element.51), channel_id=1, source_target_pairs={{0,16},{16,32},{32,48},{48,0},{64,80},{80,96},{96,112},{112,64},{1... | collective-permute-start | bytes 786440 | tf_op jit(solution)/shard_map/ppermute | solution.py:47
  89.0 83.1 %collective-permute-start.14 = (f32[16,64,64]{2,0,1:T(8,128)}, f32[16,64,64]{2,0,1:T(8,128)S(1)}, u32[]{:S(2)}, u32[]{:S(2)}) collective-permute-start(f32[16,64,64]{2,0,1:T(8,128)} %get-tuple-element.56), channel_id=1, source_target_pairs={{0,48},{16,0},{32,16},{48,32},{64,112},{80,64},{96,80},{112,96},{1... | collective-permute-start | bytes 786440 | tf_op jit(solution)/shard_map/ppermute | solution.py:47
  90.1 84.0 %collective-permute-start.15 = (f32[16,64,64]{2,0,1:T(8,128)}, f32[16,64,64]{2,0,1:T(8,128)S(1)}, u32[]{:S(2)}, u32[]{:S(2)}) collective-permute-start(f32[16,64,64]{2,0,1:T(8,128)} %get-tuple-element.48), channel_id=1, source_target_pairs={{0,32},{16,48},{32,0},{48,16},{64,96},{80,112},{96,64},{112,80},{1... | collective-permute-start | bytes 786440 | tf_op jit(solution)/shard_map/ppermute | solution.py:47
  105.3 10.4 %collective-permute-start.11 = (f32[64,2,4,64]{0,3,2,1:T(8,128)S(1)}, f32[64,2,4,64]{0,3,2,1:T(8,128)S(1)}, u32[]{:S(2)}, u32[]{:S(2)}) collective-permute-start(f32[64,2,4,64]{0,3,2,1:T(8,128)S(1)} %pad_maximum_fusion.14), channel_id=1, source_target_pairs={{0,8},{1,9},{2,10},{3,11},{4,12},{5,13},{6,14},{7,15},{8,0},{9,1},... | collective-permute-start | bytes 393224 | tf_op jit(solution)/shard_map/ppermute | solution.py:156
  113.1 14.2 %collective-permute-start.29 = (f32[16,64,64]{2,0,1:T(8,128)S(1)}, f32[16,64,64]{2,0,1:T(8,128)S(1)}, u32[]{:S(2)}, u32[]{:S(2)}) collective-permute-start(f32[16,64,64]{2,0,1:T(8,128)S(1)} %get-tuple-element.27), channel_id=1, source_target_pairs={{0,192},{16,208},{32,224},{48,240},{64,0},{80,16},{96,32},{112,48}... | collective-permute-start | bytes 786440 | tf_op jit(solution)/shard_map/ppermute | solution.py:57
  114.5 47.3 %collective-permute-start.30 = (f32[16,64,64]{2,0,1:T(8,128)S(1)}, f32[16,64,64]{2,0,1:T(8,128)S(1)}, u32[]{:S(2)}, u32[]{:S(2)}) collective-permute-start(f32[16,64,64]{2,0,1:T(8,128)S(1)} %get-tuple-element.26), channel_id=1, source_target_pairs={{0,128},{16,144},{32,160},{48,176},{64,192},{80,208},{96,224},{112... | collective-permute-start | bytes 786440 | tf_op jit(solution)/shard_map/ppermute | solution.py:57
  115.7 47.7 %collective-permute-start.31 = (f32[16,64,64]{2,0,1:T(8,128)S(1)}, f32[16,64,64]{2,0,1:T(8,128)S(1)}, u32[]{:S(2)}, u32[]{:S(2)}) collective-permute-start(f32[16,64,64]{2,0,1:T(8,128)S(1)} %get-tuple-element.25), channel_id=1, source_target_pairs={{0,64},{16,80},{32,96},{48,112},{64,128},{80,144},{96,160},{112,17... | collective-permute-start | bytes 786440 | tf_op jit(solution)/shard_map/ppermute | solution.py:57
  127.3 139.2 %collective-permute-start.20 = (f32[16,64,64]{2,0,1:T(8,128)}, f32[16,64,64]{2,0,1:T(8,128)S(1)}, u32[]{:S(2)}, u32[]{:S(2)}) collective-permute-start(f32[16,64,64]{2,0,1:T(8,128)} %get-tuple-element.55), channel_id=1, source_target_pairs={{0,192},{64,0},{128,64},{192,128},{16,208},{80,16},{144,80},{208,1... | collective-permute-start | bytes 786440 | tf_op jit(solution)/shard_map/ppermute | solution.py:47
  161.9 9.2 %collective-permute-start.12 = (f32[64,2,2,4,64]{0,4,3,2,1:T(8,128)S(1)}, f32[64,2,2,4,64]{0,4,3,2,1:T(8,128)S(1)}, u32[]{:S(2)}, u32[]{:S(2)}) collective-permute-start(f32[64,2,2,4,64]{0,4,3,2,1:T(8,128)S(1)} %pad_maximum_fusion.13), channel_id=1, source_target_pairs={{0,4},{1,5},{2,6},{3,7},{4,0},{5,1},{6,2},{7,3},{8,12},{9,13},{10,... | collective-permute-start | bytes 786440 | tf_op jit(solution)/shard_map/ppermute | solution.py:156
  164.6 9.5 %collective-permute-start.16 = (f32[16,64,64]{2,0,1:T(8,128)S(1)}, f32[16,64,64]{2,0,1:T(8,128)S(1)}, u32[]{:S(2)}, u32[]{:S(2)}) collective-permute-start(f32[16,64,64]{2,0,1:T(8,128)S(1)} %get-tuple-element.46), channel_id=1, source_target_pairs={{0,16},{16,32},{32,48},{48,0},{64,80},{80,96},{96,112},{112,64},{1... | collective-permute-start | bytes 786440 | tf_op jit(solution)/shard_map/ppermute | solution.py:47
  171.3 16.1 %collective-permute-start.13 = (f32[64,2,2,2,4,64]{0,5,4,3,1,2:T(8,128)S(1)}, f32[64,2,2,2,4,64]{0,5,4,3,1,2:T(8,128)S(1)}, u32[]{:S(2)}, u32[]{:S(2)}) collective-permute-start(f32[64,2,2,2,4,64]{0,5,4,3,1,2:T(8,128)S(1)} %pad_maximum_fusion.11), channel_id=1, source_target_pairs={{0,1},{1,0},{2,3},{3,2},{4,5},{5,4},{6,7},{7,6},{8,9},{9,8},{10,11... | collective-permute-start | bytes 1572872 | tf_op jit(solution)/shard_map/ppermute | solution.py:156
  172.9 93.6 %collective-permute-start.22 = (f32[16,64,64]{2,0,1:T(8,128)}, f32[16,64,64]{2,0,1:T(8,128)S(1)}, u32[]{:S(2)}, u32[]{:S(2)}) collective-permute-start(f32[16,64,64]{2,0,1:T(8,128)} %get-tuple-element.49), channel_id=1, source_target_pairs={{0,64},{64,128},{128,192},{192,0},{16,80},{80,144},{144,208},{208,... | collective-permute-start | bytes 786440 | tf_op jit(solution)/shard_map/ppermute | solution.py:47
  176.8 58.3 %collective-permute-start.17 = (f32[16,64,64]{2,0,1:T(8,128)}, f32[16,64,64]{2,0,1:T(8,128)}, u32[]{:S(2)}, u32[]{:S(2)}) collective-permute-start(f32[16,64,64]{2,0,1:T(8,128)} %get-tuple-element.21), channel_id=1, source_target_pairs={{0,192},{16,208},{32,224},{48,240},{64,0},{80,16},{96,32},{112,48}... | collective-permute-start | bytes 786440 | tf_op jit(solution)/shard_map/ppermute | solution.py:57
  179.5 58.3 %collective-permute-start.18 = (f32[16,64,64]{2,0,1:T(8,128)}, f32[16,64,64]{2,0,1:T(8,128)}, u32[]{:S(2)}, u32[]{:S(2)}) collective-permute-start(f32[16,64,64]{2,0,1:T(8,128)} %get-tuple-element.20), channel_id=1, source_target_pairs={{0,128},{16,144},{32,160},{48,176},{64,192},{80,208},{96,224},{112... | collective-permute-start | bytes 786440 | tf_op jit(solution)/shard_map/ppermute | solution.py:57
  195.9 5.9 collective-permute-start.40
  206.4 32.7 %collective-permute-start.19 = (f32[16,64,64]{2,0,1:T(8,128)}, f32[16,64,64]{2,0,1:T(8,128)}, u32[]{:S(2)}, u32[]{:S(2)}) collective-permute-start(f32[16,64,64]{2,0,1:T(8,128)} %get-tuple-element.19), channel_id=1, source_target_pairs={{0,64},{16,80},{32,96},{48,112},{64,128},{80,144},{96,160},{112,17... | collective-permute-start | bytes 786440 | tf_op jit(solution)/shard_map/ppermute | solution.py:57
  235.2 17.9 %collective-permute-start.41 = (f32[7,64,64]{1,2,0:T(8,128)}, f32[7,64,64]{1,2,0:T(8,128)}, u32[]{:S(2)}, u32[]{:S(2)}) collective-permute-start(f32[7,64,64]{1,2,0:T(8,128)} %get-tuple-element.57), channel_id=1, source_target_pairs={{0,64},{16,80},{32,96},{48,112},{64,128},{80,144},{96,160},{112,17... | collective-permute-start | bytes 344072 | tf_op jit(solution)/shard_map/ppermute | solution.py:126
  237.8 19.1 %collective-permute-start.42 = (f32[7,64,64]{1,2,0:T(8,128)}, f32[7,64,64]{1,2,0:T(8,128)}, u32[]{:S(2)}, u32[]{:S(2)}) collective-permute-start(f32[7,64,64]{1,2,0:T(8,128)} %get-tuple-element.58), channel_id=1, source_target_pairs={{64,0},{80,16},{96,32},{112,48},{128,64},{144,80},{160,96},{176,11... | collective-permute-start | bytes 344072 | tf_op jit(solution)/shard_map/ppermute | solution.py:127
  241.6 51.5 %collective-permute-start.21 = (f32[16,64,64]{2,0,1:T(8,128)}, f32[16,64,64]{2,0,1:T(8,128)}, u32[]{:S(2)}, u32[]{:S(2)}) collective-permute-start(f32[16,64,64]{2,0,1:T(8,128)} %get-tuple-element.44), channel_id=1, source_target_pairs={{0,128},{64,192},{128,0},{192,64},{16,144},{80,208},{144,16},{208,... | collective-permute-start | bytes 786440 | tf_op jit(solution)/shard_map/ppermute | solution.py:47
  253.0 44.4 %collective-permute-start.32 = (f32[16,64,64]{2,0,1:T(8,128)}, f32[16,64,64]{2,0,1:T(8,128)}, u32[]{:S(2)}, u32[]{:S(2)}) collective-permute-start(f32[16,64,64]{2,0,1:T(8,128)} %get-tuple-element.53), channel_id=1, source_target_pairs={{0,192},{64,0},{128,64},{192,128},{16,208},{80,16},{144,80},{208,1... | collective-permute-start | bytes 786440 | tf_op jit(solution)/shard_map/ppermute | solution.py:47
  256.9 42.0 %collective-permute-start.34 = (f32[16,64,64]{2,0,1:T(8,128)}, f32[16,64,64]{2,0,1:T(8,128)}, u32[]{:S(2)}, u32[]{:S(2)}) collective-permute-start(f32[16,64,64]{2,0,1:T(8,128)} %get-tuple-element.52), channel_id=1, source_target_pairs={{0,64},{64,128},{128,192},{192,0},{16,80},{80,144},{144,208},{208,... | collective-permute-start | bytes 786440 | tf_op jit(solution)/shard_map/ppermute | solution.py:47
  266.5 45.2 %collective-permute-start.33 = (f32[16,64,64]{2,0,1:T(8,128)}, f32[16,64,64]{2,0,1:T(8,128)S(1)}, u32[]{:S(2)}, u32[]{:S(2)}) collective-permute-start(f32[16,64,64]{2,0,1:T(8,128)} %get-tuple-element.45), channel_id=1, source_target_pairs={{0,128},{64,192},{128,0},{192,64},{16,144},{80,208},{144,16},{208,... | collective-permute-start | bytes 786440 | tf_op jit(solution)/shard_map/ppermute | solution.py:47
  294.4 20.7 %collective-permute-start.23 = (f32[16,64,64]{2,0,1:T(8,128)S(1)}, f32[16,64,64]{2,0,1:T(8,128)S(1)}, u32[]{:S(2)}, u32[]{:S(2)}) collective-permute-start(f32[16,64,64]{2,0,1:T(8,128)S(1)} %get-tuple-element.24), channel_id=1, source_target_pairs={{0,48},{64,112},{128,176},{192,240},{16,0},{80,64},{144,128},{208,... | collective-permute-start | bytes 786440 | tf_op jit(solution)/shard_map/ppermute | solution.py:57
  296.8 19.8 %collective-permute-start.24 = (f32[16,64,64]{2,0,1:T(8,128)S(1)}, f32[16,64,64]{2,0,1:T(8,128)S(1)}, u32[]{:S(2)}, u32[]{:S(2)}) collective-permute-start(f32[16,64,64]{2,0,1:T(8,128)S(1)} %get-tuple-element.23), channel_id=1, source_target_pairs={{0,32},{64,96},{128,160},{192,224},{16,48},{80,112},{144,176},{208... | collective-permute-start | bytes 786440 | tf_op jit(solution)/shard_map/ppermute | solution.py:57
  297.4 19.2 %collective-permute-start.25 = (f32[16,64,64]{2,0,1:T(8,128)S(1)}, f32[16,64,64]{2,0,1:T(8,128)S(1)}, u32[]{:S(2)}, u32[]{:S(2)}) collective-permute-start(f32[16,64,64]{2,0,1:T(8,128)S(1)} %get-tuple-element.22), channel_id=1, source_target_pairs={{0,16},{64,80},{128,144},{192,208},{16,32},{80,96},{144,160},{208,... | collective-permute-start | bytes 786440 | tf_op jit(solution)/shard_map/ppermute | solution.py:57
  313.1 21.5 %collective-permute-start.35 = (f32[16,64,64]{2,0,1:T(8,128)S(1)}, f32[16,64,64]{2,0,1:T(8,128)S(1)}, u32[]{:S(2)}, u32[]{:S(2)}) collective-permute-start(f32[16,64,64]{2,0,1:T(8,128)S(1)} %get-tuple-element.30), channel_id=1, source_target_pairs={{0,48},{64,112},{128,176},{192,240},{16,0},{80,64},{144,128},{208,... | collective-permute-start | bytes 786440 | tf_op jit(solution)/shard_map/ppermute | solution.py:57
  314.5 20.2 %collective-permute-start.36 = (f32[16,64,64]{2,0,1:T(8,128)S(1)}, f32[16,64,64]{2,0,1:T(8,128)S(1)}, u32[]{:S(2)}, u32[]{:S(2)}) collective-permute-start(f32[16,64,64]{2,0,1:T(8,128)S(1)} %get-tuple-element.29), channel_id=1, source_target_pairs={{0,32},{64,96},{128,160},{192,224},{16,48},{80,112},{144,176},{208... | collective-permute-start | bytes 786440 | tf_op jit(solution)/shard_map/ppermute | solution.py:57
  315.1 21.4 %collective-permute-start.37 = (f32[16,64,64]{2,0,1:T(8,128)S(1)}, f32[16,64,64]{2,0,1:T(8,128)S(1)}, u32[]{:S(2)}, u32[]{:S(2)}) collective-permute-start(f32[16,64,64]{2,0,1:T(8,128)S(1)} %get-tuple-element.28), channel_id=1, source_target_pairs={{0,16},{64,80},{128,144},{192,208},{16,32},{80,96},{144,160},{208,... | collective-permute-start | bytes 786440 | tf_op jit(solution)/shard_map/ppermute | solution.py:57
  343.0 6.7 %collective-permute-start.43 = (f32[7,64,64]{2,0,1:T(8,128)S(1)}, f32[7,64,64]{2,0,1:T(8,128)S(1)}, u32[]{:S(2)}, u32[]{:S(2)}) collective-permute-start(f32[7,64,64]{2,0,1:T(8,128)S(1)} %get-tuple-element.41), channel_id=1, source_target_pairs={{0,64},{16,80},{32,96},{48,112},{64,128},{80,144},{96,160},{112,17... | collective-permute-start | bytes 344072 | tf_op jit(solution)/shard_map/ppermute | solution.py:126
  345.0 8.8 %collective-permute-start.44 = (f32[7,64,64]{2,0,1:T(8,128)S(1)}, f32[7,64,64]{2,0,1:T(8,128)S(1)}, u32[]{:S(2)}, u32[]{:S(2)}) collective-permute-start(f32[7,64,64]{2,0,1:T(8,128)S(1)} %get-tuple-element.42), channel_id=1, source_target_pairs={{64,0},{80,16},{96,32},{112,48},{128,64},{144,80},{160,96},{176,11... | collective-permute-start | bytes 344072 | tf_op jit(solution)/shard_map/ppermute | solution.py:127
  360.4 10.9 %collective-permute-start.47 = (f32[64,64,3]{0,2,1:T(4,128)S(1)}, f32[64,64,3]{0,2,1:T(4,128)S(1)}, u32[]{:S(2)}, u32[]{:S(2)}) collective-permute-start(f32[64,64,3]{0,2,1:T(4,128)S(1)} %slice_select_fusion.18), channel_id=1, source_target_pairs={{0,16},{16,0},{32,48},{48,32},{64,80},{80,64},{96,112},{112,96},{1... | collective-permute-start | bytes 147464 | tf_op jit(solution)/shard_map/ppermute | solution.py:105
  365.3 5.3 collective-permute-start.45
  366.0 6.0 collective-permute-start.46
  390.8 14.1 %collective-permute-start.49 = (f32[64,2,2,4,64]{0,4,3,2,1:T(8,128)S(1)}, f32[64,2,2,4,64]{0,4,3,2,1:T(8,128)S(1)}, u32[]{:S(2)}, u32[]{:S(2)}) collective-permute-start(f32[64,2,2,4,64]{0,4,3,2,1:T(8,128)S(1)} %select_bitcast_fusion.9), channel_id=1, source_target_pairs={{0,4},{1,5},{2,6},{3,7},{4,0},{5,1},{6,2},{7,3},{8,12},{9,13},{10,... | collective-permute-start | bytes 786440 | tf_op jit(solution)/shard_map/ppermute | solution.py:148
  404.9 14.7 %collective-permute-start.50 = (f32[64,2,2,4,64]{0,4,3,2,1:T(8,128)S(1)}, f32[64,2,2,4,64]{0,4,3,2,1:T(8,128)S(1)}, u32[]{:S(2)}, u32[]{:S(2)}) collective-permute-start(f32[64,2,2,4,64]{0,4,3,2,1:T(8,128)S(1)} %bitcast_add_fusion.3), channel_id=1, source_target_pairs={{0,8},{1,9},{2,10},{3,11},{4,12},{5,13},{6,14},{7,15},{8,0},{9,1},... | collective-permute-start | bytes 786440 | tf_op jit(solution)/shard_map/ppermute | solution.py:243
  419.7 16.4 %collective-permute-start.51 = (f32[64,2,2,4,64]{0,4,3,2,1:T(8,128)S(1)}, f32[64,2,2,4,64]{0,4,3,2,1:T(8,128)S(1)}, u32[]{:S(2)}, u32[]{:S(2)}) collective-permute-start(f32[64,2,2,4,64]{0,4,3,2,1:T(8,128)S(1)} %add.495), channel_id=1, source_target_pairs={{0,2},{1,3},{2,0},{3,1},{4,6},{5,7},{6,4},{7,5},{8,10},{9,11},{10,... | collective-permute-start | bytes 786440 | tf_op jit(solution)/shard_map/ppermute | solution.py:243
  437.0 11.5 %collective-permute-start.52 = (f32[64,2,2,4,64]{0,4,3,2,1:T(8,128)S(1)}, f32[64,2,2,4,64]{0,4,3,2,1:T(8,128)S(1)}, u32[]{:S(2)}, u32[]{:S(2)}) collective-permute-start(f32[64,2,2,4,64]{0,4,3,2,1:T(8,128)S(1)} %fusion.6), channel_id=1, source_target_pairs={{0,4},{1,5},{2,6},{3,7},{4,0},{5,1},{6,2},{7,3},{8,12},{9,13},{10,... | collective-permute-start | bytes 786440 | tf_op jit(solution)/shard_map/ppermute | solution.py:156
  452.8 8.3 %collective-permute-start.56 = (f32[64,64,3]{0,2,1:T(4,128)S(1)}, f32[64,64,3]{0,2,1:T(4,128)S(1)}, u32[]{:S(2)}, u32[]{:S(2)}) collective-permute-start(f32[64,64,3]{0,2,1:T(4,128)S(1)} %slice_select_fusion.17), channel_id=1, source_target_pairs={{0,16},{16,0},{32,48},{48,32},{64,80},{80,64},{96,112},{112,96},{1... | collective-permute-start | bytes 147464 | tf_op jit(solution)/shard_map/ppermute | solution.py:105
  455.1 5.3 collective-permute-start.54
  476.0 22.0 %collective-permute-start.57 = (f32[7,64,64]{1,2,0:T(8,128)S(1)}, f32[7,64,64]{1,2,0:T(8,128)S(1)}, u32[]{:S(2)}, u32[]{:S(2)}) collective-permute-start(f32[7,64,64]{1,2,0:T(8,128)S(1)} %get-tuple-element.35), channel_id=1, source_target_pairs={{0,64},{16,80},{32,96},{48,112},{64,128},{80,144},{96,160},{112,17... | collective-permute-start | bytes 344072 | tf_op jit(solution)/shard_map/ppermute | solution.py:126
  494.4 7.9 %collective-permute-start.58 = (f32[7,64,64]{1,2,0:T(8,128)S(1)}, f32[7,64,64]{1,2,0:T(8,128)S(1)}, u32[]{:S(2)}, u32[]{:S(2)}) collective-permute-start(f32[7,64,64]{1,2,0:T(8,128)S(1)} %get-tuple-element.36), channel_id=1, source_target_pairs={{64,0},{80,16},{96,32},{112,48},{128,64},{144,80},{160,96},{176,11... | collective-permute-start | bytes 344072 | tf_op jit(solution)/shard_map/ppermute | solution.py:127
  514.0 6.0 collective-permute-start.59
  516.1 8.3 %collective-permute-start.60 = (f32[7,64,64]{2,0,1:T(8,128)S(1)}, f32[7,64,64]{2,0,1:T(8,128)S(1)}, u32[]{:S(2)}, u32[]{:S(2)}) collective-permute-start(f32[7,64,64]{2,0,1:T(8,128)S(1)} %get-tuple-element.34), channel_id=1, source_target_pairs={{64,0},{80,16},{96,32},{112,48},{128,64},{144,80},{160,96},{176,11... | collective-permute-start | bytes 344072 | tf_op jit(solution)/shard_map/ppermute | solution.py:127
  530.9 10.6 %collective-permute-start.63 = (f32[64,64,3]{0,2,1:T(4,128)S(1)}, f32[64,64,3]{0,2,1:T(4,128)S(1)}, u32[]{:S(2)}, u32[]{:S(2)}) collective-permute-start(f32[64,64,3]{0,2,1:T(4,128)S(1)} %slice_select_fusion.16), channel_id=1, source_target_pairs={{0,16},{16,0},{32,48},{48,32},{64,80},{80,64},{96,112},{112,96},{1... | collective-permute-start | bytes 147464 | tf_op jit(solution)/shard_map/ppermute | solution.py:105
  536.3 6.0 collective-permute-start.62
  561.0 14.1 %collective-permute-start.65 = (f32[64,2,2,4,64]{0,4,3,2,1:T(8,128)S(1)}, f32[64,2,2,4,64]{0,4,3,2,1:T(8,128)S(1)}, u32[]{:S(2)}, u32[]{:S(2)}) collective-permute-start(f32[64,2,2,4,64]{0,4,3,2,1:T(8,128)S(1)} %select_bitcast_fusion.6), channel_id=1, source_target_pairs={{0,4},{1,5},{2,6},{3,7},{4,0},{5,1},{6,2},{7,3},{8,12},{9,13},{10,... | collective-permute-start | bytes 786440 | tf_op jit(solution)/shard_map/ppermute | solution.py:148
  575.2 9.1 %collective-permute-start.66 = (f32[64,2,4,64]{0,3,2,1:T(8,128)S(1)}, f32[64,2,4,64]{0,3,2,1:T(8,128)S(1)}, u32[]{:S(2)}, u32[]{:S(2)}) collective-permute-start(f32[64,2,4,64]{0,3,2,1:T(8,128)S(1)} %select_bitcast_fusion.12), channel_id=1, source_target_pairs={{0,8},{1,9},{2,10},{3,11},{4,12},{5,13},{6,14},{7,15},{8,0},{9,1},... | collective-permute-start | bytes 393224 | tf_op jit(solution)/shard_map/ppermute | solution.py:148
  584.4 9.6 %collective-permute-start.67 = (f32[64,4,64]{0,2,1:T(8,128)S(1)}, f32[64,4,64]{0,2,1:T(8,128)S(1)}, u32[]{:S(2)}, u32[]{:S(2)}) collective-permute-start(f32[64,4,64]{0,2,1:T(8,128)S(1)} %select_bitcast_fusion.16), channel_id=1, source_target_pairs={{0,2},{1,3},{2,0},{3,1},{4,6},{5,7},{6,4},{7,5},{8,10},{9,11},{10,... | collective-permute-start | bytes 196616 | tf_op jit(solution)/shard_map/ppermute | solution.py:148
  595.7 14.3 %collective-permute-start.68 = (f32[64,4,64]{0,2,1:T(8,128)S(1)}, f32[64,4,64]{0,2,1:T(8,128)S(1)}, u32[]{:S(2)}, u32[]{:S(2)}) collective-permute-start(f32[64,4,64]{0,2,1:T(8,128)S(1)} %get-tuple-element.76), channel_id=1, source_target_pairs={{0,48},{16,0},{32,16},{48,32},{64,112},{80,64},{96,80},{112,96},{1... | collective-permute-start | bytes 196616 | tf_op jit(solution)/shard_map/ppermute | solution.py:47
  597.3 12.6 %collective-permute-start.69 = (f32[64,4,64]{0,2,1:T(8,128)S(1)}, f32[64,4,64]{0,2,1:T(8,128)S(1)}, u32[]{:S(2)}, u32[]{:S(2)}) collective-permute-start(f32[64,4,64]{0,2,1:T(8,128)S(1)} %get-tuple-element.75), channel_id=1, source_target_pairs={{0,32},{16,48},{32,0},{48,16},{64,96},{80,112},{96,64},{112,80},{1... | collective-permute-start | bytes 196616 | tf_op jit(solution)/shard_map/ppermute | solution.py:47
  599.6 10.3 %collective-permute-start.70 = (f32[64,4,64]{0,2,1:T(8,128)S(1)}, f32[64,4,64]{0,2,1:T(8,128)S(1)}, u32[]{:S(2)}, u32[]{:S(2)}) collective-permute-start(f32[64,4,64]{0,2,1:T(8,128)S(1)} %get-tuple-element.17), channel_id=1, source_target_pairs={{0,16},{16,32},{32,48},{48,0},{64,80},{80,96},{96,112},{112,64},{1... | collective-permute-start | bytes 196616 | tf_op jit(solution)/shard_map/ppermute | solution.py:47
  610.0 5.5 collective-permute-start.71
  610.1 11.1 %collective-permute-start.72 = (f32[64,4,64]{0,2,1:T(8,128)S(1)}, f32[64,4,64]{0,2,1:T(8,128)S(1)}, u32[]{:S(2)}, u32[]{:S(2)}) collective-permute-start(f32[64,4,64]{0,2,1:T(8,128)S(1)} %get-tuple-element.66), channel_id=1, source_target_pairs={{0,128},{16,144},{32,160},{48,176},{64,192},{80,208},{96,224},{112... | collective-permute-start | bytes 196616 | tf_op jit(solution)/shard_map/ppermute | solution.py:57
  611.2 10.0 %collective-permute-start.73 = (f32[64,4,64]{0,2,1:T(8,128)S(1)}, f32[64,4,64]{0,2,1:T(8,128)S(1)}, u32[]{:S(2)}, u32[]{:S(2)}) collective-permute-start(f32[64,4,64]{0,2,1:T(8,128)S(1)} %get-tuple-element.65), channel_id=1, source_target_pairs={{0,64},{16,80},{32,96},{48,112},{64,128},{80,144},{96,160},{112,17... | collective-permute-start | bytes 196616 | tf_op jit(solution)/shard_map/ppermute | solution.py:57
  (30 other events, 320.0 us)

commit v12 on v10

--- a/solution.py
+++ b/solution.py
@@ -18,10 +18,9 @@
 def gather_rows(row, axis, n):
     me = lax.axis_index(axis)
     buf = jnp.where(jnp.arange(n)[:, None] == me, row, jnp.zeros_like(row))
-    m = 1
-    while m < n:
-        buf = buf + lax.ppermute(buf, axis, xor_pairs(n, m))
-        m *= 2
+    for shift in (0, 2):
+        step = [lax.ppermute(buf, axis, xor_pairs(n, t << shift)) for t in (1, 2, 3)]
+        buf = buf + step[0] + step[1] + step[2]
     return buf
 
 

time: 624 us -> 624 us (level)
  starting transfers between devices: 147 us -> 129 us
  waiting for transfers between devices: 257 us -> 275 us
    ppermute x36, starting transfers between devices: 70.2 us -> 60.9 us  [route(): part = lax.ppermute(part, 'space', pairs)]
    ppermute x8, starting transfers between devices: 15.7 us -> 6.67 us  [view_reduce_scatter(): x = keep + lax.ppermute(send, 'view', xor_pairs(nv, m))]
    ppermute x12, starting transfers between devices: 20.1 us -> 28.8 us  [swap(): return lax.ppermute(x, 'space', [(i, i ^ partner) for i in range(nsp)])]
    ppermute x8, starting transfers between devices: 18.4 us -> 10.2 us  [view_all_gather(): recv = lax.ppermute(x, 'view', xor_pairs(nv, m))]
    ppermute x8, waiting for transfers between devices: 56.4 us -> 64.6 us  [view_reduce_scatter(): x = keep + lax.ppermute(send, 'view', xor_pairs(nv, m))]
    ppermute x8, waiting for transfers between devices: 30.5 us -> 38.5 us  [view_all_gather(): recv = lax.ppermute(x, 'view', xor_pairs(nv, m))]
  transfers between devices with their start and end apart: 76 -> 78, of which waited for: 42 -> 39; matrix products, arithmetic and copies ran while one was open for 14% -> 14% of each run, Pallas kernels for 0% -> 0%
where the time goes in v12:
time: 624 us; the launch traced here: 614 us
  waiting for transfers between devices  275 us (44%)
  starting transfers between devices  129 us (21%)
  other arithmetic  69.9 us (11%)
  matrix products  61.5 us (10%)
  local copies, waits for them, and re-layouts  39.4 us (6%)
  between operations  38.6 us (6%)
    ppermute x36, waiting for transfers between devices, route(): part = lax.ppermute(part, 'space', pairs)  128 us
    ppermute x8, waiting for transfers between devices, view_reduce_scatter(): x = keep + lax.ppermute(send, 'view', xor_pairs(nv, m))  64.6 us
    ppermute x36, starting transfers between devices, route(): part = lax.ppermute(part, 'space', pairs)  60.9 us
    ppermute x8, waiting for transfers between devices, view_all_gather(): recv = lax.ppermute(x, 'view', xor_pairs(nv, m))  38.5 us
    ppermute x12, starting transfers between devices, swap(): return lax.ppermute(x, 'space', [(i, i ^ partner) for i in range(nsp)])  28.8 us
    dot_general x4, matrix products, convolve(): return jnp.einsum('ot,atb->aob', band, extended, precision=hi)  20.9 us
    dot_general x4, matrix products, convolve(): return jnp.einsum('abt,ot->abo', extended, band, precision=hi)  19.6 us
    select_n x3, other arithmetic, band_matrix(): band = jnp.where(offset == position, weight, band)  18.9 us
  transfers between devices with their start and end apart: 78, of which 39 were waited for; matrix products, arithmetic and copies ran while one was open for 14% of the time, Pallas kernels for 0%

profile of v12, /device:TPU:8, one launch (start us, length us, event | category | flops | bytes accessed | tf_op | source)
XLA Modules:
  0.0 613.6 jit_solution(13060296971650938680)
XLA Ops:
  12.9 4.4 select_select_fusion.25
  17.4 4.4 select_select_fusion.23
  23.7 3.3 collective-permute-start.4
  28.5 3.8 collective-permute-done.5
  43.7 2.6 collective-permute-start.8
  46.3 10.1 %select_select_fusion.27 = (f32[64,78]{1,0:T(8,128)S(1)}, f32[64,78]{1,0:T(8,128)}) fusion(f32[]{:T(128)} %bitcast.40, f32[]{:T(128)} %bitcast.39, f32[]{:T(128)} %bitcast.38, f32[]{:T(128)} %bitcast.37, f32[]{:T(128)} %bitcast.36, f32[]{:T(128)} %bitcast.35, f32[]{:T(128)} %bitcast.34, f32[]{:T(128)} %bitcast.33, f32[]{:T(128)} %bitcast.32, f32[]{:T(128)} %bitcast.31, ...), kind=kLoop, calls=%fused_computation.182 | loop fusion | flops 229632 | bytes 39996 | tf_op jit(solution)/shard_map/jit(_where)/select_n | solution.py:67
  63.1 3.3 collective-permute-start.9
  73.7 4.6 collective-permute-start.36
  89.2 18.3 %collective-permute-done.24 = f32[16,64,64]{2,0,1:T(8,128)S(1)} collective-permute-done((f32[16,64,64]{2,0,1:T(8,128)}, f32[16,64,64]{2,0,1:T(8,128)S(1)}, u32[]{:S(2)}, u32[]{:S(2)}) %collective-permute-start.24) | collective-permute-done | bytes 262176 | tf_op jit(solution)/shard_map/ppermute | solution.py:46
  107.6 3.0 collective-permute-start.37
  112.8 3.0 collective-permute-start.28
  117.8 13.3 %collective-permute-done.27 = f32[16,64,64]{2,0,1:T(8,128)S(1)} collective-permute-done((f32[16,64,64]{2,0,1:T(8,128)S(1)}, f32[16,64,64]{2,0,1:T(8,128)S(1)}, u32[]{:S(2)}, u32[]{:S(2)}) %collective-permute-start.27) | collective-permute-done | bytes 262176 | tf_op jit(solution)/shard_map/ppermute | solution.py:56
  131.1 30.0 %collective-permute-done.28 = f32[16,64,64]{2,0,1:T(8,128)S(1)} collective-permute-done((f32[16,64,64]{2,0,1:T(8,128)S(1)}, f32[16,64,64]{2,0,1:T(8,128)S(1)}, u32[]{:S(2)}, u32[]{:S(2)}) %collective-permute-start.28) | collective-permute-done | bytes 262176 | tf_op jit(solution)/shard_map/ppermute | solution.py:56
  163.8 6.4 %collective-permute-done.38 = f32[64,2,2,4,64]{0,4,3,2,1:T(8,128)S(1)} collective-permute-done((f32[64,2,2,4,64]{0,4,3,2,1:T(8,128)S(1)}, f32[64,2,2,4,64]{0,4,3,2,1:T(8,128)S(1)}, u32[]{:S(2)}, u32[]{:S(2)}) %collective-permute-start.38) | collective-permute-done | bytes 262176 | tf_op jit(solution)/shard_map/ppermute | solution.py:160
  172.9 2.6 select_select_fusion.13
  175.5 3.2 collective-permute-start.15
  178.7 6.6 %collective-permute-start.16 = (f32[16,64,64]{2,0,1:T(8,128)}, f32[16,64,64]{2,0,1:T(8,128)}, u32[]{:S(2)}, u32[]{:S(2)}) collective-permute-start(f32[16,64,64]{2,0,1:T(8,128)} %get-tuple-element.20), channel_id=1, source_target_pairs={{0,128},{16,144},{32,160},{48,176},{64,192},{80,208},{96,224},{112... | collective-permute-start | bytes 786440 | tf_op jit(solution)/shard_map/ppermute | solution.py:56
  189.6 3.1 collective-permute-done.40
  192.7 11.5 %collective-permute-start.42 = (f32[64,64,3]{0,2,1:T(4,128)S(1)}, f32[64,64,3]{0,2,1:T(4,128)S(1)}, u32[]{:S(2)}, u32[]{:S(2)}) collective-permute-start(f32[64,64,3]{0,2,1:T(4,128)S(1)} %slice_select_fusion.19), channel_id=1, source_target_pairs={{0,16},{16,0},{32,48},{48,32},{64,80},{80,64},{96,112},{112,96},{1... | collective-permute-start | bytes 147464 | tf_op jit(solution)/shard_map/ppermute | solution.py:104
  208.2 3.6 collective-permute-done.41
  216.4 3.4 copy.52
  219.8 7.9 %fusion.40 = f32[64,70,64]{1,2,0:T(8,128)S(1)} fusion(f32[64,70,70]{2,1,0:T(8,128)} %copy.52, f32[64,70]{1,0:T(8,128)S(1)} %get-tuple-element.13), kind=kOutput, calls=%fused_computation.166 | convolution fusion | flops 240844800 | bytes 2419200 | tf_op jit(solution)/shard_map/abt,ot->abo/dot_general | solution.py:77
  227.8 3.2 convolution_bitcast_fusion.1
  232.8 2.6 collective-permute-start.43
  251.7 2.8 collective-permute-start.30
  256.2 3.6 pad_maximum_fusion.6
  259.8 4.4 copy.39
  264.7 25.9 %collective-permute-done.19 = f32[16,64,64]{2,0,1:T(8,128)} collective-permute-done((f32[16,64,64]{2,0,1:T(8,128)}, f32[16,64,64]{2,0,1:T(8,128)}, u32[]{:S(2)}, u32[]{:S(2)}) %collective-permute-start.19) | collective-permute-done | bytes 262176 | tf_op jit(solution)/shard_map/ppermute | solution.py:46
  291.9 3.5 collective-permute-start.21
  297.0 13.7 %collective-permute-done.31 = f32[16,64,64]{2,0,1:T(8,128)S(1)} collective-permute-done((f32[16,64,64]{2,0,1:T(8,128)}, f32[16,64,64]{2,0,1:T(8,128)S(1)}, u32[]{:S(2)}, u32[]{:S(2)}) %collective-permute-start.31) | collective-permute-done | bytes 262176 | tf_op jit(solution)/shard_map/ppermute | solution.py:46
  314.4 2.5 collective-permute-start.35
  317.3 9.0 %collective-permute-done.33 = f32[16,64,64]{2,0,1:T(8,128)S(1)} collective-permute-done((f32[16,64,64]{2,0,1:T(8,128)S(1)}, f32[16,64,64]{2,0,1:T(8,128)S(1)}, u32[]{:S(2)}, u32[]{:S(2)}) %collective-permute-start.33) | collective-permute-done | bytes 262176 | tf_op jit(solution)/shard_map/ppermute | solution.py:56
  326.3 9.2 %collective-permute-done.34 = f32[16,64,64]{2,0,1:T(8,128)S(1)} collective-permute-done((f32[16,64,64]{2,0,1:T(8,128)S(1)}, f32[16,64,64]{2,0,1:T(8,128)S(1)}, u32[]{:S(2)}, u32[]{:S(2)}) %collective-permute-start.34) | collective-permute-done | bytes 262176 | tf_op jit(solution)/shard_map/ppermute | solution.py:56
  338.4 6.1 convolution_divide_fusion.1
  347.1 3.6 collective-permute-done.45
  350.8 4.1 collective-permute-done.46
  357.4 3.4 fusion.91
  361.4 4.0 collective-permute-start.49
  368.5 3.0 collective-permute-done.47
  376.2 7.9 %fusion.34 = f32[64,70,64]{1,2,0:T(8,128)S(1)} fusion(f32[64,70,70]{1,2,0:T(8,128)} %copy.53, f32[64,70]{1,0:T(8,128)S(1)} %get-tuple-element.15), kind=kOutput, calls=%fused_computation.160 | convolution fusion | flops 240844800 | bytes 2419200 | tf_op jit(solution)/shard_map/ot,atb->aob/dot_general | solution.py:76
  388.6 2.6 collective-permute-done.50
  391.7 14.0 %collective-permute-done.51 = f32[64,2,2,4,64]{0,4,3,2,1:T(8,128)S(1)} collective-permute-done((f32[64,2,2,4,64]{0,4,3,2,1:T(8,128)S(1)}, f32[64,2,2,4,64]{0,4,3,2,1:T(8,128)S(1)}, u32[]{:S(2)}, u32[]{:S(2)}) %collective-permute-start.51) | collective-permute-done | bytes 262176 | tf_op jit(solution)/shard_map/ppermute | solution.py:150
  406.6 8.5 %collective-permute-done.52 = f32[64,2,4,64]{0,3,2,1:T(8,128)S(1)} collective-permute-done((f32[64,2,4,64]{0,3,2,1:T(8,128)S(1)}, f32[64,2,4,64]{0,3,2,1:T(8,128)S(1)}, u32[]{:S(2)}, u32[]{:S(2)}) %collective-permute-start.52) | collective-permute-done | bytes 131104 | tf_op jit(solution)/shard_map/ppermute | solution.py:150
  416.0 8.8 %collective-permute-done.53 = f32[64,4,64]{0,2,1:T(8,128)S(1)} collective-permute-done((f32[64,4,64]{0,2,1:T(8,128)S(1)}, f32[64,4,64]{0,2,1:T(8,128)S(1)}, u32[]{:S(2)}, u32[]{:S(2)}) %collective-permute-start.53) | collective-permute-done | bytes 65568 | tf_op jit(solution)/shard_map/ppermute | solution.py:150
  425.5 10.2 %collective-permute-done.54 = f32[64,4,64]{0,2,1:T(8,128)S(1)} collective-permute-done((f32[64,4,64]{0,2,1:T(8,128)S(1)}, f32[64,4,64]{0,2,1:T(8,128)S(1)}, u32[]{:S(2)}, u32[]{:S(2)}) %collective-permute-start.54) | collective-permute-done | bytes 65568 | tf_op jit(solution)/shard_map/ppermute | solution.py:160
  435.9 10.6 %collective-permute-done.55 = f32[64,2,4,64]{0,3,2,1:T(8,128)S(1)} collective-permute-done((f32[64,2,4,64]{0,3,2,1:T(8,128)S(1)}, f32[64,2,4,64]{0,3,2,1:T(8,128)S(1)}, u32[]{:S(2)}, u32[]{:S(2)}) %collective-permute-start.55) | collective-permute-done | bytes 131104 | tf_op jit(solution)/shard_map/ppermute | solution.py:160
  447.4 8.5 %collective-permute-done.56 = f32[64,2,2,4,64]{0,4,3,2,1:T(8,128)S(1)} collective-permute-done((f32[64,2,2,4,64]{0,4,3,2,1:T(8,128)S(1)}, f32[64,2,2,4,64]{0,4,3,2,1:T(8,128)S(1)}, u32[]{:S(2)}, u32[]{:S(2)}) %collective-permute-start.56) | collective-permute-done | bytes 262176 | tf_op jit(solution)/shard_map/ppermute | solution.py:160
  456.2 2.6 collective-permute-done.57
  473.8 7.9 %fusion.38 = f32[64,70,64]{1,2,0:T(8,128)S(1)} fusion(f32[64,70,70]{2,1,0:T(8,128)} %copy.54, f32[64,70]{1,0:T(8,128)S(1)} %get-tuple-element.13), kind=kOutput, calls=%fused_computation.164 | convolution fusion | flops 240844800 | bytes 2419200 | tf_op jit(solution)/shard_map/abt,ot->abo/dot_general | solution.py:77
  489.8 4.2 collective-permute-done.62
  494.3 3.3 copy.47
  497.6 8.1 %convolution_divide_fusion = f32[64,64,64]{2,0,1:T(8,128)S(1)} fusion(f32[78,64,64]{0,2,1:T(8,128)} %copy.47, f32[16,64,64]{2,0,1:T(8,128)} %copy-done.12, f32[16,64,64]{2,0,1:T(8,128)S(1)} %copy-done.9, f32[16,64,64]{2,0,1:T(8,128)} %copy-done.11, f32[16,64,64]{2,0,1:T(8,128)} %get-tuple-element.43, f32[64,78]{1,0:T(8,128)S(1)} %copy-done.17), kind=kOutput, calls=%fused_computation.18 | convolution fusion | flops 246415360 | bytes 3395072 | tf_op jit(solution)/shard_map/ot,tab->oab/dot_general | solution.py:74
  509.1 2.6 collective-permute-done.63
  511.7 4.4 collective-permute-done.64
  518.6 3.4 fusion.92
  522.7 3.6 collective-permute-start.67
  529.4 2.8 collective-permute-done.65
  536.9 7.9 %fusion.32 = f32[64,70,64]{1,2,0:T(8,128)S(1)} fusion(f32[64,70,70]{1,2,0:T(8,128)} %copy.55, f32[64,70]{1,0:T(8,128)S(1)} %get-tuple-element.15), kind=kOutput, calls=%fused_computation.158 | convolution fusion | flops 240844800 | bytes 2419200 | tf_op jit(solution)/shard_map/ot,atb->aob/dot_general | solution.py:76
  549.3 2.6 collective-permute-done.68
  553.6 12.8 %collective-permute-done.69 = f32[64,2,2,4,64]{0,4,3,2,1:T(8,128)S(1)} collective-permute-done((f32[64,2,2,4,64]{0,4,3,2,1:T(8,128)S(1)}, f32[64,2,2,4,64]{0,4,3,2,1:T(8,128)S(1)}, u32[]{:S(2)}, u32[]{:S(2)}) %collective-permute-start.69) | collective-permute-done | bytes 262176 | tf_op jit(solution)/shard_map/ppermute | solution.py:150
  566.5 2.6 collective-permute-start.70
  569.1 6.5 %collective-permute-done.70 = f32[64,2,4,64]{0,3,2,1:T(8,128)S(1)} collective-permute-done((f32[64,2,4,64]{0,3,2,1:T(8,128)S(1)}, f32[64,2,4,64]{0,3,2,1:T(8,128)S(1)}, u32[]{:S(2)}, u32[]{:S(2)}) %collective-permute-start.70) | collective-permute-done | bytes 131104 | tf_op jit(solution)/shard_map/ppermute | solution.py:150
  577.2 8.7 %collective-permute-done.71 = f32[64,4,64]{0,2,1:T(8,128)S(1)} collective-permute-done((f32[64,4,64]{0,2,1:T(8,128)S(1)}, f32[64,4,64]{0,2,1:T(8,128)S(1)}, u32[]{:S(2)}, u32[]{:S(2)}) %collective-permute-start.71) | collective-permute-done | bytes 65568 | tf_op jit(solution)/shard_map/ppermute | solution.py:150
  608.1 4.4 collective-permute-done.76
  (287 shorter events, 158.1 us)
Async XLA Ops:
  1.5 20.3 %collective-permute-start = (s32[16,7]{0,1:T(8,128)S(1)}, s32[16,7]{0,1:T(8,128)S(1)}, u32[]{:S(2)}, u32[]{:S(2)}) collective-permute-start(s32[16,7]{0,1:T(8,128)S(1)} %broadcast_select_fusion.22), channel_id=1, source_target_pairs={{0,16},{16,0},{32,48},{48,32},{64,80},{80,64},{96,112},{112,96},{1... | collective-permute-start | bytes 1352 | tf_op jit(solution)/shard_map/ppermute | solution.py:22
  3.7 18.2 %collective-permute-start.1 = (s32[16,7]{0,1:T(8,128)S(1)}, s32[16,7]{0,1:T(8,128)S(1)}, u32[]{:S(2)}, u32[]{:S(2)}) collective-permute-start(s32[16,7]{0,1:T(8,128)S(1)} %broadcast_select_fusion.22), channel_id=1, source_target_pairs={{0,32},{16,48},{32,0},{48,16},{64,96},{80,112},{96,64},{112,80},{1... | collective-permute-start | bytes 1352 | tf_op jit(solution)/shard_map/ppermute | solution.py:22
  4.5 17.3 %collective-permute-start.2 = (s32[16,7]{0,1:T(8,128)S(1)}, s32[16,7]{0,1:T(8,128)S(1)}, u32[]{:S(2)}, u32[]{:S(2)}) collective-permute-start(s32[16,7]{0,1:T(8,128)S(1)} %broadcast_select_fusion.22), channel_id=1, source_target_pairs={{0,48},{16,32},{32,16},{48,0},{64,112},{80,96},{96,80},{112,64},{1... | collective-permute-start | bytes 1352 | tf_op jit(solution)/shard_map/ppermute | solution.py:22
  39.1 23.2 %collective-permute-start.6 = (f32[64,4,64]{0,2,1:T(8,128)S(1)}, f32[64,4,64]{0,2,1:T(8,128)S(1)}, u32[]{:S(2)}, u32[]{:S(2)}) collective-permute-start(f32[64,4,64]{0,2,1:T(8,128)S(1)} %bitcast.290), channel_id=1, source_target_pairs={{0,48},{16,0},{32,16},{48,32},{64,112},{80,64},{96,80},{112,96},{1... | collective-permute-start | bytes 196616 | tf_op jit(solution)/shard_map/ppermute | solution.py:46
  40.9 21.4 %collective-permute-start.7 = (f32[64,4,64]{0,2,1:T(8,128)S(1)}, f32[64,4,64]{0,2,1:T(8,128)S(1)}, u32[]{:S(2)}, u32[]{:S(2)}) collective-permute-start(f32[64,4,64]{0,2,1:T(8,128)S(1)} %bitcast.291), channel_id=1, source_target_pairs={{0,32},{16,48},{32,0},{48,16},{64,96},{80,112},{96,64},{112,80},{1... | collective-permute-start | bytes 196616 | tf_op jit(solution)/shard_map/ppermute | solution.py:46
  43.7 18.7 %collective-permute-start.8 = (f32[64,4,64]{0,2,1:T(8,128)}, f32[64,4,64]{0,2,1:T(8,128)S(1)}, u32[]{:S(2)}, u32[]{:S(2)}) collective-permute-start(f32[64,4,64]{0,2,1:T(8,128)} %bitcast.259), channel_id=1, source_target_pairs={{0,16},{16,32},{32,48},{48,0},{64,80},{80,96},{96,112},{112,64},{1... | collective-permute-start | bytes 196616 | tf_op jit(solution)/shard_map/ppermute | solution.py:46
  62.4 10.3 %collective-permute-start.10 = (f32[64,4,64]{0,2,1:T(8,128)S(1)}, f32[64,4,64]{0,2,1:T(8,128)S(1)}, u32[]{:S(2)}, u32[]{:S(2)}) collective-permute-start(f32[64,4,64]{0,2,1:T(8,128)S(1)} %get-tuple-element.73), channel_id=1, source_target_pairs={{0,128},{16,144},{32,160},{48,176},{64,192},{80,208},{96,224},{112... | collective-permute-start | bytes 196616 | tf_op jit(solution)/shard_map/ppermute | solution.py:56
  62.5 10.2 %collective-permute-start.11 = (f32[64,4,64]{0,2,1:T(8,128)S(1)}, f32[64,4,64]{0,2,1:T(8,128)S(1)}, u32[]{:S(2)}, u32[]{:S(2)}) collective-permute-start(f32[64,4,64]{0,2,1:T(8,128)S(1)} %get-tuple-element.72), channel_id=1, source_target_pairs={{0,64},{16,80},{32,96},{48,112},{64,128},{80,144},{96,160},{112,17... | collective-permute-start | bytes 196616 | tf_op jit(solution)/shard_map/ppermute | solution.py:56
  63.1 9.6 %collective-permute-start.9 = (f32[64,4,64]{0,2,1:T(8,128)S(1)}, f32[64,4,64]{0,2,1:T(8,128)}, u32[]{:S(2)}, u32[]{:S(2)}) collective-permute-start(f32[64,4,64]{0,2,1:T(8,128)S(1)} %get-tuple-element.74), channel_id=1, source_target_pairs={{0,192},{16,208},{32,224},{48,240},{64,0},{80,16},{96,32},{112,48}... | collective-permute-start | bytes 196616 | tf_op jit(solution)/shard_map/ppermute | solution.py:56
  73.7 12.4 %collective-permute-start.36 = (f32[64,4,64]{0,2,1:T(8,128)S(1)}, f32[64,4,64]{0,2,1:T(8,128)}, u32[]{:S(2)}, u32[]{:S(2)}) collective-permute-start(f32[64,4,64]{0,2,1:T(8,128)S(1)} %fusion.15), channel_id=1, source_target_pairs={{0,2},{1,3},{2,0},{3,1},{4,6},{5,7},{6,4},{7,5},{8,10},{9,11},{10,... | collective-permute-start | bytes 196616 | tf_op jit(solution)/shard_map/ppermute | solution.py:160
  81.1 26.4 %collective-permute-start.24 = (f32[16,64,64]{2,0,1:T(8,128)}, f32[16,64,64]{2,0,1:T(8,128)S(1)}, u32[]{:S(2)}, u32[]{:S(2)}) collective-permute-start(f32[16,64,64]{2,0,1:T(8,128)} %get-tuple-element.54), channel_id=1, source_target_pairs={{0,48},{16,0},{32,16},{48,32},{64,112},{80,64},{96,80},{112,96},{1... | collective-permute-start | bytes 786440 | tf_op jit(solution)/shard_map/ppermute | solution.py:46
  81.6 29.0 %collective-permute-start.25 = (f32[16,64,64]{2,0,1:T(8,128)}, f32[16,64,64]{2,0,1:T(8,128)}, u32[]{:S(2)}, u32[]{:S(2)}) collective-permute-start(f32[16,64,64]{2,0,1:T(8,128)} %get-tuple-element.50), channel_id=1, source_target_pairs={{0,32},{16,48},{32,0},{48,16},{64,96},{80,112},{96,64},{112,80},{1... | collective-permute-start | bytes 786440 | tf_op jit(solution)/shard_map/ppermute | solution.py:46
  82.3 28.3 %collective-permute-start.26 = (f32[16,64,64]{2,0,1:T(8,128)}, f32[16,64,64]{2,0,1:T(8,128)}, u32[]{:S(2)}, u32[]{:S(2)}) collective-permute-start(f32[16,64,64]{2,0,1:T(8,128)} %get-tuple-element.51), channel_id=1, source_target_pairs={{0,16},{16,32},{32,48},{48,0},{64,80},{80,96},{96,112},{112,64},{1... | collective-permute-start | bytes 786440 | tf_op jit(solution)/shard_map/ppermute | solution.py:46
  84.8 86.5 %collective-permute-start.12 = (f32[16,64,64]{2,0,1:T(8,128)}, f32[16,64,64]{2,0,1:T(8,128)S(1)}, u32[]{:S(2)}, u32[]{:S(2)}) collective-permute-start(f32[16,64,64]{2,0,1:T(8,128)} %get-tuple-element.56), channel_id=1, source_target_pairs={{0,48},{16,0},{32,16},{48,32},{64,112},{80,64},{96,80},{112,96},{1... | collective-permute-start | bytes 786440 | tf_op jit(solution)/shard_map/ppermute | solution.py:46
  86.1 85.9 %collective-permute-start.13 = (f32[16,64,64]{2,0,1:T(8,128)}, f32[16,64,64]{2,0,1:T(8,128)S(1)}, u32[]{:S(2)}, u32[]{:S(2)}) collective-permute-start(f32[16,64,64]{2,0,1:T(8,128)} %get-tuple-element.48), channel_id=1, source_target_pairs={{0,32},{16,48},{32,0},{48,16},{64,96},{80,112},{96,64},{112,80},{1... | collective-permute-start | bytes 786440 | tf_op jit(solution)/shard_map/ppermute | solution.py:46
  107.6 8.2 %collective-permute-start.37 = (f32[64,2,4,64]{0,3,2,1:T(8,128)S(1)}, f32[64,2,4,64]{0,3,2,1:T(8,128)S(1)}, u32[]{:S(2)}, u32[]{:S(2)}) collective-permute-start(f32[64,2,4,64]{0,3,2,1:T(8,128)S(1)} %pad_maximum_fusion.15), channel_id=1, source_target_pairs={{0,8},{1,9},{2,10},{3,11},{4,12},{5,13},{6,14},{7,15},{8,0},{9,1},... | collective-permute-start | bytes 393224 | tf_op jit(solution)/shard_map/ppermute | solution.py:160
  112.0 19.1 %collective-permute-start.27 = (f32[16,64,64]{2,0,1:T(8,128)S(1)}, f32[16,64,64]{2,0,1:T(8,128)S(1)}, u32[]{:S(2)}, u32[]{:S(2)}) collective-permute-start(f32[16,64,64]{2,0,1:T(8,128)S(1)} %get-tuple-element.27), channel_id=1, source_target_pairs={{0,192},{16,208},{32,224},{48,240},{64,0},{80,16},{96,32},{112,48}... | collective-permute-start | bytes 786440 | tf_op jit(solution)/shard_map/ppermute | solution.py:56
  112.8 48.3 %collective-permute-start.28 = (f32[16,64,64]{2,0,1:T(8,128)S(1)}, f32[16,64,64]{2,0,1:T(8,128)S(1)}, u32[]{:S(2)}, u32[]{:S(2)}) collective-permute-start(f32[16,64,64]{2,0,1:T(8,128)S(1)} %get-tuple-element.26), channel_id=1, source_target_pairs={{0,128},{16,144},{32,160},{48,176},{64,192},{80,208},{96,224},{112... | collective-permute-start | bytes 786440 | tf_op jit(solution)/shard_map/ppermute | solution.py:56
  115.8 46.7 %collective-permute-start.29 = (f32[16,64,64]{2,0,1:T(8,128)S(1)}, f32[16,64,64]{2,0,1:T(8,128)S(1)}, u32[]{:S(2)}, u32[]{:S(2)}) collective-permute-start(f32[16,64,64]{2,0,1:T(8,128)S(1)} %get-tuple-element.25), channel_id=1, source_target_pairs={{0,64},{16,80},{32,96},{48,112},{64,128},{80,144},{96,160},{112,17... | collective-permute-start | bytes 786440 | tf_op jit(solution)/shard_map/ppermute | solution.py:56
  131.1 133.2 %collective-permute-start.18 = (f32[16,64,64]{2,0,1:T(8,128)}, f32[16,64,64]{2,0,1:T(8,128)S(1)}, u32[]{:S(2)}, u32[]{:S(2)}) collective-permute-start(f32[16,64,64]{2,0,1:T(8,128)} %get-tuple-element.55), channel_id=1, source_target_pairs={{0,192},{64,0},{128,64},{192,128},{16,208},{80,16},{144,80},{208,1... | collective-permute-start | bytes 786440 | tf_op jit(solution)/shard_map/ppermute | solution.py:46
  161.1 9.2 %collective-permute-start.38 = (f32[64,2,2,4,64]{0,4,3,2,1:T(8,128)S(1)}, f32[64,2,2,4,64]{0,4,3,2,1:T(8,128)S(1)}, u32[]{:S(2)}, u32[]{:S(2)}) collective-permute-start(f32[64,2,2,4,64]{0,4,3,2,1:T(8,128)S(1)} %pad_maximum_fusion.13), channel_id=1, source_target_pairs={{0,4},{1,5},{2,6},{3,7},{4,0},{5,1},{6,2},{7,3},{8,12},{9,13},{10,... | collective-permute-start | bytes 786440 | tf_op jit(solution)/shard_map/ppermute | solution.py:160
  163.7 9.2 %collective-permute-start.14 = (f32[16,64,64]{2,0,1:T(8,128)S(1)}, f32[16,64,64]{2,0,1:T(8,128)S(1)}, u32[]{:S(2)}, u32[]{:S(2)}) collective-permute-start(f32[16,64,64]{2,0,1:T(8,128)S(1)} %get-tuple-element.46), channel_id=1, source_target_pairs={{0,16},{16,32},{32,48},{48,0},{64,80},{80,96},{96,112},{112,64},{1... | collective-permute-start | bytes 786440 | tf_op jit(solution)/shard_map/ppermute | solution.py:46
  170.4 14.8 %collective-permute-start.39 = (f32[64,2,2,2,4,64]{0,5,4,3,1,2:T(8,128)S(1)}, f32[64,2,2,2,4,64]{0,5,4,3,1,2:T(8,128)S(1)}, u32[]{:S(2)}, u32[]{:S(2)}) collective-permute-start(f32[64,2,2,2,4,64]{0,5,4,3,1,2:T(8,128)S(1)} %pad_maximum_fusion.11), channel_id=1, source_target_pairs={{0,1},{1,0},{2,3},{3,2},{4,5},{5,4},{6,7},{7,6},{8,9},{9,8},{10,11... | collective-permute-start | bytes 1572872 | tf_op jit(solution)/shard_map/ppermute | solution.py:160
  172.0 92.7 %collective-permute-start.20 = (f32[16,64,64]{2,0,1:T(8,128)}, f32[16,64,64]{2,0,1:T(8,128)S(1)}, u32[]{:S(2)}, u32[]{:S(2)}) collective-permute-start(f32[16,64,64]{2,0,1:T(8,128)} %get-tuple-element.49), channel_id=1, source_target_pairs={{0,64},{64,128},{128,192},{192,0},{16,80},{80,144},{144,208},{208,... | collective-permute-start | bytes 786440 | tf_op jit(solution)/shard_map/ppermute | solution.py:46
  175.5 57.3 %collective-permute-start.15 = (f32[16,64,64]{2,0,1:T(8,128)}, f32[16,64,64]{2,0,1:T(8,128)}, u32[]{:S(2)}, u32[]{:S(2)}) collective-permute-start(f32[16,64,64]{2,0,1:T(8,128)} %get-tuple-element.21), channel_id=1, source_target_pairs={{0,192},{16,208},{32,224},{48,240},{64,0},{80,16},{96,32},{112,48}... | collective-permute-start | bytes 786440 | tf_op jit(solution)/shard_map/ppermute | solution.py:56
  178.7 56.8 %collective-permute-start.16 = (f32[16,64,64]{2,0,1:T(8,128)}, f32[16,64,64]{2,0,1:T(8,128)}, u32[]{:S(2)}, u32[]{:S(2)}) collective-permute-start(f32[16,64,64]{2,0,1:T(8,128)} %get-tuple-element.20), channel_id=1, source_target_pairs={{0,128},{16,144},{32,160},{48,176},{64,192},{80,208},{96,224},{112... | collective-permute-start | bytes 786440 | tf_op jit(solution)/shard_map/ppermute | solution.py:56
  192.7 14.4 %collective-permute-start.42 = (f32[64,64,3]{0,2,1:T(4,128)S(1)}, f32[64,64,3]{0,2,1:T(4,128)S(1)}, u32[]{:S(2)}, u32[]{:S(2)}) collective-permute-start(f32[64,64,3]{0,2,1:T(4,128)S(1)} %slice_select_fusion.19), channel_id=1, source_target_pairs={{0,16},{16,0},{32,48},{48,32},{64,80},{80,64},{96,112},{112,96},{1... | collective-permute-start | bytes 147464 | tf_op jit(solution)/shard_map/ppermute | solution.py:104
  211.8 24.9 %collective-permute-start.17 = (f32[16,64,64]{2,0,1:T(8,128)}, f32[16,64,64]{2,0,1:T(8,128)}, u32[]{:S(2)}, u32[]{:S(2)}) collective-permute-start(f32[16,64,64]{2,0,1:T(8,128)} %get-tuple-element.19), channel_id=1, source_target_pairs={{0,64},{16,80},{32,96},{48,112},{64,128},{80,144},{96,160},{112,17... | collective-permute-start | bytes 786440 | tf_op jit(solution)/shard_map/ppermute | solution.py:56
  232.8 18.9 %collective-permute-start.43 = (f32[7,64,64]{1,2,0:T(8,128)}, f32[7,64,64]{1,2,0:T(8,128)}, u32[]{:S(2)}, u32[]{:S(2)}) collective-permute-start(f32[7,64,64]{1,2,0:T(8,128)} %get-tuple-element.57), channel_id=1, source_target_pairs={{0,64},{16,80},{32,96},{48,112},{64,128},{80,144},{96,160},{112,17... | collective-permute-start | bytes 344072 | tf_op jit(solution)/shard_map/ppermute | solution.py:125
  235.4 19.0 %collective-permute-start.44 = (f32[7,64,64]{1,2,0:T(8,128)}, f32[7,64,64]{1,2,0:T(8,128)}, u32[]{:S(2)}, u32[]{:S(2)}) collective-permute-start(f32[7,64,64]{1,2,0:T(8,128)} %get-tuple-element.58), channel_id=1, source_target_pairs={{64,0},{80,16},{96,32},{112,48},{128,64},{144,80},{160,96},{176,11... | collective-permute-start | bytes 344072 | tf_op jit(solution)/shard_map/ppermute | solution.py:126
  239.2 51.4 %collective-permute-start.19 = (f32[16,64,64]{2,0,1:T(8,128)}, f32[16,64,64]{2,0,1:T(8,128)}, u32[]{:S(2)}, u32[]{:S(2)}) collective-permute-start(f32[16,64,64]{2,0,1:T(8,128)} %get-tuple-element.44), channel_id=1, source_target_pairs={{0,128},{64,192},{128,0},{192,64},{16,144},{80,208},{144,16},{208,... | collective-permute-start | bytes 786440 | tf_op jit(solution)/shard_map/ppermute | solution.py:46
  251.7 43.7 %collective-permute-start.30 = (f32[16,64,64]{2,0,1:T(8,128)}, f32[16,64,64]{2,0,1:T(8,128)}, u32[]{:S(2)}, u32[]{:S(2)}) collective-permute-start(f32[16,64,64]{2,0,1:T(8,128)} %get-tuple-element.53), channel_id=1, source_target_pairs={{0,192},{64,0},{128,64},{192,128},{16,208},{80,16},{144,80},{208,1... | collective-permute-start | bytes 786440 | tf_op jit(solution)/shard_map/ppermute | solution.py:46
  254.5 42.5 %collective-permute-start.32 = (f32[16,64,64]{2,0,1:T(8,128)}, f32[16,64,64]{2,0,1:T(8,128)}, u32[]{:S(2)}, u32[]{:S(2)}) collective-permute-start(f32[16,64,64]{2,0,1:T(8,128)} %get-tuple-element.52), channel_id=1, source_target_pairs={{0,64},{64,128},{128,192},{192,0},{16,80},{80,144},{144,208},{208,... | collective-permute-start | bytes 786440 | tf_op jit(solution)/shard_map/ppermute | solution.py:46
  264.3 46.4 %collective-permute-start.31 = (f32[16,64,64]{2,0,1:T(8,128)}, f32[16,64,64]{2,0,1:T(8,128)S(1)}, u32[]{:S(2)}, u32[]{:S(2)}) collective-permute-start(f32[16,64,64]{2,0,1:T(8,128)} %get-tuple-element.45), channel_id=1, source_target_pairs={{0,128},{64,192},{128,0},{192,64},{16,144},{80,208},{144,16},{208,... | collective-permute-start | bytes 786440 | tf_op jit(solution)/shard_map/ppermute | solution.py:46
  291.9 22.5 %collective-permute-start.21 = (f32[16,64,64]{2,0,1:T(8,128)S(1)}, f32[16,64,64]{2,0,1:T(8,128)S(1)}, u32[]{:S(2)}, u32[]{:S(2)}) collective-permute-start(f32[16,64,64]{2,0,1:T(8,128)S(1)} %get-tuple-element.24), channel_id=1, source_target_pairs={{0,48},{64,112},{128,176},{192,240},{16,0},{80,64},{144,128},{208,... | collective-permute-start | bytes 786440 | tf_op jit(solution)/shard_map/ppermute | solution.py:56
  295.4 21.5 %collective-permute-start.22 = (f32[16,64,64]{2,0,1:T(8,128)S(1)}, f32[16,64,64]{2,0,1:T(8,128)S(1)}, u32[]{:S(2)}, u32[]{:S(2)}) collective-permute-start(f32[16,64,64]{2,0,1:T(8,128)S(1)} %get-tuple-element.23), channel_id=1, source_target_pairs={{0,32},{64,96},{128,160},{192,224},{16,48},{80,112},{144,176},{208... | collective-permute-start | bytes 786440 | tf_op jit(solution)/shard_map/ppermute | solution.py:56
  295.4 21.5 %collective-permute-start.23 = (f32[16,64,64]{2,0,1:T(8,128)S(1)}, f32[16,64,64]{2,0,1:T(8,128)S(1)}, u32[]{:S(2)}, u32[]{:S(2)}) collective-permute-start(f32[16,64,64]{2,0,1:T(8,128)S(1)} %get-tuple-element.22), channel_id=1, source_target_pairs={{0,16},{64,80},{128,144},{192,208},{16,32},{80,96},{144,160},{208,... | collective-permute-start | bytes 786440 | tf_op jit(solution)/shard_map/ppermute | solution.py:56
  312.1 14.2 %collective-permute-start.33 = (f32[16,64,64]{2,0,1:T(8,128)S(1)}, f32[16,64,64]{2,0,1:T(8,128)S(1)}, u32[]{:S(2)}, u32[]{:S(2)}) collective-permute-start(f32[16,64,64]{2,0,1:T(8,128)S(1)} %get-tuple-element.30), channel_id=1, source_target_pairs={{0,48},{64,112},{128,176},{192,240},{16,0},{80,64},{144,128},{208,... | collective-permute-start | bytes 786440 | tf_op jit(solution)/shard_map/ppermute | solution.py:56
  313.9 21.6 %collective-permute-start.34 = (f32[16,64,64]{2,0,1:T(8,128)S(1)}, f32[16,64,64]{2,0,1:T(8,128)S(1)}, u32[]{:S(2)}, u32[]{:S(2)}) collective-permute-start(f32[16,64,64]{2,0,1:T(8,128)S(1)} %get-tuple-element.29), channel_id=1, source_target_pairs={{0,32},{64,96},{128,160},{192,224},{16,48},{80,112},{144,176},{208... | collective-permute-start | bytes 786440 | tf_op jit(solution)/shard_map/ppermute | solution.py:56
  314.4 22.5 %collective-permute-start.35 = (f32[16,64,64]{2,0,1:T(8,128)S(1)}, f32[16,64,64]{2,0,1:T(8,128)S(1)}, u32[]{:S(2)}, u32[]{:S(2)}) collective-permute-start(f32[16,64,64]{2,0,1:T(8,128)S(1)} %get-tuple-element.28), channel_id=1, source_target_pairs={{0,16},{64,80},{128,144},{192,208},{16,32},{80,96},{144,160},{208,... | collective-permute-start | bytes 786440 | tf_op jit(solution)/shard_map/ppermute | solution.py:56
  344.5 6.2 %collective-permute-start.45 = (f32[7,64,64]{2,0,1:T(8,128)S(1)}, f32[7,64,64]{2,0,1:T(8,128)S(1)}, u32[]{:S(2)}, u32[]{:S(2)}) collective-permute-start(f32[7,64,64]{2,0,1:T(8,128)S(1)} %get-tuple-element.41), channel_id=1, source_target_pairs={{0,64},{16,80},{32,96},{48,112},{64,128},{80,144},{96,160},{112,17... | collective-permute-start | bytes 344072 | tf_op jit(solution)/shard_map/ppermute | solution.py:125
  345.8 9.1 %collective-permute-start.46 = (f32[7,64,64]{2,0,1:T(8,128)S(1)}, f32[7,64,64]{2,0,1:T(8,128)S(1)}, u32[]{:S(2)}, u32[]{:S(2)}) collective-permute-start(f32[7,64,64]{2,0,1:T(8,128)S(1)} %get-tuple-element.42), channel_id=1, source_target_pairs={{64,0},{80,16},{96,32},{112,48},{128,64},{144,80},{160,96},{176,11... | collective-permute-start | bytes 344072 | tf_op jit(solution)/shard_map/ppermute | solution.py:126
  361.4 10.7 %collective-permute-start.49 = (f32[64,64,3]{0,2,1:T(4,128)S(1)}, f32[64,64,3]{0,2,1:T(4,128)S(1)}, u32[]{:S(2)}, u32[]{:S(2)}) collective-permute-start(f32[64,64,3]{0,2,1:T(4,128)S(1)} %slice_select_fusion.18), channel_id=1, source_target_pairs={{0,16},{16,0},{32,48},{48,32},{64,80},{80,64},{96,112},{112,96},{1... | collective-permute-start | bytes 147464 | tf_op jit(solution)/shard_map/ppermute | solution.py:104
  391.6 14.1 %collective-permute-start.51 = (f32[64,2,2,4,64]{0,4,3,2,1:T(8,128)S(1)}, f32[64,2,2,4,64]{0,4,3,2,1:T(8,128)S(1)}, u32[]{:S(2)}, u32[]{:S(2)}) collective-permute-start(f32[64,2,2,4,64]{0,4,3,2,1:T(8,128)S(1)} %select_bitcast_fusion.9), channel_id=1, source_target_pairs={{0,4},{1,5},{2,6},{3,7},{4,0},{5,1},{6,2},{7,3},{8,12},{9,13},{10,... | collective-permute-start | bytes 786440 | tf_op jit(solution)/shard_map/ppermute | solution.py:150
  405.8 9.3 %collective-permute-start.52 = (f32[64,2,4,64]{0,3,2,1:T(8,128)S(1)}, f32[64,2,4,64]{0,3,2,1:T(8,128)S(1)}, u32[]{:S(2)}, u32[]{:S(2)}) collective-permute-start(f32[64,2,4,64]{0,3,2,1:T(8,128)S(1)} %select_bitcast_fusion.15), channel_id=1, source_target_pairs={{0,8},{1,9},{2,10},{3,11},{4,12},{5,13},{6,14},{7,15},{8,0},{9,1},... | collective-permute-start | bytes 393224 | tf_op jit(solution)/shard_map/ppermute | solution.py:150
  415.2 9.6 %collective-permute-start.53 = (f32[64,4,64]{0,2,1:T(8,128)S(1)}, f32[64,4,64]{0,2,1:T(8,128)S(1)}, u32[]{:S(2)}, u32[]{:S(2)}) collective-permute-start(f32[64,4,64]{0,2,1:T(8,128)S(1)} %select_bitcast_fusion.22), channel_id=1, source_target_pairs={{0,2},{1,3},{2,0},{3,1},{4,6},{5,7},{6,4},{7,5},{8,10},{9,11},{10,... | collective-permute-start | bytes 196616 | tf_op jit(solution)/shard_map/ppermute | solution.py:150
  425.4 10.3 %collective-permute-start.54 = (f32[64,4,64]{0,2,1:T(8,128)S(1)}, f32[64,4,64]{0,2,1:T(8,128)S(1)}, u32[]{:S(2)}, u32[]{:S(2)}) collective-permute-start(f32[64,4,64]{0,2,1:T(8,128)S(1)} %fusion.9), channel_id=1, source_target_pairs={{0,2},{1,3},{2,0},{3,1},{4,6},{5,7},{6,4},{7,5},{8,10},{9,11},{10,... | collective-permute-start | bytes 196616 | tf_op jit(solution)/shard_map/ppermute | solution.py:160
  435.8 10.7 %collective-permute-start.55 = (f32[64,2,4,64]{0,3,2,1:T(8,128)S(1)}, f32[64,2,4,64]{0,3,2,1:T(8,128)S(1)}, u32[]{:S(2)}, u32[]{:S(2)}) collective-permute-start(f32[64,2,4,64]{0,3,2,1:T(8,128)S(1)} %pad_maximum_fusion.16), channel_id=1, source_target_pairs={{0,8},{1,9},{2,10},{3,11},{4,12},{5,13},{6,14},{7,15},{8,0},{9,1},... | collective-permute-start | bytes 393224 | tf_op jit(solution)/shard_map/ppermute | solution.py:160
  446.6 9.3 %collective-permute-start.56 = (f32[64,2,2,4,64]{0,4,3,2,1:T(8,128)S(1)}, f32[64,2,2,4,64]{0,4,3,2,1:T(8,128)S(1)}, u32[]{:S(2)}, u32[]{:S(2)}) collective-permute-start(f32[64,2,2,4,64]{0,4,3,2,1:T(8,128)S(1)} %pad_maximum_fusion.14), channel_id=1, source_target_pairs={{0,4},{1,5},{2,6},{3,7},{4,0},{5,1},{6,2},{7,3},{8,12},{9,13},{10,... | collective-permute-start | bytes 786440 | tf_op jit(solution)/shard_map/ppermute | solution.py:160
  460.2 8.3 %collective-permute-start.60 = (f32[64,64,3]{0,2,1:T(4,128)S(1)}, f32[64,64,3]{0,2,1:T(4,128)S(1)}, u32[]{:S(2)}, u32[]{:S(2)}) collective-permute-start(f32[64,64,3]{0,2,1:T(4,128)S(1)} %slice_select_fusion.17), channel_id=1, source_target_pairs={{0,16},{16,0},{32,48},{48,32},{64,80},{80,64},{96,112},{112,96},{1... | collective-permute-start | bytes 147464 | tf_op jit(solution)/shard_map/ppermute | solution.py:104
  483.6 6.2 %collective-permute-start.61 = (f32[7,64,64]{1,2,0:T(8,128)S(1)}, f32[7,64,64]{1,2,0:T(8,128)S(1)}, u32[]{:S(2)}, u32[]{:S(2)}) collective-permute-start(f32[7,64,64]{1,2,0:T(8,128)S(1)} %get-tuple-element.35), channel_id=1, source_target_pairs={{0,64},{16,80},{32,96},{48,112},{64,128},{80,144},{96,160},{112,17... | collective-permute-start | bytes 344072 | tf_op jit(solution)/shard_map/ppermute | solution.py:125
  486.1 7.9 %collective-permute-start.62 = (f32[7,64,64]{1,2,0:T(8,128)S(1)}, f32[7,64,64]{1,2,0:T(8,128)S(1)}, u32[]{:S(2)}, u32[]{:S(2)}) collective-permute-start(f32[7,64,64]{1,2,0:T(8,128)S(1)} %get-tuple-element.36), channel_id=1, source_target_pairs={{64,0},{80,16},{96,32},{112,48},{128,64},{144,80},{160,96},{176,11... | collective-permute-start | bytes 344072 | tf_op jit(solution)/shard_map/ppermute | solution.py:126
  505.7 6.0 collective-permute-start.63
  507.8 8.3 %collective-permute-start.64 = (f32[7,64,64]{2,0,1:T(8,128)S(1)}, f32[7,64,64]{2,0,1:T(8,128)S(1)}, u32[]{:S(2)}, u32[]{:S(2)}) collective-permute-start(f32[7,64,64]{2,0,1:T(8,128)S(1)} %get-tuple-element.34), channel_id=1, source_target_pairs={{64,0},{80,16},{96,32},{112,48},{128,64},{144,80},{160,96},{176,11... | collective-permute-start | bytes 344072 | tf_op jit(solution)/shard_map/ppermute | solution.py:126
  522.7 10.2 %collective-permute-start.67 = (f32[64,64,3]{0,2,1:T(4,128)S(1)}, f32[64,64,3]{0,2,1:T(4,128)S(1)}, u32[]{:S(2)}, u32[]{:S(2)}) collective-permute-start(f32[64,64,3]{0,2,1:T(4,128)S(1)} %slice_select_fusion.16), channel_id=1, source_target_pairs={{0,16},{16,0},{32,48},{48,32},{64,80},{80,64},{96,112},{112,96},{1... | collective-permute-start | bytes 147464 | tf_op jit(solution)/shard_map/ppermute | solution.py:104
  552.3 14.1 %collective-permute-start.69 = (f32[64,2,2,4,64]{0,4,3,2,1:T(8,128)S(1)}, f32[64,2,2,4,64]{0,4,3,2,1:T(8,128)S(1)}, u32[]{:S(2)}, u32[]{:S(2)}) collective-permute-start(f32[64,2,2,4,64]{0,4,3,2,1:T(8,128)S(1)} %select_bitcast_fusion.6), channel_id=1, source_target_pairs={{0,4},{1,5},{2,6},{3,7},{4,0},{5,1},{6,2},{7,3},{8,12},{9,13},{10,... | collective-permute-start | bytes 786440 | tf_op jit(solution)/shard_map/ppermute | solution.py:150
  566.5 9.1 %collective-permute-start.70 = (f32[64,2,4,64]{0,3,2,1:T(8,128)S(1)}, f32[64,2,4,64]{0,3,2,1:T(8,128)S(1)}, u32[]{:S(2)}, u32[]{:S(2)}) collective-permute-start(f32[64,2,4,64]{0,3,2,1:T(8,128)S(1)} %select_bitcast_fusion.12), channel_id=1, source_target_pairs={{0,8},{1,9},{2,10},{3,11},{4,12},{5,13},{6,14},{7,15},{8,0},{9,1},... | collective-permute-start | bytes 393224 | tf_op jit(solution)/shard_map/ppermute | solution.py:150
  575.7 10.2 %collective-permute-start.71 = (f32[64,4,64]{0,2,1:T(8,128)S(1)}, f32[64,4,64]{0,2,1:T(8,128)S(1)}, u32[]{:S(2)}, u32[]{:S(2)}) collective-permute-start(f32[64,4,64]{0,2,1:T(8,128)S(1)} %select_bitcast_fusion.19), channel_id=1, source_target_pairs={{0,2},{1,3},{2,0},{3,1},{4,6},{5,7},{6,4},{7,5},{8,10},{9,11},{10,... | collective-permute-start | bytes 196616 | tf_op jit(solution)/shard_map/ppermute | solution.py:150
  586.5 14.3 %collective-permute-start.72 = (f32[64,4,64]{0,2,1:T(8,128)S(1)}, f32[64,4,64]{0,2,1:T(8,128)S(1)}, u32[]{:S(2)}, u32[]{:S(2)}) collective-permute-start(f32[64,4,64]{0,2,1:T(8,128)S(1)} %get-tuple-element.80), channel_id=1, source_target_pairs={{0,48},{16,0},{32,16},{48,32},{64,112},{80,64},{96,80},{112,96},{1... | collective-permute-start | bytes 196616 | tf_op jit(solution)/shard_map/ppermute | solution.py:46
  588.6 12.2 %collective-permute-start.73 = (f32[64,4,64]{0,2,1:T(8,128)S(1)}, f32[64,4,64]{0,2,1:T(8,128)S(1)}, u32[]{:S(2)}, u32[]{:S(2)}) collective-permute-start(f32[64,4,64]{0,2,1:T(8,128)S(1)} %get-tuple-element.79), channel_id=1, source_target_pairs={{0,32},{16,48},{32,0},{48,16},{64,96},{80,112},{96,64},{112,80},{1... | collective-permute-start | bytes 196616 | tf_op jit(solution)/shard_map/ppermute | solution.py:46
  590.7 10.1 %collective-permute-start.74 = (f32[64,4,64]{0,2,1:T(8,128)S(1)}, f32[64,4,64]{0,2,1:T(8,128)S(1)}, u32[]{:S(2)}, u32[]{:S(2)}) collective-permute-start(f32[64,4,64]{0,2,1:T(8,128)S(1)} %get-tuple-element.17), channel_id=1, source_target_pairs={{0,16},{16,32},{32,48},{48,0},{64,80},{80,96},{96,112},{112,64},{1... | collective-permute-start | bytes 196616 | tf_op jit(solution)/shard_map/ppermute | solution.py:46
  600.9 7.2 %collective-permute-start.75 = (f32[64,4,64]{0,2,1:T(8,128)S(1)}, f32[64,4,64]{0,2,1:T(8,128)S(1)}, u32[]{:S(2)}, u32[]{:S(2)}) collective-permute-start(f32[64,4,64]{0,2,1:T(8,128)S(1)} %get-tuple-element.67), channel_id=1, source_target_pairs={{0,192},{16,208},{32,224},{48,240},{64,0},{80,16},{96,32},{112,48}... | collective-permute-start | bytes 196616 | tf_op jit(solution)/shard_map/ppermute | solution.py:56
  602.2 10.3 %collective-permute-start.76 = (f32[64,4,64]{0,2,1:T(8,128)S(1)}, f32[64,4,64]{0,2,1:T(8,128)S(1)}, u32[]{:S(2)}, u32[]{:S(2)}) collective-permute-start(f32[64,4,64]{0,2,1:T(8,128)S(1)} %get-tuple-element.66), channel_id=1, source_target_pairs={{0,128},{16,144},{32,160},{48,176},{64,192},{80,208},{96,224},{112... | collective-permute-start | bytes 196616 | tf_op jit(solution)/shard_map/ppermute | solution.py:56
  603.2 9.3 %collective-permute-start.77 = (f32[64,4,64]{0,2,1:T(8,128)S(1)}, f32[64,4,64]{0,2,1:T(8,128)S(1)}, u32[]{:S(2)}, u32[]{:S(2)}) collective-permute-start(f32[64,4,64]{0,2,1:T(8,128)S(1)} %get-tuple-element.65), channel_id=1, source_target_pairs={{0,64},{16,80},{32,96},{48,112},{64,128},{80,144},{96,160},{112,17... | collective-permute-start | bytes 196616 | tf_op jit(solution)/shard_map/ppermute | solution.py:56
  (35 other events, 611.3 us)

commit v13 on v12

--- a/solution.py
+++ b/solution.py
@@ -197,11 +197,11 @@
     share = jnp.transpose(estimate[0].reshape(side, estimate.shape[2] // side, side), (2, 1, 0))
     share = route(share, place, my_brick, nsp)
     recorded = jnp.transpose(measured[0, 0].reshape(side, side, side), (2, 1, 0))
-    chunk = side // 4
+    chunk = side // 8
     recorded = jnp.concatenate(
         [
             route(recorded[c * chunk:(c + 1) * chunk], place, my_brick, nsp, columns_first=c % 2 == 1)
-            for c in range(4)
+            for c in range(8)
         ],
         axis=0,
     )

time: 624 us -> 655 us (1.050)
  starting transfers between devices: 129 us -> 204 us
  waiting for transfers between devices: 275 us -> 237 us
  other arithmetic: 69.9 us -> 62.9 us
    ppermute x36 -> x60, starting transfers between devices: 60.9 us -> 110 us  [route(): part = lax.ppermute(part, 'space', pairs)]
    ppermute x8, starting transfers between devices: 6.67 us -> 22.7 us  [view_reduce_scatter(): x = keep + lax.ppermute(send, 'view', xor_pairs(nv, m))]
    ppermute x8, waiting for transfers between devices: 64.6 us -> 52.7 us  [view_reduce_scatter(): x = keep + lax.ppermute(send, 'view', xor_pairs(nv, m))]
    ppermute x4, starting transfers between devices: 8.5 us -> 19.5 us  [z_halo(): low = lax.ppermute(last, 'space', [(i, i + ROW) for i in range(nsp - ROW)])]
    ppermute x36 -> x60, waiting for transfers between devices: 128 us -> 119 us  [route(): part = lax.ppermute(part, 'space', pairs)]
    ppermute x12, starting transfers between devices: 28.8 us -> 21 us  [swap(): return lax.ppermute(x, 'space', [(i, i ^ partner) for i in range(nsp)])]
    ppermute x8, starting transfers between devices: 10.2 us -> 16.8 us  [view_all_gather(): recv = lax.ppermute(x, 'view', xor_pairs(nv, m))]
  transfers between devices with their start and end apart: 78 -> 102, of which waited for: 39 -> 58; matrix products, arithmetic and copies ran while one was open for 14% -> 11% of each run, Pallas kernels for 0% -> 0%
where the time goes in v13:
time: 655 us; the launch traced here: 643 us
  waiting for transfers between devices  237 us (36%)
  starting transfers between devices  204 us (31%)
  other arithmetic  62.9 us (10%)
  matrix products  62.6 us (10%)
  between operations  39.1 us (6%)
  local copies, waits for them, and re-layouts  37.6 us (6%)
    ppermute x60, waiting for transfers between devices, route(): part = lax.ppermute(part, 'space', pairs)  119 us
    ppermute x60, starting transfers between devices, route(): part = lax.ppermute(part, 'space', pairs)  110 us
    ppermute x8, waiting for transfers between devices, view_reduce_scatter(): x = keep + lax.ppermute(send, 'view', xor_pairs(nv, m))  52.7 us
    ppermute x8, waiting for transfers between devices, view_all_gather(): recv = lax.ppermute(x, 'view', xor_pairs(nv, m))  36.4 us
    ppermute x8, starting transfers between devices, view_reduce_scatter(): x = keep + lax.ppermute(send, 'view', xor_pairs(nv, m))  22.7 us
    ppermute x12, starting transfers between devices, swap(): return lax.ppermute(x, 'space', [(i, i ^ partner) for i in range(nsp)])  21 us
    select_n x3, other arithmetic, band_matrix(): band = jnp.where(offset == position, weight, band)  19.9 us
    dot_general x4, matrix products, convolve(): return jnp.einsum('abt,ot->abo', extended, band, precision=hi)  19.6 us
  transfers between devices with their start and end apart: 102, of which 58 were waited for; matrix products, arithmetic and copies ran while one was open for 11% of the time, Pallas kernels for 0%

profile of v13, /device:TPU:8, one launch (start us, length us, event | category | flops | bytes accessed | tf_op | source)
XLA Modules:
  0.0 643.5 jit_solution(8807593692037598630)
XLA Ops:
  15.5 4.9 select_select_fusion.33
  20.4 5.1 select_select_fusion.31
  25.5 9.9 %select_select_fusion.35 = (f32[64,78]{1,0:T(8,128)}, f32[64,78]{1,0:T(8,128)}) fusion(f32[]{:T(128)} %bitcast.40, f32[]{:T(128)} %bitcast.39, f32[]{:T(128)} %bitcast.38, f32[]{:T(128)} %bitcast.37, f32[]{:T(128)} %bitcast.36, f32[]{:T(128)} %bitcast.35, f32[]{:T(128)} %bitcast.34, f32[]{:T(128)} %bitcast.33, f32[]{:T(128)} %bitcast.32, f32[]{:T(128)} %bitcast.31, ...), kind=kLoop, calls=%fused_computation.213 | loop fusion | flops 229632 | bytes 39996 | tf_op jit(solution)/shard_map/jit(_where)/select_n | solution.py:67
  37.4 4.5 collective-permute-start.5
  96.4 3.1 collective-permute-done.13
  104.3 3.6 collective-permute-done.24
  121.1 4.9 collective-permute-done.38
  126.8 3.3 collective-permute-start.30
  130.1 7.1 %collective-permute-done.10 = f32[64,4,64]{0,2,1:T(8,128)S(1)} collective-permute-done((f32[64,4,64]{0,2,1:T(8,128)S(1)}, f32[64,4,64]{0,2,1:T(8,128)S(1)}, u32[]{:S(2)}, u32[]{:S(2)}) %collective-permute-start.10) | collective-permute-done | bytes 65568 | tf_op jit(solution)/shard_map/ppermute | solution.py:56
  137.2 8.5 %collective-permute-start.32 = (f32[8,64,64]{2,0,1:T(8,128)S(1)}, f32[8,64,64]{2,0,1:T(8,128)S(1)}, u32[]{:S(2)}, u32[]{:S(2)}) collective-permute-start(f32[8,64,64]{2,0,1:T(8,128)S(1)} %copy-done.14), channel_id=1, source_target_pairs={{0,64},{64,128},{128,192},{192,0},{16,80},{80,144},{144,208},{208,... | collective-permute-start | bytes 393224 | tf_op jit(solution)/shard_map/ppermute | solution.py:46
  145.9 13.3 %collective-permute-done.31 = f32[8,64,64]{2,0,1:T(8,128)S(1)} collective-permute-done((f32[8,64,64]{2,0,1:T(8,128)S(1)}, f32[8,64,64]{2,0,1:T(8,128)S(1)}, u32[]{:S(2)}, u32[]{:S(2)}) %collective-permute-start.31) | collective-permute-done | bytes 131104 | tf_op jit(solution)/shard_map/ppermute | solution.py:46
  159.3 4.7 collective-permute-start.60
  164.0 8.3 %collective-permute-done.60 = f32[64,4,64]{0,2,1:T(8,128)S(1)} collective-permute-done((f32[64,4,64]{0,2,1:T(8,128)S(1)}, f32[64,4,64]{0,2,1:T(8,128)S(1)}, u32[]{:S(2)}, u32[]{:S(2)}) %collective-permute-start.60) | collective-permute-done | bytes 65568 | tf_op jit(solution)/shard_map/ppermute | solution.py:160
  172.3 8.4 %collective-permute-start.17 = (f32[8,64,64]{2,0,1:T(8,128)S(1)}, f32[8,64,64]{2,0,1:T(8,128)S(1)}, u32[]{:S(2)}, u32[]{:S(2)}) collective-permute-start(f32[8,64,64]{2,0,1:T(8,128)S(1)} %get-tuple-element.40), channel_id=1, source_target_pairs={{0,64},{16,80},{32,96},{48,112},{64,128},{80,144},{96,160},{112,17... | collective-permute-start | bytes 393224 | tf_op jit(solution)/shard_map/ppermute | solution.py:56
  180.9 4.9 collective-permute-done.16
  185.8 3.3 collective-permute-start.61
  189.2 4.7 collective-permute-done.61
  194.0 8.8 %collective-permute-start.20 = (f32[8,64,64]{2,0,1:T(8,128)S(1)}, f32[8,64,64]{2,0,1:T(8,128)S(1)}, u32[]{:S(2)}, u32[]{:S(2)}) collective-permute-start(f32[8,64,64]{2,0,1:T(8,128)S(1)} %get-tuple-element.73), channel_id=1, source_target_pairs={{0,64},{64,128},{128,192},{192,0},{16,80},{80,144},{144,208},{208,... | collective-permute-start | bytes 393224 | tf_op jit(solution)/shard_map/ppermute | solution.py:46
  203.0 9.5 %collective-permute-start.28 = (f32[8,64,64]{2,0,1:T(8,128)S(1)}, f32[8,64,64]{2,0,1:T(8,128)S(1)}, u32[]{:S(2)}, u32[]{:S(2)}) collective-permute-start(f32[8,64,64]{2,0,1:T(8,128)S(1)} %get-tuple-element.35), channel_id=1, source_target_pairs={{0,128},{16,144},{32,160},{48,176},{64,192},{80,208},{96,224},{112... | collective-permute-start | bytes 393224 | tf_op jit(solution)/shard_map/ppermute | solution.py:56
  212.5 9.3 %collective-permute-start.44 = (f32[8,64,64]{2,0,1:T(8,128)S(1)}, f32[8,64,64]{2,0,1:T(8,128)S(1)}, u32[]{:S(2)}, u32[]{:S(2)}) collective-permute-start(f32[8,64,64]{2,0,1:T(8,128)S(1)} %get-tuple-element.71), channel_id=1, source_target_pairs={{0,64},{64,128},{128,192},{192,0},{16,80},{80,144},{144,208},{208,... | collective-permute-start | bytes 393224 | tf_op jit(solution)/shard_map/ppermute | solution.py:46
  222.3 3.4 collective-permute-done.44
  225.9 3.8 collective-permute-done.21
  233.5 5.2 collective-permute-done.23
  244.9 4.6 collective-permute-done.34
  256.5 3.9 collective-permute-done.40
  262.5 7.5 %collective-permute-start.49 = (f32[8,64,64]{2,0,1:T(8,128)S(1)}, f32[8,64,64]{2,0,1:T(8,128)S(1)}, u32[]{:S(2)}, u32[]{:S(2)}) collective-permute-start(f32[8,64,64]{2,0,1:T(8,128)S(1)} %get-tuple-element.67), channel_id=1, source_target_pairs={{0,32},{16,48},{32,0},{48,16},{64,96},{80,112},{96,64},{112,80},{1... | collective-permute-start | bytes 393224 | tf_op jit(solution)/shard_map/ppermute | solution.py:46
  274.5 3.7 collective-permute-done.50
  280.5 6.3 collective-permute-done.51
  286.9 19.9 %collective-permute-done.52 = f32[8,64,64]{2,0,1:T(8,128)S(1)} collective-permute-done((f32[8,64,64]{2,0,1:T(8,128)S(1)}, f32[8,64,64]{2,0,1:T(8,128)S(1)}, u32[]{:S(2)}, u32[]{:S(2)}) %collective-permute-start.52) | collective-permute-done | bytes 131104 | tf_op jit(solution)/shard_map/ppermute | solution.py:56
  307.8 7.3 %collective-permute-done.56 = f32[8,64,64]{2,0,1:T(8,128)S(1)} collective-permute-done((f32[8,64,64]{2,0,1:T(8,128)S(1)}, f32[8,64,64]{2,0,1:T(8,128)S(1)}, u32[]{:S(2)}, u32[]{:S(2)}) %collective-permute-start.56) | collective-permute-done | bytes 131104 | tf_op jit(solution)/shard_map/ppermute | solution.py:46
  335.8 3.4 copy.52
  339.2 8.0 %fusion.40 = f32[64,70,64]{1,2,0:T(8,128)S(1)} fusion(f32[64,70,70]{2,1,0:T(8,128)} %copy.52, f32[64,70]{1,0:T(8,128)S(1)} %copy-done.10), kind=kOutput, calls=%fused_computation.197 | convolution fusion | flops 240844800 | bytes 2419200 | tf_op jit(solution)/shard_map/abt,ot->abo/dot_general | solution.py:77
  350.3 4.7 collective-permute-start.67
  358.6 3.3 copy.39
  361.9 8.3 %convolution_divide_fusion.1 = f32[64,64,64]{2,0,1:T(8,128)S(1)} fusion(f32[64,64,64]{2,0,1:T(8,128)} %select_dynamic-update-slice_fusion, f32[78,64,64]{0,2,1:T(8,128)} %copy.39, f32[64,78]{1,0:T(8,128)S(1)} %copy-done.22), kind=kOutput, calls=%fused_computation.19 | convolution fusion | flops 245628928 | bytes 3395072 | tf_op jit(solution)/shard_map/ot,tab->oab/dot_general | solution.py:74
  371.6 5.0 collective-permute-start.69
  383.0 3.4 fusion.91
  387.8 3.1 collective-permute-start.71
  400.9 8.0 %fusion.34 = f32[64,70,64]{1,2,0:T(8,128)S(1)} fusion(f32[64,70,70]{1,2,0:T(8,128)} %copy.53, f32[64,70]{1,0:T(8,128)S(1)} %copy-done.6), kind=kOutput, calls=%fused_computation.191 | convolution fusion | flops 240844800 | bytes 2419200 | tf_op jit(solution)/shard_map/ot,atb->aob/dot_general | solution.py:76
  418.5 12.2 %collective-permute-done.75 = f32[64,2,2,4,64]{0,4,3,2,1:T(8,128)S(1)} collective-permute-done((f32[64,2,2,4,64]{0,4,3,2,1:T(8,128)S(1)}, f32[64,2,2,4,64]{0,4,3,2,1:T(8,128)S(1)}, u32[]{:S(2)}, u32[]{:S(2)}) %collective-permute-start.75) | collective-permute-done | bytes 262176 | tf_op jit(solution)/shard_map/ppermute | solution.py:150
  430.9 5.3 collective-permute-start.76
  436.1 5.8 collective-permute-done.76
  442.0 6.5 %collective-permute-start.77 = (f32[64,4,64]{0,2,1:T(8,128)S(1)}, f32[64,4,64]{0,2,1:T(8,128)S(1)}, u32[]{:S(2)}, u32[]{:S(2)}) collective-permute-start(f32[64,4,64]{0,2,1:T(8,128)S(1)} %select_bitcast_fusion.22), channel_id=1, source_target_pairs={{0,2},{1,3},{2,0},{3,1},{4,6},{5,7},{6,4},{7,5},{8,10},{9,11},{10,... | collective-permute-start | bytes 196616 | tf_op jit(solution)/shard_map/ppermute | solution.py:150
  449.1 3.9 collective-permute-done.77
  453.6 6.8 %collective-permute-start.78 = (f32[64,4,64]{0,2,1:T(8,128)S(1)}, f32[64,4,64]{0,2,1:T(8,128)S(1)}, u32[]{:S(2)}, u32[]{:S(2)}) collective-permute-start(f32[64,4,64]{0,2,1:T(8,128)S(1)} %fusion.9), channel_id=1, source_target_pairs={{0,2},{1,3},{2,0},{3,1},{4,6},{5,7},{6,4},{7,5},{8,10},{9,11},{10,... | collective-permute-start | bytes 196616 | tf_op jit(solution)/shard_map/ppermute | solution.py:160
  460.5 3.9 collective-permute-done.78
  464.6 9.3 %collective-permute-done.79 = f32[64,2,4,64]{0,3,2,1:T(8,128)S(1)} collective-permute-done((f32[64,2,4,64]{0,3,2,1:T(8,128)S(1)}, f32[64,2,4,64]{0,3,2,1:T(8,128)S(1)}, u32[]{:S(2)}, u32[]{:S(2)}) %collective-permute-start.79) | collective-permute-done | bytes 131104 | tf_op jit(solution)/shard_map/ppermute | solution.py:160
  475.7 7.5 %collective-permute-done.80 = f32[64,2,2,4,64]{0,4,3,2,1:T(8,128)S(1)} collective-permute-done((f32[64,2,2,4,64]{0,4,3,2,1:T(8,128)S(1)}, f32[64,2,2,4,64]{0,4,3,2,1:T(8,128)S(1)}, u32[]{:S(2)}, u32[]{:S(2)}) %collective-permute-start.80) | collective-permute-done | bytes 262176 | tf_op jit(solution)/shard_map/ppermute | solution.py:160
  488.3 4.2 collective-permute-start.82
  494.7 3.8 collective-permute-done.84
  502.8 7.9 %fusion.38 = f32[64,70,64]{1,2,0:T(8,128)S(1)} fusion(f32[64,70,70]{2,1,0:T(8,128)} %copy.54, f32[64,70]{1,0:T(8,128)S(1)} %copy-done.11), kind=kOutput, calls=%fused_computation.195 | convolution fusion | flops 240844800 | bytes 2419200 | tf_op jit(solution)/shard_map/abt,ot->abo/dot_general | solution.py:77
  514.0 4.7 collective-permute-start.85
  522.6 3.3 copy.47
  525.9 8.3 %convolution_divide_fusion = f32[64,64,64]{2,0,1:T(8,128)S(1)} fusion(f32[64,64,64]{2,0,1:T(8,128)} %select_dynamic-update-slice_fusion, f32[78,64,64]{0,2,1:T(8,128)} %copy.47, f32[64,78]{1,0:T(8,128)S(1)} %copy-done.23), kind=kOutput, calls=%fused_computation.17 | convolution fusion | flops 245628928 | bytes 3395072 | tf_op jit(solution)/shard_map/ot,tab->oab/dot_general | solution.py:74
  535.6 5.0 collective-permute-start.87
  547.0 3.4 fusion.92
  551.7 3.0 collective-permute-start.89
  564.9 7.9 %fusion.32 = f32[64,70,64]{1,2,0:T(8,128)S(1)} fusion(f32[64,70,70]{1,2,0:T(8,128)} %copy.55, f32[64,70]{1,0:T(8,128)S(1)} %copy-done.6), kind=kOutput, calls=%fused_computation.189 | convolution fusion | flops 240844800 | bytes 2419200 | tf_op jit(solution)/shard_map/ot,atb->aob/dot_general | solution.py:76
  580.4 14.0 %collective-permute-done.93 = f32[64,2,2,4,64]{0,4,3,2,1:T(8,128)S(1)} collective-permute-done((f32[64,2,2,4,64]{0,4,3,2,1:T(8,128)S(1)}, f32[64,2,2,4,64]{0,4,3,2,1:T(8,128)S(1)}, u32[]{:S(2)}, u32[]{:S(2)}) %collective-permute-start.93) | collective-permute-done | bytes 262176 | tf_op jit(solution)/shard_map/ppermute | solution.py:150
  596.6 7.0 %collective-permute-done.94 = f32[64,2,4,64]{0,3,2,1:T(8,128)S(1)} collective-permute-done((f32[64,2,4,64]{0,3,2,1:T(8,128)S(1)}, f32[64,2,4,64]{0,3,2,1:T(8,128)S(1)}, u32[]{:S(2)}, u32[]{:S(2)}) %collective-permute-start.94) | collective-permute-done | bytes 131104 | tf_op jit(solution)/shard_map/ppermute | solution.py:150
  603.7 6.5 %collective-permute-start.95 = (f32[64,4,64]{0,2,1:T(8,128)S(1)}, f32[64,4,64]{0,2,1:T(8,128)S(1)}, u32[]{:S(2)}, u32[]{:S(2)}) collective-permute-start(f32[64,4,64]{0,2,1:T(8,128)S(1)} %select_bitcast_fusion.19), channel_id=1, source_target_pairs={{0,2},{1,3},{2,0},{3,1},{4,6},{5,7},{6,4},{7,5},{8,10},{9,11},{10,... | collective-permute-start | bytes 196616 | tf_op jit(solution)/shard_map/ppermute | solution.py:150
  610.2 4.5 collective-permute-done.95
  628.8 4.6 collective-permute-start.99
  636.5 5.6 collective-permute-done.100
  (350 shorter events, 206.6 us)
Async XLA Ops:
  1.5 35.8 %collective-permute-start.2 = (s32[16,7]{0,1:T(8,128)S(1)}, s32[16,7]{0,1:T(8,128)S(1)}, u32[]{:S(2)}, u32[]{:S(2)}) collective-permute-start(s32[16,7]{0,1:T(8,128)S(1)} %broadcast_select_fusion.22), channel_id=1, source_target_pairs={{0,48},{16,32},{32,16},{48,0},{64,112},{80,96},{96,80},{112,64},{1... | collective-permute-start | bytes 1352 | tf_op jit(solution)/shard_map/ppermute | solution.py:22
  3.0 34.3 %collective-permute-start.1 = (s32[16,7]{0,1:T(8,128)S(1)}, s32[16,7]{0,1:T(8,128)S(1)}, u32[]{:S(2)}, u32[]{:S(2)}) collective-permute-start(s32[16,7]{0,1:T(8,128)S(1)} %broadcast_select_fusion.22), channel_id=1, source_target_pairs={{0,32},{16,48},{32,0},{48,16},{64,96},{80,112},{96,64},{112,80},{1... | collective-permute-start | bytes 1352 | tf_op jit(solution)/shard_map/ppermute | solution.py:22
  5.7 31.6 %collective-permute-start = (s32[16,7]{0,1:T(8,128)S(1)}, s32[16,7]{0,1:T(8,128)S(1)}, u32[]{:S(2)}, u32[]{:S(2)}) collective-permute-start(s32[16,7]{0,1:T(8,128)S(1)} %broadcast_select_fusion.22), channel_id=1, source_target_pairs={{0,16},{16,0},{32,48},{48,32},{64,80},{80,64},{96,112},{112,96},{1... | collective-permute-start | bytes 1352 | tf_op jit(solution)/shard_map/ppermute | solution.py:22
  76.5 12.4 %collective-permute-start.6 = (f32[64,4,64]{0,2,1:T(8,128)}, f32[64,4,64]{0,2,1:T(8,128)S(1)}, u32[]{:S(2)}, u32[]{:S(2)}) collective-permute-start(f32[64,4,64]{0,2,1:T(8,128)} %bitcast.261), channel_id=1, source_target_pairs={{0,48},{16,0},{32,16},{48,32},{64,112},{80,64},{96,80},{112,96},{1... | collective-permute-start | bytes 196616 | tf_op jit(solution)/shard_map/ppermute | solution.py:46
  77.7 13.7 %collective-permute-start.7 = (f32[64,4,64]{0,2,1:T(8,128)}, f32[64,4,64]{0,2,1:T(8,128)S(1)}, u32[]{:S(2)}, u32[]{:S(2)}) collective-permute-start(f32[64,4,64]{0,2,1:T(8,128)} %bitcast.260), channel_id=1, source_target_pairs={{0,32},{16,48},{32,0},{48,16},{64,96},{80,112},{96,64},{112,80},{1... | collective-permute-start | bytes 196616 | tf_op jit(solution)/shard_map/ppermute | solution.py:46
  81.1 11.8 %collective-permute-start.8 = (f32[64,4,64]{0,2,1:T(8,128)}, f32[64,4,64]{0,2,1:T(8,128)S(1)}, u32[]{:S(2)}, u32[]{:S(2)}) collective-permute-start(f32[64,4,64]{0,2,1:T(8,128)} %bitcast.259), channel_id=1, source_target_pairs={{0,16},{16,32},{32,48},{48,0},{64,80},{80,96},{96,112},{112,64},{1... | collective-permute-start | bytes 196616 | tf_op jit(solution)/shard_map/ppermute | solution.py:46
  85.1 11.0 %collective-permute-start.12 = (f32[8,64,64]{2,0,1:T(8,128)}, f32[8,64,64]{2,0,1:T(8,128)S(1)}, u32[]{:S(2)}, u32[]{:S(2)}) collective-permute-start(f32[8,64,64]{2,0,1:T(8,128)} %get-tuple-element.89), channel_id=1, source_target_pairs={{0,48},{16,0},{32,16},{48,32},{64,112},{80,64},{96,80},{112,96},{1... | collective-permute-start | bytes 393224 | tf_op jit(solution)/shard_map/ppermute | solution.py:46
  87.0 12.5 %collective-permute-start.13 = (f32[8,64,64]{2,0,1:T(8,128)}, f32[8,64,64]{2,0,1:T(8,128)S(1)}, u32[]{:S(2)}, u32[]{:S(2)}) collective-permute-start(f32[8,64,64]{2,0,1:T(8,128)} %get-tuple-element.75), channel_id=1, source_target_pairs={{0,32},{16,48},{32,0},{48,16},{64,96},{80,112},{96,64},{112,80},{1... | collective-permute-start | bytes 393224 | tf_op jit(solution)/shard_map/ppermute | solution.py:46
  88.9 14.7 %collective-permute-start.14 = (f32[8,64,64]{2,0,1:T(8,128)}, f32[8,64,64]{2,0,1:T(8,128)S(1)}, u32[]{:S(2)}, u32[]{:S(2)}) collective-permute-start(f32[8,64,64]{2,0,1:T(8,128)} %get-tuple-element.76), channel_id=1, source_target_pairs={{0,16},{16,32},{32,48},{48,0},{64,80},{80,96},{96,112},{112,64},{1... | collective-permute-start | bytes 393224 | tf_op jit(solution)/shard_map/ppermute | solution.py:46
  91.4 111.5 %collective-permute-start.18 = (f32[8,64,64]{2,0,1:T(8,128)}, f32[8,64,64]{2,0,1:T(8,128)S(1)}, u32[]{:S(2)}, u32[]{:S(2)}) collective-permute-start(f32[8,64,64]{2,0,1:T(8,128)} %get-tuple-element.88), channel_id=1, source_target_pairs={{0,192},{64,0},{128,64},{192,128},{16,208},{80,16},{144,80},{208,1... | collective-permute-start | bytes 393224 | tf_op jit(solution)/shard_map/ppermute | solution.py:46
  92.9 110.1 %collective-permute-start.19 = (f32[8,64,64]{2,0,1:T(8,128)}, f32[8,64,64]{2,0,1:T(8,128)S(1)}, u32[]{:S(2)}, u32[]{:S(2)}) collective-permute-start(f32[8,64,64]{2,0,1:T(8,128)} %get-tuple-element.77), channel_id=1, source_target_pairs={{0,128},{64,192},{128,0},{192,64},{16,144},{80,208},{144,16},{208,... | collective-permute-start | bytes 393224 | tf_op jit(solution)/shard_map/ppermute | solution.py:46
  96.1 11.8 %collective-permute-start.24 = (f32[8,64,64]{2,0,1:T(8,128)}, f32[8,64,64]{2,0,1:T(8,128)S(1)}, u32[]{:S(2)}, u32[]{:S(2)}) collective-permute-start(f32[8,64,64]{2,0,1:T(8,128)} %get-tuple-element.87), channel_id=1, source_target_pairs={{0,48},{16,0},{32,16},{48,32},{64,112},{80,64},{96,80},{112,96},{1... | collective-permute-start | bytes 393224 | tf_op jit(solution)/shard_map/ppermute | solution.py:46
  99.5 11.2 %collective-permute-start.25 = (f32[8,64,64]{2,0,1:T(8,128)}, f32[8,64,64]{2,0,1:T(8,128)S(1)}, u32[]{:S(2)}, u32[]{:S(2)}) collective-permute-start(f32[8,64,64]{2,0,1:T(8,128)} %get-tuple-element.78), channel_id=1, source_target_pairs={{0,32},{16,48},{32,0},{48,16},{64,96},{80,112},{96,64},{112,80},{1... | collective-permute-start | bytes 393224 | tf_op jit(solution)/shard_map/ppermute | solution.py:46
  103.7 12.1 %collective-permute-start.26 = (f32[8,64,64]{2,0,1:T(8,128)}, f32[8,64,64]{2,0,1:T(8,128)S(1)}, u32[]{:S(2)}, u32[]{:S(2)}) collective-permute-start(f32[8,64,64]{2,0,1:T(8,128)} %get-tuple-element.79), channel_id=1, source_target_pairs={{0,16},{16,32},{32,48},{48,0},{64,80},{80,96},{96,112},{112,64},{1... | collective-permute-start | bytes 393224 | tf_op jit(solution)/shard_map/ppermute | solution.py:46
  107.8 11.3 %collective-permute-start.36 = (f32[8,64,64]{2,0,1:T(8,128)S(1)}, f32[8,64,64]{2,0,1:T(8,128)S(1)}, u32[]{:S(2)}, u32[]{:S(2)}) collective-permute-start(f32[8,64,64]{2,0,1:T(8,128)S(1)} %copy-done.19), channel_id=1, source_target_pairs={{0,48},{16,0},{32,16},{48,32},{64,112},{80,64},{96,80},{112,96},{1... | collective-permute-start | bytes 393224 | tf_op jit(solution)/shard_map/ppermute | solution.py:46
  110.8 9.8 %collective-permute-start.37 = (f32[8,64,64]{2,0,1:T(8,128)S(1)}, f32[8,64,64]{2,0,1:T(8,128)S(1)}, u32[]{:S(2)}, u32[]{:S(2)}) collective-permute-start(f32[8,64,64]{2,0,1:T(8,128)S(1)} %copy-done.18), channel_id=1, source_target_pairs={{0,32},{16,48},{32,0},{48,16},{64,96},{80,112},{96,64},{112,80},{1... | collective-permute-start | bytes 393224 | tf_op jit(solution)/shard_map/ppermute | solution.py:46
  115.8 10.2 %collective-permute-start.38 = (f32[8,64,64]{2,0,1:T(8,128)S(1)}, f32[8,64,64]{2,0,1:T(8,128)S(1)}, u32[]{:S(2)}, u32[]{:S(2)}) collective-permute-start(f32[8,64,64]{2,0,1:T(8,128)S(1)} %copy-done.17), channel_id=1, source_target_pairs={{0,16},{16,32},{32,48},{48,0},{64,80},{80,96},{96,112},{112,64},{1... | collective-permute-start | bytes 393224 | tf_op jit(solution)/shard_map/ppermute | solution.py:46
  120.6 16.6 %collective-permute-start.10 = (f32[64,4,64]{0,2,1:T(8,128)S(1)}, f32[64,4,64]{0,2,1:T(8,128)S(1)}, u32[]{:S(2)}, u32[]{:S(2)}) collective-permute-start(f32[64,4,64]{0,2,1:T(8,128)S(1)} %get-tuple-element.102), channel_id=1, source_target_pairs={{0,128},{16,144},{32,160},{48,176},{64,192},{80,208},{96,224},{112... | collective-permute-start | bytes 196616 | tf_op jit(solution)/shard_map/ppermute | solution.py:56
  126.0 11.2 %collective-permute-start.11 = (f32[64,4,64]{0,2,1:T(8,128)S(1)}, f32[64,4,64]{0,2,1:T(8,128)S(1)}, u32[]{:S(2)}, u32[]{:S(2)}) collective-permute-start(f32[64,4,64]{0,2,1:T(8,128)S(1)} %get-tuple-element.101), channel_id=1, source_target_pairs={{0,64},{16,80},{32,96},{48,112},{64,128},{80,144},{96,160},{112,17... | collective-permute-start | bytes 196616 | tf_op jit(solution)/shard_map/ppermute | solution.py:56
  126.8 19.0 %collective-permute-start.30 = (f32[8,64,64]{2,0,1:T(8,128)S(1)}, f32[8,64,64]{2,0,1:T(8,128)S(1)}, u32[]{:S(2)}, u32[]{:S(2)}) collective-permute-start(f32[8,64,64]{2,0,1:T(8,128)S(1)} %copy-done.16), channel_id=1, source_target_pairs={{0,192},{64,0},{128,64},{192,128},{16,208},{80,16},{144,80},{208,1... | collective-permute-start | bytes 393224 | tf_op jit(solution)/shard_map/ppermute | solution.py:46
  137.2 22.0 %collective-permute-start.31 = (f32[8,64,64]{2,0,1:T(8,128)S(1)}, f32[8,64,64]{2,0,1:T(8,128)S(1)}, u32[]{:S(2)}, u32[]{:S(2)}) collective-permute-start(f32[8,64,64]{2,0,1:T(8,128)S(1)} %copy-done.15), channel_id=1, source_target_pairs={{0,128},{64,192},{128,0},{192,64},{16,144},{80,208},{144,16},{208,... | collective-permute-start | bytes 393224 | tf_op jit(solution)/shard_map/ppermute | solution.py:46
  137.2 22.0 %collective-permute-start.32 = (f32[8,64,64]{2,0,1:T(8,128)S(1)}, f32[8,64,64]{2,0,1:T(8,128)S(1)}, u32[]{:S(2)}, u32[]{:S(2)}) collective-permute-start(f32[8,64,64]{2,0,1:T(8,128)S(1)} %copy-done.14), channel_id=1, source_target_pairs={{0,64},{64,128},{128,192},{192,0},{16,80},{80,144},{144,208},{208,... | collective-permute-start | bytes 393224 | tf_op jit(solution)/shard_map/ppermute | solution.py:46
  145.8 34.9 %collective-permute-start.15 = (f32[8,64,64]{2,0,1:T(8,128)S(1)}, f32[8,64,64]{2,0,1:T(8,128)S(1)}, u32[]{:S(2)}, u32[]{:S(2)}) collective-permute-start(f32[8,64,64]{2,0,1:T(8,128)S(1)} %get-tuple-element.42), channel_id=1, source_target_pairs={{0,192},{16,208},{32,224},{48,240},{64,0},{80,16},{96,32},{112,48}... | collective-permute-start | bytes 393224 | tf_op jit(solution)/shard_map/ppermute | solution.py:56
  159.2 26.6 %collective-permute-start.16 = (f32[8,64,64]{2,0,1:T(8,128)S(1)}, f32[8,64,64]{2,0,1:T(8,128)S(1)}, u32[]{:S(2)}, u32[]{:S(2)}) collective-permute-start(f32[8,64,64]{2,0,1:T(8,128)S(1)} %get-tuple-element.41), channel_id=1, source_target_pairs={{0,128},{16,144},{32,160},{48,176},{64,192},{80,208},{96,224},{112... | collective-permute-start | bytes 393224 | tf_op jit(solution)/shard_map/ppermute | solution.py:56
  159.3 13.1 %collective-permute-start.60 = (f32[64,4,64]{0,2,1:T(8,128)S(1)}, f32[64,4,64]{0,2,1:T(8,128)S(1)}, u32[]{:S(2)}, u32[]{:S(2)}) collective-permute-start(f32[64,4,64]{0,2,1:T(8,128)S(1)} %fusion.15), channel_id=1, source_target_pairs={{0,2},{1,3},{2,0},{3,1},{4,6},{5,7},{6,4},{7,5},{8,10},{9,11},{10,... | collective-permute-start | bytes 196616 | tf_op jit(solution)/shard_map/ppermute | solution.py:160
  172.3 13.5 %collective-permute-start.17 = (f32[8,64,64]{2,0,1:T(8,128)S(1)}, f32[8,64,64]{2,0,1:T(8,128)S(1)}, u32[]{:S(2)}, u32[]{:S(2)}) collective-permute-start(f32[8,64,64]{2,0,1:T(8,128)S(1)} %get-tuple-element.40), channel_id=1, source_target_pairs={{0,64},{16,80},{32,96},{48,112},{64,128},{80,144},{96,160},{112,17... | collective-permute-start | bytes 393224 | tf_op jit(solution)/shard_map/ppermute | solution.py:56
  180.8 41.2 %collective-permute-start.42 = (f32[8,64,64]{2,0,1:T(8,128)S(1)}, f32[8,64,64]{2,0,1:T(8,128)S(1)}, u32[]{:S(2)}, u32[]{:S(2)}) collective-permute-start(f32[8,64,64]{2,0,1:T(8,128)S(1)} %copy-done.13), channel_id=1, source_target_pairs={{0,192},{64,0},{128,64},{192,128},{16,208},{80,16},{144,80},{208,1... | collective-permute-start | bytes 393224 | tf_op jit(solution)/shard_map/ppermute | solution.py:46
  185.8 36.2 %collective-permute-start.43 = (f32[8,64,64]{2,0,1:T(8,128)S(1)}, f32[8,64,64]{2,0,1:T(8,128)S(1)}, u32[]{:S(2)}, u32[]{:S(2)}) collective-permute-start(f32[8,64,64]{2,0,1:T(8,128)S(1)} %copy-done.12), channel_id=1, source_target_pairs={{0,128},{64,192},{128,0},{192,64},{16,144},{80,208},{144,16},{208,... | collective-permute-start | bytes 393224 | tf_op jit(solution)/shard_map/ppermute | solution.py:46
  194.0 18.5 %collective-permute-start.20 = (f32[8,64,64]{2,0,1:T(8,128)S(1)}, f32[8,64,64]{2,0,1:T(8,128)S(1)}, u32[]{:S(2)}, u32[]{:S(2)}) collective-permute-start(f32[8,64,64]{2,0,1:T(8,128)S(1)} %get-tuple-element.73), channel_id=1, source_target_pairs={{0,64},{64,128},{128,192},{192,0},{16,80},{80,144},{144,208},{208,... | collective-permute-start | bytes 393224 | tf_op jit(solution)/shard_map/ppermute | solution.py:46
  202.9 35.9 %collective-permute-start.27 = (f32[8,64,64]{2,0,1:T(8,128)S(1)}, f32[8,64,64]{2,0,1:T(8,128)S(1)}, u32[]{:S(2)}, u32[]{:S(2)}) collective-permute-start(f32[8,64,64]{2,0,1:T(8,128)S(1)} %get-tuple-element.36), channel_id=1, source_target_pairs={{0,192},{16,208},{32,224},{48,240},{64,0},{80,16},{96,32},{112,48}... | collective-permute-start | bytes 393224 | tf_op jit(solution)/shard_map/ppermute | solution.py:56
  203.0 38.4 %collective-permute-start.28 = (f32[8,64,64]{2,0,1:T(8,128)S(1)}, f32[8,64,64]{2,0,1:T(8,128)S(1)}, u32[]{:S(2)}, u32[]{:S(2)}) collective-permute-start(f32[8,64,64]{2,0,1:T(8,128)S(1)} %get-tuple-element.35), channel_id=1, source_target_pairs={{0,128},{16,144},{32,160},{48,176},{64,192},{80,208},{96,224},{112... | collective-permute-start | bytes 393224 | tf_op jit(solution)/shard_map/ppermute | solution.py:56
  212.5 13.2 %collective-permute-start.44 = (f32[8,64,64]{2,0,1:T(8,128)S(1)}, f32[8,64,64]{2,0,1:T(8,128)S(1)}, u32[]{:S(2)}, u32[]{:S(2)}) collective-permute-start(f32[8,64,64]{2,0,1:T(8,128)S(1)} %get-tuple-element.71), channel_id=1, source_target_pairs={{0,64},{64,128},{128,192},{192,0},{16,80},{80,144},{144,208},{208,... | collective-permute-start | bytes 393224 | tf_op jit(solution)/shard_map/ppermute | solution.py:46
  222.1 11.4 %collective-permute-start.22 = (f32[8,64,64]{2,0,1:T(8,128)S(1)}, f32[8,64,64]{2,0,1:T(8,128)S(1)}, u32[]{:S(2)}, u32[]{:S(2)}) collective-permute-start(f32[8,64,64]{2,0,1:T(8,128)S(1)} %get-tuple-element.38), channel_id=1, source_target_pairs={{0,32},{64,96},{128,160},{192,224},{16,48},{80,112},{144,176},{208... | collective-permute-start | bytes 393224 | tf_op jit(solution)/shard_map/ppermute | solution.py:56
  225.7 13.0 %collective-permute-start.23 = (f32[8,64,64]{2,0,1:T(8,128)S(1)}, f32[8,64,64]{2,0,1:T(8,128)S(1)}, u32[]{:S(2)}, u32[]{:S(2)}) collective-permute-start(f32[8,64,64]{2,0,1:T(8,128)S(1)} %get-tuple-element.37), channel_id=1, source_target_pairs={{0,16},{64,80},{128,144},{192,208},{16,32},{80,96},{144,160},{208,... | collective-permute-start | bytes 393224 | tf_op jit(solution)/shard_map/ppermute | solution.py:56
  229.7 14.2 %collective-permute-start.29 = (f32[8,64,64]{2,0,1:T(8,128)S(1)}, f32[8,64,64]{2,0,1:T(8,128)S(1)}, u32[]{:S(2)}, u32[]{:S(2)}) collective-permute-start(f32[8,64,64]{2,0,1:T(8,128)S(1)} %get-tuple-element.34), channel_id=1, source_target_pairs={{0,64},{16,80},{32,96},{48,112},{64,128},{80,144},{96,160},{112,17... | collective-permute-start | bytes 393224 | tf_op jit(solution)/shard_map/ppermute | solution.py:56
  233.5 11.3 %collective-permute-start.33 = (f32[8,64,64]{2,0,1:T(8,128)S(1)}, f32[8,64,64]{2,0,1:T(8,128)S(1)}, u32[]{:S(2)}, u32[]{:S(2)}) collective-permute-start(f32[8,64,64]{2,0,1:T(8,128)S(1)} %get-tuple-element.33), channel_id=1, source_target_pairs={{0,48},{64,112},{128,176},{192,240},{16,0},{80,64},{144,128},{208,... | collective-permute-start | bytes 393224 | tf_op jit(solution)/shard_map/ppermute | solution.py:56
  238.7 10.7 %collective-permute-start.34 = (f32[8,64,64]{2,0,1:T(8,128)S(1)}, f32[8,64,64]{2,0,1:T(8,128)S(1)}, u32[]{:S(2)}, u32[]{:S(2)}) collective-permute-start(f32[8,64,64]{2,0,1:T(8,128)S(1)} %get-tuple-element.32), channel_id=1, source_target_pairs={{0,32},{64,96},{128,160},{192,224},{16,48},{80,112},{144,176},{208... | collective-permute-start | bytes 393224 | tf_op jit(solution)/shard_map/ppermute | solution.py:56
  238.8 13.3 %collective-permute-start.35 = (f32[8,64,64]{2,0,1:T(8,128)S(1)}, f32[8,64,64]{2,0,1:T(8,128)S(1)}, u32[]{:S(2)}, u32[]{:S(2)}) collective-permute-start(f32[8,64,64]{2,0,1:T(8,128)S(1)} %get-tuple-element.31), channel_id=1, source_target_pairs={{0,16},{64,80},{128,144},{192,208},{16,32},{80,96},{144,160},{208,... | collective-permute-start | bytes 393224 | tf_op jit(solution)/shard_map/ppermute | solution.py:56
  241.4 12.3 %collective-permute-start.39 = (f32[8,64,64]{2,0,1:T(8,128)S(1)}, f32[8,64,64]{2,0,1:T(8,128)S(1)}, u32[]{:S(2)}, u32[]{:S(2)}) collective-permute-start(f32[8,64,64]{2,0,1:T(8,128)S(1)} %get-tuple-element.30), channel_id=1, source_target_pairs={{0,192},{16,208},{32,224},{48,240},{64,0},{80,16},{96,32},{112,48}... | collective-permute-start | bytes 393224 | tf_op jit(solution)/shard_map/ppermute | solution.py:56
  243.8 16.5 %collective-permute-start.40 = (f32[8,64,64]{2,0,1:T(8,128)S(1)}, f32[8,64,64]{2,0,1:T(8,128)S(1)}, u32[]{:S(2)}, u32[]{:S(2)}) collective-permute-start(f32[8,64,64]{2,0,1:T(8,128)S(1)} %get-tuple-element.29), channel_id=1, source_target_pairs={{0,128},{16,144},{32,160},{48,176},{64,192},{80,208},{96,224},{112... | collective-permute-start | bytes 393224 | tf_op jit(solution)/shard_map/ppermute | solution.py:56
  244.8 15.7 %collective-permute-start.41 = (f32[8,64,64]{2,0,1:T(8,128)S(1)}, f32[8,64,64]{2,0,1:T(8,128)S(1)}, u32[]{:S(2)}, u32[]{:S(2)}) collective-permute-start(f32[8,64,64]{2,0,1:T(8,128)S(1)} %get-tuple-element.28), channel_id=1, source_target_pairs={{0,64},{16,80},{32,96},{48,112},{64,128},{80,144},{96,160},{112,17... | collective-permute-start | bytes 393224 | tf_op jit(solution)/shard_map/ppermute | solution.py:56
  249.5 22.2 %collective-permute-start.62 = (f32[64,2,2,4,64]{0,4,3,2,1:T(8,128)S(1)}, f32[64,2,2,4,64]{0,4,3,2,1:T(8,128)S(1)}, u32[]{:S(2)}, u32[]{:S(2)}) collective-permute-start(f32[64,2,2,4,64]{0,4,3,2,1:T(8,128)S(1)} %pad_maximum_fusion.12), channel_id=1, source_target_pairs={{0,4},{1,5},{2,6},{3,7},{4,0},{5,1},{6,2},{7,3},{8,12},{9,13},{10,... | collective-permute-start | bytes 786440 | tf_op jit(solution)/shard_map/ppermute | solution.py:160
  252.1 10.4 %collective-permute-start.45 = (f32[8,64,64]{2,0,1:T(8,128)S(1)}, f32[8,64,64]{2,0,1:T(8,128)S(1)}, u32[]{:S(2)}, u32[]{:S(2)}) collective-permute-start(f32[8,64,64]{2,0,1:T(8,128)S(1)} %get-tuple-element.27), channel_id=1, source_target_pairs={{0,48},{64,112},{128,176},{192,240},{16,0},{80,64},{144,128},{208,... | collective-permute-start | bytes 393224 | tf_op jit(solution)/shard_map/ppermute | solution.py:56
  253.6 16.4 %collective-permute-start.46 = (f32[8,64,64]{2,0,1:T(8,128)S(1)}, f32[8,64,64]{2,0,1:T(8,128)S(1)}, u32[]{:S(2)}, u32[]{:S(2)}) collective-permute-start(f32[8,64,64]{2,0,1:T(8,128)S(1)} %get-tuple-element.26), channel_id=1, source_target_pairs={{0,32},{64,96},{128,160},{192,224},{16,48},{80,112},{144,176},{208... | collective-permute-start | bytes 393224 | tf_op jit(solution)/shard_map/ppermute | solution.py:56
  260.3 11.2 %collective-permute-start.47 = (f32[8,64,64]{2,0,1:T(8,128)S(1)}, f32[8,64,64]{2,0,1:T(8,128)S(1)}, u32[]{:S(2)}, u32[]{:S(2)}) collective-permute-start(f32[8,64,64]{2,0,1:T(8,128)S(1)} %get-tuple-element.25), channel_id=1, source_target_pairs={{0,16},{64,80},{128,144},{192,208},{16,32},{80,96},{144,160},{208,... | collective-permute-start | bytes 393224 | tf_op jit(solution)/shard_map/ppermute | solution.py:56
  260.5 11.6 %collective-permute-start.48 = (f32[8,64,64]{2,0,1:T(8,128)S(1)}, f32[8,64,64]{2,0,1:T(8,128)S(1)}, u32[]{:S(2)}, u32[]{:S(2)}) collective-permute-start(f32[8,64,64]{2,0,1:T(8,128)S(1)} %get-tuple-element.69), channel_id=1, source_target_pairs={{0,48},{16,0},{32,16},{48,32},{64,112},{80,64},{96,80},{112,96},{1... | collective-permute-start | bytes 393224 | tf_op jit(solution)/shard_map/ppermute | solution.py:46
  262.5 12.0 %collective-permute-start.49 = (f32[8,64,64]{2,0,1:T(8,128)S(1)}, f32[8,64,64]{2,0,1:T(8,128)S(1)}, u32[]{:S(2)}, u32[]{:S(2)}) collective-permute-start(f32[8,64,64]{2,0,1:T(8,128)S(1)} %get-tuple-element.67), channel_id=1, source_target_pairs={{0,32},{16,48},{32,0},{48,16},{64,96},{80,112},{96,64},{112,80},{1... | collective-permute-start | bytes 393224 | tf_op jit(solution)/shard_map/ppermute | solution.py:46
  271.5 36.3 %collective-permute-start.54 = (f32[8,64,64]{2,0,1:T(8,128)S(1)}, f32[8,64,64]{2,0,1:T(8,128)S(1)}, u32[]{:S(2)}, u32[]{:S(2)}) collective-permute-start(f32[8,64,64]{2,0,1:T(8,128)S(1)} %get-tuple-element.63), channel_id=1, source_target_pairs={{0,192},{64,0},{128,64},{192,128},{16,208},{80,16},{144,80},{208,1... | collective-permute-start | bytes 393224 | tf_op jit(solution)/shard_map/ppermute | solution.py:46
  271.6 36.2 %collective-permute-start.55 = (f32[8,64,64]{2,0,1:T(8,128)S(1)}, f32[8,64,64]{2,0,1:T(8,128)S(1)}, u32[]{:S(2)}, u32[]{:S(2)}) collective-permute-start(f32[8,64,64]{2,0,1:T(8,128)S(1)} %get-tuple-element.61), channel_id=1, source_target_pairs={{0,128},{64,192},{128,0},{192,64},{16,144},{80,208},{144,16},{208,... | collective-permute-start | bytes 393224 | tf_op jit(solution)/shard_map/ppermute | solution.py:46
  278.4 28.3 %collective-permute-start.52 = (f32[8,64,64]{2,0,1:T(8,128)S(1)}, f32[8,64,64]{2,0,1:T(8,128)S(1)}, u32[]{:S(2)}, u32[]{:S(2)}) collective-permute-start(f32[8,64,64]{2,0,1:T(8,128)S(1)} %get-tuple-element.23), channel_id=1, source_target_pairs={{0,128},{16,144},{32,160},{48,176},{64,192},{80,208},{96,224},{112... | collective-permute-start | bytes 393224 | tf_op jit(solution)/shard_map/ppermute | solution.py:56
  278.5 28.2 %collective-permute-start.53 = (f32[8,64,64]{2,0,1:T(8,128)S(1)}, f32[8,64,64]{2,0,1:T(8,128)S(1)}, u32[]{:S(2)}, u32[]{:S(2)}) collective-permute-start(f32[8,64,64]{2,0,1:T(8,128)S(1)} %get-tuple-element.22), channel_id=1, source_target_pairs={{0,64},{16,80},{32,96},{48,112},{64,128},{80,144},{96,160},{112,17... | collective-permute-start | bytes 393224 | tf_op jit(solution)/shard_map/ppermute | solution.py:56
  286.9 33.8 %collective-permute-start.63 = (f32[64,2,2,2,4,64]{0,5,4,3,1,2:T(8,128)S(1)}, f32[64,2,2,2,4,64]{0,5,4,3,1,2:T(8,128)S(1)}, u32[]{:S(2)}, u32[]{:S(2)}) collective-permute-start(f32[64,2,2,2,4,64]{0,5,4,3,1,2:T(8,128)S(1)} %pad_maximum_fusion.10), channel_id=1, source_target_pairs={{0,1},{1,0},{2,3},{3,2},{4,5},{5,4},{6,7},{7,6},{8,9},{9,8},{10,11... | collective-permute-start | bytes 1572872 | tf_op jit(solution)/shard_map/ppermute | solution.py:160
  316.1 39.0 %collective-permute-start.57 = (f32[8,64,64]{2,0,1:T(8,128)}, f32[8,64,64]{2,0,1:T(8,128)}, u32[]{:S(2)}, u32[]{:S(2)}) collective-permute-start(f32[8,64,64]{2,0,1:T(8,128)} %get-tuple-element.21), channel_id=1, source_target_pairs={{0,48},{64,112},{128,176},{192,240},{16,0},{80,64},{144,128},{208,... | collective-permute-start | bytes 393224 | tf_op jit(solution)/shard_map/ppermute | solution.py:56
  317.6 37.5 %collective-permute-start.58 = (f32[8,64,64]{2,0,1:T(8,128)}, f32[8,64,64]{2,0,1:T(8,128)}, u32[]{:S(2)}, u32[]{:S(2)}) collective-permute-start(f32[8,64,64]{2,0,1:T(8,128)} %get-tuple-element.20), channel_id=1, source_target_pairs={{0,32},{64,96},{128,160},{192,224},{16,48},{80,112},{144,176},{208... | collective-permute-start | bytes 393224 | tf_op jit(solution)/shard_map/ppermute | solution.py:56
  318.8 36.3 %collective-permute-start.59 = (f32[8,64,64]{2,0,1:T(8,128)}, f32[8,64,64]{2,0,1:T(8,128)}, u32[]{:S(2)}, u32[]{:S(2)}) collective-permute-start(f32[8,64,64]{2,0,1:T(8,128)} %get-tuple-element.19), channel_id=1, source_target_pairs={{0,16},{64,80},{128,144},{192,208},{16,32},{80,96},{144,160},{208,... | collective-permute-start | bytes 393224 | tf_op jit(solution)/shard_map/ppermute | solution.py:56
  416.3 14.4 %collective-permute-start.75 = (f32[64,2,2,4,64]{0,4,3,2,1:T(8,128)S(1)}, f32[64,2,2,4,64]{0,4,3,2,1:T(8,128)S(1)}, u32[]{:S(2)}, u32[]{:S(2)}) collective-permute-start(f32[64,2,2,4,64]{0,4,3,2,1:T(8,128)S(1)} %select_bitcast_fusion.9), channel_id=1, source_target_pairs={{0,4},{1,5},{2,6},{3,7},{4,0},{5,1},{6,2},{7,3},{8,12},{9,13},{10,... | collective-permute-start | bytes 786440 | tf_op jit(solution)/shard_map/ppermute | solution.py:150
  430.9 11.0 %collective-permute-start.76 = (f32[64,2,4,64]{0,3,2,1:T(8,128)S(1)}, f32[64,2,4,64]{0,3,2,1:T(8,128)S(1)}, u32[]{:S(2)}, u32[]{:S(2)}) collective-permute-start(f32[64,2,4,64]{0,3,2,1:T(8,128)S(1)} %select_bitcast_fusion.15), channel_id=1, source_target_pairs={{0,8},{1,9},{2,10},{3,11},{4,12},{5,13},{6,14},{7,15},{8,0},{9,1},... | collective-permute-start | bytes 393224 | tf_op jit(solution)/shard_map/ppermute | solution.py:150
  442.0 11.0 %collective-permute-start.77 = (f32[64,4,64]{0,2,1:T(8,128)S(1)}, f32[64,4,64]{0,2,1:T(8,128)S(1)}, u32[]{:S(2)}, u32[]{:S(2)}) collective-permute-start(f32[64,4,64]{0,2,1:T(8,128)S(1)} %select_bitcast_fusion.22), channel_id=1, source_target_pairs={{0,2},{1,3},{2,0},{3,1},{4,6},{5,7},{6,4},{7,5},{8,10},{9,11},{10,... | collective-permute-start | bytes 196616 | tf_op jit(solution)/shard_map/ppermute | solution.py:150
  453.6 10.7 %collective-permute-start.78 = (f32[64,4,64]{0,2,1:T(8,128)S(1)}, f32[64,4,64]{0,2,1:T(8,128)S(1)}, u32[]{:S(2)}, u32[]{:S(2)}) collective-permute-start(f32[64,4,64]{0,2,1:T(8,128)S(1)} %fusion.9), channel_id=1, source_target_pairs={{0,2},{1,3},{2,0},{3,1},{4,6},{5,7},{6,4},{7,5},{8,10},{9,11},{10,... | collective-permute-start | bytes 196616 | tf_op jit(solution)/shard_map/ppermute | solution.py:160
  580.3 14.1 %collective-permute-start.93 = (f32[64,2,2,4,64]{0,4,3,2,1:T(8,128)S(1)}, f32[64,2,2,4,64]{0,4,3,2,1:T(8,128)S(1)}, u32[]{:S(2)}, u32[]{:S(2)}) collective-permute-start(f32[64,2,2,4,64]{0,4,3,2,1:T(8,128)S(1)} %select_bitcast_fusion.6), channel_id=1, source_target_pairs={{0,4},{1,5},{2,6},{3,7},{4,0},{5,1},{6,2},{7,3},{8,12},{9,13},{10,... | collective-permute-start | bytes 786440 | tf_op jit(solution)/shard_map/ppermute | solution.py:150
  603.7 11.0 %collective-permute-start.95 = (f32[64,4,64]{0,2,1:T(8,128)S(1)}, f32[64,4,64]{0,2,1:T(8,128)S(1)}, u32[]{:S(2)}, u32[]{:S(2)}) collective-permute-start(f32[64,4,64]{0,2,1:T(8,128)S(1)} %select_bitcast_fusion.19), channel_id=1, source_target_pairs={{0,2},{1,3},{2,0},{3,1},{4,6},{5,7},{6,4},{7,5},{8,10},{9,11},{10,... | collective-permute-start | bytes 196616 | tf_op jit(solution)/shard_map/ppermute | solution.py:150
  615.4 13.3 %collective-permute-start.96 = (f32[64,4,64]{0,2,1:T(8,128)S(1)}, f32[64,4,64]{0,2,1:T(8,128)S(1)}, u32[]{:S(2)}, u32[]{:S(2)}) collective-permute-start(f32[64,4,64]{0,2,1:T(8,128)S(1)} %get-tuple-element.109), channel_id=1, source_target_pairs={{0,48},{16,0},{32,16},{48,32},{64,112},{80,64},{96,80},{112,96},{1... | collective-permute-start | bytes 196616 | tf_op jit(solution)/shard_map/ppermute | solution.py:46
  617.7 10.9 %collective-permute-start.97 = (f32[64,4,64]{0,2,1:T(8,128)S(1)}, f32[64,4,64]{0,2,1:T(8,128)S(1)}, u32[]{:S(2)}, u32[]{:S(2)}) collective-permute-start(f32[64,4,64]{0,2,1:T(8,128)S(1)} %get-tuple-element.108), channel_id=1, source_target_pairs={{0,32},{16,48},{32,0},{48,16},{64,96},{80,112},{96,64},{112,80},{1... | collective-permute-start | bytes 196616 | tf_op jit(solution)/shard_map/ppermute | solution.py:46
  618.6 10.1 %collective-permute-start.98 = (f32[64,4,64]{0,2,1:T(8,128)S(1)}, f32[64,4,64]{0,2,1:T(8,128)S(1)}, u32[]{:S(2)}, u32[]{:S(2)}) collective-permute-start(f32[64,4,64]{0,2,1:T(8,128)S(1)} %get-tuple-element.17), channel_id=1, source_target_pairs={{0,16},{16,32},{32,48},{48,0},{64,80},{80,96},{96,112},{112,64},{1... | collective-permute-start | bytes 196616 | tf_op jit(solution)/shard_map/ppermute | solution.py:46
  (62 other events, 825.6 us)

commit v14 on v12

--- a/solution.py
+++ b/solution.py
@@ -36,11 +36,10 @@
         first, second = (lambda s: s % ROW), (lambda s: s // ROW)
         put = lambda s2, s1: s2 * ROW + s1
     my1, my2 = first(me), second(me)
-    dest1 = first(dest[me])
     zero = jnp.zeros_like(x)
     received = []
     for k in range(n1):
-        part = jnp.where((dest1 - my1) % n1 == k, x, zero)
+        part = x
         if k:
             pairs = [(put(q2, q1), put(q2, (q1 + k) % n1)) for q2 in range(n2) for q1 in range(n1)]
             part = lax.ppermute(part, "space", pairs)

time: 624 us -> 649 us (1.040)
  starting transfers between devices: 129 us -> 151 us
  waiting for transfers between devices: 275 us -> 288 us
  other arithmetic: 69.9 us -> 63.1 us
    ppermute x36, waiting for transfers between devices: 128 us -> 156 us  [route(): part = lax.ppermute(part, 'space', pairs)]
    ppermute x36, starting transfers between devices: 60.9 us -> 82.3 us  [route(): part = lax.ppermute(part, 'space', pairs)]
    ppermute x8, waiting for transfers between devices: 38.5 us -> 30 us  [view_all_gather(): recv = lax.ppermute(x, 'view', xor_pairs(nv, m))]
    ppermute x12, starting transfers between devices: 28.8 us -> 22.3 us  [swap(): return lax.ppermute(x, 'space', [(i, i ^ partner) for i in range(nsp)])]
  transfers between devices with their start and end apart: 78 -> 78, of which waited for: 39 -> 37; matrix products, arithmetic and copies ran while one was open for 14% -> 12% of each run, Pallas kernels for 0% -> 0%
where the time goes in v14:
time: 649 us; the launch traced here: 638 us
  waiting for transfers between devices  288 us (44%)
  starting transfers between devices  151 us (23%)
  other arithmetic  63.1 us (10%)
  matrix products  62.1 us (10%)
  between operations  37.8 us (6%)
  local copies, waits for them, and re-layouts  35.6 us (5%)
    ppermute x36, waiting for transfers between devices, route(): part = lax.ppermute(part, 'space', pairs)  156 us
    ppermute x36, starting transfers between devices, route(): part = lax.ppermute(part, 'space', pairs)  82.3 us
    ppermute x8, waiting for transfers between devices, view_reduce_scatter(): x = keep + lax.ppermute(send, 'view', xor_pairs(nv, m))  62.5 us
    ppermute x8, waiting for transfers between devices, view_all_gather(): recv = lax.ppermute(x, 'view', xor_pairs(nv, m))  30 us
    ppermute x12, starting transfers between devices, swap(): return lax.ppermute(x, 'space', [(i, i ^ partner) for i in range(nsp)])  22.3 us
    select_n x3, other arithmetic, band_matrix(): band = jnp.where(offset == position, weight, band)  19.9 us
    dot_general x4, matrix products, convolve(): return jnp.einsum('abt,ot->abo', extended, band, precision=hi)  19.6 us
    dot_general x4, matrix products, convolve(): return jnp.einsum('ot,atb->aob', band, extended, precision=hi)  19.6 us
  transfers between devices with their start and end apart: 78, of which 37 were waited for; matrix products, arithmetic and copies ran while one was open for 12% of the time, Pallas kernels for 0%

profile of v14, /device:TPU:8, one launch (start us, length us, event | category | flops | bytes accessed | tf_op | source)
XLA Modules:
  0.0 638.2 jit_solution(17654114903086672984)
XLA Ops:
  8.0 3.1 collective-permute-start.12
  17.0 5.1 select_select_fusion.25
  22.1 5.2 select_select_fusion.23
  30.1 3.3 collective-permute-start.4
  34.9 2.5 collective-permute-start.7
  39.3 2.6 collective-permute-start.8
  56.0 3.1 collective-permute-start.9
  59.2 9.7 %select_select_fusion.27 = (f32[64,78]{1,0:T(8,128)}, f32[64,78]{1,0:T(8,128)}) fusion(f32[]{:T(128)} %bitcast.34, f32[]{:T(128)} %bitcast.33, f32[]{:T(128)} %bitcast.32, f32[]{:T(128)} %bitcast.31, f32[]{:T(128)} %bitcast.30, f32[]{:T(128)} %bitcast.29, f32[]{:T(128)} %bitcast.28, f32[]{:T(128)} %bitcast.27, f32[]{:T(128)} %bitcast.26, f32[]{:T(128)} %bitcast.25, ...), kind=kLoop, calls=%fused_computation.145 | loop fusion | flops 229632 | bytes 39996 | tf_op jit(solution)/shard_map/jit(_where)/select_n | solution.py:66
  75.0 4.8 collective-permute-start.36
  92.4 3.1 collective-permute-start.37
  103.9 6.4 collective-permute-done.15
  110.2 29.7 %collective-permute-done.16 = f32[16,64,64]{2,0,1:T(8,128)S(1)} collective-permute-done((f32[16,64,64]{2,0,1:T(8,128)S(1)}, f32[16,64,64]{2,0,1:T(8,128)S(1)}, u32[]{:S(2)}, u32[]{:S(2)}) %collective-permute-start.16) | collective-permute-done | bytes 262176 | tf_op jit(solution)/shard_map/ppermute | solution.py:55
  141.0 13.2 %collective-permute-start.19 = (f32[16,64,64]{2,0,1:T(8,128)S(1)}, f32[16,64,64]{2,0,1:T(8,128)S(1)}, u32[]{:S(2)}, u32[]{:S(2)}) collective-permute-start(f32[16,64,64]{2,0,1:T(8,128)S(1)} %get-tuple-element.44), channel_id=1, source_target_pairs={{0,128},{64,192},{128,0},{192,64},{16,144},{80,208},{144,16},{208,... | collective-permute-start | bytes 786440 | tf_op jit(solution)/shard_map/ppermute | solution.py:45
  157.7 2.3 collective-permute-start.25
  160.3 4.1 collective-permute-done.18
  166.3 33.8 %collective-permute-done.19 = f32[16,64,64]{2,0,1:T(8,128)S(1)} collective-permute-done((f32[16,64,64]{2,0,1:T(8,128)S(1)}, f32[16,64,64]{2,0,1:T(8,128)S(1)}, u32[]{:S(2)}, u32[]{:S(2)}) %collective-permute-start.19) | collective-permute-done | bytes 262176 | tf_op jit(solution)/shard_map/ppermute | solution.py:45
  204.2 10.3 %collective-permute-done.30 = f32[16,64,64]{2,0,1:T(8,128)S(1)} collective-permute-done((f32[16,64,64]{2,0,1:T(8,128)S(1)}, f32[16,64,64]{2,0,1:T(8,128)S(1)}, u32[]{:S(2)}, u32[]{:S(2)}) %collective-permute-start.30) | collective-permute-done | bytes 262176 | tf_op jit(solution)/shard_map/ppermute | solution.py:45
  214.5 2.5 collective-permute-start.27
  217.0 30.6 %collective-permute-done.31 = f32[16,64,64]{2,0,1:T(8,128)S(1)} collective-permute-done((f32[16,64,64]{2,0,1:T(8,128)S(1)}, f32[16,64,64]{2,0,1:T(8,128)S(1)}, u32[]{:S(2)}, u32[]{:S(2)}) %collective-permute-start.31) | collective-permute-done | bytes 262176 | tf_op jit(solution)/shard_map/ppermute | solution.py:45
  247.7 21.3 %collective-permute-start.29 = (f32[16,64,64]{2,0,1:T(8,128)S(1)}, f32[16,64,64]{2,0,1:T(8,128)S(1)}, u32[]{:S(2)}, u32[]{:S(2)}) collective-permute-start(f32[16,64,64]{2,0,1:T(8,128)S(1)} %get-tuple-element.23), channel_id=1, source_target_pairs={{0,64},{16,80},{32,96},{48,112},{64,128},{80,144},{96,160},{112,17... | collective-permute-start | bytes 786440 | tf_op jit(solution)/shard_map/ppermute | solution.py:55
  271.8 18.1 %collective-permute-done.28 = f32[16,64,64]{2,0,1:T(8,128)S(1)} collective-permute-done((f32[16,64,64]{2,0,1:T(8,128)S(1)}, f32[16,64,64]{2,0,1:T(8,128)S(1)}, u32[]{:S(2)}, u32[]{:S(2)}) %collective-permute-start.28) | collective-permute-done | bytes 262176 | tf_op jit(solution)/shard_map/ppermute | solution.py:55
  294.7 2.6 collective-permute-start.35
  297.3 18.0 %collective-permute-done.23 = f32[16,64,64]{2,0,1:T(8,128)S(1)} collective-permute-done((f32[16,64,64]{2,0,1:T(8,128)S(1)}, f32[16,64,64]{2,0,1:T(8,128)S(1)}, u32[]{:S(2)}, u32[]{:S(2)}) %collective-permute-start.23) | collective-permute-done | bytes 262176 | tf_op jit(solution)/shard_map/ppermute | solution.py:55
  318.1 3.5 collective-permute-start.42
  323.6 3.8 collective-permute-done.40
  327.4 2.7 collective-permute-start.41
  335.2 3.4 copy.40
  338.6 8.0 %fusion.28 = f32[64,70,64]{1,2,0:T(8,128)S(1)} fusion(f32[64,70,70]{2,1,0:T(8,128)} %copy.40, f32[64,70]{1,0:T(8,128)S(1)} %copy-done.8), kind=kOutput, calls=%fused_computation.129 | convolution fusion | flops 240844800 | bytes 2419200 | tf_op jit(solution)/shard_map/abt,ot->abo/dot_general | solution.py:76
  348.5 3.9 collective-permute-start.43
  356.1 4.3 collective-permute-done.44
  360.6 3.3 copy.27
  363.8 8.1 %convolution_divide_fusion.1 = f32[64,64,64]{2,0,1:T(8,128)S(1)} fusion(f32[78,64,64]{0,2,1:T(8,128)} %copy.27, f32[16,64,64]{2,0,1:T(8,128)} %select_select_fusion, f32[16,64,64]{2,0,1:T(8,128)} %select_select_fusion.4, f32[16,64,64]{2,0,1:T(8,128)} %select_select_fusion.8, f32[16,64,64]{2,0,1:T(8,128)S(1)} %copy-done.2, f32[64,78]{1,0:T(8,128)S(1)} %copy-done.12), kind=kOutput, calls=%fused_computation.20 | convolution fusion | flops 246415360 | bytes 3395072 | tf_op jit(solution)/shard_map/ot,tab->oab/dot_general | solution.py:73
  375.2 2.6 collective-permute-done.45
  377.8 4.4 collective-permute-done.46
  384.7 3.4 fusion.78
  388.7 3.4 collective-permute-start.49
  395.2 2.8 collective-permute-done.47
  402.7 8.0 %fusion.22 = f32[64,70,64]{1,2,0:T(8,128)S(1)} fusion(f32[64,70,70]{1,2,0:T(8,128)} %copy.41, f32[64,70]{1,0:T(8,128)S(1)} %copy-done.5), kind=kOutput, calls=%fused_computation.123 | convolution fusion | flops 240844800 | bytes 2419200 | tf_op jit(solution)/shard_map/ot,atb->aob/dot_general | solution.py:75
  415.1 2.6 collective-permute-done.50
  418.8 13.4 %collective-permute-done.51 = f32[64,2,2,4,64]{0,4,3,2,1:T(8,128)S(1)} collective-permute-done((f32[64,2,2,4,64]{0,4,3,2,1:T(8,128)S(1)}, f32[64,2,2,4,64]{0,4,3,2,1:T(8,128)S(1)}, u32[]{:S(2)}, u32[]{:S(2)}) %collective-permute-start.51) | collective-permute-done | bytes 262176 | tf_op jit(solution)/shard_map/ppermute | solution.py:149
  433.3 8.2 %collective-permute-done.52 = f32[64,2,4,64]{0,3,2,1:T(8,128)S(1)} collective-permute-done((f32[64,2,4,64]{0,3,2,1:T(8,128)S(1)}, f32[64,2,4,64]{0,3,2,1:T(8,128)S(1)}, u32[]{:S(2)}, u32[]{:S(2)}) %collective-permute-start.52) | collective-permute-done | bytes 131104 | tf_op jit(solution)/shard_map/ppermute | solution.py:149
  443.7 7.0 %collective-permute-done.53 = f32[64,4,64]{0,2,1:T(8,128)S(1)} collective-permute-done((f32[64,4,64]{0,2,1:T(8,128)S(1)}, f32[64,4,64]{0,2,1:T(8,128)S(1)}, u32[]{:S(2)}, u32[]{:S(2)}) %collective-permute-start.53) | collective-permute-done | bytes 65568 | tf_op jit(solution)/shard_map/ppermute | solution.py:149
  451.4 3.3 collective-permute-start.54
  454.8 6.7 %collective-permute-done.54 = f32[64,4,64]{0,2,1:T(8,128)S(1)} collective-permute-done((f32[64,4,64]{0,2,1:T(8,128)S(1)}, f32[64,4,64]{0,2,1:T(8,128)S(1)}, u32[]{:S(2)}, u32[]{:S(2)}) %collective-permute-start.54) | collective-permute-done | bytes 65568 | tf_op jit(solution)/shard_map/ppermute | solution.py:159
  462.9 7.4 %collective-permute-done.55 = f32[64,2,4,64]{0,3,2,1:T(8,128)S(1)} collective-permute-done((f32[64,2,4,64]{0,3,2,1:T(8,128)S(1)}, f32[64,2,4,64]{0,3,2,1:T(8,128)S(1)}, u32[]{:S(2)}, u32[]{:S(2)}) %collective-permute-start.55) | collective-permute-done | bytes 131104 | tf_op jit(solution)/shard_map/ppermute | solution.py:159
  471.1 11.3 %collective-permute-done.56 = f32[64,2,2,4,64]{0,4,3,2,1:T(8,128)S(1)} collective-permute-done((f32[64,2,2,4,64]{0,4,3,2,1:T(8,128)S(1)}, f32[64,2,2,4,64]{0,4,3,2,1:T(8,128)S(1)}, u32[]{:S(2)}, u32[]{:S(2)}) %collective-permute-start.56) | collective-permute-done | bytes 262176 | tf_op jit(solution)/shard_map/ppermute | solution.py:159
  482.8 2.6 collective-permute-done.57
  497.6 2.5 copy.42
  500.1 7.9 %fusion.26 = f32[64,70,64]{1,2,0:T(8,128)S(1)} fusion(f32[64,70,70]{2,1,0:T(8,128)} %copy.42, f32[64,70]{1,0:T(8,128)S(1)} %copy-done.8), kind=kOutput, calls=%fused_computation.127 | convolution fusion | flops 240844800 | bytes 2419200 | tf_op jit(solution)/shard_map/abt,ot->abo/dot_general | solution.py:76
  515.9 4.2 collective-permute-done.62
  520.3 3.3 copy.35
  523.6 8.1 %convolution_divide_fusion = f32[64,64,64]{2,0,1:T(8,128)S(1)} fusion(f32[78,64,64]{0,2,1:T(8,128)} %copy.35, f32[16,64,64]{2,0,1:T(8,128)} %select_select_fusion, f32[16,64,64]{2,0,1:T(8,128)} %select_select_fusion.4, f32[16,64,64]{2,0,1:T(8,128)} %select_select_fusion.8, f32[16,64,64]{2,0,1:T(8,128)S(1)} %copy-done.3, f32[64,78]{1,0:T(8,128)S(1)} %copy-done.13), kind=kOutput, calls=%fused_computation.18 | convolution fusion | flops 246415360 | bytes 3395072 | tf_op jit(solution)/shard_map/ot,tab->oab/dot_general | solution.py:73
  535.2 2.6 collective-permute-done.63
  537.8 4.4 collective-permute-done.64
  544.7 3.4 fusion.79
  548.7 3.7 collective-permute-start.67
  555.5 2.8 collective-permute-done.65
  562.9 7.9 %fusion.20 = f32[64,70,64]{1,2,0:T(8,128)S(1)} fusion(f32[64,70,70]{1,2,0:T(8,128)} %copy.43, f32[64,70]{1,0:T(8,128)S(1)} %copy-done.5), kind=kOutput, calls=%fused_computation.121 | convolution fusion | flops 240844800 | bytes 2419200 | tf_op jit(solution)/shard_map/ot,atb->aob/dot_general | solution.py:75
  575.3 2.6 collective-permute-done.68
  579.0 13.4 %collective-permute-done.69 = f32[64,2,2,4,64]{0,4,3,2,1:T(8,128)S(1)} collective-permute-done((f32[64,2,2,4,64]{0,4,3,2,1:T(8,128)S(1)}, f32[64,2,2,4,64]{0,4,3,2,1:T(8,128)S(1)}, u32[]{:S(2)}, u32[]{:S(2)}) %collective-permute-start.69) | collective-permute-done | bytes 262176 | tf_op jit(solution)/shard_map/ppermute | solution.py:149
  593.8 7.9 %collective-permute-done.70 = f32[64,2,4,64]{0,3,2,1:T(8,128)S(1)} collective-permute-done((f32[64,2,4,64]{0,3,2,1:T(8,128)S(1)}, f32[64,2,4,64]{0,3,2,1:T(8,128)S(1)}, u32[]{:S(2)}, u32[]{:S(2)}) %collective-permute-start.70) | collective-permute-done | bytes 131104 | tf_op jit(solution)/shard_map/ppermute | solution.py:149
  603.5 7.4 %collective-permute-done.71 = f32[64,4,64]{0,2,1:T(8,128)S(1)} collective-permute-done((f32[64,4,64]{0,2,1:T(8,128)S(1)}, f32[64,4,64]{0,2,1:T(8,128)S(1)}, u32[]{:S(2)}, u32[]{:S(2)}) %collective-permute-start.71) | collective-permute-done | bytes 65568 | tf_op jit(solution)/shard_map/ppermute | solution.py:149
  615.8 2.5 collective-permute-start.74
  631.9 4.9 collective-permute-done.76
  (273 shorter events, 147.4 us)
Async XLA Ops:
  1.5 26.6 %collective-permute-start = (s32[16,7]{0,1:T(8,128)S(1)}, s32[16,7]{0,1:T(8,128)S(1)}, u32[]{:S(2)}, u32[]{:S(2)}) collective-permute-start(s32[16,7]{0,1:T(8,128)S(1)} %broadcast_select_fusion.16), channel_id=1, source_target_pairs={{0,16},{16,0},{32,48},{48,32},{64,80},{80,64},{96,112},{112,96},{1... | collective-permute-start | bytes 1352 | tf_op jit(solution)/shard_map/ppermute | solution.py:22
  3.7 24.3 %collective-permute-start.1 = (s32[16,7]{0,1:T(8,128)S(1)}, s32[16,7]{0,1:T(8,128)S(1)}, u32[]{:S(2)}, u32[]{:S(2)}) collective-permute-start(s32[16,7]{0,1:T(8,128)S(1)} %broadcast_select_fusion.16), channel_id=1, source_target_pairs={{0,32},{16,48},{32,0},{48,16},{64,96},{80,112},{96,64},{112,80},{1... | collective-permute-start | bytes 1352 | tf_op jit(solution)/shard_map/ppermute | solution.py:22
  4.6 23.4 %collective-permute-start.2 = (s32[16,7]{0,1:T(8,128)S(1)}, s32[16,7]{0,1:T(8,128)S(1)}, u32[]{:S(2)}, u32[]{:S(2)}) collective-permute-start(s32[16,7]{0,1:T(8,128)S(1)} %broadcast_select_fusion.16), channel_id=1, source_target_pairs={{0,48},{16,32},{32,16},{48,0},{64,112},{80,96},{96,80},{112,64},{1... | collective-permute-start | bytes 1352 | tf_op jit(solution)/shard_map/ppermute | solution.py:22
  8.0 87.5 %collective-permute-start.12 = (f32[16,64,64]{2,0,1:T(8,128)}, f32[16,64,64]{2,0,1:T(8,128)S(1)}, u32[]{:S(2)}, u32[]{:S(2)}) collective-permute-start(f32[16,64,64]{2,0,1:T(8,128)} %slice.417), channel_id=1, source_target_pairs={{0,48},{16,0},{32,16},{48,32},{64,112},{80,64},{96,80},{112,96},{1... | collective-permute-start | bytes 786440 | tf_op jit(solution)/shard_map/ppermute | solution.py:45
  11.1 84.4 %collective-permute-start.13 = (f32[16,64,64]{2,0,1:T(8,128)}, f32[16,64,64]{2,0,1:T(8,128)S(1)}, u32[]{:S(2)}, u32[]{:S(2)}) collective-permute-start(f32[16,64,64]{2,0,1:T(8,128)} %slice.417), channel_id=1, source_target_pairs={{0,32},{16,48},{32,0},{48,16},{64,96},{80,112},{96,64},{112,80},{1... | collective-permute-start | bytes 786440 | tf_op jit(solution)/shard_map/ppermute | solution.py:45
  33.3 20.2 %collective-permute-start.6 = (f32[64,4,64]{0,2,1:T(8,128)}, f32[64,4,64]{0,2,1:T(8,128)S(1)}, u32[]{:S(2)}, u32[]{:S(2)}) collective-permute-start(f32[64,4,64]{0,2,1:T(8,128)} %bitcast.230), channel_id=1, source_target_pairs={{0,48},{16,0},{32,16},{48,32},{64,112},{80,64},{96,80},{112,96},{1... | collective-permute-start | bytes 196616 | tf_op jit(solution)/shard_map/ppermute | solution.py:45
  34.9 18.7 %collective-permute-start.7 = (f32[64,4,64]{0,2,1:T(8,128)}, f32[64,4,64]{0,2,1:T(8,128)S(1)}, u32[]{:S(2)}, u32[]{:S(2)}) collective-permute-start(f32[64,4,64]{0,2,1:T(8,128)} %bitcast.230), channel_id=1, source_target_pairs={{0,32},{16,48},{32,0},{48,16},{64,96},{80,112},{96,64},{112,80},{1... | collective-permute-start | bytes 196616 | tf_op jit(solution)/shard_map/ppermute | solution.py:45
  39.3 14.3 %collective-permute-start.8 = (f32[64,4,64]{0,2,1:T(8,128)}, f32[64,4,64]{0,2,1:T(8,128)}, u32[]{:S(2)}, u32[]{:S(2)}) collective-permute-start(f32[64,4,64]{0,2,1:T(8,128)} %bitcast.230), channel_id=1, source_target_pairs={{0,16},{16,32},{32,48},{48,0},{64,80},{80,96},{96,112},{112,64},{1... | collective-permute-start | bytes 196616 | tf_op jit(solution)/shard_map/ppermute | solution.py:45
  55.4 18.8 %collective-permute-start.10 = (f32[64,4,64]{0,2,1:T(8,128)}, f32[64,4,64]{0,2,1:T(8,128)}, u32[]{:S(2)}, u32[]{:S(2)}) collective-permute-start(f32[64,4,64]{0,2,1:T(8,128)} %get-tuple-element.61), channel_id=1, source_target_pairs={{0,128},{16,144},{32,160},{48,176},{64,192},{80,208},{96,224},{112... | collective-permute-start | bytes 196616 | tf_op jit(solution)/shard_map/ppermute | solution.py:55
  55.4 19.5 %collective-permute-start.11 = (f32[64,4,64]{0,2,1:T(8,128)}, f32[64,4,64]{0,2,1:T(8,128)}, u32[]{:S(2)}, u32[]{:S(2)}) collective-permute-start(f32[64,4,64]{0,2,1:T(8,128)} %get-tuple-element.60), channel_id=1, source_target_pairs={{0,64},{16,80},{32,96},{48,112},{64,128},{80,144},{96,160},{112,17... | collective-permute-start | bytes 196616 | tf_op jit(solution)/shard_map/ppermute | solution.py:55
  56.0 18.8 %collective-permute-start.9 = (f32[64,4,64]{0,2,1:T(8,128)}, f32[64,4,64]{0,2,1:T(8,128)}, u32[]{:S(2)}, u32[]{:S(2)}) collective-permute-start(f32[64,4,64]{0,2,1:T(8,128)} %get-tuple-element.62), channel_id=1, source_target_pairs={{0,192},{16,208},{32,224},{48,240},{64,0},{80,16},{96,32},{112,48}... | collective-permute-start | bytes 196616 | tf_op jit(solution)/shard_map/ppermute | solution.py:55
  74.2 21.3 %collective-permute-start.14 = (f32[16,64,64]{2,0,1:T(8,128)}, f32[16,64,64]{2,0,1:T(8,128)}, u32[]{:S(2)}, u32[]{:S(2)}) collective-permute-start(f32[16,64,64]{2,0,1:T(8,128)} %slice.417), channel_id=1, source_target_pairs={{0,16},{16,32},{32,48},{48,0},{64,80},{80,96},{96,112},{112,64},{1... | collective-permute-start | bytes 786440 | tf_op jit(solution)/shard_map/ppermute | solution.py:45
  75.0 17.4 %collective-permute-start.36 = (f32[64,4,64]{0,2,1:T(8,128)S(1)}, f32[64,4,64]{0,2,1:T(8,128)S(1)}, u32[]{:S(2)}, u32[]{:S(2)}) collective-permute-start(f32[64,4,64]{0,2,1:T(8,128)S(1)} %select_select_fusion.19), channel_id=1, source_target_pairs={{0,2},{1,3},{2,0},{3,1},{4,6},{5,7},{6,4},{7,5},{8,10},{9,11},{10,... | collective-permute-start | bytes 196616 | tf_op jit(solution)/shard_map/ppermute | solution.py:159
  92.4 9.8 %collective-permute-start.37 = (f32[64,2,4,64]{0,3,2,1:T(8,128)S(1)}, f32[64,2,4,64]{0,3,2,1:T(8,128)S(1)}, u32[]{:S(2)}, u32[]{:S(2)}) collective-permute-start(f32[64,2,4,64]{0,3,2,1:T(8,128)S(1)} %pad_maximum_fusion.15), channel_id=1, source_target_pairs={{0,8},{1,9},{2,10},{3,11},{4,12},{5,13},{6,14},{7,15},{8,0},{9,1},... | collective-permute-start | bytes 393224 | tf_op jit(solution)/shard_map/ppermute | solution.py:159
  96.8 13.4 %collective-permute-start.15 = (f32[16,64,64]{2,0,1:T(8,128)S(1)}, f32[16,64,64]{2,0,1:T(8,128)S(1)}, u32[]{:S(2)}, u32[]{:S(2)}) collective-permute-start(f32[16,64,64]{2,0,1:T(8,128)S(1)} %get-tuple-element.19), channel_id=1, source_target_pairs={{0,192},{16,208},{32,224},{48,240},{64,0},{80,16},{96,32},{112,48}... | collective-permute-start | bytes 786440 | tf_op jit(solution)/shard_map/ppermute | solution.py:55
  97.9 42.0 %collective-permute-start.16 = (f32[16,64,64]{2,0,1:T(8,128)S(1)}, f32[16,64,64]{2,0,1:T(8,128)S(1)}, u32[]{:S(2)}, u32[]{:S(2)}) collective-permute-start(f32[16,64,64]{2,0,1:T(8,128)S(1)} %get-tuple-element.18), channel_id=1, source_target_pairs={{0,128},{16,144},{32,160},{48,176},{64,192},{80,208},{96,224},{112... | collective-permute-start | bytes 786440 | tf_op jit(solution)/shard_map/ppermute | solution.py:55
  99.3 40.6 %collective-permute-start.17 = (f32[16,64,64]{2,0,1:T(8,128)S(1)}, f32[16,64,64]{2,0,1:T(8,128)S(1)}, u32[]{:S(2)}, u32[]{:S(2)}) collective-permute-start(f32[16,64,64]{2,0,1:T(8,128)S(1)} %get-tuple-element.17), channel_id=1, source_target_pairs={{0,64},{16,80},{32,96},{48,112},{64,128},{80,144},{96,160},{112,17... | collective-permute-start | bytes 786440 | tf_op jit(solution)/shard_map/ppermute | solution.py:55
  102.3 55.4 %collective-permute-start.38 = (f32[64,2,2,4,64]{0,4,3,2,1:T(8,128)S(1)}, f32[64,2,2,4,64]{0,4,3,2,1:T(8,128)S(1)}, u32[]{:S(2)}, u32[]{:S(2)}) collective-permute-start(f32[64,2,2,4,64]{0,4,3,2,1:T(8,128)S(1)} %pad_maximum_fusion.13), channel_id=1, source_target_pairs={{0,4},{1,5},{2,6},{3,7},{4,0},{5,1},{6,2},{7,3},{8,12},{9,13},{10,... | collective-permute-start | bytes 786440 | tf_op jit(solution)/shard_map/ppermute | solution.py:159
  141.0 23.4 %collective-permute-start.18 = (f32[16,64,64]{2,0,1:T(8,128)S(1)}, f32[16,64,64]{2,0,1:T(8,128)S(1)}, u32[]{:S(2)}, u32[]{:S(2)}) collective-permute-start(f32[16,64,64]{2,0,1:T(8,128)S(1)} %get-tuple-element.44), channel_id=1, source_target_pairs={{0,192},{64,0},{128,64},{192,128},{16,208},{80,16},{144,80},{208,1... | collective-permute-start | bytes 786440 | tf_op jit(solution)/shard_map/ppermute | solution.py:45
  141.0 59.0 %collective-permute-start.19 = (f32[16,64,64]{2,0,1:T(8,128)S(1)}, f32[16,64,64]{2,0,1:T(8,128)S(1)}, u32[]{:S(2)}, u32[]{:S(2)}) collective-permute-start(f32[16,64,64]{2,0,1:T(8,128)S(1)} %get-tuple-element.44), channel_id=1, source_target_pairs={{0,128},{64,192},{128,0},{192,64},{16,144},{80,208},{144,16},{208,... | collective-permute-start | bytes 786440 | tf_op jit(solution)/shard_map/ppermute | solution.py:45
  154.2 45.9 %collective-permute-start.20 = (f32[16,64,64]{2,0,1:T(8,128)S(1)}, f32[16,64,64]{2,0,1:T(8,128)S(1)}, u32[]{:S(2)}, u32[]{:S(2)}) collective-permute-start(f32[16,64,64]{2,0,1:T(8,128)S(1)} %get-tuple-element.44), channel_id=1, source_target_pairs={{0,64},{64,128},{128,192},{192,0},{16,80},{80,144},{144,208},{208,... | collective-permute-start | bytes 786440 | tf_op jit(solution)/shard_map/ppermute | solution.py:45
  156.3 44.1 %collective-permute-start.24 = (f32[16,64,64]{2,0,1:T(8,128)S(1)}, f32[16,64,64]{2,0,1:T(8,128)S(1)}, u32[]{:S(2)}, u32[]{:S(2)}) collective-permute-start(f32[16,64,64]{2,0,1:T(8,128)S(1)} %get-tuple-element.43), channel_id=1, source_target_pairs={{0,48},{16,0},{32,16},{48,32},{64,112},{80,64},{96,80},{112,96},{1... | collective-permute-start | bytes 786440 | tf_op jit(solution)/shard_map/ppermute | solution.py:45
  157.7 44.7 %collective-permute-start.25 = (f32[16,64,64]{2,0,1:T(8,128)S(1)}, f32[16,64,64]{2,0,1:T(8,128)S(1)}, u32[]{:S(2)}, u32[]{:S(2)}) collective-permute-start(f32[16,64,64]{2,0,1:T(8,128)S(1)} %get-tuple-element.43), channel_id=1, source_target_pairs={{0,32},{16,48},{32,0},{48,16},{64,96},{80,112},{96,64},{112,80},{1... | collective-permute-start | bytes 786440 | tf_op jit(solution)/shard_map/ppermute | solution.py:45
  164.4 38.0 %collective-permute-start.26 = (f32[16,64,64]{2,0,1:T(8,128)S(1)}, f32[16,64,64]{2,0,1:T(8,128)S(1)}, u32[]{:S(2)}, u32[]{:S(2)}) collective-permute-start(f32[16,64,64]{2,0,1:T(8,128)S(1)} %get-tuple-element.43), channel_id=1, source_target_pairs={{0,16},{16,32},{32,48},{48,0},{64,80},{80,96},{96,112},{112,64},{1... | collective-permute-start | bytes 786440 | tf_op jit(solution)/shard_map/ppermute | solution.py:45
  200.1 14.4 %collective-permute-start.30 = (f32[16,64,64]{2,0,1:T(8,128)S(1)}, f32[16,64,64]{2,0,1:T(8,128)S(1)}, u32[]{:S(2)}, u32[]{:S(2)}) collective-permute-start(f32[16,64,64]{2,0,1:T(8,128)S(1)} %get-tuple-element.42), channel_id=1, source_target_pairs={{0,192},{64,0},{128,64},{192,128},{16,208},{80,16},{144,80},{208,1... | collective-permute-start | bytes 786440 | tf_op jit(solution)/shard_map/ppermute | solution.py:45
  200.1 47.6 %collective-permute-start.31 = (f32[16,64,64]{2,0,1:T(8,128)S(1)}, f32[16,64,64]{2,0,1:T(8,128)S(1)}, u32[]{:S(2)}, u32[]{:S(2)}) collective-permute-start(f32[16,64,64]{2,0,1:T(8,128)S(1)} %get-tuple-element.42), channel_id=1, source_target_pairs={{0,128},{64,192},{128,0},{192,64},{16,144},{80,208},{144,16},{208,... | collective-permute-start | bytes 786440 | tf_op jit(solution)/shard_map/ppermute | solution.py:45
  200.4 47.3 %collective-permute-start.32 = (f32[16,64,64]{2,0,1:T(8,128)S(1)}, f32[16,64,64]{2,0,1:T(8,128)S(1)}, u32[]{:S(2)}, u32[]{:S(2)}) collective-permute-start(f32[16,64,64]{2,0,1:T(8,128)S(1)} %get-tuple-element.42), channel_id=1, source_target_pairs={{0,64},{64,128},{128,192},{192,0},{16,80},{80,144},{144,208},{208,... | collective-permute-start | bytes 786440 | tf_op jit(solution)/shard_map/ppermute | solution.py:45
  202.4 114.1 %collective-permute-start.39 = (f32[64,2,2,2,4,64]{0,5,4,3,1,2:T(8,128)S(1)}, f32[64,2,2,2,4,64]{0,5,4,3,1,2:T(8,128)S(1)}, u32[]{:S(2)}, u32[]{:S(2)}) collective-permute-start(f32[64,2,2,2,4,64]{0,5,4,3,1,2:T(8,128)S(1)} %pad_maximum_fusion.11), channel_id=1, source_target_pairs={{0,1},{1,0},{2,3},{3,2},{4,5},{5,4},{6,7},{7,6},{8,9},{9,8},{10,11... | collective-permute-start | bytes 1572872 | tf_op jit(solution)/shard_map/ppermute | solution.py:159
  202.5 90.7 %collective-permute-start.21 = (f32[16,64,64]{2,0,1:T(8,128)S(1)}, f32[16,64,64]{2,0,1:T(8,128)S(1)}, u32[]{:S(2)}, u32[]{:S(2)}) collective-permute-start(f32[16,64,64]{2,0,1:T(8,128)S(1)} %get-tuple-element.22), channel_id=1, source_target_pairs={{0,48},{64,112},{128,176},{192,240},{16,0},{80,64},{144,128},{208,... | collective-permute-start | bytes 786440 | tf_op jit(solution)/shard_map/ppermute | solution.py:55
  214.5 55.8 %collective-permute-start.27 = (f32[16,64,64]{2,0,1:T(8,128)S(1)}, f32[16,64,64]{2,0,1:T(8,128)S(1)}, u32[]{:S(2)}, u32[]{:S(2)}) collective-permute-start(f32[16,64,64]{2,0,1:T(8,128)S(1)} %get-tuple-element.25), channel_id=1, source_target_pairs={{0,192},{16,208},{32,224},{48,240},{64,0},{80,16},{96,32},{112,48}... | collective-permute-start | bytes 786440 | tf_op jit(solution)/shard_map/ppermute | solution.py:55
  247.7 42.3 %collective-permute-start.28 = (f32[16,64,64]{2,0,1:T(8,128)S(1)}, f32[16,64,64]{2,0,1:T(8,128)S(1)}, u32[]{:S(2)}, u32[]{:S(2)}) collective-permute-start(f32[16,64,64]{2,0,1:T(8,128)S(1)} %get-tuple-element.24), channel_id=1, source_target_pairs={{0,128},{16,144},{32,160},{48,176},{64,192},{80,208},{96,224},{112... | collective-permute-start | bytes 786440 | tf_op jit(solution)/shard_map/ppermute | solution.py:55
  247.7 44.2 %collective-permute-start.29 = (f32[16,64,64]{2,0,1:T(8,128)S(1)}, f32[16,64,64]{2,0,1:T(8,128)S(1)}, u32[]{:S(2)}, u32[]{:S(2)}) collective-permute-start(f32[16,64,64]{2,0,1:T(8,128)S(1)} %get-tuple-element.23), channel_id=1, source_target_pairs={{0,64},{16,80},{32,96},{48,112},{64,128},{80,144},{96,160},{112,17... | collective-permute-start | bytes 786440 | tf_op jit(solution)/shard_map/ppermute | solution.py:55
  270.3 24.4 %collective-permute-start.22 = (f32[16,64,64]{2,0,1:T(8,128)S(1)}, f32[16,64,64]{2,0,1:T(8,128)S(1)}, u32[]{:S(2)}, u32[]{:S(2)}) collective-permute-start(f32[16,64,64]{2,0,1:T(8,128)S(1)} %get-tuple-element.21), channel_id=1, source_target_pairs={{0,32},{64,96},{128,160},{192,224},{16,48},{80,112},{144,176},{208... | collective-permute-start | bytes 786440 | tf_op jit(solution)/shard_map/ppermute | solution.py:55
  290.0 25.4 %collective-permute-start.23 = (f32[16,64,64]{2,0,1:T(8,128)S(1)}, f32[16,64,64]{2,0,1:T(8,128)S(1)}, u32[]{:S(2)}, u32[]{:S(2)}) collective-permute-start(f32[16,64,64]{2,0,1:T(8,128)S(1)} %get-tuple-element.20), channel_id=1, source_target_pairs={{0,16},{64,80},{128,144},{192,208},{16,32},{80,96},{144,160},{208,... | collective-permute-start | bytes 786440 | tf_op jit(solution)/shard_map/ppermute | solution.py:55
  291.9 62.0 %collective-permute-start.33 = (f32[16,64,64]{2,0,1:T(8,128)}, f32[16,64,64]{2,0,1:T(8,128)}, u32[]{:S(2)}, u32[]{:S(2)}) collective-permute-start(f32[16,64,64]{2,0,1:T(8,128)} %get-tuple-element.28), channel_id=1, source_target_pairs={{0,48},{64,112},{128,176},{192,240},{16,0},{80,64},{144,128},{208,... | collective-permute-start | bytes 786440 | tf_op jit(solution)/shard_map/ppermute | solution.py:55
  293.2 60.7 %collective-permute-start.34 = (f32[16,64,64]{2,0,1:T(8,128)}, f32[16,64,64]{2,0,1:T(8,128)}, u32[]{:S(2)}, u32[]{:S(2)}) collective-permute-start(f32[16,64,64]{2,0,1:T(8,128)} %get-tuple-element.27), channel_id=1, source_target_pairs={{0,32},{64,96},{128,160},{192,224},{16,48},{80,112},{144,176},{208... | collective-permute-start | bytes 786440 | tf_op jit(solution)/shard_map/ppermute | solution.py:55
  294.7 59.2 %collective-permute-start.35 = (f32[16,64,64]{2,0,1:T(8,128)}, f32[16,64,64]{2,0,1:T(8,128)}, u32[]{:S(2)}, u32[]{:S(2)}) collective-permute-start(f32[16,64,64]{2,0,1:T(8,128)} %get-tuple-element.26), channel_id=1, source_target_pairs={{0,16},{64,80},{128,144},{192,208},{16,32},{80,96},{144,160},{208,... | collective-permute-start | bytes 786440 | tf_op jit(solution)/shard_map/ppermute | solution.py:55
  318.1 12.6 %collective-permute-start.42 = (f32[64,64,3]{0,2,1:T(4,128)S(1)}, f32[64,64,3]{0,2,1:T(4,128)S(1)}, u32[]{:S(2)}, u32[]{:S(2)}) collective-permute-start(f32[64,64,3]{0,2,1:T(4,128)S(1)} %slice_select_fusion.3), channel_id=1, source_target_pairs={{0,16},{16,0},{32,48},{48,32},{64,80},{80,64},{96,112},{112,96},{1... | collective-permute-start | bytes 147464 | tf_op jit(solution)/shard_map/ppermute | solution.py:103
  348.5 7.6 %collective-permute-start.43 = (f32[7,64,64]{1,2,0:T(8,128)S(1)}, f32[7,64,64]{1,2,0:T(8,128)S(1)}, u32[]{:S(2)}, u32[]{:S(2)}) collective-permute-start(f32[7,64,64]{1,2,0:T(8,128)S(1)} %get-tuple-element.45), channel_id=1, source_target_pairs={{0,64},{16,80},{32,96},{48,112},{64,128},{80,144},{96,160},{112,17... | collective-permute-start | bytes 344072 | tf_op jit(solution)/shard_map/ppermute | solution.py:124
  352.4 7.9 %collective-permute-start.44 = (f32[7,64,64]{1,2,0:T(8,128)S(1)}, f32[7,64,64]{1,2,0:T(8,128)S(1)}, u32[]{:S(2)}, u32[]{:S(2)}) collective-permute-start(f32[7,64,64]{1,2,0:T(8,128)S(1)} %get-tuple-element.46), channel_id=1, source_target_pairs={{64,0},{80,16},{96,32},{112,48},{128,64},{144,80},{160,96},{176,11... | collective-permute-start | bytes 344072 | tf_op jit(solution)/shard_map/ppermute | solution.py:125
  373.9 8.3 %collective-permute-start.46 = (f32[7,64,64]{2,0,1:T(8,128)S(1)}, f32[7,64,64]{2,0,1:T(8,128)S(1)}, u32[]{:S(2)}, u32[]{:S(2)}) collective-permute-start(f32[7,64,64]{2,0,1:T(8,128)S(1)} %get-tuple-element.40), channel_id=1, source_target_pairs={{64,0},{80,16},{96,32},{112,48},{128,64},{144,80},{160,96},{176,11... | collective-permute-start | bytes 344072 | tf_op jit(solution)/shard_map/ppermute | solution.py:125
  388.7 10.0 %collective-permute-start.49 = (f32[64,64,3]{0,2,1:T(4,128)S(1)}, f32[64,64,3]{0,2,1:T(4,128)S(1)}, u32[]{:S(2)}, u32[]{:S(2)}) collective-permute-start(f32[64,64,3]{0,2,1:T(4,128)S(1)} %slice_select_fusion.2), channel_id=1, source_target_pairs={{0,16},{16,0},{32,48},{48,32},{64,80},{80,64},{96,112},{112,96},{1... | collective-permute-start | bytes 147464 | tf_op jit(solution)/shard_map/ppermute | solution.py:103
  418.1 14.1 %collective-permute-start.51 = (f32[64,2,2,4,64]{0,4,3,2,1:T(8,128)S(1)}, f32[64,2,2,4,64]{0,4,3,2,1:T(8,128)S(1)}, u32[]{:S(2)}, u32[]{:S(2)}) collective-permute-start(f32[64,2,2,4,64]{0,4,3,2,1:T(8,128)S(1)} %select_bitcast_fusion.9), channel_id=1, source_target_pairs={{0,4},{1,5},{2,6},{3,7},{4,0},{5,1},{6,2},{7,3},{8,12},{9,13},{10,... | collective-permute-start | bytes 786440 | tf_op jit(solution)/shard_map/ppermute | solution.py:149
  432.3 9.1 %collective-permute-start.52 = (f32[64,2,4,64]{0,3,2,1:T(8,128)S(1)}, f32[64,2,4,64]{0,3,2,1:T(8,128)S(1)}, u32[]{:S(2)}, u32[]{:S(2)}) collective-permute-start(f32[64,2,4,64]{0,3,2,1:T(8,128)S(1)} %select_bitcast_fusion.15), channel_id=1, source_target_pairs={{0,8},{1,9},{2,10},{3,11},{4,12},{5,13},{6,14},{7,15},{8,0},{9,1},... | collective-permute-start | bytes 393224 | tf_op jit(solution)/shard_map/ppermute | solution.py:149
  441.5 9.2 %collective-permute-start.53 = (f32[64,4,64]{0,2,1:T(8,128)S(1)}, f32[64,4,64]{0,2,1:T(8,128)S(1)}, u32[]{:S(2)}, u32[]{:S(2)}) collective-permute-start(f32[64,4,64]{0,2,1:T(8,128)S(1)} %select_bitcast_fusion.22), channel_id=1, source_target_pairs={{0,2},{1,3},{2,0},{3,1},{4,6},{5,7},{6,4},{7,5},{8,10},{9,11},{10,... | collective-permute-start | bytes 196616 | tf_op jit(solution)/shard_map/ppermute | solution.py:149
  451.4 10.1 %collective-permute-start.54 = (f32[64,4,64]{0,2,1:T(8,128)S(1)}, f32[64,4,64]{0,2,1:T(8,128)S(1)}, u32[]{:S(2)}, u32[]{:S(2)}) collective-permute-start(f32[64,4,64]{0,2,1:T(8,128)S(1)} %fusion.9), channel_id=1, source_target_pairs={{0,2},{1,3},{2,0},{3,1},{4,6},{5,7},{6,4},{7,5},{8,10},{9,11},{10,... | collective-permute-start | bytes 196616 | tf_op jit(solution)/shard_map/ppermute | solution.py:159
  461.6 8.8 %collective-permute-start.55 = (f32[64,2,4,64]{0,3,2,1:T(8,128)S(1)}, f32[64,2,4,64]{0,3,2,1:T(8,128)S(1)}, u32[]{:S(2)}, u32[]{:S(2)}) collective-permute-start(f32[64,2,4,64]{0,3,2,1:T(8,128)S(1)} %pad_maximum_fusion.16), channel_id=1, source_target_pairs={{0,8},{1,9},{2,10},{3,11},{4,12},{5,13},{6,14},{7,15},{8,0},{9,1},... | collective-permute-start | bytes 393224 | tf_op jit(solution)/shard_map/ppermute | solution.py:159
  470.5 12.0 %collective-permute-start.56 = (f32[64,2,2,4,64]{0,4,3,2,1:T(8,128)S(1)}, f32[64,2,2,4,64]{0,4,3,2,1:T(8,128)S(1)}, u32[]{:S(2)}, u32[]{:S(2)}) collective-permute-start(f32[64,2,2,4,64]{0,4,3,2,1:T(8,128)S(1)} %pad_maximum_fusion.14), channel_id=1, source_target_pairs={{0,4},{1,5},{2,6},{3,7},{4,0},{5,1},{6,2},{7,3},{8,12},{9,13},{10,... | collective-permute-start | bytes 786440 | tf_op jit(solution)/shard_map/ppermute | solution.py:159
  486.8 8.4 %collective-permute-start.60 = (f32[64,64,3]{0,2,1:T(4,128)S(1)}, f32[64,64,3]{0,2,1:T(4,128)S(1)}, u32[]{:S(2)}, u32[]{:S(2)}) collective-permute-start(f32[64,64,3]{0,2,1:T(4,128)S(1)} %slice_select_fusion.1), channel_id=1, source_target_pairs={{0,16},{16,0},{32,48},{48,32},{64,80},{80,64},{96,112},{112,96},{1... | collective-permute-start | bytes 147464 | tf_op jit(solution)/shard_map/ppermute | solution.py:103
  510.0 5.9 collective-permute-start.61
  512.1 7.9 %collective-permute-start.62 = (f32[7,64,64]{1,2,0:T(8,128)S(1)}, f32[7,64,64]{1,2,0:T(8,128)S(1)}, u32[]{:S(2)}, u32[]{:S(2)}) collective-permute-start(f32[7,64,64]{1,2,0:T(8,128)S(1)} %get-tuple-element.34), channel_id=1, source_target_pairs={{64,0},{80,16},{96,32},{112,48},{128,64},{144,80},{160,96},{176,11... | collective-permute-start | bytes 344072 | tf_op jit(solution)/shard_map/ppermute | solution.py:125
  531.7 6.0 collective-permute-start.63
  533.9 8.3 %collective-permute-start.64 = (f32[7,64,64]{2,0,1:T(8,128)S(1)}, f32[7,64,64]{2,0,1:T(8,128)S(1)}, u32[]{:S(2)}, u32[]{:S(2)}) collective-permute-start(f32[7,64,64]{2,0,1:T(8,128)S(1)} %get-tuple-element.32), channel_id=1, source_target_pairs={{64,0},{80,16},{96,32},{112,48},{128,64},{144,80},{160,96},{176,11... | collective-permute-start | bytes 344072 | tf_op jit(solution)/shard_map/ppermute | solution.py:125
  548.7 10.3 %collective-permute-start.67 = (f32[64,64,3]{0,2,1:T(4,128)S(1)}, f32[64,64,3]{0,2,1:T(4,128)S(1)}, u32[]{:S(2)}, u32[]{:S(2)}) collective-permute-start(f32[64,64,3]{0,2,1:T(4,128)S(1)} %slice_select_fusion), channel_id=1, source_target_pairs={{0,16},{16,0},{32,48},{48,32},{64,80},{80,64},{96,112},{112,96},{1... | collective-permute-start | bytes 147464 | tf_op jit(solution)/shard_map/ppermute | solution.py:103
  553.7 5.9 collective-permute-start.66
  578.3 14.1 %collective-permute-start.69 = (f32[64,2,2,4,64]{0,4,3,2,1:T(8,128)S(1)}, f32[64,2,2,4,64]{0,4,3,2,1:T(8,128)S(1)}, u32[]{:S(2)}, u32[]{:S(2)}) collective-permute-start(f32[64,2,2,4,64]{0,4,3,2,1:T(8,128)S(1)} %select_bitcast_fusion.6), channel_id=1, source_target_pairs={{0,4},{1,5},{2,6},{3,7},{4,0},{5,1},{6,2},{7,3},{8,12},{9,13},{10,... | collective-permute-start | bytes 786440 | tf_op jit(solution)/shard_map/ppermute | solution.py:149
  592.5 9.1 %collective-permute-start.70 = (f32[64,2,4,64]{0,3,2,1:T(8,128)S(1)}, f32[64,2,4,64]{0,3,2,1:T(8,128)S(1)}, u32[]{:S(2)}, u32[]{:S(2)}) collective-permute-start(f32[64,2,4,64]{0,3,2,1:T(8,128)S(1)} %select_bitcast_fusion.12), channel_id=1, source_target_pairs={{0,8},{1,9},{2,10},{3,11},{4,12},{5,13},{6,14},{7,15},{8,0},{9,1},... | collective-permute-start | bytes 393224 | tf_op jit(solution)/shard_map/ppermute | solution.py:149
  601.7 9.2 %collective-permute-start.71 = (f32[64,4,64]{0,2,1:T(8,128)S(1)}, f32[64,4,64]{0,2,1:T(8,128)S(1)}, u32[]{:S(2)}, u32[]{:S(2)}) collective-permute-start(f32[64,4,64]{0,2,1:T(8,128)S(1)} %select_bitcast_fusion.19), channel_id=1, source_target_pairs={{0,2},{1,3},{2,0},{3,1},{4,6},{5,7},{6,4},{7,5},{8,10},{9,11},{10,... | collective-permute-start | bytes 196616 | tf_op jit(solution)/shard_map/ppermute | solution.py:149
  611.7 13.5 %collective-permute-start.72 = (f32[64,4,64]{0,2,1:T(8,128)S(1)}, f32[64,4,64]{0,2,1:T(8,128)S(1)}, u32[]{:S(2)}, u32[]{:S(2)}) collective-permute-start(f32[64,4,64]{0,2,1:T(8,128)S(1)} %fusion.6), channel_id=1, source_target_pairs={{0,48},{16,0},{32,16},{48,32},{64,112},{80,64},{96,80},{112,96},{1... | collective-permute-start | bytes 196616 | tf_op jit(solution)/shard_map/ppermute | solution.py:45
  613.8 11.4 %collective-permute-start.73 = (f32[64,4,64]{0,2,1:T(8,128)S(1)}, f32[64,4,64]{0,2,1:T(8,128)S(1)}, u32[]{:S(2)}, u32[]{:S(2)}) collective-permute-start(f32[64,4,64]{0,2,1:T(8,128)S(1)} %fusion.6), channel_id=1, source_target_pairs={{0,32},{16,48},{32,0},{48,16},{64,96},{80,112},{96,64},{112,80},{1... | collective-permute-start | bytes 196616 | tf_op jit(solution)/shard_map/ppermute | solution.py:45
  615.8 9.4 %collective-permute-start.74 = (f32[64,4,64]{0,2,1:T(8,128)S(1)}, f32[64,4,64]{0,2,1:T(8,128)S(1)}, u32[]{:S(2)}, u32[]{:S(2)}) collective-permute-start(f32[64,4,64]{0,2,1:T(8,128)S(1)} %fusion.6), channel_id=1, source_target_pairs={{0,16},{16,32},{32,48},{48,0},{64,80},{80,96},{96,112},{112,64},{1... | collective-permute-start | bytes 196616 | tf_op jit(solution)/shard_map/ppermute | solution.py:45
  625.3 6.6 %collective-permute-start.75 = (f32[64,4,64]{0,2,1:T(8,128)S(1)}, f32[64,4,64]{0,2,1:T(8,128)S(1)}, u32[]{:S(2)}, u32[]{:S(2)}) collective-permute-start(f32[64,4,64]{0,2,1:T(8,128)S(1)} %get-tuple-element.55), channel_id=1, source_target_pairs={{0,192},{16,208},{32,224},{48,240},{64,0},{80,16},{96,32},{112,48}... | collective-permute-start | bytes 196616 | tf_op jit(solution)/shard_map/ppermute | solution.py:55
  625.4 11.5 %collective-permute-start.76 = (f32[64,4,64]{0,2,1:T(8,128)S(1)}, f32[64,4,64]{0,2,1:T(8,128)S(1)}, u32[]{:S(2)}, u32[]{:S(2)}) collective-permute-start(f32[64,4,64]{0,2,1:T(8,128)S(1)} %get-tuple-element.54), channel_id=1, source_target_pairs={{0,128},{16,144},{32,160},{48,176},{64,192},{80,208},{96,224},{112... | collective-permute-start | bytes 196616 | tf_op jit(solution)/shard_map/ppermute | solution.py:55
  626.8 10.0 %collective-permute-start.77 = (f32[64,4,64]{0,2,1:T(8,128)S(1)}, f32[64,4,64]{0,2,1:T(8,128)S(1)}, u32[]{:S(2)}, u32[]{:S(2)}) collective-permute-start(f32[64,4,64]{0,2,1:T(8,128)S(1)} %get-tuple-element.53), channel_id=1, source_target_pairs={{0,64},{16,80},{32,96},{48,112},{64,128},{80,144},{96,160},{112,17... | collective-permute-start | bytes 196616 | tf_op jit(solution)/shard_map/ppermute | solution.py:55
  (33 other events, 241.7 us)

commit v15 on v12

--- a/solution.py
+++ b/solution.py
@@ -195,16 +195,15 @@
     my_y = cy[my_brick]
 
     share = jnp.transpose(estimate[0].reshape(side, estimate.shape[2] // side, side), (2, 1, 0))
-    share = route(share, place, my_brick, nsp)
     recorded = jnp.transpose(measured[0, 0].reshape(side, side, side), (2, 1, 0))
     chunk = side // 4
-    recorded = jnp.concatenate(
-        [
-            route(recorded[c * chunk:(c + 1) * chunk], place, my_brick, nsp, columns_first=c % 2 == 1)
-            for c in range(4)
-        ],
-        axis=0,
-    )
+    share_planes = share.size // (side * side)
+    parts = [
+        jnp.concatenate([share.reshape(share_planes, side, side), recorded[:chunk]], axis=0)
+    ] + [recorded[c * chunk:(c + 1) * chunk] for c in range(1, 4)]
+    parts = [route(p, place, my_brick, nsp, columns_first=c % 2 == 1) for c, p in enumerate(parts)]
+    share = parts[0][:share_planes].reshape(share.shape)
+    recorded = jnp.concatenate([parts[0][share_planes:]] + parts[1:], axis=0)
 
     radius_x = (kernel_x.shape[1] - 1) // 2
     radius_y = (kernel_y.shape[1] - 1) // 2

time: 624 us -> 686 us (1.099)
  local copies, waits for them, and re-layouts: 39.4 us -> 68.3 us
  starting transfers between devices: 129 us -> 155 us
  other arithmetic: 69.9 us -> 84.9 us
  matrix products: 61.5 us -> 53.7 us
    ppermute x36 -> x30, starting transfers between devices: 60.9 us -> 83.2 us  [route(): part = lax.ppermute(part, 'space', pairs)]
    ppermute x36 -> x30, waiting for transfers between devices: 128 us -> 146 us  [route(): part = lax.ppermute(part, 'space', pairs)]
    ppermute x12, starting transfers between devices: 28.8 us -> 15.7 us  [swap(): return lax.ppermute(x, 'space', [(i, i ^ partner) for i in range(nsp)])]
    select_n x0 -> x20, local copies, waits for them, and re-layouts: none -> 13 us  [the longest x10 6.53 us: place(): low = jnp.where(is_high, halo, zero)]
    dot_general x4, matrix products: 20.9 us -> 7.85 us  [convolve(): return jnp.einsum('ot,atb->aob', band, extended, precision=hi)]
    ppermute x8, starting transfers between devices: 6.67 us -> 15.7 us  [view_reduce_scatter(): x = keep + lax.ppermute(send, 'view', xor_pairs(nv, m))]
    unnamed x47 -> x45, local copies, waits for them, and re-layouts: 6.06 us -> 15 us
    ppermute x8, waiting for transfers between devices: 64.6 us -> 56.1 us  [view_reduce_scatter(): x = keep + lax.ppermute(send, 'view', xor_pairs(nv, m))]
  transfers between devices with their start and end apart: 78 -> 72, of which waited for: 39 -> 44; matrix products, arithmetic and copies ran while one was open for 14% -> 14% of each run, Pallas kernels for 0% -> 0%
where the time goes in v15:
time: 686 us; the launch traced here: 673 us
  waiting for transfers between devices  273 us (40%)
  starting transfers between devices  155 us (23%)
  other arithmetic  84.9 us (12%)
  local copies, waits for them, and re-layouts  68.3 us (10%)
  matrix products  53.7 us (8%)
  between operations  38.3 us (6%)
    ppermute x30, waiting for transfers between devices, route(): part = lax.ppermute(part, 'space', pairs)  146 us
    ppermute x30, starting transfers between devices, route(): part = lax.ppermute(part, 'space', pairs)  83.2 us
    ppermute x8, waiting for transfers between devices, view_reduce_scatter(): x = keep + lax.ppermute(send, 'view', xor_pairs(nv, m))  56.1 us
    ppermute x8, waiting for transfers between devices, view_all_gather(): recv = lax.ppermute(x, 'view', xor_pairs(nv, m))  30.3 us
    dot_general x4, matrix products, convolve(): return jnp.einsum('abt,ot->abo', extended, band, precision=hi)  22.9 us
    select_n x3, other arithmetic, band_matrix(): band = jnp.where(offset == position, weight, band)  18.7 us
    ppermute x8, starting transfers between devices, view_all_gather(): recv = lax.ppermute(x, 'view', xor_pairs(nv, m))  17.2 us
    ppermute x4, waiting for transfers between devices, z_halo(): lax.ppermute(first, 'space', [(i + ROW, i) for i in range(nsp - ROW)])  16.3 us
  transfers between devices with their start and end apart: 72, of which 44 were waited for; matrix products, arithmetic and copies ran while one was open for 14% of the time, Pallas kernels for 0%

profile of v15, /device:TPU:8, one launch (start us, length us, event | category | flops | bytes accessed | tf_op | source)
XLA Modules:
  0.0 673.5 jit_solution(3948335166415554241)
XLA Ops:
  8.8 4.0 collective-permute-start.5
  14.4 2.9 collective-permute-done.4
  25.9 3.8 collective-permute-start.24
  37.3 20.9 %collective-permute-done.25 = f32[16,64,64]{2,0,1:T(8,128)S(1)} collective-permute-done((f32[16,64,64]{2,0,1:T(8,128)}, f32[16,64,64]{2,0,1:T(8,128)S(1)}, u32[]{:S(2)}, u32[]{:S(2)}) %collective-permute-start.25) | collective-permute-done | bytes 262176 | tf_op jit(solution)/shard_map/ppermute | solution.py:46
  72.1 11.2 %collective-permute-start.13 = (f32[16,64,64]{2,0,1:T(8,128)}, f32[16,64,64]{2,0,1:T(8,128)S(1)}, u32[]{:S(2)}, u32[]{:S(2)}) collective-permute-start(f32[16,64,64]{2,0,1:T(8,128)} %get-tuple-element.57), channel_id=1, source_target_pairs={{0,128},{64,192},{128,0},{192,64},{16,144},{80,208},{144,16},{208,... | collective-permute-start | bytes 786440 | tf_op jit(solution)/shard_map/ppermute | solution.py:46
  85.0 3.7 collective-permute-done.27
  90.9 11.0 %collective-permute-start.14 = (f32[16,64,64]{2,0,1:T(8,128)S(1)}, f32[16,64,64]{2,0,1:T(8,128)S(1)}, u32[]{:S(2)}, u32[]{:S(2)}) collective-permute-start(f32[16,64,64]{2,0,1:T(8,128)S(1)} %get-tuple-element.55), channel_id=1, source_target_pairs={{0,64},{64,128},{128,192},{192,0},{16,80},{80,144},{144,208},{208,... | collective-permute-start | bytes 786440 | tf_op jit(solution)/shard_map/ppermute | solution.py:46
  101.9 16.9 %collective-permute-done.13 = f32[16,64,64]{2,0,1:T(8,128)S(1)} collective-permute-done((f32[16,64,64]{2,0,1:T(8,128)}, f32[16,64,64]{2,0,1:T(8,128)S(1)}, u32[]{:S(2)}, u32[]{:S(2)}) %collective-permute-start.13) | collective-permute-done | bytes 262176 | tf_op jit(solution)/shard_map/ppermute | solution.py:46
  121.0 2.9 collective-permute-start.16
  124.3 11.7 %collective-permute-done.17 = f32[16,64,64]{2,0,1:T(8,128)S(1)} collective-permute-done((f32[16,64,64]{2,0,1:T(8,128)}, f32[16,64,64]{2,0,1:T(8,128)S(1)}, u32[]{:S(2)}, u32[]{:S(2)}) %collective-permute-start.17) | collective-permute-done | bytes 262176 | tf_op jit(solution)/shard_map/ppermute | solution.py:56
  137.7 8.1 %collective-permute-done.15 = f32[16,64,64]{2,0,1:T(8,128)} collective-permute-done((f32[16,64,64]{2,0,1:T(8,128)}, f32[16,64,64]{2,0,1:T(8,128)}, u32[]{:S(2)}, u32[]{:S(2)}) %collective-permute-start.15) | collective-permute-done | bytes 262176 | tf_op jit(solution)/shard_map/ppermute | solution.py:56
  151.9 3.0 collective-permute-start.7
  166.0 3.2 collective-permute-done.8
  171.5 12.4 %collective-permute-done.6 = f32[20,64,64]{2,1,0:T(8,128)} collective-permute-done((f32[20,64,64]{2,1,0:T(8,128)}, f32[20,64,64]{2,1,0:T(8,128)}, u32[]{:S(2)}, u32[]{:S(2)}) %collective-permute-start.6) | collective-permute-done | bytes 327712 | tf_op jit(solution)/shard_map/ppermute | solution.py:46
  187.5 13.1 %collective-permute-start.9 = (f32[20,64,64]{2,1,0:T(8,128)}, f32[20,64,64]{2,1,0:T(8,128)}, u32[]{:S(2)}, u32[]{:S(2)}) collective-permute-start(f32[20,64,64]{2,1,0:T(8,128)} %copy.213), channel_id=1, source_target_pairs={{0,192},{16,208},{32,224},{48,240},{64,0},{80,16},{96,32},{112,48}... | collective-permute-start | bytes 983048 | tf_op jit(solution)/shard_map/ppermute | solution.py:56
  210.9 5.2 collective-permute-done.9
  216.1 40.3 %collective-permute-done.10 = f32[20,64,64]{2,1,0:T(8,128)} collective-permute-done((f32[20,64,64]{2,1,0:T(8,128)}, f32[20,64,64]{2,1,0:T(8,128)}, u32[]{:S(2)}, u32[]{:S(2)}) %collective-permute-start.10) | collective-permute-done | bytes 327712 | tf_op jit(solution)/shard_map/ppermute | solution.py:56
  256.5 5.2 fusion.27
  262.6 7.0 %collective-permute-start.30 = (f32[64,4,64]{2,1,0:T(4,128)S(1)}, f32[64,4,64]{2,1,0:T(4,128)S(1)}, u32[]{:S(2)}, u32[]{:S(2)}) collective-permute-start(f32[64,4,64]{2,1,0:T(4,128)S(1)} %bitcast.244), channel_id=1, source_target_pairs={{0,2},{1,3},{2,0},{3,1},{4,6},{5,7},{6,4},{7,5},{8,10},{9,11},{10,... | collective-permute-start | bytes 196616 | tf_op jit(solution)/shard_map/ppermute | solution.py:160
  270.3 4.5 collective-permute-done.30
  274.9 3.1 collective-permute-start.31
  278.7 4.4 select_select_fusion.15
  287.2 4.4 select_select_fusion.17
  291.6 10.0 %select_select_fusion.19 = (f32[64,78]{1,0:T(8,128)S(1)}, f32[64,78]{1,0:T(8,128)}) fusion(f32[]{:T(128)} %bitcast.38, f32[]{:T(128)} %bitcast.37, f32[]{:T(128)} %bitcast.36, f32[]{:T(128)} %bitcast.35, f32[]{:T(128)} %bitcast.34, f32[]{:T(128)} %bitcast.33, f32[]{:T(128)} %bitcast.32, f32[]{:T(128)} %bitcast.31, f32[]{:T(128)} %bitcast.30, f32[]{:T(128)} %bitcast.29, ...), kind=kLoop, calls=%fused_computation.199 | loop fusion | flops 229632 | bytes 39996 | tf_op jit(solution)/shard_map/jit(_where)/select_n | solution.py:67
  304.7 2.9 collective-permute-start.19
  310.0 6.1 collective-permute-done.20
  318.8 5.6 collective-permute-done.19
  325.9 4.7 collective-permute-start.23
  330.6 4.8 collective-permute-start.22
  335.4 3.3 collective-permute-start.21
  342.8 2.7 fusion.91
  356.3 3.1 collective-permute-done.34
  369.2 9.9 %fusion = f32[64,70,64]{1,2,0:T(8,128)S(1)} fusion(f32[64,3,70]{2,1,0:T(4,128)S(1)} %get-tuple-element.91, f32[64,64,3]{2,1,0:T(8,128)} %copy.238, f32[64,64,64]{2,1,0:T(8,128)} %copy.232, f32[64,64,3]{2,1,0:T(8,128)} %copy.236, f32[64,3,70]{2,1,0:T(4,128)S(1)} %get-tuple-element.90, f32[64,70]{1,0:T(8,128)S(1)} %get-tuple-element.13), kind=kOutput, calls=%fused_computation.9 | convolution fusion | flops 242099200 | bytes 2419200 | tf_op jit(solution)/shard_map/abt,ot->abo/dot_general | solution.py:77
  387.0 3.3 collective-permute-done.38
  390.6 3.3 copy.239
  393.9 8.1 %convolution_divide_fusion.1 = f32[64,64,64]{2,0,1:T(8,128)S(1)} fusion(f32[78,64,64]{0,2,1:T(8,128)} %copy.239, f32[16,64,64]{2,0,1:T(8,128)S(1)} %copy-done.8, f32[16,64,64]{2,0,1:T(8,128)} %select_select_fusion.4, f32[16,64,64]{2,0,1:T(8,128)} %get-tuple-element.52, f32[16,64,64]{2,0,1:T(8,128)} %slice.427, f32[64,78]{1,0:T(8,128)S(1)} %copy-done.12), kind=kOutput, calls=%fused_computation.38 | convolution fusion | flops 246415360 | bytes 3395072 | tf_op jit(solution)/shard_map/ot,tab->oab/dot_general | solution.py:74
  408.1 4.4 collective-permute-done.40
  415.0 3.4 fusion.101
  444.0 13.4 %collective-permute-done.45 = f32[64,2,2,4,64]{4,3,0,2,1:T(4,128)S(1)} collective-permute-done((f32[64,2,2,4,64]{4,3,0,2,1:T(4,128)S(1)}, f32[64,2,2,4,64]{4,3,0,2,1:T(4,128)S(1)}, u32[]{:S(2)}, u32[]{:S(2)}) %collective-permute-start.45) | collective-permute-done | bytes 262176 | tf_op jit(solution)/shard_map/ppermute | solution.py:150
  457.7 2.8 collective-permute-start.46
  460.5 6.3 collective-permute-done.46
  467.0 2.8 collective-permute-start.47
  470.3 7.3 %collective-permute-done.47 = f32[64,4,64]{2,1,0:T(4,128)S(1)} collective-permute-done((f32[64,4,64]{2,1,0:T(4,128)S(1)}, f32[64,4,64]{2,1,0:T(4,128)S(1)}, u32[]{:S(2)}, u32[]{:S(2)}) %collective-permute-start.47) | collective-permute-done | bytes 65568 | tf_op jit(solution)/shard_map/ppermute | solution.py:150
  480.8 7.4 %collective-permute-done.48 = f32[64,4,64]{2,1,0:T(4,128)S(1)} collective-permute-done((f32[64,4,64]{2,1,0:T(4,128)S(1)}, f32[64,4,64]{2,1,0:T(4,128)S(1)}, u32[]{:S(2)}, u32[]{:S(2)}) %collective-permute-start.48) | collective-permute-done | bytes 65568 | tf_op jit(solution)/shard_map/ppermute | solution.py:160
  488.4 2.8 collective-permute-start.49
  491.2 6.6 collective-permute-done.49
  498.2 9.2 %collective-permute-done.50 = f32[64,2,2,4,64]{4,3,0,2,1:T(4,128)S(1)} collective-permute-done((f32[64,2,2,4,64]{4,3,0,2,1:T(4,128)S(1)}, f32[64,2,2,4,64]{4,3,0,2,1:T(4,128)S(1)}, u32[]{:S(2)}, u32[]{:S(2)}) %collective-permute-start.50) | collective-permute-done | bytes 262176 | tf_op jit(solution)/shard_map/ppermute | solution.py:160
  513.5 2.8 fusion.85
  528.0 3.7 collective-permute-done.52
  538.9 9.3 %fusion.10 = f32[64,70,64]{1,2,0:T(8,128)S(1)} fusion(f32[64,3,70]{2,1,0:T(4,128)S(1)} %get-tuple-element.87, f32[64,64,3]{2,1,0:T(8,128)} %copy.263, f32[64,64,64]{2,1,0:T(8,128)S(1)} %copy.257, f32[64,64,3]{2,1,0:T(8,128)} %copy.261, f32[64,3,70]{2,1,0:T(4,128)S(1)} %get-tuple-element.86, f32[64,70]{1,0:T(8,128)S(1)} %get-tuple-element.13), kind=kOutput, calls=%fused_computation.19 | convolution fusion | flops 242099200 | bytes 2419200 | tf_op jit(solution)/shard_map/abt,ot->abo/dot_general | solution.py:77
  555.7 4.2 collective-permute-done.56
  560.1 3.3 copy.264
  563.4 8.1 %convolution_divide_fusion = f32[64,64,64]{2,0,1:T(8,128)S(1)} fusion(f32[78,64,64]{0,2,1:T(8,128)} %copy.264, f32[16,64,64]{2,0,1:T(8,128)S(1)} %copy-done.9, f32[16,64,64]{2,0,1:T(8,128)} %select_select_fusion.4, f32[16,64,64]{2,0,1:T(8,128)} %get-tuple-element.52, f32[16,64,64]{2,0,1:T(8,128)} %slice.427, f32[64,78]{1,0:T(8,128)S(1)} %copy-done.12), kind=kOutput, calls=%fused_computation.36 | convolution fusion | flops 246415360 | bytes 3395072 | tf_op jit(solution)/shard_map/ot,tab->oab/dot_general | solution.py:74
  571.5 2.9 collective-permute-start.57
  578.3 4.4 collective-permute-done.58
  585.2 3.4 fusion.102
  595.1 3.3 collective-permute-done.59
  615.6 13.1 %collective-permute-done.63 = f32[64,2,2,4,64]{4,3,0,2,1:T(4,128)S(1)} collective-permute-done((f32[64,2,2,4,64]{4,3,0,2,1:T(4,128)S(1)}, f32[64,2,2,4,64]{4,3,0,2,1:T(4,128)S(1)}, u32[]{:S(2)}, u32[]{:S(2)}) %collective-permute-start.63) | collective-permute-done | bytes 262176 | tf_op jit(solution)/shard_map/ppermute | solution.py:150
  629.0 3.7 collective-permute-start.64
  632.7 5.8 collective-permute-done.64
  638.6 4.7 collective-permute-start.65
  643.3 4.9 collective-permute-done.65
  662.5 2.9 collective-permute-start.69
  669.5 2.8 collective-permute-done.70
  (299 shorter events, 214.7 us)
Async XLA Ops:
  1.5 6.5 collective-permute-start.1
  23.9 34.3 %collective-permute-start.25 = (f32[16,64,64]{2,0,1:T(8,128)}, f32[16,64,64]{2,0,1:T(8,128)S(1)}, u32[]{:S(2)}, u32[]{:S(2)}) collective-permute-start(f32[16,64,64]{2,0,1:T(8,128)} %get-tuple-element.59), channel_id=1, source_target_pairs={{0,128},{64,192},{128,0},{192,64},{16,144},{80,208},{144,16},{208,... | collective-permute-start | bytes 786440 | tf_op jit(solution)/shard_map/ppermute | solution.py:46
  25.9 32.3 %collective-permute-start.26 = (f32[16,64,64]{2,0,1:T(8,128)}, f32[16,64,64]{2,0,1:T(8,128)S(1)}, u32[]{:S(2)}, u32[]{:S(2)}) collective-permute-start(f32[16,64,64]{2,0,1:T(8,128)} %get-tuple-element.60), channel_id=1, source_target_pairs={{0,64},{64,128},{128,192},{192,0},{16,80},{80,144},{144,208},{208,... | collective-permute-start | bytes 786440 | tf_op jit(solution)/shard_map/ppermute | solution.py:46
  25.9 33.6 %collective-permute-start.24 = (f32[16,64,64]{2,0,1:T(8,128)}, f32[16,64,64]{2,0,1:T(8,128)}, u32[]{:S(2)}, u32[]{:S(2)}) collective-permute-start(f32[16,64,64]{2,0,1:T(8,128)} %get-tuple-element.61), channel_id=1, source_target_pairs={{0,192},{64,0},{128,64},{192,128},{16,208},{80,16},{144,80},{208,1... | collective-permute-start | bytes 786440 | tf_op jit(solution)/shard_map/ppermute | solution.py:46
  61.9 23.1 %collective-permute-start.29 = (f32[16,64,64]{2,0,1:T(8,128)}, f32[16,64,64]{2,0,1:T(8,128)}, u32[]{:S(2)}, u32[]{:S(2)}) collective-permute-start(f32[16,64,64]{2,0,1:T(8,128)} %get-tuple-element.25), channel_id=1, source_target_pairs={{0,16},{64,80},{128,144},{192,208},{16,32},{80,96},{144,160},{208,... | collective-permute-start | bytes 786440 | tf_op jit(solution)/shard_map/ppermute | solution.py:56
  63.4 21.5 %collective-permute-start.28 = (f32[16,64,64]{2,0,1:T(8,128)}, f32[16,64,64]{2,0,1:T(8,128)}, u32[]{:S(2)}, u32[]{:S(2)}) collective-permute-start(f32[16,64,64]{2,0,1:T(8,128)} %get-tuple-element.26), channel_id=1, source_target_pairs={{0,32},{64,96},{128,160},{192,224},{16,48},{80,112},{144,176},{208... | collective-permute-start | bytes 786440 | tf_op jit(solution)/shard_map/ppermute | solution.py:56
  65.3 23.4 %collective-permute-start.27 = (f32[16,64,64]{2,0,1:T(8,128)}, f32[16,64,64]{2,0,1:T(8,128)}, u32[]{:S(2)}, u32[]{:S(2)}) collective-permute-start(f32[16,64,64]{2,0,1:T(8,128)} %get-tuple-element.27), channel_id=1, source_target_pairs={{0,48},{64,112},{128,176},{192,240},{16,0},{80,64},{144,128},{208,... | collective-permute-start | bytes 786440 | tf_op jit(solution)/shard_map/ppermute | solution.py:56
  72.1 46.7 %collective-permute-start.13 = (f32[16,64,64]{2,0,1:T(8,128)}, f32[16,64,64]{2,0,1:T(8,128)S(1)}, u32[]{:S(2)}, u32[]{:S(2)}) collective-permute-start(f32[16,64,64]{2,0,1:T(8,128)} %get-tuple-element.57), channel_id=1, source_target_pairs={{0,128},{64,192},{128,0},{192,64},{16,144},{80,208},{144,16},{208,... | collective-permute-start | bytes 786440 | tf_op jit(solution)/shard_map/ppermute | solution.py:46
  83.3 35.5 %collective-permute-start.12 = (f32[16,64,64]{2,0,1:T(8,128)}, f32[16,64,64]{2,0,1:T(8,128)S(1)}, u32[]{:S(2)}, u32[]{:S(2)}) collective-permute-start(f32[16,64,64]{2,0,1:T(8,128)} %get-tuple-element.63), channel_id=1, source_target_pairs={{0,192},{64,0},{128,64},{192,128},{16,208},{80,16},{144,80},{208,1... | collective-permute-start | bytes 786440 | tf_op jit(solution)/shard_map/ppermute | solution.py:46
  90.9 27.9 %collective-permute-start.14 = (f32[16,64,64]{2,0,1:T(8,128)S(1)}, f32[16,64,64]{2,0,1:T(8,128)S(1)}, u32[]{:S(2)}, u32[]{:S(2)}) collective-permute-start(f32[16,64,64]{2,0,1:T(8,128)S(1)} %get-tuple-element.55), channel_id=1, source_target_pairs={{0,64},{64,128},{128,192},{192,0},{16,80},{80,144},{144,208},{208,... | collective-permute-start | bytes 786440 | tf_op jit(solution)/shard_map/ppermute | solution.py:46
  120.9 15.1 %collective-permute-start.17 = (f32[16,64,64]{2,0,1:T(8,128)}, f32[16,64,64]{2,0,1:T(8,128)S(1)}, u32[]{:S(2)}, u32[]{:S(2)}) collective-permute-start(f32[16,64,64]{2,0,1:T(8,128)} %get-tuple-element.19), channel_id=1, source_target_pairs={{0,16},{64,80},{128,144},{192,208},{16,32},{80,96},{144,160},{208,... | collective-permute-start | bytes 786440 | tf_op jit(solution)/shard_map/ppermute | solution.py:56
  121.0 16.7 %collective-permute-start.16 = (f32[16,64,64]{2,0,1:T(8,128)}, f32[16,64,64]{2,0,1:T(8,128)}, u32[]{:S(2)}, u32[]{:S(2)}) collective-permute-start(f32[16,64,64]{2,0,1:T(8,128)} %get-tuple-element.20), channel_id=1, source_target_pairs={{0,32},{64,96},{128,160},{192,224},{16,48},{80,112},{144,176},{208... | collective-permute-start | bytes 786440 | tf_op jit(solution)/shard_map/ppermute | solution.py:56
  123.9 21.9 %collective-permute-start.15 = (f32[16,64,64]{2,0,1:T(8,128)}, f32[16,64,64]{2,0,1:T(8,128)}, u32[]{:S(2)}, u32[]{:S(2)}) collective-permute-start(f32[16,64,64]{2,0,1:T(8,128)} %get-tuple-element.21), channel_id=1, source_target_pairs={{0,48},{64,112},{128,176},{192,240},{16,0},{80,64},{144,128},{208,... | collective-permute-start | bytes 786440 | tf_op jit(solution)/shard_map/ppermute | solution.py:56
  151.3 17.8 %collective-permute-start.8 = (f32[20,64,64]{2,1,0:T(8,128)}, f32[20,64,64]{2,1,0:T(8,128)S(1)}, u32[]{:S(2)}, u32[]{:S(2)}) collective-permute-start(f32[20,64,64]{2,1,0:T(8,128)} %copy.209), channel_id=1, source_target_pairs={{0,16},{16,32},{32,48},{48,0},{64,80},{80,96},{96,112},{112,64},{1... | collective-permute-start | bytes 983048 | tf_op jit(solution)/shard_map/ppermute | solution.py:46
  151.9 19.5 %collective-permute-start.7 = (f32[20,64,64]{2,1,0:T(8,128)}, f32[20,64,64]{2,1,0:T(8,128)}, u32[]{:S(2)}, u32[]{:S(2)}) collective-permute-start(f32[20,64,64]{2,1,0:T(8,128)} %copy.208), channel_id=1, source_target_pairs={{0,32},{16,48},{32,0},{48,16},{64,96},{80,112},{96,64},{112,80},{1... | collective-permute-start | bytes 983048 | tf_op jit(solution)/shard_map/ppermute | solution.py:46
  154.9 28.9 %collective-permute-start.6 = (f32[20,64,64]{2,1,0:T(8,128)}, f32[20,64,64]{2,1,0:T(8,128)}, u32[]{:S(2)}, u32[]{:S(2)}) collective-permute-start(f32[20,64,64]{2,1,0:T(8,128)} %copy.207), channel_id=1, source_target_pairs={{0,48},{16,0},{32,16},{48,32},{64,112},{80,64},{96,80},{112,96},{1... | collective-permute-start | bytes 983048 | tf_op jit(solution)/shard_map/ppermute | solution.py:46
  187.5 28.7 %collective-permute-start.9 = (f32[20,64,64]{2,1,0:T(8,128)}, f32[20,64,64]{2,1,0:T(8,128)}, u32[]{:S(2)}, u32[]{:S(2)}) collective-permute-start(f32[20,64,64]{2,1,0:T(8,128)} %copy.213), channel_id=1, source_target_pairs={{0,192},{16,208},{32,224},{48,240},{64,0},{80,16},{96,32},{112,48}... | collective-permute-start | bytes 983048 | tf_op jit(solution)/shard_map/ppermute | solution.py:56
  205.2 51.3 %collective-permute-start.10 = (f32[20,64,64]{2,1,0:T(8,128)}, f32[20,64,64]{2,1,0:T(8,128)}, u32[]{:S(2)}, u32[]{:S(2)}) collective-permute-start(f32[20,64,64]{2,1,0:T(8,128)} %copy.217), channel_id=1, source_target_pairs={{0,128},{16,144},{32,160},{48,176},{64,192},{80,208},{96,224},{112... | collective-permute-start | bytes 983048 | tf_op jit(solution)/shard_map/ppermute | solution.py:56
  205.2 51.3 %collective-permute-start.11 = (f32[20,64,64]{2,1,0:T(8,128)}, f32[20,64,64]{2,1,0:T(8,128)}, u32[]{:S(2)}, u32[]{:S(2)}) collective-permute-start(f32[20,64,64]{2,1,0:T(8,128)} %copy.221), channel_id=1, source_target_pairs={{0,64},{16,80},{32,96},{48,112},{64,128},{80,144},{96,160},{112,17... | collective-permute-start | bytes 983048 | tf_op jit(solution)/shard_map/ppermute | solution.py:56
  262.6 12.1 %collective-permute-start.30 = (f32[64,4,64]{2,1,0:T(4,128)S(1)}, f32[64,4,64]{2,1,0:T(4,128)S(1)}, u32[]{:S(2)}, u32[]{:S(2)}) collective-permute-start(f32[64,4,64]{2,1,0:T(4,128)S(1)} %bitcast.244), channel_id=1, source_target_pairs={{0,2},{1,3},{2,0},{3,1},{4,6},{5,7},{6,4},{7,5},{8,10},{9,11},{10,... | collective-permute-start | bytes 196616 | tf_op jit(solution)/shard_map/ppermute | solution.py:160
  274.9 8.2 %collective-permute-start.31 = (f32[64,2,4,64]{3,2,0,1:T(4,128)S(1)}, f32[64,2,4,64]{3,2,0,1:T(4,128)}, u32[]{:S(2)}, u32[]{:S(2)}) collective-permute-start(f32[64,2,4,64]{3,2,0,1:T(4,128)S(1)} %pad_maximum_fusion.14), channel_id=1, source_target_pairs={{0,8},{1,9},{2,10},{3,11},{4,12},{5,13},{6,14},{7,15},{8,0},{9,1},... | collective-permute-start | bytes 393224 | tf_op jit(solution)/shard_map/ppermute | solution.py:160
  285.1 22.6 %collective-permute-start.32 = (f32[64,2,2,4,64]{4,3,0,2,1:T(4,128)}, f32[64,2,2,4,64]{4,3,0,2,1:T(4,128)}, u32[]{:S(2)}, u32[]{:S(2)}) collective-permute-start(f32[64,2,2,4,64]{4,3,0,2,1:T(4,128)} %pad_maximum_fusion.12), channel_id=1, source_target_pairs={{0,4},{1,5},{2,6},{3,7},{4,0},{5,1},{6,2},{7,3},{8,12},{9,13},{10,... | collective-permute-start | bytes 786440 | tf_op jit(solution)/shard_map/ppermute | solution.py:160
  302.6 13.5 %collective-permute-start.20 = (f32[16,64,64]{2,0,1:T(8,128)}, f32[16,64,64]{2,0,1:T(8,128)S(1)}, u32[]{:S(2)}, u32[]{:S(2)}) collective-permute-start(f32[16,64,64]{2,0,1:T(8,128)} %get-tuple-element.58), channel_id=1, source_target_pairs={{0,16},{16,32},{32,48},{48,0},{64,80},{80,96},{96,112},{112,64},{1... | collective-permute-start | bytes 786440 | tf_op jit(solution)/shard_map/ppermute | solution.py:46
  303.4 15.4 %collective-permute-start.18 = (f32[16,64,64]{2,0,1:T(8,128)}, f32[16,64,64]{2,0,1:T(8,128)S(1)}, u32[]{:S(2)}, u32[]{:S(2)}) collective-permute-start(f32[16,64,64]{2,0,1:T(8,128)} %get-tuple-element.62), channel_id=1, source_target_pairs={{0,48},{16,0},{32,16},{48,32},{64,112},{80,64},{96,80},{112,96},{1... | collective-permute-start | bytes 786440 | tf_op jit(solution)/shard_map/ppermute | solution.py:46
  304.7 19.7 %collective-permute-start.19 = (f32[16,64,64]{2,0,1:T(8,128)}, f32[16,64,64]{2,0,1:T(8,128)S(1)}, u32[]{:S(2)}, u32[]{:S(2)}) collective-permute-start(f32[16,64,64]{2,0,1:T(8,128)} %get-tuple-element.53), channel_id=1, source_target_pairs={{0,32},{16,48},{32,0},{48,16},{64,96},{80,112},{96,64},{112,80},{1... | collective-permute-start | bytes 786440 | tf_op jit(solution)/shard_map/ppermute | solution.py:46
  309.3 29.5 %collective-permute-start.33 = (f32[64,2,2,2,4,64]{5,4,0,3,1,2:T(4,128)S(1)}, f32[64,2,2,2,4,64]{5,4,0,3,1,2:T(4,128)S(1)}, u32[]{:S(2)}, u32[]{:S(2)}) collective-permute-start(f32[64,2,2,2,4,64]{5,4,0,3,1,2:T(4,128)S(1)} %pad_maximum_fusion.9), channel_id=1, source_target_pairs={{0,1},{1,0},{2,3},{3,2},{4,5},{5,4},{6,7},{7,6},{8,9},{9,8},{10,11... | collective-permute-start | bytes 1572872 | tf_op jit(solution)/shard_map/ppermute | solution.py:160
  325.9 58.0 %collective-permute-start.23 = (f32[16,64,64]{2,0,1:T(8,128)}, f32[16,64,64]{2,0,1:T(8,128)}, u32[]{:S(2)}, u32[]{:S(2)}) collective-permute-start(f32[16,64,64]{2,0,1:T(8,128)} %get-tuple-element.22), channel_id=1, source_target_pairs={{0,64},{16,80},{32,96},{48,112},{64,128},{80,144},{96,160},{112,17... | collective-permute-start | bytes 786440 | tf_op jit(solution)/shard_map/ppermute | solution.py:56
  330.6 53.3 %collective-permute-start.22 = (f32[16,64,64]{2,0,1:T(8,128)}, f32[16,64,64]{2,0,1:T(8,128)}, u32[]{:S(2)}, u32[]{:S(2)}) collective-permute-start(f32[16,64,64]{2,0,1:T(8,128)} %get-tuple-element.23), channel_id=1, source_target_pairs={{0,128},{16,144},{32,160},{48,176},{64,192},{80,208},{96,224},{112... | collective-permute-start | bytes 786440 | tf_op jit(solution)/shard_map/ppermute | solution.py:56
  335.4 48.5 %collective-permute-start.21 = (f32[16,64,64]{2,0,1:T(8,128)}, f32[16,64,64]{2,0,1:T(8,128)}, u32[]{:S(2)}, u32[]{:S(2)}) collective-permute-start(f32[16,64,64]{2,0,1:T(8,128)} %get-tuple-element.24), channel_id=1, source_target_pairs={{0,192},{16,208},{32,224},{48,240},{64,0},{80,16},{96,32},{112,48}... | collective-permute-start | bytes 786440 | tf_op jit(solution)/shard_map/ppermute | solution.py:56
  351.5 11.2 %collective-permute-start.36 = (f32[64,64,3]{1,0,2:T(8,128)S(1)}, f32[64,64,3]{1,0,2:T(8,128)S(1)}, u32[]{:S(2)}, u32[]{:S(2)}) collective-permute-start(f32[64,64,3]{1,0,2:T(8,128)S(1)} %broadcast_select_fusion.35), channel_id=1, source_target_pairs={{0,16},{16,0},{32,48},{48,32},{64,80},{80,64},{96,112},{112,96},{1... | collective-permute-start | bytes 147464 | tf_op jit(solution)/shard_map/ppermute | solution.py:104
  353.2 6.3 collective-permute-start.34
  359.4 8.0 %collective-permute-start.35 = (f32[64,3,64]{2,1,0:T(4,128)}, f32[64,3,64]{2,1,0:T(4,128)}, u32[]{:S(2)}, u32[]{:S(2)}) collective-permute-start(f32[64,3,64]{2,1,0:T(4,128)} %slice_select_fusion.13), channel_id=1, source_target_pairs={{0,48},{16,32},{32,16},{48,0},{64,112},{80,96},{96,80},{112,64},{1... | collective-permute-start | bytes 147464 | tf_op jit(solution)/shard_map/ppermute | solution.py:104
  381.0 6.0 collective-permute-start.37
  382.3 8.0 %collective-permute-start.38 = (f32[7,64,64]{1,2,0:T(8,128)S(1)}, f32[7,64,64]{1,2,0:T(8,128)S(1)}, u32[]{:S(2)}, u32[]{:S(2)}) collective-permute-start(f32[7,64,64]{1,2,0:T(8,128)S(1)} %get-tuple-element.65), channel_id=1, source_target_pairs={{64,0},{80,16},{96,32},{112,48},{128,64},{144,80},{160,96},{176,11... | collective-permute-start | bytes 344072 | tf_op jit(solution)/shard_map/ppermute | solution.py:126
  402.0 6.1 collective-permute-start.39
  404.2 8.3 %collective-permute-start.40 = (f32[7,64,64]{2,0,1:T(8,128)S(1)}, f32[7,64,64]{2,0,1:T(8,128)S(1)}, u32[]{:S(2)}, u32[]{:S(2)}) collective-permute-start(f32[7,64,64]{2,0,1:T(8,128)S(1)} %get-tuple-element.51), channel_id=1, source_target_pairs={{64,0},{80,16},{96,32},{112,48},{128,64},{144,80},{160,96},{176,11... | collective-permute-start | bytes 344072 | tf_op jit(solution)/shard_map/ppermute | solution.py:126
  420.1 8.8 %collective-permute-start.43 = (f32[64,64,3]{1,0,2:T(8,128)S(1)}, f32[64,64,3]{1,0,2:T(8,128)S(1)}, u32[]{:S(2)}, u32[]{:S(2)}) collective-permute-start(f32[64,64,3]{1,0,2:T(8,128)S(1)} %broadcast_select_fusion.34), channel_id=1, source_target_pairs={{0,16},{16,0},{32,48},{48,32},{64,80},{80,64},{96,112},{112,96},{1... | collective-permute-start | bytes 147464 | tf_op jit(solution)/shard_map/ppermute | solution.py:104
  420.9 6.2 collective-permute-start.41
  423.2 6.6 collective-permute-start.42
  443.4 14.1 %collective-permute-start.45 = (f32[64,2,2,4,64]{4,3,0,2,1:T(4,128)S(1)}, f32[64,2,2,4,64]{4,3,0,2,1:T(4,128)S(1)}, u32[]{:S(2)}, u32[]{:S(2)}) collective-permute-start(f32[64,2,2,4,64]{4,3,0,2,1:T(4,128)S(1)} %select_bitcast_fusion.9), channel_id=1, source_target_pairs={{0,4},{1,5},{2,6},{3,7},{4,0},{5,1},{6,2},{7,3},{8,12},{9,13},{10,... | collective-permute-start | bytes 786440 | tf_op jit(solution)/shard_map/ppermute | solution.py:150
  457.7 9.1 %collective-permute-start.46 = (f32[64,2,4,64]{3,2,0,1:T(4,128)S(1)}, f32[64,2,4,64]{3,2,0,1:T(4,128)S(1)}, u32[]{:S(2)}, u32[]{:S(2)}) collective-permute-start(f32[64,2,4,64]{3,2,0,1:T(4,128)S(1)} %select_bitcast_fusion.15), channel_id=1, source_target_pairs={{0,8},{1,9},{2,10},{3,11},{4,12},{5,13},{6,14},{7,15},{8,0},{9,1},... | collective-permute-start | bytes 393224 | tf_op jit(solution)/shard_map/ppermute | solution.py:150
  467.0 10.6 %collective-permute-start.47 = (f32[64,4,64]{2,1,0:T(4,128)S(1)}, f32[64,4,64]{2,1,0:T(4,128)S(1)}, u32[]{:S(2)}, u32[]{:S(2)}) collective-permute-start(f32[64,4,64]{2,1,0:T(4,128)S(1)} %select_bitcast_fusion.22), channel_id=1, source_target_pairs={{0,2},{1,3},{2,0},{3,1},{4,6},{5,7},{6,4},{7,5},{8,10},{9,11},{10,... | collective-permute-start | bytes 196616 | tf_op jit(solution)/shard_map/ppermute | solution.py:150
  478.4 9.9 %collective-permute-start.48 = (f32[64,4,64]{2,1,0:T(4,128)S(1)}, f32[64,4,64]{2,1,0:T(4,128)S(1)}, u32[]{:S(2)}, u32[]{:S(2)}) collective-permute-start(f32[64,4,64]{2,1,0:T(4,128)S(1)} %fusion.33), channel_id=1, source_target_pairs={{0,2},{1,3},{2,0},{3,1},{4,6},{5,7},{6,4},{7,5},{8,10},{9,11},{10,... | collective-permute-start | bytes 196616 | tf_op jit(solution)/shard_map/ppermute | solution.py:160
  488.4 9.4 %collective-permute-start.49 = (f32[64,2,4,64]{3,2,0,1:T(4,128)S(1)}, f32[64,2,4,64]{3,2,0,1:T(4,128)S(1)}, u32[]{:S(2)}, u32[]{:S(2)}) collective-permute-start(f32[64,2,4,64]{3,2,0,1:T(4,128)S(1)} %pad_maximum_fusion.15), channel_id=1, source_target_pairs={{0,8},{1,9},{2,10},{3,11},{4,12},{5,13},{6,14},{7,15},{8,0},{9,1},... | collective-permute-start | bytes 393224 | tf_op jit(solution)/shard_map/ppermute | solution.py:160
  498.1 9.3 %collective-permute-start.50 = (f32[64,2,2,4,64]{4,3,0,2,1:T(4,128)S(1)}, f32[64,2,2,4,64]{4,3,0,2,1:T(4,128)S(1)}, u32[]{:S(2)}, u32[]{:S(2)}) collective-permute-start(f32[64,2,2,4,64]{4,3,0,2,1:T(4,128)S(1)} %pad_maximum_fusion.13), channel_id=1, source_target_pairs={{0,4},{1,5},{2,6},{3,7},{4,0},{5,1},{6,2},{7,3},{8,12},{9,13},{10,... | collective-permute-start | bytes 786440 | tf_op jit(solution)/shard_map/ppermute | solution.py:160
  523.0 10.4 %collective-permute-start.54 = (f32[64,64,3]{1,0,2:T(8,128)S(1)}, f32[64,64,3]{1,0,2:T(8,128)S(1)}, u32[]{:S(2)}, u32[]{:S(2)}) collective-permute-start(f32[64,64,3]{1,0,2:T(8,128)S(1)} %broadcast_select_fusion.33), channel_id=1, source_target_pairs={{0,16},{16,0},{32,48},{48,32},{64,80},{80,64},{96,112},{112,96},{1... | collective-permute-start | bytes 147464 | tf_op jit(solution)/shard_map/ppermute | solution.py:104
  525.5 6.2 collective-permute-start.52
  527.1 11.0 %collective-permute-start.53 = (f32[64,3,64]{2,1,0:T(4,128)S(1)}, f32[64,3,64]{2,1,0:T(4,128)S(1)}, u32[]{:S(2)}, u32[]{:S(2)}) collective-permute-start(f32[64,3,64]{2,1,0:T(4,128)S(1)} %slice_select_fusion.12), channel_id=1, source_target_pairs={{0,48},{16,32},{32,16},{48,0},{64,112},{80,96},{96,80},{112,64},{1... | collective-permute-start | bytes 147464 | tf_op jit(solution)/shard_map/ppermute | solution.py:104
  550.1 5.6 collective-permute-start.55
  551.9 7.9 %collective-permute-start.56 = (f32[7,64,64]{1,2,0:T(8,128)S(1)}, f32[7,64,64]{1,2,0:T(8,128)S(1)}, u32[]{:S(2)}, u32[]{:S(2)}) collective-permute-start(f32[7,64,64]{1,2,0:T(8,128)S(1)} %get-tuple-element.39), channel_id=1, source_target_pairs={{64,0},{80,16},{96,32},{112,48},{128,64},{144,80},{160,96},{176,11... | collective-permute-start | bytes 344072 | tf_op jit(solution)/shard_map/ppermute | solution.py:126
  571.5 6.7 %collective-permute-start.57 = (f32[7,64,64]{2,0,1:T(8,128)S(1)}, f32[7,64,64]{2,0,1:T(8,128)S(1)}, u32[]{:S(2)}, u32[]{:S(2)}) collective-permute-start(f32[7,64,64]{2,0,1:T(8,128)S(1)} %get-tuple-element.36), channel_id=1, source_target_pairs={{0,64},{16,80},{32,96},{48,112},{64,128},{80,144},{96,160},{112,17... | collective-permute-start | bytes 344072 | tf_op jit(solution)/shard_map/ppermute | solution.py:125
  574.4 8.3 %collective-permute-start.58 = (f32[7,64,64]{2,0,1:T(8,128)S(1)}, f32[7,64,64]{2,0,1:T(8,128)S(1)}, u32[]{:S(2)}, u32[]{:S(2)}) collective-permute-start(f32[7,64,64]{2,0,1:T(8,128)S(1)} %get-tuple-element.37), channel_id=1, source_target_pairs={{64,0},{80,16},{96,32},{112,48},{128,64},{144,80},{160,96},{176,11... | collective-permute-start | bytes 344072 | tf_op jit(solution)/shard_map/ppermute | solution.py:126
  590.3 9.9 %collective-permute-start.61 = (f32[64,64,3]{1,0,2:T(8,128)S(1)}, f32[64,64,3]{1,0,2:T(8,128)S(1)}, u32[]{:S(2)}, u32[]{:S(2)}) collective-permute-start(f32[64,64,3]{1,0,2:T(8,128)S(1)} %broadcast_select_fusion.32), channel_id=1, source_target_pairs={{0,16},{16,0},{32,48},{48,32},{64,80},{80,64},{96,112},{112,96},{1... | collective-permute-start | bytes 147464 | tf_op jit(solution)/shard_map/ppermute | solution.py:104
  592.2 6.3 collective-permute-start.59
  594.1 7.0 %collective-permute-start.60 = (f32[64,3,64]{2,1,0:T(4,128)S(1)}, f32[64,3,64]{2,1,0:T(4,128)S(1)}, u32[]{:S(2)}, u32[]{:S(2)}) collective-permute-start(f32[64,3,64]{2,1,0:T(4,128)S(1)} %broadcast_select_fusion.14), channel_id=1, source_target_pairs={{0,48},{16,32},{32,16},{48,0},{64,112},{80,96},{96,80},{112,64},{1... | collective-permute-start | bytes 147464 | tf_op jit(solution)/shard_map/ppermute | solution.py:104
  614.7 14.1 %collective-permute-start.63 = (f32[64,2,2,4,64]{4,3,0,2,1:T(4,128)S(1)}, f32[64,2,2,4,64]{4,3,0,2,1:T(4,128)S(1)}, u32[]{:S(2)}, u32[]{:S(2)}) collective-permute-start(f32[64,2,2,4,64]{4,3,0,2,1:T(4,128)S(1)} %select_bitcast_fusion.6), channel_id=1, source_target_pairs={{0,4},{1,5},{2,6},{3,7},{4,0},{5,1},{6,2},{7,3},{8,12},{9,13},{10,... | collective-permute-start | bytes 786440 | tf_op jit(solution)/shard_map/ppermute | solution.py:150
  629.0 9.5 %collective-permute-start.64 = (f32[64,2,4,64]{3,2,0,1:T(4,128)S(1)}, f32[64,2,4,64]{3,2,0,1:T(4,128)S(1)}, u32[]{:S(2)}, u32[]{:S(2)}) collective-permute-start(f32[64,2,4,64]{3,2,0,1:T(4,128)S(1)} %select_bitcast_fusion.12), channel_id=1, source_target_pairs={{0,8},{1,9},{2,10},{3,11},{4,12},{5,13},{6,14},{7,15},{8,0},{9,1},... | collective-permute-start | bytes 393224 | tf_op jit(solution)/shard_map/ppermute | solution.py:150
  638.6 9.6 %collective-permute-start.65 = (f32[64,4,64]{2,1,0:T(4,128)S(1)}, f32[64,4,64]{2,1,0:T(4,128)S(1)}, u32[]{:S(2)}, u32[]{:S(2)}) collective-permute-start(f32[64,4,64]{2,1,0:T(4,128)S(1)} %select_bitcast_fusion.19), channel_id=1, source_target_pairs={{0,2},{1,3},{2,0},{3,1},{4,6},{5,7},{6,4},{7,5},{8,10},{9,11},{10,... | collective-permute-start | bytes 196616 | tf_op jit(solution)/shard_map/ppermute | solution.py:150
  648.9 12.5 %collective-permute-start.68 = (f32[64,4,64]{2,1,0:T(4,128)S(1)}, f32[64,4,64]{2,1,0:T(4,128)S(1)}, u32[]{:S(2)}, u32[]{:S(2)}) collective-permute-start(f32[64,4,64]{2,1,0:T(4,128)S(1)} %get-tuple-element.17), channel_id=1, source_target_pairs={{0,16},{16,32},{32,48},{48,0},{64,80},{80,96},{96,112},{112,64},{1... | collective-permute-start | bytes 196616 | tf_op jit(solution)/shard_map/ppermute | solution.py:46
  651.0 10.4 %collective-permute-start.67 = (f32[64,4,64]{2,1,0:T(4,128)S(1)}, f32[64,4,64]{2,1,0:T(4,128)S(1)}, u32[]{:S(2)}, u32[]{:S(2)}) collective-permute-start(f32[64,4,64]{2,1,0:T(4,128)S(1)} %get-tuple-element.96), channel_id=1, source_target_pairs={{0,32},{16,48},{32,0},{48,16},{64,96},{80,112},{96,64},{112,80},{1... | collective-permute-start | bytes 196616 | tf_op jit(solution)/shard_map/ppermute | solution.py:46
  653.4 8.0 %collective-permute-start.66 = (f32[64,4,64]{2,1,0:T(4,128)S(1)}, f32[64,4,64]{2,1,0:T(4,128)S(1)}, u32[]{:S(2)}, u32[]{:S(2)}) collective-permute-start(f32[64,4,64]{2,1,0:T(4,128)S(1)} %get-tuple-element.97), channel_id=1, source_target_pairs={{0,48},{16,0},{32,16},{48,32},{64,112},{80,64},{96,80},{112,96},{1... | collective-permute-start | bytes 196616 | tf_op jit(solution)/shard_map/ppermute | solution.py:46
  661.5 8.0 %collective-permute-start.71 = (f32[64,4,64]{2,1,0:T(4,128)S(1)}, f32[64,4,64]{2,1,0:T(4,128)S(1)}, u32[]{:S(2)}, u32[]{:S(2)}) collective-permute-start(f32[64,4,64]{2,1,0:T(4,128)S(1)} %get-tuple-element.77), channel_id=1, source_target_pairs={{0,64},{16,80},{32,96},{48,112},{64,128},{80,144},{96,160},{112,17... | collective-permute-start | bytes 196616 | tf_op jit(solution)/shard_map/ppermute | solution.py:56
  661.9 10.4 %collective-permute-start.70 = (f32[64,4,64]{2,1,0:T(4,128)S(1)}, f32[64,4,64]{2,1,0:T(4,128)S(1)}, u32[]{:S(2)}, u32[]{:S(2)}) collective-permute-start(f32[64,4,64]{2,1,0:T(4,128)S(1)} %get-tuple-element.78), channel_id=1, source_target_pairs={{0,128},{16,144},{32,160},{48,176},{64,192},{80,208},{96,224},{112... | collective-permute-start | bytes 196616 | tf_op jit(solution)/shard_map/ppermute | solution.py:56
  662.5 9.7 %collective-permute-start.69 = (f32[64,4,64]{2,1,0:T(4,128)S(1)}, f32[64,4,64]{2,1,0:T(4,128)S(1)}, u32[]{:S(2)}, u32[]{:S(2)}) collective-permute-start(f32[64,4,64]{2,1,0:T(4,128)S(1)} %get-tuple-element.79), channel_id=1, source_target_pairs={{0,192},{16,208},{32,224},{48,240},{64,0},{80,16},{96,32},{112,48}... | collective-permute-start | bytes 196616 | tf_op jit(solution)/shard_map/ppermute | solution.py:56
  (24 other events, 148.3 us)
